TPU v7x, 32 devices: a whole 2x2x4 slice. The times are simulated.
32 devices in a mesh: gx: 4 (over x, core), gy: 8 (over z, y).
Axes of the slice: x: 2, y: 2, z: 4, core: 2. Of those that a mesh axis runs over, the one named last changes fastest.
Arguments:
- forcing: float32 [16, 16, 2, 4096], P('gx', 'gy'), may hold values from -6 to 6
- initial: float32 [16, 16, 2, 4096], P('gx', 'gy'), may hold values from -6 to 6
- blocks: float32 [16, 16, 2, 4096], P('gx', 'gy'), as said below
- face_blocks: float32 [6, 64, 64], replicated, may hold values from -0.75 to 0.75
- strength: float32 [6, 16, 16, 2], P(None, 'gx', 'gy'), may hold values from 0.2 to 2
- strong: int32 [6, 16, 16, 2], P(None, 'gx', 'gy'), may hold values 0 or 1
- colour: int32 [16, 16, 2], P('gx', 'gy'), may hold values from 0 to 1, as said below
- neighbours: int32 [6, 16, 16, 2], P(None, 'gx', 'gy'), may hold values from 2 to 48, as said below
Outputs:
- smoothed: float32 [16, 16, 2, 4096], P('gx', 'gy')
Inputs may be any that keep to these rules, and one draw needn't show every extreme that they name: Elements of a column along z are stored in an order drawn per column. colour is (global x index + global y index + physical position along z + one flip common to all elements) mod 2, so elements that share a face differ in colour and every column holds one element of each colour. `neighbours`: Slots of the four corner columns are never named. `blocks`: each block is symmetric, and each diagonal entry exceeds the sum of the magnitudes of the other entries of its row by 0.5 or more.
All inputs are finite; a program needn't handle non-finite values. No bound on the sum of `strong` on one device may be relied on, other than what follows from the above.
Results may differ from a plain program's by a relative error of at most 0.00011.
Values sent between devices are 32-bit elements; how exact they have to be, the bound alone decides.
No kernel may reach another device: no remote copies, remote signals or barrier semaphores. Data moves between devices by JAX's collectives and lax.ppermute only.
A program may use at most 64 MiB of HBM per device.

v0:
```python
import functools

import jax
import jax.numpy as jnp
from jax import lax
from jax.experimental import pallas as pl
from jax.experimental.pallas import tpu as pltpu
from jax.sharding import PartitionSpec as P

P_SIZE = 64
R = 64
SWEEPS = 4


def padded(block, sides, width):
    for axis, dim in sides:
        count = lax.axis_size(axis)
        forward = [(i, i + 1) for i in range(count - 1)]
        backward = [(target, source) for source, target in forward]
        low = lax.ppermute(
            lax.slice_in_dim(block, block.shape[dim] - width, None, axis=dim), axis, forward
        )
        high = lax.ppermute(lax.slice_in_dim(block, 0, width, axis=dim), axis, backward)
        block = jnp.concatenate([low, block, high], axis=dim)
    return block


def _gauss_jordan_kernel(a_ref, o_ref, *, n, nb):
    lanes = n * nb
    tiles = lanes // 128
    o_ref[...] = a_ref[...]
    lane_t = lax.broadcasted_iota(jnp.int32, (n, 128), 1)
    lane_r = lax.broadcasted_iota(jnp.int32, (1, 128), 1)
    row_i = lax.broadcasted_iota(jnp.int32, (n, 128), 0)

    def spread(x):
        shift = nb
        while shift < 128:
            x = x + pltpu.roll(x, shift, 1)
            shift *= 2
        return x

    def step(k, carry):
        start = k * nb
        tile = start // 128
        off = start % 128
        tile_start = pl.multiple_of(tile * 128, 128)
        column = spread(
            jnp.where((lane_t >= off) & (lane_t < off + nb), o_ref[:, pl.ds(tile_start, 128)], 0.0)
        )
        pivot = jnp.sum(jnp.where(row_i == k, column, 0.0), axis=0, keepdims=True)
        base = pl.multiple_of((k // 8) * 8, 8)
        band = o_ref[pl.ds(base, 8), :]
        band_i = lax.broadcasted_iota(jnp.int32, band.shape, 0)
        row = jnp.sum(jnp.where(band_i == k - base, band, 0.0), axis=0, keepdims=True)
        for t in range(tiles):
            in_col = (t == tile) & (lane_r >= off) & (lane_r < off + nb)
            scaled = jnp.where(in_col, 1.0 / pivot, row[:, t * 128:(t + 1) * 128] / pivot)
            kept = jnp.where(in_col, 0.0, o_ref[:, t * 128:(t + 1) * 128])
            o_ref[:, t * 128:(t + 1) * 128] = jnp.where(row_i == k, scaled, kept - column * scaled)
        return carry

    lax.fori_loop(0, n, step, 0)


def block_inverses(matrices):
    nb, n, _ = matrices.shape
    if 128 % nb or (n * nb) % 128:
        lower_factor = jnp.linalg.cholesky(matrices)
        identity = jnp.broadcast_to(jnp.eye(n, dtype=matrices.dtype), matrices.shape)
        solved = jax.scipy.linalg.solve_triangular(lower_factor, identity, lower=True)
        return jnp.einsum("eqp,eqr->epr", solved, solved, precision=lax.Precision.HIGHEST)
    packed = jnp.transpose(matrices, (1, 2, 0)).reshape(n, n * nb)
    inverted = pl.pallas_call(
        functools.partial(_gauss_jordan_kernel, n=n, nb=nb),
        out_shape=jax.ShapeDtypeStruct((n, n * nb), jnp.float32),
        in_specs=[pl.BlockSpec(memory_space=pltpu.VMEM)],
        out_specs=pl.BlockSpec(memory_space=pltpu.VMEM),
    )(packed)
    return jnp.transpose(inverted.reshape(n, n, nb), (2, 0, 1))


def shifted(values, halo, dim, lower):
    width = values.shape[dim]
    if lower:
        return jnp.concatenate([halo, lax.slice_in_dim(values, 0, width - 1, axis=dim)], axis=dim)
    return jnp.concatenate([lax.slice_in_dim(values, 1, width, axis=dim), halo], axis=dim)


def exchange(values, axis, dim):
    count = lax.axis_size(axis)
    forward = [(i, i + 1) for i in range(count - 1)]
    backward = [(target, source) for source, target in forward]
    width = values.shape[dim]
    from_lower = lax.ppermute(lax.slice_in_dim(values, width - 1, width, axis=dim), axis, forward)
    from_upper = lax.ppermute(lax.slice_in_dim(values, 0, 1, axis=dim), axis, backward)
    return from_lower, from_upper


def body(forcing, initial, blocks, face_blocks, strength, strong, colour, neighbours):
    span_x, span_y, span_z, width = forcing.shape
    count = span_x * span_y * span_z
    columns = span_x * span_y
    empty_slot = (span_x + 2) * (span_y + 2) * span_z
    inverse = block_inverses(blocks.reshape(count, P_SIZE, P_SIZE)).reshape(
        span_x, span_y, span_z, P_SIZE, P_SIZE
    )
    weight = jnp.where(neighbours == empty_slot, 0.0, strength * strong.astype(jnp.float32))
    first_is = [colour[:, :, 0] == paint for paint in (0, 1)]

    def pick(values, paint, axis=2):
        lead = (1,) * (axis - 2)
        mask = first_is[paint].reshape(lead + first_is[paint].shape + (1,) * (values.ndim - axis - 1))
        low = lax.index_in_dim(values, 0, axis=axis, keepdims=False)
        high = lax.index_in_dim(values, 1, axis=axis, keepdims=False)
        return jnp.where(mask, low, high)

    member_inverse = [pick(inverse, paint).reshape(columns, P_SIZE, P_SIZE) for paint in (0, 1)]
    member_target = [pick(forcing, paint).reshape(columns, P_SIZE, R) for paint in (0, 1)]
    member_weight = [pick(weight, paint, axis=3)[..., None] for paint in (0, 1)]
    state = [pick(initial, 0), pick(initial, 1)]
    for sweep_index in range(SWEEPS):
        for paint_now in (0, 1):
            other = state[1 - paint_now]
            low_x, high_x = exchange(other, "gx", 0)
            low_y, high_y = exchange(other, "gy", 1)
            nearby = jnp.stack(
                [
                    shifted(other, low_x, 0, True),
                    shifted(other, high_x, 0, False),
                    shifted(other, low_y, 1, True),
                    shifted(other, high_y, 1, False),
                    other,
                    other,
                ]
            )
            nearby = (nearby * member_weight[paint_now]).reshape(6, columns, P_SIZE, R)
            coupled = jnp.einsum(
                "fpq,feqr->epr", face_blocks, nearby, precision=lax.Precision.HIGHEST
            )
            update = jnp.einsum(
                "epq,eqr->epr",
                member_inverse[paint_now],
                member_target[paint_now] - coupled,
                precision=lax.Precision.HIGHEST,
            )
            state[paint_now] = update.reshape(span_x, span_y, width)
    first = first_is[0][..., None]
    return jnp.stack(
        [jnp.where(first, state[0], state[1]), jnp.where(first, state[1], state[0])], axis=2
    )


def _half_sweep_kernel(
    other_ref, lo_x_ref, hi_x_ref, lo_y_ref, hi_y_ref, face_ref, weight_ref, inverse_ref,
    target_ref, out_ref, send_lo_x_ref, send_hi_x_ref, send_lo_y_ref, send_hi_y_ref, *, span_x
):
    tile = 2 * R
    highest = lax.Precision.HIGHEST
    other = other_ref[...]
    lanes = other.shape[1]
    lane = lax.broadcasted_iota(jnp.int32, (P_SIZE, tile), 1)
    low_half = lane < R
    tiles = [other[:, t * tile:(t + 1) * tile] for t in range(span_x)]
    lo_y = lo_y_ref[...]
    hi_y = hi_y_ref[...]

    def y_block(packed, x):
        held = packed[:, (x // 2) * tile:(x // 2 + 1) * tile]
        return held if x % 2 == 0 else pltpu.roll(held, R, 1)

    below, above = [], []
    for x in range(span_x):
        rolled = pltpu.roll(tiles[x], R, 1)
        below.append(jnp.where(low_half, y_block(lo_y, x), rolled))
        above.append(jnp.where(low_half, rolled, pltpu.roll(y_block(hi_y, x), R, 1)))
    nearby = [
        jnp.concatenate([lo_x_ref[...], other[:, :lanes - tile]], axis=1),
        jnp.concatenate([other[:, tile:], hi_x_ref[...]], axis=1),
        jnp.concatenate(below, axis=1),
        jnp.concatenate(above, axis=1),
        other,
        other,
    ]
    coupled = jnp.zeros_like(other)
    for face in range(6):
        product = jnp.dot(
            face_ref[face], nearby[face], precision=highest, preferred_element_type=jnp.float32
        )
        coupled = coupled + weight_ref[face] * product
    rhs = target_ref[...] - coupled
    outs = []
    for x in range(span_x):
        part = rhs[:, x * tile:(x + 1) * tile]
        first = jnp.dot(inverse_ref[2 * x], part, precision=highest, preferred_element_type=jnp.float32)
        second = jnp.dot(
            inverse_ref[2 * x + 1], part, precision=highest, preferred_element_type=jnp.float32
        )
        outs.append(jnp.where(low_half, first, second))
    out_ref[...] = jnp.concatenate(outs, axis=1)
    send_lo_x_ref[...] = outs[-1]
    send_hi_x_ref[...] = outs[0]
    for t in range(span_x // 2):
        even, odd = outs[2 * t], outs[2 * t + 1]
        send_lo_y_ref[:, t * tile:(t + 1) * tile] = jnp.where(low_half, pltpu.roll(even, R, 1), odd)
        send_hi_y_ref[:, t * tile:(t + 1) * tile] = jnp.where(low_half, even, pltpu.roll(odd, R, 1))


def half_sweep(other, halos, face_blocks, weight, inverse, target, span_x):
    lanes = other.shape[1]
    x_shape = jax.ShapeDtypeStruct((P_SIZE, 2 * R), jnp.float32)
    y_shape = jax.ShapeDtypeStruct((P_SIZE, span_x * R), jnp.float32)
    vmem = pl.BlockSpec(memory_space=pltpu.VMEM)
    return pl.pallas_call(
        functools.partial(_half_sweep_kernel, span_x=span_x),
        out_shape=(jax.ShapeDtypeStruct((P_SIZE, lanes), jnp.float32), x_shape, x_shape, y_shape, y_shape),
        in_specs=[vmem] * 9,
        out_specs=(vmem,) * 5,
    )(other, *halos, face_blocks, weight, inverse, target)


def send_buffers(state, span_x):
    blocks = state.reshape(P_SIZE, span_x, 2, R)
    return (
        blocks[:, -1].reshape(P_SIZE, 2 * R),
        blocks[:, 0].reshape(P_SIZE, 2 * R),
        blocks[:, :, 1].reshape(P_SIZE, span_x * R),
        blocks[:, :, 0].reshape(P_SIZE, span_x * R),
    )


def trade(sends):
    lo_x, hi_x = (
        lax.ppermute(sends[0], "gx", shift_pairs("gx", 1)),
        lax.ppermute(sends[1], "gx", shift_pairs("gx", -1)),
    )
    lo_y, hi_y = (
        lax.ppermute(sends[2], "gy", shift_pairs("gy", 1)),
        lax.ppermute(sends[3], "gy", shift_pairs("gy", -1)),
    )
    return lo_x, hi_x, lo_y, hi_y


def shift_pairs(axis, step):
    count = lax.axis_size(axis)
    return [(i, i + step) for i in range(count) if 0 <= i + step < count]


def lane_body(forcing, initial, blocks, face_blocks, strength, strong, colour, neighbours):
    span_x, span_y, span_z, width = forcing.shape
    count = span_x * span_y * span_z
    columns = span_x * span_y
    empty_slot = (span_x + 2) * (span_y + 2) * span_z
    inverse = block_inverses(blocks.reshape(count, P_SIZE, P_SIZE)).reshape(
        span_x, span_y, span_z, P_SIZE, P_SIZE
    )
    weight = jnp.where(neighbours == empty_slot, 0.0, strength * strong.astype(jnp.float32))
    first_is = [colour[:, :, 0] == paint for paint in (0, 1)]

    def pick(values, paint, axis=2):
        lead = (1,) * (axis - 2)
        mask = first_is[paint].reshape(lead + first_is[paint].shape + (1,) * (values.ndim - axis - 1))
        low = lax.index_in_dim(values, 0, axis=axis, keepdims=False)
        high = lax.index_in_dim(values, 1, axis=axis, keepdims=False)
        return jnp.where(mask, low, high)

    def to_lanes(values):
        return jnp.transpose(values.reshape(columns, P_SIZE, R), (1, 0, 2)).reshape(P_SIZE, columns * R)

    member_inverse = [pick(inverse, paint).reshape(columns, P_SIZE, P_SIZE) for paint in (0, 1)]
    member_target = [to_lanes(pick(forcing, paint)) for paint in (0, 1)]
    member_weight = [
        jnp.repeat(pick(weight, paint, axis=3).reshape(6, columns), R, axis=1).reshape(6, 1, columns * R)
        for paint in (0, 1)
    ]
    state = [None, to_lanes(pick(initial, 1))]
    sends = send_buffers(state[1], span_x)
    for sweep_index in range(SWEEPS):
        for paint_now in (0, 1):
            halos = trade(sends)
            state[paint_now], *sends = half_sweep(
                state[1 - paint_now],
                halos,
                face_blocks,
                member_weight[paint_now],
                member_inverse[paint_now],
                member_target[paint_now],
                span_x,
            )
    first = first_is[0][..., None]
    whole = [
        jnp.transpose(part.reshape(P_SIZE, columns, R), (1, 0, 2)).reshape(span_x, span_y, width)
        for part in state
    ]
    return jnp.stack(
        [jnp.where(first, whole[0], whole[1]), jnp.where(first, whole[1], whole[0])], axis=2
    )


def dispatch(forcing, *rest):
    span_x, span_y, span_z, width = forcing.shape
    if span_y == 2 and span_z == 2 and span_x % 2 == 0 and width == P_SIZE * R:
        return lane_body(forcing, *rest)
    return body(forcing, *rest)


def solution(mesh):
    in_specs = (
        P("gx", "gy", None, None),
        P("gx", "gy", None, None),
        P("gx", "gy", None, None),
        P(),
        P(None, "gx", "gy", None),
        P(None, "gx", "gy", None),
        P("gx", "gy", None),
        P(None, "gx", "gy", None),
    )
    out_specs = P("gx", "gy", None, None)
    return jax.shard_map(dispatch, mesh=mesh, in_specs=in_specs, out_specs=out_specs, check_vma=False)
```

profile of v0, /device:TPU:9, one launch (start us, length us, event | category | flops | bytes accessed | tf_op | source)
XLA Modules:
  0.0 179.3 jit_solution(14758513786846156898)
XLA Ops:
  1.1 1.3 reshape.134
  2.7 0.9 copy.52.a_ref
  3.6 19.2 %shard_map.82 = f32[64,1024]{1,0:T(8,128)} custom-call(f32[64,1024]{1,0:T(8,128)} %copy.52.a_ref), custom_call_target="tpu_custom_call" | custom-call | tf_op jit(solution)/shard_map/pallas_call | solution.py:74
  22.7 1.1 copy.53
  24.2 0.9 copy-done
  25.1 0.8 slice_reduce_fusion.2
  26.3 0.7 copy-done.1
  27.1 0.8 slice_reduce_fusion
  28.3 0.9 bitcast_select_fusion
  29.4 3.1 %collective-permute-start.2 = (f32[64,256]{1,0:T(8,128)S(1)}, f32[64,256]{1,0:T(8,128)S(1)}, u32[]{:S(2)}, u32[]{:S(2)}) collective-permute-start(f32[64,256]{1,0:T(8,128)S(1)} %reshape_squeeze.14), channel_id=1, source_target_pairs={{0,1},{1,2},{2,3},{3,4},{4,5},{5,6},{6,7},{8,9},{9,10},{10,11},{11... | collective-permute-start | bytes 196616 | tf_op jit(solution)/shard_map/ppermute | solution.py:238
  32.8 3.0 %collective-permute-start.3 = (f32[64,256]{1,0:T(8,128)S(1)}, f32[64,256]{1,0:T(8,128)S(1)}, u32[]{:S(2)}, u32[]{:S(2)}) collective-permute-start(f32[64,256]{1,0:T(8,128)S(1)} %reshape_squeeze.15), channel_id=1, source_target_pairs={{1,0},{2,1},{3,2},{4,3},{5,4},{6,5},{7,6},{9,8},{10,9},{11,10},{12... | collective-permute-start | bytes 196616 | tf_op jit(solution)/shard_map/ppermute | solution.py:239
  36.0 4.2 %collective-permute-start = (f32[64,128]{1,0:T(8,128)S(1)}, f32[64,128]{1,0:T(8,128)S(1)}, u32[]{:S(2)}, u32[]{:S(2)}) collective-permute-start(f32[64,128]{1,0:T(8,128)S(1)} %reshape_squeeze.12), channel_id=1, source_target_pairs={{0,8},{8,16},{16,24},{1,9},{9,17},{17,25},{2,10},{10,18},{18,26},{... | collective-permute-start | bytes 98312 | tf_op jit(solution)/shard_map/ppermute | solution.py:234
  40.5 1.9 %collective-permute-start.1 = (f32[64,128]{1,0:T(8,128)S(1)}, f32[64,128]{1,0:T(8,128)S(1)}, u32[]{:S(2)}, u32[]{:S(2)}) collective-permute-start(f32[64,128]{1,0:T(8,128)S(1)} %reshape_squeeze.13), channel_id=1, source_target_pairs={{8,0},{16,8},{24,16},{9,1},{17,9},{25,17},{10,2},{18,10},{26,18},{... | collective-permute-start | bytes 98312 | tf_op jit(solution)/shard_map/ppermute | solution.py:235
  42.7 0.8 reshape.138.target_ref
  43.6 0.8 reshape.133.other_ref
  44.5 0.7 reshape_reshape.10.weight_ref
  46.4 3.1 %shard_map.83 = (f32[64,512]{1,0:T(8,128)}, f32[64,128]{1,0:T(8,128)}, f32[64,128]{1,0:T(8,128)}, f32[64,256]{1,0:T(8,128)}, f32[64,256]{1,0:T(8,128)}) custom-call(f32[64,512]{1,0:T(8,128)} %reshape.133.other_ref, f32[64,128]{1,0:T(8,128)} %copy-done.18, f32[64,128]{1,0:T(8,128)} %copy-done.19, f32[64,256]{1,0:T(8,128)} %copy-done.2, f32[64,256]{1,0:T(8,128)} %copy-done.3, ...), custom_call_target="tpu_custom_call" | custom-call | tf_op jit(solution)/shard_map/pallas_call | solution.py:214
  49.4 2.2 %collective-permute-start.6 = (f32[64,256]{1,0:T(8,128)}, f32[64,256]{1,0:T(8,128)S(1)}, u32[]{:S(2)}, u32[]{:S(2)}) collective-permute-start(f32[64,256]{1,0:T(8,128)} %get-tuple-element.44), channel_id=1, source_target_pairs={{0,1},{1,2},{2,3},{3,4},{4,5},{5,6},{6,7},{8,9},{9,10},{10,11},{11... | collective-permute-start | bytes 196616 | tf_op jit(solution)/shard_map/ppermute | solution.py:238
  51.7 3.9 %collective-permute-start.7 = (f32[64,256]{1,0:T(8,128)}, f32[64,256]{1,0:T(8,128)S(1)}, u32[]{:S(2)}, u32[]{:S(2)}) collective-permute-start(f32[64,256]{1,0:T(8,128)} %get-tuple-element.45), channel_id=1, source_target_pairs={{1,0},{2,1},{3,2},{4,3},{5,4},{6,5},{7,6},{9,8},{10,9},{11,10},{12... | collective-permute-start | bytes 196616 | tf_op jit(solution)/shard_map/ppermute | solution.py:239
  55.6 3.7 %collective-permute-start.4 = (f32[64,128]{1,0:T(8,128)}, f32[64,128]{1,0:T(8,128)S(1)}, u32[]{:S(2)}, u32[]{:S(2)}) collective-permute-start(f32[64,128]{1,0:T(8,128)} %get-tuple-element.42), channel_id=1, source_target_pairs={{0,8},{8,16},{16,24},{1,9},{9,17},{17,25},{2,10},{10,18},{18,26},{... | collective-permute-start | bytes 98312 | tf_op jit(solution)/shard_map/ppermute | solution.py:234
  59.4 1.9 %collective-permute-start.5 = (f32[64,128]{1,0:T(8,128)}, f32[64,128]{1,0:T(8,128)S(1)}, u32[]{:S(2)}, u32[]{:S(2)}) collective-permute-start(f32[64,128]{1,0:T(8,128)} %get-tuple-element.43), channel_id=1, source_target_pairs={{8,0},{16,8},{24,16},{9,1},{17,9},{25,17},{10,2},{18,10},{26,18},{... | collective-permute-start | bytes 98312 | tf_op jit(solution)/shard_map/ppermute | solution.py:235
  61.5 0.8 reshape.139.target_ref
  62.4 0.7 reshape_reshape.11.weight_ref
  63.1 1.8 collective-permute-done.5.hi_x_ref
  65.5 3.1 %shard_map.84 = (f32[64,512]{1,0:T(8,128)}, f32[64,128]{1,0:T(8,128)}, f32[64,128]{1,0:T(8,128)}, f32[64,256]{1,0:T(8,128)}, f32[64,256]{1,0:T(8,128)}) custom-call(f32[64,512]{1,0:T(8,128)} %get-tuple-element.41.other_ref, f32[64,128]{1,0:T(8,128)} %copy-done.20, f32[64,128]{1,0:T(8,128)} %copy-done.21, f32[64,256]{1,0:T(8,128)} %copy-done.4, ...), custom_call_target="tpu_custom_call" | custom-call | tf_op jit(solution)/shard_map/pallas_call | solution.py:214
  68.6 1.9 %collective-permute-start.10 = (f32[64,256]{1,0:T(8,128)}, f32[64,256]{1,0:T(8,128)S(1)}, u32[]{:S(2)}, u32[]{:S(2)}) collective-permute-start(f32[64,256]{1,0:T(8,128)} %get-tuple-element.49), channel_id=1, source_target_pairs={{0,1},{1,2},{2,3},{3,4},{4,5},{5,6},{6,7},{8,9},{9,10},{10,11},{11... | collective-permute-start | bytes 196616 | tf_op jit(solution)/shard_map/ppermute | solution.py:238
  70.5 4.3 %collective-permute-start.11 = (f32[64,256]{1,0:T(8,128)}, f32[64,256]{1,0:T(8,128)S(1)}, u32[]{:S(2)}, u32[]{:S(2)}) collective-permute-start(f32[64,256]{1,0:T(8,128)} %get-tuple-element.50), channel_id=1, source_target_pairs={{1,0},{2,1},{3,2},{4,3},{5,4},{6,5},{7,6},{9,8},{10,9},{11,10},{12... | collective-permute-start | bytes 196616 | tf_op jit(solution)/shard_map/ppermute | solution.py:239
  74.7 2.6 %collective-permute-start.8 = (f32[64,128]{1,0:T(8,128)}, f32[64,128]{1,0:T(8,128)S(1)}, u32[]{:S(2)}, u32[]{:S(2)}) collective-permute-start(f32[64,128]{1,0:T(8,128)} %get-tuple-element.47), channel_id=1, source_target_pairs={{0,8},{8,16},{16,24},{1,9},{9,17},{17,25},{2,10},{10,18},{18,26},{... | collective-permute-start | bytes 98312 | tf_op jit(solution)/shard_map/ppermute | solution.py:234
  77.3 1.9 %collective-permute-start.9 = (f32[64,128]{1,0:T(8,128)}, f32[64,128]{1,0:T(8,128)S(1)}, u32[]{:S(2)}, u32[]{:S(2)}) collective-permute-start(f32[64,128]{1,0:T(8,128)} %get-tuple-element.48), channel_id=1, source_target_pairs={{8,0},{16,8},{24,16},{9,1},{17,9},{25,17},{10,2},{18,10},{26,18},{... | collective-permute-start | bytes 98312 | tf_op jit(solution)/shard_map/ppermute | solution.py:235
  79.3 3.5 %collective-permute-done.9.hi_x_ref = f32[64,128]{1,0:T(8,128)S(1)} collective-permute-done((f32[64,128]{1,0:T(8,128)}, f32[64,128]{1,0:T(8,128)S(1)}, u32[]{:S(2)}, u32[]{:S(2)}) %collective-permute-start.9) | collective-permute-done | bytes 32800 | tf_op jit(solution)/shard_map/ppermute | solution.py:235
  83.4 3.1 %shard_map.85 = (f32[64,512]{1,0:T(8,128)}, f32[64,128]{1,0:T(8,128)}, f32[64,128]{1,0:T(8,128)}, f32[64,256]{1,0:T(8,128)}, f32[64,256]{1,0:T(8,128)}) custom-call(f32[64,512]{1,0:T(8,128)} %get-tuple-element.46.other_ref, f32[64,128]{1,0:T(8,128)} %copy-done.25, f32[64,128]{1,0:T(8,128)} %copy-done.30, f32[64,256]{1,0:T(8,128)} %copy-done.9, ...), custom_call_target="tpu_custom_call" | custom-call | tf_op jit(solution)/shard_map/pallas_call | solution.py:214
  86.5 1.9 %collective-permute-start.14 = (f32[64,256]{1,0:T(8,128)}, f32[64,256]{1,0:T(8,128)S(1)}, u32[]{:S(2)}, u32[]{:S(2)}) collective-permute-start(f32[64,256]{1,0:T(8,128)} %get-tuple-element.54), channel_id=1, source_target_pairs={{0,1},{1,2},{2,3},{3,4},{4,5},{5,6},{6,7},{8,9},{9,10},{10,11},{11... | collective-permute-start | bytes 196616 | tf_op jit(solution)/shard_map/ppermute | solution.py:238
  88.4 4.3 %collective-permute-start.15 = (f32[64,256]{1,0:T(8,128)}, f32[64,256]{1,0:T(8,128)S(1)}, u32[]{:S(2)}, u32[]{:S(2)}) collective-permute-start(f32[64,256]{1,0:T(8,128)} %get-tuple-element.55), channel_id=1, source_target_pairs={{1,0},{2,1},{3,2},{4,3},{5,4},{6,5},{7,6},{9,8},{10,9},{11,10},{12... | collective-permute-start | bytes 196616 | tf_op jit(solution)/shard_map/ppermute | solution.py:239
  92.7 2.6 %collective-permute-start.12 = (f32[64,128]{1,0:T(8,128)}, f32[64,128]{1,0:T(8,128)S(1)}, u32[]{:S(2)}, u32[]{:S(2)}) collective-permute-start(f32[64,128]{1,0:T(8,128)} %get-tuple-element.52), channel_id=1, source_target_pairs={{0,8},{8,16},{16,24},{1,9},{9,17},{17,25},{2,10},{10,18},{18,26},{... | collective-permute-start | bytes 98312 | tf_op jit(solution)/shard_map/ppermute | solution.py:234
  95.3 1.9 %collective-permute-start.13 = (f32[64,128]{1,0:T(8,128)}, f32[64,128]{1,0:T(8,128)S(1)}, u32[]{:S(2)}, u32[]{:S(2)}) collective-permute-start(f32[64,128]{1,0:T(8,128)} %get-tuple-element.53), channel_id=1, source_target_pairs={{8,0},{16,8},{24,16},{9,1},{17,9},{25,17},{10,2},{18,10},{26,18},{... | collective-permute-start | bytes 98312 | tf_op jit(solution)/shard_map/ppermute | solution.py:235
  97.2 3.5 %collective-permute-done.13.hi_x_ref = f32[64,128]{1,0:T(8,128)S(1)} collective-permute-done((f32[64,128]{1,0:T(8,128)}, f32[64,128]{1,0:T(8,128)S(1)}, u32[]{:S(2)}, u32[]{:S(2)}) %collective-permute-start.13) | collective-permute-done | bytes 32800 | tf_op jit(solution)/shard_map/ppermute | solution.py:235
  101.4 3.1 %shard_map.86 = (f32[64,512]{1,0:T(8,128)}, f32[64,128]{1,0:T(8,128)}, f32[64,128]{1,0:T(8,128)}, f32[64,256]{1,0:T(8,128)}, f32[64,256]{1,0:T(8,128)}) custom-call(f32[64,512]{1,0:T(8,128)} %get-tuple-element.51.other_ref, f32[64,128]{1,0:T(8,128)} %copy-done.26, f32[64,128]{1,0:T(8,128)} %copy-done.31, f32[64,256]{1,0:T(8,128)} %copy-done.10, ...), custom_call_target="tpu_custom_call" | custom-call | tf_op jit(solution)/shard_map/pallas_call | solution.py:214
  104.4 1.9 %collective-permute-start.18 = (f32[64,256]{1,0:T(8,128)}, f32[64,256]{1,0:T(8,128)S(1)}, u32[]{:S(2)}, u32[]{:S(2)}) collective-permute-start(f32[64,256]{1,0:T(8,128)} %get-tuple-element.59), channel_id=1, source_target_pairs={{0,1},{1,2},{2,3},{3,4},{4,5},{5,6},{6,7},{8,9},{9,10},{10,11},{11... | collective-permute-start | bytes 196616 | tf_op jit(solution)/shard_map/ppermute | solution.py:238
  106.4 4.3 %collective-permute-start.19 = (f32[64,256]{1,0:T(8,128)}, f32[64,256]{1,0:T(8,128)S(1)}, u32[]{:S(2)}, u32[]{:S(2)}) collective-permute-start(f32[64,256]{1,0:T(8,128)} %get-tuple-element.60), channel_id=1, source_target_pairs={{1,0},{2,1},{3,2},{4,3},{5,4},{6,5},{7,6},{9,8},{10,9},{11,10},{12... | collective-permute-start | bytes 196616 | tf_op jit(solution)/shard_map/ppermute | solution.py:239
  110.6 2.6 %collective-permute-start.16 = (f32[64,128]{1,0:T(8,128)}, f32[64,128]{1,0:T(8,128)S(1)}, u32[]{:S(2)}, u32[]{:S(2)}) collective-permute-start(f32[64,128]{1,0:T(8,128)} %get-tuple-element.57), channel_id=1, source_target_pairs={{0,8},{8,16},{16,24},{1,9},{9,17},{17,25},{2,10},{10,18},{18,26},{... | collective-permute-start | bytes 98312 | tf_op jit(solution)/shard_map/ppermute | solution.py:234
  113.2 2.1 %collective-permute-start.17 = (f32[64,128]{1,0:T(8,128)}, f32[64,128]{1,0:T(8,128)S(1)}, u32[]{:S(2)}, u32[]{:S(2)}) collective-permute-start(f32[64,128]{1,0:T(8,128)} %get-tuple-element.58), channel_id=1, source_target_pairs={{8,0},{16,8},{24,16},{9,1},{17,9},{25,17},{10,2},{18,10},{26,18},{... | collective-permute-start | bytes 98312 | tf_op jit(solution)/shard_map/ppermute | solution.py:235
  115.3 3.3 %collective-permute-done.17.hi_x_ref = f32[64,128]{1,0:T(8,128)S(1)} collective-permute-done((f32[64,128]{1,0:T(8,128)}, f32[64,128]{1,0:T(8,128)S(1)}, u32[]{:S(2)}, u32[]{:S(2)}) %collective-permute-start.17) | collective-permute-done | bytes 32800 | tf_op jit(solution)/shard_map/ppermute | solution.py:235
  119.3 3.1 %shard_map.87 = (f32[64,512]{1,0:T(8,128)}, f32[64,128]{1,0:T(8,128)}, f32[64,128]{1,0:T(8,128)}, f32[64,256]{1,0:T(8,128)}, f32[64,256]{1,0:T(8,128)}) custom-call(f32[64,512]{1,0:T(8,128)} %get-tuple-element.56.other_ref, f32[64,128]{1,0:T(8,128)} %copy-done.27, f32[64,128]{1,0:T(8,128)} %copy-done.32, f32[64,256]{1,0:T(8,128)} %copy-done.11, ...), custom_call_target="tpu_custom_call" | custom-call | tf_op jit(solution)/shard_map/pallas_call | solution.py:214
  122.4 1.9 %collective-permute-start.22 = (f32[64,256]{1,0:T(8,128)}, f32[64,256]{1,0:T(8,128)S(1)}, u32[]{:S(2)}, u32[]{:S(2)}) collective-permute-start(f32[64,256]{1,0:T(8,128)} %get-tuple-element.64), channel_id=1, source_target_pairs={{0,1},{1,2},{2,3},{3,4},{4,5},{5,6},{6,7},{8,9},{9,10},{10,11},{11... | collective-permute-start | bytes 196616 | tf_op jit(solution)/shard_map/ppermute | solution.py:238
  124.3 4.3 %collective-permute-start.23 = (f32[64,256]{1,0:T(8,128)}, f32[64,256]{1,0:T(8,128)S(1)}, u32[]{:S(2)}, u32[]{:S(2)}) collective-permute-start(f32[64,256]{1,0:T(8,128)} %get-tuple-element.65), channel_id=1, source_target_pairs={{1,0},{2,1},{3,2},{4,3},{5,4},{6,5},{7,6},{9,8},{10,9},{11,10},{12... | collective-permute-start | bytes 196616 | tf_op jit(solution)/shard_map/ppermute | solution.py:239
  128.6 2.6 %collective-permute-start.20 = (f32[64,128]{1,0:T(8,128)}, f32[64,128]{1,0:T(8,128)S(1)}, u32[]{:S(2)}, u32[]{:S(2)}) collective-permute-start(f32[64,128]{1,0:T(8,128)} %get-tuple-element.62), channel_id=1, source_target_pairs={{0,8},{8,16},{16,24},{1,9},{9,17},{17,25},{2,10},{10,18},{18,26},{... | collective-permute-start | bytes 98312 | tf_op jit(solution)/shard_map/ppermute | solution.py:234
  131.2 1.9 %collective-permute-start.21 = (f32[64,128]{1,0:T(8,128)}, f32[64,128]{1,0:T(8,128)S(1)}, u32[]{:S(2)}, u32[]{:S(2)}) collective-permute-start(f32[64,128]{1,0:T(8,128)} %get-tuple-element.63), channel_id=1, source_target_pairs={{8,0},{16,8},{24,16},{9,1},{17,9},{25,17},{10,2},{18,10},{26,18},{... | collective-permute-start | bytes 98312 | tf_op jit(solution)/shard_map/ppermute | solution.py:235
  133.1 3.5 %collective-permute-done.21.hi_x_ref = f32[64,128]{1,0:T(8,128)S(1)} collective-permute-done((f32[64,128]{1,0:T(8,128)}, f32[64,128]{1,0:T(8,128)S(1)}, u32[]{:S(2)}, u32[]{:S(2)}) %collective-permute-start.21) | collective-permute-done | bytes 32800 | tf_op jit(solution)/shard_map/ppermute | solution.py:235
  137.3 3.1 %shard_map.88 = (f32[64,512]{1,0:T(8,128)}, f32[64,128]{1,0:T(8,128)}, f32[64,128]{1,0:T(8,128)}, f32[64,256]{1,0:T(8,128)}, f32[64,256]{1,0:T(8,128)}) custom-call(f32[64,512]{1,0:T(8,128)} %get-tuple-element.61.other_ref, f32[64,128]{1,0:T(8,128)} %copy-done.28, f32[64,128]{1,0:T(8,128)} %copy-done.33, f32[64,256]{1,0:T(8,128)} %copy-done.12, ...), custom_call_target="tpu_custom_call" | custom-call | tf_op jit(solution)/shard_map/pallas_call | solution.py:214
  140.3 1.9 %collective-permute-start.26 = (f32[64,256]{1,0:T(8,128)}, f32[64,256]{1,0:T(8,128)S(1)}, u32[]{:S(2)}, u32[]{:S(2)}) collective-permute-start(f32[64,256]{1,0:T(8,128)} %get-tuple-element.69), channel_id=1, source_target_pairs={{0,1},{1,2},{2,3},{3,4},{4,5},{5,6},{6,7},{8,9},{9,10},{10,11},{11... | collective-permute-start | bytes 196616 | tf_op jit(solution)/shard_map/ppermute | solution.py:238
  142.3 4.3 %collective-permute-start.27 = (f32[64,256]{1,0:T(8,128)}, f32[64,256]{1,0:T(8,128)S(1)}, u32[]{:S(2)}, u32[]{:S(2)}) collective-permute-start(f32[64,256]{1,0:T(8,128)} %get-tuple-element.70), channel_id=1, source_target_pairs={{1,0},{2,1},{3,2},{4,3},{5,4},{6,5},{7,6},{9,8},{10,9},{11,10},{12... | collective-permute-start | bytes 196616 | tf_op jit(solution)/shard_map/ppermute | solution.py:239
  146.5 2.6 %collective-permute-start.24 = (f32[64,128]{1,0:T(8,128)}, f32[64,128]{1,0:T(8,128)S(1)}, u32[]{:S(2)}, u32[]{:S(2)}) collective-permute-start(f32[64,128]{1,0:T(8,128)} %get-tuple-element.67), channel_id=1, source_target_pairs={{0,8},{8,16},{16,24},{1,9},{9,17},{17,25},{2,10},{10,18},{18,26},{... | collective-permute-start | bytes 98312 | tf_op jit(solution)/shard_map/ppermute | solution.py:234
  149.1 1.9 %collective-permute-start.25 = (f32[64,128]{1,0:T(8,128)}, f32[64,128]{1,0:T(8,128)S(1)}, u32[]{:S(2)}, u32[]{:S(2)}) collective-permute-start(f32[64,128]{1,0:T(8,128)} %get-tuple-element.68), channel_id=1, source_target_pairs={{8,0},{16,8},{24,16},{9,1},{17,9},{25,17},{10,2},{18,10},{26,18},{... | collective-permute-start | bytes 98312 | tf_op jit(solution)/shard_map/ppermute | solution.py:235
  151.1 3.5 %collective-permute-done.25.hi_x_ref = f32[64,128]{1,0:T(8,128)S(1)} collective-permute-done((f32[64,128]{1,0:T(8,128)}, f32[64,128]{1,0:T(8,128)S(1)}, u32[]{:S(2)}, u32[]{:S(2)}) %collective-permute-start.25) | collective-permute-done | bytes 32800 | tf_op jit(solution)/shard_map/ppermute | solution.py:235
  155.2 3.1 %shard_map.89 = (f32[64,512]{1,0:T(8,128)}, f32[64,128]{1,0:T(8,128)}, f32[64,128]{1,0:T(8,128)}, f32[64,256]{1,0:T(8,128)}, f32[64,256]{1,0:T(8,128)}) custom-call(f32[64,512]{1,0:T(8,128)} %get-tuple-element.66.other_ref, f32[64,128]{1,0:T(8,128)} %copy-done.24, f32[64,128]{1,0:T(8,128)} %copy-done.29, f32[64,256]{1,0:T(8,128)} %copy-done.8, ...), custom_call_target="tpu_custom_call" | custom-call | tf_op jit(solution)/shard_map/pallas_call | solution.py:214
  158.3 1.9 %collective-permute-start.30 = (f32[64,256]{1,0:T(8,128)}, f32[64,256]{1,0:T(8,128)S(1)}, u32[]{:S(2)}, u32[]{:S(2)}) collective-permute-start(f32[64,256]{1,0:T(8,128)} %get-tuple-element.74), channel_id=1, source_target_pairs={{0,1},{1,2},{2,3},{3,4},{4,5},{5,6},{6,7},{8,9},{9,10},{10,11},{11... | collective-permute-start | bytes 196616 | tf_op jit(solution)/shard_map/ppermute | solution.py:238
  160.2 4.3 %collective-permute-start.31 = (f32[64,256]{1,0:T(8,128)}, f32[64,256]{1,0:T(8,128)S(1)}, u32[]{:S(2)}, u32[]{:S(2)}) collective-permute-start(f32[64,256]{1,0:T(8,128)} %get-tuple-element.75), channel_id=1, source_target_pairs={{1,0},{2,1},{3,2},{4,3},{5,4},{6,5},{7,6},{9,8},{10,9},{11,10},{12... | collective-permute-start | bytes 196616 | tf_op jit(solution)/shard_map/ppermute | solution.py:239
  164.5 2.6 %collective-permute-start.28 = (f32[64,128]{1,0:T(8,128)}, f32[64,128]{1,0:T(8,128)S(1)}, u32[]{:S(2)}, u32[]{:S(2)}) collective-permute-start(f32[64,128]{1,0:T(8,128)} %get-tuple-element.72), channel_id=1, source_target_pairs={{0,8},{8,16},{16,24},{1,9},{9,17},{17,25},{2,10},{10,18},{18,26},{... | collective-permute-start | bytes 98312 | tf_op jit(solution)/shard_map/ppermute | solution.py:234
  167.1 1.9 %collective-permute-start.29 = (f32[64,128]{1,0:T(8,128)}, f32[64,128]{1,0:T(8,128)S(1)}, u32[]{:S(2)}, u32[]{:S(2)}) collective-permute-start(f32[64,128]{1,0:T(8,128)} %get-tuple-element.73), channel_id=1, source_target_pairs={{8,0},{16,8},{24,16},{9,1},{17,9},{25,17},{10,2},{18,10},{26,18},{... | collective-permute-start | bytes 98312 | tf_op jit(solution)/shard_map/ppermute | solution.py:235
  169.0 1.0 reshape.140
  170.2 2.3 %collective-permute-done.29.hi_x_ref = f32[64,128]{1,0:T(8,128)S(1)} collective-permute-done((f32[64,128]{1,0:T(8,128)}, f32[64,128]{1,0:T(8,128)S(1)}, u32[]{:S(2)}, u32[]{:S(2)}) %collective-permute-start.29) | collective-permute-done | bytes 32800 | tf_op jit(solution)/shard_map/ppermute | solution.py:235
  173.8 3.1 %shard_map.90 = (f32[64,512]{1,0:T(8,128)}, f32[64,128]{1,0:T(8,128)}, f32[64,128]{1,0:T(8,128)}, f32[64,256]{1,0:T(8,128)}, f32[64,256]{1,0:T(8,128)}) custom-call(f32[64,512]{1,0:T(8,128)} %get-tuple-element.71.other_ref, f32[64,128]{1,0:T(8,128)} %copy-done.22, f32[64,128]{1,0:T(8,128)} %copy-done.23, f32[64,256]{1,0:T(8,128)} %copy-done.6, ...), custom_call_target="tpu_custom_call" | custom-call | tf_op jit(solution)/shard_map/pallas_call | solution.py:214
  176.9 1.0 reshape.142
  178.4 0.9 copy.60
  (137 shorter events, 11.1 us)
Async XLA Ops:
  0.0 0.7 slice-start
  24.1 1.0 copy-start
  26.1 1.0 copy-start.1
  29.4 16.3 %collective-permute-start.2 = (f32[64,256]{1,0:T(8,128)S(1)}, f32[64,256]{1,0:T(8,128)S(1)}, u32[]{:S(2)}, u32[]{:S(2)}) collective-permute-start(f32[64,256]{1,0:T(8,128)S(1)} %reshape_squeeze.14), channel_id=1, source_target_pairs={{0,1},{1,2},{2,3},{3,4},{4,5},{5,6},{6,7},{8,9},{9,10},{10,11},{11... | collective-permute-start | bytes 196616 | tf_op jit(solution)/shard_map/ppermute | solution.py:238
  32.8 12.9 %collective-permute-start.3 = (f32[64,256]{1,0:T(8,128)S(1)}, f32[64,256]{1,0:T(8,128)S(1)}, u32[]{:S(2)}, u32[]{:S(2)}) collective-permute-start(f32[64,256]{1,0:T(8,128)S(1)} %reshape_squeeze.15), channel_id=1, source_target_pairs={{1,0},{2,1},{3,2},{4,3},{5,4},{6,5},{7,6},{9,8},{10,9},{11,10},{12... | collective-permute-start | bytes 196616 | tf_op jit(solution)/shard_map/ppermute | solution.py:239
  36.0 9.2 %collective-permute-start = (f32[64,128]{1,0:T(8,128)S(1)}, f32[64,128]{1,0:T(8,128)S(1)}, u32[]{:S(2)}, u32[]{:S(2)}) collective-permute-start(f32[64,128]{1,0:T(8,128)S(1)} %reshape_squeeze.12), channel_id=1, source_target_pairs={{0,8},{8,16},{16,24},{1,9},{9,17},{17,25},{2,10},{10,18},{18,26},{... | collective-permute-start | bytes 98312 | tf_op jit(solution)/shard_map/ppermute | solution.py:234
  40.3 2.1 %copy-start.34 = (s32[6,4,2,2]{0,3,2,1:T(2,128)S(1)}, s32[6,4,2,2]{0,3,2,1:T(2,128)}, u32[]{:S(2)}) copy-start(s32[6,4,2,2]{0,3,2,1:T(2,128)} %param.15) | copy-start | bytes 1156
  40.3 2.1 %copy-start.35 = (f32[6,4,2,2]{0,3,2,1:T(2,128)S(1)}, f32[6,4,2,2]{0,3,2,1:T(2,128)}, u32[]{:S(2)}) copy-start(f32[6,4,2,2]{0,3,2,1:T(2,128)} %param.12) | copy-start | bytes 1156
  40.4 2.1 %copy-start.36 = (s32[6,4,2,2]{0,3,2,1:T(2,128)S(1)}, s32[6,4,2,2]{0,3,2,1:T(2,128)}, u32[]{:S(2)}) copy-start(s32[6,4,2,2]{0,3,2,1:T(2,128)} %param.13) | copy-start | bytes 1156
  40.5 5.2 %collective-permute-start.1 = (f32[64,128]{1,0:T(8,128)S(1)}, f32[64,128]{1,0:T(8,128)S(1)}, u32[]{:S(2)}, u32[]{:S(2)}) collective-permute-start(f32[64,128]{1,0:T(8,128)S(1)} %reshape_squeeze.13), channel_id=1, source_target_pairs={{8,0},{16,8},{24,16},{9,1},{17,9},{25,17},{10,2},{18,10},{26,18},{... | collective-permute-start | bytes 98312 | tf_op jit(solution)/shard_map/ppermute | solution.py:235
  45.2 0.6 copy-start.18
  45.7 0.6 copy-start.19
  45.7 0.6 copy-start.2
  45.7 0.6 copy-start.3
  49.4 15.4 %collective-permute-start.6 = (f32[64,256]{1,0:T(8,128)}, f32[64,256]{1,0:T(8,128)S(1)}, u32[]{:S(2)}, u32[]{:S(2)}) collective-permute-start(f32[64,256]{1,0:T(8,128)} %get-tuple-element.44), channel_id=1, source_target_pairs={{0,1},{1,2},{2,3},{3,4},{4,5},{5,6},{6,7},{8,9},{9,10},{10,11},{11... | collective-permute-start | bytes 196616 | tf_op jit(solution)/shard_map/ppermute | solution.py:238
  51.7 13.1 %collective-permute-start.7 = (f32[64,256]{1,0:T(8,128)}, f32[64,256]{1,0:T(8,128)S(1)}, u32[]{:S(2)}, u32[]{:S(2)}) collective-permute-start(f32[64,256]{1,0:T(8,128)} %get-tuple-element.45), channel_id=1, source_target_pairs={{1,0},{2,1},{3,2},{4,3},{5,4},{6,5},{7,6},{9,8},{10,9},{11,10},{12... | collective-permute-start | bytes 196616 | tf_op jit(solution)/shard_map/ppermute | solution.py:239
  55.6 7.4 %collective-permute-start.4 = (f32[64,128]{1,0:T(8,128)}, f32[64,128]{1,0:T(8,128)S(1)}, u32[]{:S(2)}, u32[]{:S(2)}) collective-permute-start(f32[64,128]{1,0:T(8,128)} %get-tuple-element.42), channel_id=1, source_target_pairs={{0,8},{8,16},{16,24},{1,9},{9,17},{17,25},{2,10},{10,18},{18,26},{... | collective-permute-start | bytes 98312 | tf_op jit(solution)/shard_map/ppermute | solution.py:234
  59.4 5.4 %collective-permute-start.5 = (f32[64,128]{1,0:T(8,128)}, f32[64,128]{1,0:T(8,128)S(1)}, u32[]{:S(2)}, u32[]{:S(2)}) collective-permute-start(f32[64,128]{1,0:T(8,128)} %get-tuple-element.43), channel_id=1, source_target_pairs={{8,0},{16,8},{24,16},{9,1},{17,9},{25,17},{10,2},{18,10},{26,18},{... | collective-permute-start | bytes 98312 | tf_op jit(solution)/shard_map/ppermute | solution.py:235
  63.0 1.8 copy-start.20
  64.8 0.6 copy-start.4
  64.8 0.7 copy-start.5
  68.6 14.2 %collective-permute-start.10 = (f32[64,256]{1,0:T(8,128)}, f32[64,256]{1,0:T(8,128)S(1)}, u32[]{:S(2)}, u32[]{:S(2)}) collective-permute-start(f32[64,256]{1,0:T(8,128)} %get-tuple-element.49), channel_id=1, source_target_pairs={{0,1},{1,2},{2,3},{3,4},{4,5},{5,6},{6,7},{8,9},{9,10},{10,11},{11... | collective-permute-start | bytes 196616 | tf_op jit(solution)/shard_map/ppermute | solution.py:238
  70.5 12.3 %collective-permute-start.11 = (f32[64,256]{1,0:T(8,128)}, f32[64,256]{1,0:T(8,128)S(1)}, u32[]{:S(2)}, u32[]{:S(2)}) collective-permute-start(f32[64,256]{1,0:T(8,128)} %get-tuple-element.50), channel_id=1, source_target_pairs={{1,0},{2,1},{3,2},{4,3},{5,4},{6,5},{7,6},{9,8},{10,9},{11,10},{12... | collective-permute-start | bytes 196616 | tf_op jit(solution)/shard_map/ppermute | solution.py:239
  74.7 4.5 %collective-permute-start.8 = (f32[64,128]{1,0:T(8,128)}, f32[64,128]{1,0:T(8,128)S(1)}, u32[]{:S(2)}, u32[]{:S(2)}) collective-permute-start(f32[64,128]{1,0:T(8,128)} %get-tuple-element.47), channel_id=1, source_target_pairs={{0,8},{8,16},{16,24},{1,9},{9,17},{17,25},{2,10},{10,18},{18,26},{... | collective-permute-start | bytes 98312 | tf_op jit(solution)/shard_map/ppermute | solution.py:234
  77.3 5.4 %collective-permute-start.9 = (f32[64,128]{1,0:T(8,128)}, f32[64,128]{1,0:T(8,128)S(1)}, u32[]{:S(2)}, u32[]{:S(2)}) collective-permute-start(f32[64,128]{1,0:T(8,128)} %get-tuple-element.48), channel_id=1, source_target_pairs={{8,0},{16,8},{24,16},{9,1},{17,9},{25,17},{10,2},{18,10},{26,18},{... | collective-permute-start | bytes 98312 | tf_op jit(solution)/shard_map/ppermute | solution.py:235
  79.3 3.5 %copy-start.25 = (f32[64,128]{1,0:T(8,128)}, f32[64,128]{1,0:T(8,128)S(1)}, u32[]{:S(2)}) copy-start(f32[64,128]{1,0:T(8,128)S(1)} %collective-permute-done.8.lo_x_ref) | copy-start | bytes 98308
  82.8 0.6 copy-start.30
  82.8 0.6 copy-start.9
  82.8 0.7 copy-start.14
  86.5 14.2 %collective-permute-start.14 = (f32[64,256]{1,0:T(8,128)}, f32[64,256]{1,0:T(8,128)S(1)}, u32[]{:S(2)}, u32[]{:S(2)}) collective-permute-start(f32[64,256]{1,0:T(8,128)} %get-tuple-element.54), channel_id=1, source_target_pairs={{0,1},{1,2},{2,3},{3,4},{4,5},{5,6},{6,7},{8,9},{9,10},{10,11},{11... | collective-permute-start | bytes 196616 | tf_op jit(solution)/shard_map/ppermute | solution.py:238
  88.4 12.3 %collective-permute-start.15 = (f32[64,256]{1,0:T(8,128)}, f32[64,256]{1,0:T(8,128)S(1)}, u32[]{:S(2)}, u32[]{:S(2)}) collective-permute-start(f32[64,256]{1,0:T(8,128)} %get-tuple-element.55), channel_id=1, source_target_pairs={{1,0},{2,1},{3,2},{4,3},{5,4},{6,5},{7,6},{9,8},{10,9},{11,10},{12... | collective-permute-start | bytes 196616 | tf_op jit(solution)/shard_map/ppermute | solution.py:239
  92.7 4.5 %collective-permute-start.12 = (f32[64,128]{1,0:T(8,128)}, f32[64,128]{1,0:T(8,128)S(1)}, u32[]{:S(2)}, u32[]{:S(2)}) collective-permute-start(f32[64,128]{1,0:T(8,128)} %get-tuple-element.52), channel_id=1, source_target_pairs={{0,8},{8,16},{16,24},{1,9},{9,17},{17,25},{2,10},{10,18},{18,26},{... | collective-permute-start | bytes 98312 | tf_op jit(solution)/shard_map/ppermute | solution.py:234
  95.3 5.4 %collective-permute-start.13 = (f32[64,128]{1,0:T(8,128)}, f32[64,128]{1,0:T(8,128)S(1)}, u32[]{:S(2)}, u32[]{:S(2)}) collective-permute-start(f32[64,128]{1,0:T(8,128)} %get-tuple-element.53), channel_id=1, source_target_pairs={{8,0},{16,8},{24,16},{9,1},{17,9},{25,17},{10,2},{18,10},{26,18},{... | collective-permute-start | bytes 98312 | tf_op jit(solution)/shard_map/ppermute | solution.py:235
  97.2 3.5 %copy-start.26 = (f32[64,128]{1,0:T(8,128)}, f32[64,128]{1,0:T(8,128)S(1)}, u32[]{:S(2)}) copy-start(f32[64,128]{1,0:T(8,128)S(1)} %collective-permute-done.12.lo_x_ref) | copy-start | bytes 98308
  100.7 0.6 copy-start.10
  100.7 0.7 copy-start.15
  104.4 14.2 %collective-permute-start.18 = (f32[64,256]{1,0:T(8,128)}, f32[64,256]{1,0:T(8,128)S(1)}, u32[]{:S(2)}, u32[]{:S(2)}) collective-permute-start(f32[64,256]{1,0:T(8,128)} %get-tuple-element.59), channel_id=1, source_target_pairs={{0,1},{1,2},{2,3},{3,4},{4,5},{5,6},{6,7},{8,9},{9,10},{10,11},{11... | collective-permute-start | bytes 196616 | tf_op jit(solution)/shard_map/ppermute | solution.py:238
  106.4 12.3 %collective-permute-start.19 = (f32[64,256]{1,0:T(8,128)}, f32[64,256]{1,0:T(8,128)S(1)}, u32[]{:S(2)}, u32[]{:S(2)}) collective-permute-start(f32[64,256]{1,0:T(8,128)} %get-tuple-element.60), channel_id=1, source_target_pairs={{1,0},{2,1},{3,2},{4,3},{5,4},{6,5},{7,6},{9,8},{10,9},{11,10},{12... | collective-permute-start | bytes 196616 | tf_op jit(solution)/shard_map/ppermute | solution.py:239
  110.6 4.7 %collective-permute-start.16 = (f32[64,128]{1,0:T(8,128)}, f32[64,128]{1,0:T(8,128)S(1)}, u32[]{:S(2)}, u32[]{:S(2)}) collective-permute-start(f32[64,128]{1,0:T(8,128)} %get-tuple-element.57), channel_id=1, source_target_pairs={{0,8},{8,16},{16,24},{1,9},{9,17},{17,25},{2,10},{10,18},{18,26},{... | collective-permute-start | bytes 98312 | tf_op jit(solution)/shard_map/ppermute | solution.py:234
  113.2 5.4 %collective-permute-start.17 = (f32[64,128]{1,0:T(8,128)}, f32[64,128]{1,0:T(8,128)S(1)}, u32[]{:S(2)}, u32[]{:S(2)}) collective-permute-start(f32[64,128]{1,0:T(8,128)} %get-tuple-element.58), channel_id=1, source_target_pairs={{8,0},{16,8},{24,16},{9,1},{17,9},{25,17},{10,2},{18,10},{26,18},{... | collective-permute-start | bytes 98312 | tf_op jit(solution)/shard_map/ppermute | solution.py:235
  115.3 3.4 %copy-start.27 = (f32[64,128]{1,0:T(8,128)}, f32[64,128]{1,0:T(8,128)S(1)}, u32[]{:S(2)}) copy-start(f32[64,128]{1,0:T(8,128)S(1)} %collective-permute-done.16.lo_x_ref) | copy-start | bytes 98308
  118.7 0.6 copy-start.11
  118.7 0.7 copy-start.16
  122.4 14.2 %collective-permute-start.22 = (f32[64,256]{1,0:T(8,128)}, f32[64,256]{1,0:T(8,128)S(1)}, u32[]{:S(2)}, u32[]{:S(2)}) collective-permute-start(f32[64,256]{1,0:T(8,128)} %get-tuple-element.64), channel_id=1, source_target_pairs={{0,1},{1,2},{2,3},{3,4},{4,5},{5,6},{6,7},{8,9},{9,10},{10,11},{11... | collective-permute-start | bytes 196616 | tf_op jit(solution)/shard_map/ppermute | solution.py:238
  124.3 12.3 %collective-permute-start.23 = (f32[64,256]{1,0:T(8,128)}, f32[64,256]{1,0:T(8,128)S(1)}, u32[]{:S(2)}, u32[]{:S(2)}) collective-permute-start(f32[64,256]{1,0:T(8,128)} %get-tuple-element.65), channel_id=1, source_target_pairs={{1,0},{2,1},{3,2},{4,3},{5,4},{6,5},{7,6},{9,8},{10,9},{11,10},{12... | collective-permute-start | bytes 196616 | tf_op jit(solution)/shard_map/ppermute | solution.py:239
  128.6 4.5 %collective-permute-start.20 = (f32[64,128]{1,0:T(8,128)}, f32[64,128]{1,0:T(8,128)S(1)}, u32[]{:S(2)}, u32[]{:S(2)}) collective-permute-start(f32[64,128]{1,0:T(8,128)} %get-tuple-element.62), channel_id=1, source_target_pairs={{0,8},{8,16},{16,24},{1,9},{9,17},{17,25},{2,10},{10,18},{18,26},{... | collective-permute-start | bytes 98312 | tf_op jit(solution)/shard_map/ppermute | solution.py:234
  131.2 5.4 %collective-permute-start.21 = (f32[64,128]{1,0:T(8,128)}, f32[64,128]{1,0:T(8,128)S(1)}, u32[]{:S(2)}, u32[]{:S(2)}) collective-permute-start(f32[64,128]{1,0:T(8,128)} %get-tuple-element.63), channel_id=1, source_target_pairs={{8,0},{16,8},{24,16},{9,1},{17,9},{25,17},{10,2},{18,10},{26,18},{... | collective-permute-start | bytes 98312 | tf_op jit(solution)/shard_map/ppermute | solution.py:235
  133.1 3.5 %copy-start.28 = (f32[64,128]{1,0:T(8,128)}, f32[64,128]{1,0:T(8,128)S(1)}, u32[]{:S(2)}) copy-start(f32[64,128]{1,0:T(8,128)S(1)} %collective-permute-done.20.lo_x_ref) | copy-start | bytes 98308
  136.6 0.6 copy-start.12
  136.6 0.7 copy-start.17
  140.3 14.2 %collective-permute-start.26 = (f32[64,256]{1,0:T(8,128)}, f32[64,256]{1,0:T(8,128)S(1)}, u32[]{:S(2)}, u32[]{:S(2)}) collective-permute-start(f32[64,256]{1,0:T(8,128)} %get-tuple-element.69), channel_id=1, source_target_pairs={{0,1},{1,2},{2,3},{3,4},{4,5},{5,6},{6,7},{8,9},{9,10},{10,11},{11... | collective-permute-start | bytes 196616 | tf_op jit(solution)/shard_map/ppermute | solution.py:238
  142.3 12.3 %collective-permute-start.27 = (f32[64,256]{1,0:T(8,128)}, f32[64,256]{1,0:T(8,128)S(1)}, u32[]{:S(2)}, u32[]{:S(2)}) collective-permute-start(f32[64,256]{1,0:T(8,128)} %get-tuple-element.70), channel_id=1, source_target_pairs={{1,0},{2,1},{3,2},{4,3},{5,4},{6,5},{7,6},{9,8},{10,9},{11,10},{12... | collective-permute-start | bytes 196616 | tf_op jit(solution)/shard_map/ppermute | solution.py:239
  146.5 4.5 %collective-permute-start.24 = (f32[64,128]{1,0:T(8,128)}, f32[64,128]{1,0:T(8,128)S(1)}, u32[]{:S(2)}, u32[]{:S(2)}) collective-permute-start(f32[64,128]{1,0:T(8,128)} %get-tuple-element.67), channel_id=1, source_target_pairs={{0,8},{8,16},{16,24},{1,9},{9,17},{17,25},{2,10},{10,18},{18,26},{... | collective-permute-start | bytes 98312 | tf_op jit(solution)/shard_map/ppermute | solution.py:234
  149.1 5.4 %collective-permute-start.25 = (f32[64,128]{1,0:T(8,128)}, f32[64,128]{1,0:T(8,128)S(1)}, u32[]{:S(2)}, u32[]{:S(2)}) collective-permute-start(f32[64,128]{1,0:T(8,128)} %get-tuple-element.68), channel_id=1, source_target_pairs={{8,0},{16,8},{24,16},{9,1},{17,9},{25,17},{10,2},{18,10},{26,18},{... | collective-permute-start | bytes 98312 | tf_op jit(solution)/shard_map/ppermute | solution.py:235
  151.1 3.5 %copy-start.24 = (f32[64,128]{1,0:T(8,128)}, f32[64,128]{1,0:T(8,128)S(1)}, u32[]{:S(2)}) copy-start(f32[64,128]{1,0:T(8,128)S(1)} %collective-permute-done.24.lo_x_ref) | copy-start | bytes 98308
  154.6 0.6 copy-start.8
  154.6 0.7 copy-start.13
  158.3 14.2 %collective-permute-start.30 = (f32[64,256]{1,0:T(8,128)}, f32[64,256]{1,0:T(8,128)S(1)}, u32[]{:S(2)}, u32[]{:S(2)}) collective-permute-start(f32[64,256]{1,0:T(8,128)} %get-tuple-element.74), channel_id=1, source_target_pairs={{0,1},{1,2},{2,3},{3,4},{4,5},{5,6},{6,7},{8,9},{9,10},{10,11},{11... | collective-permute-start | bytes 196616 | tf_op jit(solution)/shard_map/ppermute | solution.py:238
  160.2 12.3 %collective-permute-start.31 = (f32[64,256]{1,0:T(8,128)}, f32[64,256]{1,0:T(8,128)S(1)}, u32[]{:S(2)}, u32[]{:S(2)}) collective-permute-start(f32[64,256]{1,0:T(8,128)} %get-tuple-element.75), channel_id=1, source_target_pairs={{1,0},{2,1},{3,2},{4,3},{5,4},{6,5},{7,6},{9,8},{10,9},{11,10},{12... | collective-permute-start | bytes 196616 | tf_op jit(solution)/shard_map/ppermute | solution.py:239
  164.5 5.7 %collective-permute-start.28 = (f32[64,128]{1,0:T(8,128)}, f32[64,128]{1,0:T(8,128)S(1)}, u32[]{:S(2)}, u32[]{:S(2)}) collective-permute-start(f32[64,128]{1,0:T(8,128)} %get-tuple-element.72), channel_id=1, source_target_pairs={{0,8},{8,16},{16,24},{1,9},{9,17},{17,25},{2,10},{10,18},{18,26},{... | collective-permute-start | bytes 98312 | tf_op jit(solution)/shard_map/ppermute | solution.py:234
  167.1 5.4 %collective-permute-start.29 = (f32[64,128]{1,0:T(8,128)}, f32[64,128]{1,0:T(8,128)S(1)}, u32[]{:S(2)}, u32[]{:S(2)}) collective-permute-start(f32[64,128]{1,0:T(8,128)} %get-tuple-element.73), channel_id=1, source_target_pairs={{8,0},{16,8},{24,16},{9,1},{17,9},{25,17},{10,2},{18,10},{26,18},{... | collective-permute-start | bytes 98312 | tf_op jit(solution)/shard_map/ppermute | solution.py:235
  170.2 2.3 %copy-start.22 = (f32[64,128]{1,0:T(8,128)}, f32[64,128]{1,0:T(8,128)S(1)}, u32[]{:S(2)}) copy-start(f32[64,128]{1,0:T(8,128)S(1)} %collective-permute-done.28.lo_x_ref) | copy-start | bytes 98308
  172.5 0.6 copy-start.6
  173.1 0.6 copy-start.7
  (6 other events, 3.6 us)
where the time goes:
time: 181 us; the launch traced here: 179 us
  starting transfers between devices  88.3 us (49%)
  Pallas kernels  43.8 us (24%)
  local copies, waits for them, and re-layouts  23.3 us (13%)
  waiting for transfers between devices  21.9 us (12%)
    ppermute x8, starting transfers between devices, trade(): lax.ppermute(sends[3], 'gy', shift_pairs('gy', -1))  32.5 us
    pallas_call x8, Pallas kernels, half_sweep(): pl.pallas_call(functools.partial(_half_sweep_kernel, span_x=span_x), out_...  24.6 us
    ppermute x8, starting transfers between devices, trade(): lax.ppermute(sends[0], 'gx', shift_pairs('gx', 1))  23.4 us
    ppermute x8, waiting for transfers between devices, trade(): lax.ppermute(sends[1], 'gx', shift_pairs('gx', -1))  21.8 us
    pallas_call x1, Pallas kernels, block_inverses(): pl.pallas_call(functools.partial(_gauss_jordan_kernel, n=n, nb=nb), out_s...  19.2 us
    ppermute x8, starting transfers between devices, trade(): lax.ppermute(sends[2], 'gy', shift_pairs('gy', 1))  16.8 us
    ppermute x8, starting transfers between devices, trade(): lax.ppermute(sends[1], 'gx', shift_pairs('gx', -1))  15.5 us
    unnamed x74, local copies, waits for them, and re-layouts  7.39 us
  transfers between devices with their start and end apart: 32, of which 8 were waited for; matrix products, arithmetic and copies ran while one was open for 3% of the time, Pallas kernels for 0%

commit v1 on v0

--- a/solution.py
+++ b/solution.py
@@ -76,6 +76,9 @@
         out_shape=jax.ShapeDtypeStruct((n, n * nb), jnp.float32),
         in_specs=[pl.BlockSpec(memory_space=pltpu.VMEM)],
         out_specs=pl.BlockSpec(memory_space=pltpu.VMEM),
+        cost_estimate=pl.CostEstimate(
+            flops=2000 * n ** 3 * nb, transcendentals=0, bytes_accessed=8 * n * n * nb
+        ),
     )(packed)
     return jnp.transpose(inverted.reshape(n, n, nb), (2, 0, 1))
 
@@ -243,7 +246,7 @@
 
 def shift_pairs(axis, step):
     count = lax.axis_size(axis)
-    return [(i, i + step) for i in range(count) if 0 <= i + step < count]
+    return [(i, (i + step) % count) for i in range(count)]
 
 
 def lane_body(forcing, initial, blocks, face_blocks, strength, strong, colour, neighbours):
@@ -251,10 +254,6 @@
     count = span_x * span_y * span_z
     columns = span_x * span_y
     empty_slot = (span_x + 2) * (span_y + 2) * span_z
-    inverse = block_inverses(blocks.reshape(count, P_SIZE, P_SIZE)).reshape(
-        span_x, span_y, span_z, P_SIZE, P_SIZE
-    )
-    weight = jnp.where(neighbours == empty_slot, 0.0, strength * strong.astype(jnp.float32))
     first_is = [colour[:, :, 0] == paint for paint in (0, 1)]
 
     def pick(values, paint, axis=2):
@@ -267,17 +266,23 @@
     def to_lanes(values):
         return jnp.transpose(values.reshape(columns, P_SIZE, R), (1, 0, 2)).reshape(P_SIZE, columns * R)
 
+    start_state = to_lanes(pick(initial, 1))
+    first_halos = trade(send_buffers(start_state, span_x))
+    inverse = block_inverses(blocks.reshape(count, P_SIZE, P_SIZE)).reshape(
+        span_x, span_y, span_z, P_SIZE, P_SIZE
+    )
+    weight = jnp.where(neighbours == empty_slot, 0.0, strength * strong.astype(jnp.float32))
     member_inverse = [pick(inverse, paint).reshape(columns, P_SIZE, P_SIZE) for paint in (0, 1)]
     member_target = [to_lanes(pick(forcing, paint)) for paint in (0, 1)]
     member_weight = [
         jnp.repeat(pick(weight, paint, axis=3).reshape(6, columns), R, axis=1).reshape(6, 1, columns * R)
         for paint in (0, 1)
     ]
-    state = [None, to_lanes(pick(initial, 1))]
-    sends = send_buffers(state[1], span_x)
+    state = [None, start_state]
+    sends = None
     for sweep_index in range(SWEEPS):
         for paint_now in (0, 1):
-            halos = trade(sends)
+            halos = first_halos if sends is None else trade(sends)
             state[paint_now], *sends = half_sweep(
                 state[1 - paint_now],
                 halos,

time: 181 us -> 134 us (0.74)
  the two profiles are of different devices: /device:TPU:9 before, /device:TPU:1 now
where the time goes in v1:
time: 134 us
  Pallas kernels  43.8 us (33%)
  starting transfers between devices  42.4 us (32%)
  local copies, waits for them, and re-layouts  23.8 us (18%)
  waiting for transfers between devices  21.9 us (16%)
    ppermute x8, starting transfers between devices, trade(): lax.ppermute(sends[3], 'gy', shift_pairs('gy', -1))  32.2 us
    pallas_call x8, Pallas kernels, half_sweep(): pl.pallas_call(functools.partial(_half_sweep_kernel, span_x=span_x), out_...  24.6 us
    pallas_call x1, Pallas kernels, block_inverses(): pl.pallas_call(functools.partial(_gauss_jordan_kernel, n=n, nb=nb), out_s...  19.2 us
    ppermute x8, waiting for transfers between devices, trade(): lax.ppermute(sends[1], 'gx', shift_pairs('gx', -1))  15 us
    ppermute x8, starting transfers between devices, trade(): lax.ppermute(sends[0], 'gx', shift_pairs('gx', 1))  8.01 us
    unnamed x74, local copies, waits for them, and re-layouts  7.93 us
    ppermute x8, waiting for transfers between devices, trade(): lax.ppermute(sends[0], 'gx', shift_pairs('gx', 1))  6.81 us
  transfers between devices with their start and end apart: 32, of which 13 were waited for; matrix products, arithmetic and copies ran while one was open for 5% of the time, Pallas kernels for 0%

profile of v1, /device:TPU:1, one launch (start us, length us, event | category | flops | bytes accessed | tf_op | source)
XLA Modules:
  0.0 133.6 jit_solution(2058088998965088895)
XLA Ops:
  0.0 0.7 slice-done
  1.1 1.3 reshape.134
  2.7 0.9 copy.52.a_ref
  3.6 19.2 %shard_map.82 = f32[64,1024]{1,0:T(8,128)} custom-call(f32[64,1024]{1,0:T(8,128)} %copy.52.a_ref), custom_call_target="tpu_custom_call" | custom-call | flops 8388608000 | bytes 524288 | tf_op jit(solution)/shard_map/pallas_call | solution.py:74
  22.7 1.1 copy.53
  24.2 0.9 copy-done
  25.1 0.8 slice_reduce_fusion.2
  26.3 0.7 copy-done.1
  27.1 0.8 slice_reduce_fusion
  28.3 0.9 bitcast_select_fusion
  29.4 2.1 %collective-permute-start.2 = (f32[64,256]{1,0:T(8,128)S(1)}, f32[64,256]{1,0:T(8,128)S(1)}, u32[]{:S(2)}, u32[]{:S(2)}) collective-permute-start(f32[64,256]{1,0:T(8,128)S(1)} %reshape_squeeze.14), channel_id=1, source_target_pairs={{0,1},{1,2},{2,3},{3,4},{4,5},{5,6},{6,7},{7,0},{8,9},{9,10},{10,1... | collective-permute-start | bytes 196616 | tf_op jit(solution)/shard_map/ppermute | solution.py:241
  31.8 3.1 %collective-permute-start.3 = (f32[64,256]{1,0:T(8,128)S(1)}, f32[64,256]{1,0:T(8,128)S(1)}, u32[]{:S(2)}, u32[]{:S(2)}) collective-permute-start(f32[64,256]{1,0:T(8,128)S(1)} %reshape_squeeze.15), channel_id=1, source_target_pairs={{0,7},{1,0},{2,1},{3,2},{4,3},{5,4},{6,5},{7,6},{8,15},{9,8},{10,9... | collective-permute-start | bytes 196616 | tf_op jit(solution)/shard_map/ppermute | solution.py:242
  35.0 2.2 %collective-permute-start = (f32[64,128]{1,0:T(8,128)S(1)}, f32[64,128]{1,0:T(8,128)S(1)}, u32[]{:S(2)}, u32[]{:S(2)}) collective-permute-start(f32[64,128]{1,0:T(8,128)S(1)} %reshape_squeeze.12), channel_id=1, source_target_pairs={{0,8},{8,16},{16,24},{24,0},{1,9},{9,17},{17,25},{25,1},{2,10},{10... | collective-permute-start | bytes 98312 | tf_op jit(solution)/shard_map/ppermute | solution.py:237
  38.3 0.8 reshape.138.target_ref
  39.2 0.8 reshape.133.other_ref
  40.1 0.7 reshape_reshape.10.weight_ref
  40.9 0.5 copy-done.18
  41.5 3.1 %shard_map.83 = (f32[64,512]{1,0:T(8,128)}, f32[64,128]{1,0:T(8,128)}, f32[64,128]{1,0:T(8,128)}, f32[64,256]{1,0:T(8,128)}, f32[64,256]{1,0:T(8,128)}) custom-call(f32[64,512]{1,0:T(8,128)} %reshape.133.other_ref, f32[64,128]{1,0:T(8,128)} %copy-done.18, f32[64,128]{1,0:T(8,128)} %copy-done.19, f32[64,256]{1,0:T(8,128)} %copy-done.2, f32[64,256]{1,0:T(8,128)} %copy-done.3, ...), custom_call_target="tpu_custom_call" | custom-call | tf_op jit(solution)/shard_map/pallas_call | solution.py:217
  44.6 4.2 %collective-permute-start.7 = (f32[64,256]{1,0:T(8,128)}, f32[64,256]{1,0:T(8,128)S(1)}, u32[]{:S(2)}, u32[]{:S(2)}) collective-permute-start(f32[64,256]{1,0:T(8,128)} %get-tuple-element.45), channel_id=1, source_target_pairs={{0,7},{1,0},{2,1},{3,2},{4,3},{5,4},{6,5},{7,6},{8,15},{9,8},{10,9... | collective-permute-start | bytes 196616 | tf_op jit(solution)/shard_map/ppermute | solution.py:242
  48.8 1.7 %collective-permute-start.4 = (f32[64,128]{1,0:T(8,128)}, f32[64,128]{1,0:T(8,128)S(1)}, u32[]{:S(2)}, u32[]{:S(2)}) collective-permute-start(f32[64,128]{1,0:T(8,128)} %get-tuple-element.42), channel_id=1, source_target_pairs={{0,8},{8,16},{16,24},{24,0},{1,9},{9,17},{17,25},{25,1},{2,10},{10... | collective-permute-start | bytes 98312 | tf_op jit(solution)/shard_map/ppermute | solution.py:237
  50.7 0.8 reshape.139.target_ref
  51.6 0.7 reshape_reshape.11.weight_ref
  52.3 1.8 %collective-permute-done.5.hi_x_ref = f32[64,128]{1,0:T(8,128)S(1)} collective-permute-done((f32[64,128]{1,0:T(8,128)}, f32[64,128]{1,0:T(8,128)S(1)}, u32[]{:S(2)}, u32[]{:S(2)}) %collective-permute-start.5) | collective-permute-done | bytes 32800 | tf_op jit(solution)/shard_map/ppermute | solution.py:238
  54.1 0.6 copy-done.21
  54.7 3.1 %shard_map.84 = (f32[64,512]{1,0:T(8,128)}, f32[64,128]{1,0:T(8,128)}, f32[64,128]{1,0:T(8,128)}, f32[64,256]{1,0:T(8,128)}, f32[64,256]{1,0:T(8,128)}) custom-call(f32[64,512]{1,0:T(8,128)} %get-tuple-element.41.other_ref, f32[64,128]{1,0:T(8,128)} %copy-done.20, f32[64,128]{1,0:T(8,128)} %copy-done.21, f32[64,256]{1,0:T(8,128)} %copy-done.4, ...), custom_call_target="tpu_custom_call" | custom-call | tf_op jit(solution)/shard_map/pallas_call | solution.py:217
  57.8 4.2 %collective-permute-start.11 = (f32[64,256]{1,0:T(8,128)}, f32[64,256]{1,0:T(8,128)S(1)}, u32[]{:S(2)}, u32[]{:S(2)}) collective-permute-start(f32[64,256]{1,0:T(8,128)} %get-tuple-element.50), channel_id=1, source_target_pairs={{0,7},{1,0},{2,1},{3,2},{4,3},{5,4},{6,5},{7,6},{8,15},{9,8},{10,9... | collective-permute-start | bytes 196616 | tf_op jit(solution)/shard_map/ppermute | solution.py:242
  62.0 0.7 collective-permute-start.8
  62.7 1.3 %collective-permute-done.8.lo_x_ref = f32[64,128]{1,0:T(8,128)S(1)} collective-permute-done((f32[64,128]{1,0:T(8,128)}, f32[64,128]{1,0:T(8,128)S(1)}, u32[]{:S(2)}, u32[]{:S(2)}) %collective-permute-start.8) | collective-permute-done | bytes 32800 | tf_op jit(solution)/shard_map/ppermute | solution.py:237
  64.0 2.2 %collective-permute-done.9.hi_x_ref = f32[64,128]{1,0:T(8,128)S(1)} collective-permute-done((f32[64,128]{1,0:T(8,128)}, f32[64,128]{1,0:T(8,128)S(1)}, u32[]{:S(2)}, u32[]{:S(2)}) %collective-permute-start.9) | collective-permute-done | bytes 32800 | tf_op jit(solution)/shard_map/ppermute | solution.py:238
  66.2 0.6 copy-done.30
  66.9 3.1 %shard_map.85 = (f32[64,512]{1,0:T(8,128)}, f32[64,128]{1,0:T(8,128)}, f32[64,128]{1,0:T(8,128)}, f32[64,256]{1,0:T(8,128)}, f32[64,256]{1,0:T(8,128)}) custom-call(f32[64,512]{1,0:T(8,128)} %get-tuple-element.46.other_ref, f32[64,128]{1,0:T(8,128)} %copy-done.25, f32[64,128]{1,0:T(8,128)} %copy-done.30, f32[64,256]{1,0:T(8,128)} %copy-done.9, ...), custom_call_target="tpu_custom_call" | custom-call | tf_op jit(solution)/shard_map/pallas_call | solution.py:217
  69.9 4.2 %collective-permute-start.15 = (f32[64,256]{1,0:T(8,128)}, f32[64,256]{1,0:T(8,128)S(1)}, u32[]{:S(2)}, u32[]{:S(2)}) collective-permute-start(f32[64,256]{1,0:T(8,128)} %get-tuple-element.55), channel_id=1, source_target_pairs={{0,7},{1,0},{2,1},{3,2},{4,3},{5,4},{6,5},{7,6},{8,15},{9,8},{10,9... | collective-permute-start | bytes 196616 | tf_op jit(solution)/shard_map/ppermute | solution.py:242
  74.1 0.7 collective-permute-start.12
  74.8 1.3 %collective-permute-done.12.lo_x_ref = f32[64,128]{1,0:T(8,128)S(1)} collective-permute-done((f32[64,128]{1,0:T(8,128)}, f32[64,128]{1,0:T(8,128)S(1)}, u32[]{:S(2)}, u32[]{:S(2)}) %collective-permute-start.12) | collective-permute-done | bytes 32800 | tf_op jit(solution)/shard_map/ppermute | solution.py:237
  76.1 2.2 %collective-permute-done.13.hi_x_ref = f32[64,128]{1,0:T(8,128)S(1)} collective-permute-done((f32[64,128]{1,0:T(8,128)}, f32[64,128]{1,0:T(8,128)S(1)}, u32[]{:S(2)}, u32[]{:S(2)}) %collective-permute-start.13) | collective-permute-done | bytes 32800 | tf_op jit(solution)/shard_map/ppermute | solution.py:238
  78.4 0.6 copy-done.31
  79.0 3.1 %shard_map.86 = (f32[64,512]{1,0:T(8,128)}, f32[64,128]{1,0:T(8,128)}, f32[64,128]{1,0:T(8,128)}, f32[64,256]{1,0:T(8,128)}, f32[64,256]{1,0:T(8,128)}) custom-call(f32[64,512]{1,0:T(8,128)} %get-tuple-element.51.other_ref, f32[64,128]{1,0:T(8,128)} %copy-done.26, f32[64,128]{1,0:T(8,128)} %copy-done.31, f32[64,256]{1,0:T(8,128)} %copy-done.10, ...), custom_call_target="tpu_custom_call" | custom-call | tf_op jit(solution)/shard_map/pallas_call | solution.py:217
  82.1 4.2 %collective-permute-start.19 = (f32[64,256]{1,0:T(8,128)}, f32[64,256]{1,0:T(8,128)S(1)}, u32[]{:S(2)}, u32[]{:S(2)}) collective-permute-start(f32[64,256]{1,0:T(8,128)} %get-tuple-element.60), channel_id=1, source_target_pairs={{0,7},{1,0},{2,1},{3,2},{4,3},{5,4},{6,5},{7,6},{8,15},{9,8},{10,9... | collective-permute-start | bytes 196616 | tf_op jit(solution)/shard_map/ppermute | solution.py:242
  86.2 0.7 collective-permute-start.16
  86.9 1.3 %collective-permute-done.16.lo_x_ref = f32[64,128]{1,0:T(8,128)S(1)} collective-permute-done((f32[64,128]{1,0:T(8,128)}, f32[64,128]{1,0:T(8,128)S(1)}, u32[]{:S(2)}, u32[]{:S(2)}) %collective-permute-start.16) | collective-permute-done | bytes 32800 | tf_op jit(solution)/shard_map/ppermute | solution.py:237
  88.3 2.2 %collective-permute-done.17.hi_x_ref = f32[64,128]{1,0:T(8,128)S(1)} collective-permute-done((f32[64,128]{1,0:T(8,128)}, f32[64,128]{1,0:T(8,128)S(1)}, u32[]{:S(2)}, u32[]{:S(2)}) %collective-permute-start.17) | collective-permute-done | bytes 32800 | tf_op jit(solution)/shard_map/ppermute | solution.py:238
  90.5 0.6 copy-done.32
  91.1 3.1 %shard_map.87 = (f32[64,512]{1,0:T(8,128)}, f32[64,128]{1,0:T(8,128)}, f32[64,128]{1,0:T(8,128)}, f32[64,256]{1,0:T(8,128)}, f32[64,256]{1,0:T(8,128)}) custom-call(f32[64,512]{1,0:T(8,128)} %get-tuple-element.56.other_ref, f32[64,128]{1,0:T(8,128)} %copy-done.27, f32[64,128]{1,0:T(8,128)} %copy-done.32, f32[64,256]{1,0:T(8,128)} %copy-done.11, ...), custom_call_target="tpu_custom_call" | custom-call | tf_op jit(solution)/shard_map/pallas_call | solution.py:217
  94.2 4.2 %collective-permute-start.23 = (f32[64,256]{1,0:T(8,128)}, f32[64,256]{1,0:T(8,128)S(1)}, u32[]{:S(2)}, u32[]{:S(2)}) collective-permute-start(f32[64,256]{1,0:T(8,128)} %get-tuple-element.65), channel_id=1, source_target_pairs={{0,7},{1,0},{2,1},{3,2},{4,3},{5,4},{6,5},{7,6},{8,15},{9,8},{10,9... | collective-permute-start | bytes 196616 | tf_op jit(solution)/shard_map/ppermute | solution.py:242
  98.4 0.7 collective-permute-start.20
  99.0 1.3 %collective-permute-done.20.lo_x_ref = f32[64,128]{1,0:T(8,128)S(1)} collective-permute-done((f32[64,128]{1,0:T(8,128)}, f32[64,128]{1,0:T(8,128)S(1)}, u32[]{:S(2)}, u32[]{:S(2)}) %collective-permute-start.20) | collective-permute-done | bytes 32800 | tf_op jit(solution)/shard_map/ppermute | solution.py:237
  100.4 2.2 %collective-permute-done.21.hi_x_ref = f32[64,128]{1,0:T(8,128)S(1)} collective-permute-done((f32[64,128]{1,0:T(8,128)}, f32[64,128]{1,0:T(8,128)S(1)}, u32[]{:S(2)}, u32[]{:S(2)}) %collective-permute-start.21) | collective-permute-done | bytes 32800 | tf_op jit(solution)/shard_map/ppermute | solution.py:238
  102.6 0.6 copy-done.33
  103.2 3.1 %shard_map.88 = (f32[64,512]{1,0:T(8,128)}, f32[64,128]{1,0:T(8,128)}, f32[64,128]{1,0:T(8,128)}, f32[64,256]{1,0:T(8,128)}, f32[64,256]{1,0:T(8,128)}) custom-call(f32[64,512]{1,0:T(8,128)} %get-tuple-element.61.other_ref, f32[64,128]{1,0:T(8,128)} %copy-done.28, f32[64,128]{1,0:T(8,128)} %copy-done.33, f32[64,256]{1,0:T(8,128)} %copy-done.12, ...), custom_call_target="tpu_custom_call" | custom-call | tf_op jit(solution)/shard_map/pallas_call | solution.py:217
  106.3 4.2 %collective-permute-start.27 = (f32[64,256]{1,0:T(8,128)}, f32[64,256]{1,0:T(8,128)S(1)}, u32[]{:S(2)}, u32[]{:S(2)}) collective-permute-start(f32[64,256]{1,0:T(8,128)} %get-tuple-element.70), channel_id=1, source_target_pairs={{0,7},{1,0},{2,1},{3,2},{4,3},{5,4},{6,5},{7,6},{8,15},{9,8},{10,9... | collective-permute-start | bytes 196616 | tf_op jit(solution)/shard_map/ppermute | solution.py:242
  110.5 0.7 collective-permute-start.24
  111.2 1.3 %collective-permute-done.24.lo_x_ref = f32[64,128]{1,0:T(8,128)S(1)} collective-permute-done((f32[64,128]{1,0:T(8,128)}, f32[64,128]{1,0:T(8,128)S(1)}, u32[]{:S(2)}, u32[]{:S(2)}) %collective-permute-start.24) | collective-permute-done | bytes 32800 | tf_op jit(solution)/shard_map/ppermute | solution.py:237
  112.5 2.2 %collective-permute-done.25.hi_x_ref = f32[64,128]{1,0:T(8,128)S(1)} collective-permute-done((f32[64,128]{1,0:T(8,128)}, f32[64,128]{1,0:T(8,128)S(1)}, u32[]{:S(2)}, u32[]{:S(2)}) %collective-permute-start.25) | collective-permute-done | bytes 32800 | tf_op jit(solution)/shard_map/ppermute | solution.py:238
  114.7 0.6 copy-done.29
  115.4 3.1 %shard_map.89 = (f32[64,512]{1,0:T(8,128)}, f32[64,128]{1,0:T(8,128)}, f32[64,128]{1,0:T(8,128)}, f32[64,256]{1,0:T(8,128)}, f32[64,256]{1,0:T(8,128)}) custom-call(f32[64,512]{1,0:T(8,128)} %get-tuple-element.66.other_ref, f32[64,128]{1,0:T(8,128)} %copy-done.24, f32[64,128]{1,0:T(8,128)} %copy-done.29, f32[64,256]{1,0:T(8,128)} %copy-done.8, ...), custom_call_target="tpu_custom_call" | custom-call | tf_op jit(solution)/shard_map/pallas_call | solution.py:217
  118.4 4.2 %collective-permute-start.31 = (f32[64,256]{1,0:T(8,128)}, f32[64,256]{1,0:T(8,128)S(1)}, u32[]{:S(2)}, u32[]{:S(2)}) collective-permute-start(f32[64,256]{1,0:T(8,128)} %get-tuple-element.75), channel_id=1, source_target_pairs={{0,7},{1,0},{2,1},{3,2},{4,3},{5,4},{6,5},{7,6},{8,15},{9,8},{10,9... | collective-permute-start | bytes 196616 | tf_op jit(solution)/shard_map/ppermute | solution.py:242
  122.6 0.7 collective-permute-start.28
  123.3 1.0 reshape.140
  124.6 2.2 %collective-permute-done.29.hi_x_ref = f32[64,128]{1,0:T(8,128)S(1)} collective-permute-done((f32[64,128]{1,0:T(8,128)}, f32[64,128]{1,0:T(8,128)S(1)}, u32[]{:S(2)}, u32[]{:S(2)}) %collective-permute-start.29) | collective-permute-done | bytes 32800 | tf_op jit(solution)/shard_map/ppermute | solution.py:238
  126.8 0.6 copy-done.23
  127.5 0.6 copy-done.7
  128.1 3.1 %shard_map.90 = (f32[64,512]{1,0:T(8,128)}, f32[64,128]{1,0:T(8,128)}, f32[64,128]{1,0:T(8,128)}, f32[64,256]{1,0:T(8,128)}, f32[64,256]{1,0:T(8,128)}) custom-call(f32[64,512]{1,0:T(8,128)} %get-tuple-element.71.other_ref, f32[64,128]{1,0:T(8,128)} %copy-done.22, f32[64,128]{1,0:T(8,128)} %copy-done.23, f32[64,256]{1,0:T(8,128)} %copy-done.6, ...), custom_call_target="tpu_custom_call" | custom-call | tf_op jit(solution)/shard_map/pallas_call | solution.py:217
  131.2 1.0 reshape.142
  132.7 0.9 copy.60
  (137 shorter events, 5.5 us)
Async XLA Ops:
  0.0 0.7 slice-start
  24.1 1.0 copy-start
  26.1 1.0 copy-start.1
  29.4 11.4 %collective-permute-start.2 = (f32[64,256]{1,0:T(8,128)S(1)}, f32[64,256]{1,0:T(8,128)S(1)}, u32[]{:S(2)}, u32[]{:S(2)}) collective-permute-start(f32[64,256]{1,0:T(8,128)S(1)} %reshape_squeeze.14), channel_id=1, source_target_pairs={{0,1},{1,2},{2,3},{3,4},{4,5},{5,6},{6,7},{7,0},{8,9},{9,10},{10,1... | collective-permute-start | bytes 196616 | tf_op jit(solution)/shard_map/ppermute | solution.py:241
  31.8 9.1 %collective-permute-start.3 = (f32[64,256]{1,0:T(8,128)S(1)}, f32[64,256]{1,0:T(8,128)S(1)}, u32[]{:S(2)}, u32[]{:S(2)}) collective-permute-start(f32[64,256]{1,0:T(8,128)S(1)} %reshape_squeeze.15), channel_id=1, source_target_pairs={{0,7},{1,0},{2,1},{3,2},{4,3},{5,4},{6,5},{7,6},{8,15},{9,8},{10,9... | collective-permute-start | bytes 196616 | tf_op jit(solution)/shard_map/ppermute | solution.py:242
  35.0 5.8 %collective-permute-start = (f32[64,128]{1,0:T(8,128)S(1)}, f32[64,128]{1,0:T(8,128)S(1)}, u32[]{:S(2)}, u32[]{:S(2)}) collective-permute-start(f32[64,128]{1,0:T(8,128)S(1)} %reshape_squeeze.12), channel_id=1, source_target_pairs={{0,8},{8,16},{16,24},{24,0},{1,9},{9,17},{17,25},{25,1},{2,10},{10... | collective-permute-start | bytes 98312 | tf_op jit(solution)/shard_map/ppermute | solution.py:237
  37.3 0.7 copy-start.34
  37.3 0.7 copy-start.35
  37.3 0.7 copy-start.36
  37.5 3.4 %collective-permute-start.1 = (f32[64,128]{1,0:T(8,128)S(1)}, f32[64,128]{1,0:T(8,128)S(1)}, u32[]{:S(2)}, u32[]{:S(2)}) collective-permute-start(f32[64,128]{1,0:T(8,128)S(1)} %reshape_squeeze.13), channel_id=1, source_target_pairs={{0,24},{8,0},{16,8},{24,16},{1,25},{9,1},{17,9},{25,17},{2,26},{10... | collective-permute-start | bytes 98312 | tf_op jit(solution)/shard_map/ppermute | solution.py:238
  40.8 0.6 copy-start.18
  40.8 0.6 copy-start.19
  40.9 0.6 copy-start.2
  40.9 0.6 copy-start.3
  44.6 9.5 %collective-permute-start.6 = (f32[64,256]{1,0:T(8,128)}, f32[64,256]{1,0:T(8,128)S(1)}, u32[]{:S(2)}, u32[]{:S(2)}) collective-permute-start(f32[64,256]{1,0:T(8,128)} %get-tuple-element.44), channel_id=1, source_target_pairs={{0,1},{1,2},{2,3},{3,4},{4,5},{5,6},{6,7},{7,0},{8,9},{9,10},{10,1... | collective-permute-start | bytes 196616 | tf_op jit(solution)/shard_map/ppermute | solution.py:241
  44.6 9.5 %collective-permute-start.7 = (f32[64,256]{1,0:T(8,128)}, f32[64,256]{1,0:T(8,128)S(1)}, u32[]{:S(2)}, u32[]{:S(2)}) collective-permute-start(f32[64,256]{1,0:T(8,128)} %get-tuple-element.45), channel_id=1, source_target_pairs={{0,7},{1,0},{2,1},{3,2},{4,3},{5,4},{6,5},{7,6},{8,15},{9,8},{10,9... | collective-permute-start | bytes 196616 | tf_op jit(solution)/shard_map/ppermute | solution.py:242
  48.8 3.5 %collective-permute-start.4 = (f32[64,128]{1,0:T(8,128)}, f32[64,128]{1,0:T(8,128)S(1)}, u32[]{:S(2)}, u32[]{:S(2)}) collective-permute-start(f32[64,128]{1,0:T(8,128)} %get-tuple-element.42), channel_id=1, source_target_pairs={{0,8},{8,16},{16,24},{24,0},{1,9},{9,17},{17,25},{25,1},{2,10},{10... | collective-permute-start | bytes 98312 | tf_op jit(solution)/shard_map/ppermute | solution.py:237
  50.5 3.6 %collective-permute-start.5 = (f32[64,128]{1,0:T(8,128)}, f32[64,128]{1,0:T(8,128)S(1)}, u32[]{:S(2)}, u32[]{:S(2)}) collective-permute-start(f32[64,128]{1,0:T(8,128)} %get-tuple-element.43), channel_id=1, source_target_pairs={{0,24},{8,0},{16,8},{24,16},{1,25},{9,1},{17,9},{25,17},{2,26},{10... | collective-permute-start | bytes 98312 | tf_op jit(solution)/shard_map/ppermute | solution.py:238
  52.3 1.8 %copy-start.20 = (f32[64,128]{1,0:T(8,128)}, f32[64,128]{1,0:T(8,128)S(1)}, u32[]{:S(2)}) copy-start(f32[64,128]{1,0:T(8,128)S(1)} %collective-permute-done.4.lo_x_ref) | copy-start | bytes 98308
  54.0 0.6 copy-start.21
  54.1 0.6 copy-start.4
  54.1 0.7 copy-start.5
  57.8 8.4 %collective-permute-start.10 = (f32[64,256]{1,0:T(8,128)}, f32[64,256]{1,0:T(8,128)S(1)}, u32[]{:S(2)}, u32[]{:S(2)}) collective-permute-start(f32[64,256]{1,0:T(8,128)} %get-tuple-element.49), channel_id=1, source_target_pairs={{0,1},{1,2},{2,3},{3,4},{4,5},{5,6},{6,7},{7,0},{8,9},{9,10},{10,1... | collective-permute-start | bytes 196616 | tf_op jit(solution)/shard_map/ppermute | solution.py:241
  57.8 8.4 %collective-permute-start.11 = (f32[64,256]{1,0:T(8,128)}, f32[64,256]{1,0:T(8,128)S(1)}, u32[]{:S(2)}, u32[]{:S(2)}) collective-permute-start(f32[64,256]{1,0:T(8,128)} %get-tuple-element.50), channel_id=1, source_target_pairs={{0,7},{1,0},{2,1},{3,2},{4,3},{5,4},{6,5},{7,6},{8,15},{9,8},{10,9... | collective-permute-start | bytes 196616 | tf_op jit(solution)/shard_map/ppermute | solution.py:242
  62.0 2.0 %collective-permute-start.8 = (f32[64,128]{1,0:T(8,128)}, f32[64,128]{1,0:T(8,128)S(1)}, u32[]{:S(2)}, u32[]{:S(2)}) collective-permute-start(f32[64,128]{1,0:T(8,128)} %get-tuple-element.47), channel_id=1, source_target_pairs={{0,8},{8,16},{16,24},{24,0},{1,9},{9,17},{17,25},{25,1},{2,10},{10... | collective-permute-start | bytes 98312 | tf_op jit(solution)/shard_map/ppermute | solution.py:237
  62.7 3.6 %collective-permute-start.9 = (f32[64,128]{1,0:T(8,128)}, f32[64,128]{1,0:T(8,128)S(1)}, u32[]{:S(2)}, u32[]{:S(2)}) collective-permute-start(f32[64,128]{1,0:T(8,128)} %get-tuple-element.48), channel_id=1, source_target_pairs={{0,24},{8,0},{16,8},{24,16},{1,25},{9,1},{17,9},{25,17},{2,26},{10... | collective-permute-start | bytes 98312 | tf_op jit(solution)/shard_map/ppermute | solution.py:238
  64.0 2.2 %copy-start.25 = (f32[64,128]{1,0:T(8,128)}, f32[64,128]{1,0:T(8,128)S(1)}, u32[]{:S(2)}) copy-start(f32[64,128]{1,0:T(8,128)S(1)} %collective-permute-done.8.lo_x_ref) | copy-start | bytes 98308
  66.2 0.6 copy-start.9
  66.2 0.7 copy-start.14
  69.9 8.4 %collective-permute-start.14 = (f32[64,256]{1,0:T(8,128)}, f32[64,256]{1,0:T(8,128)S(1)}, u32[]{:S(2)}, u32[]{:S(2)}) collective-permute-start(f32[64,256]{1,0:T(8,128)} %get-tuple-element.54), channel_id=1, source_target_pairs={{0,1},{1,2},{2,3},{3,4},{4,5},{5,6},{6,7},{7,0},{8,9},{9,10},{10,1... | collective-permute-start | bytes 196616 | tf_op jit(solution)/shard_map/ppermute | solution.py:241
  69.9 8.4 %collective-permute-start.15 = (f32[64,256]{1,0:T(8,128)}, f32[64,256]{1,0:T(8,128)S(1)}, u32[]{:S(2)}, u32[]{:S(2)}) collective-permute-start(f32[64,256]{1,0:T(8,128)} %get-tuple-element.55), channel_id=1, source_target_pairs={{0,7},{1,0},{2,1},{3,2},{4,3},{5,4},{6,5},{7,6},{8,15},{9,8},{10,9... | collective-permute-start | bytes 196616 | tf_op jit(solution)/shard_map/ppermute | solution.py:242
  74.1 2.0 %collective-permute-start.12 = (f32[64,128]{1,0:T(8,128)}, f32[64,128]{1,0:T(8,128)S(1)}, u32[]{:S(2)}, u32[]{:S(2)}) collective-permute-start(f32[64,128]{1,0:T(8,128)} %get-tuple-element.52), channel_id=1, source_target_pairs={{0,8},{8,16},{16,24},{24,0},{1,9},{9,17},{17,25},{25,1},{2,10},{10... | collective-permute-start | bytes 98312 | tf_op jit(solution)/shard_map/ppermute | solution.py:237
  74.8 3.6 %collective-permute-start.13 = (f32[64,128]{1,0:T(8,128)}, f32[64,128]{1,0:T(8,128)S(1)}, u32[]{:S(2)}, u32[]{:S(2)}) collective-permute-start(f32[64,128]{1,0:T(8,128)} %get-tuple-element.53), channel_id=1, source_target_pairs={{0,24},{8,0},{16,8},{24,16},{1,25},{9,1},{17,9},{25,17},{2,26},{10... | collective-permute-start | bytes 98312 | tf_op jit(solution)/shard_map/ppermute | solution.py:238
  76.1 2.2 %copy-start.26 = (f32[64,128]{1,0:T(8,128)}, f32[64,128]{1,0:T(8,128)S(1)}, u32[]{:S(2)}) copy-start(f32[64,128]{1,0:T(8,128)S(1)} %collective-permute-done.12.lo_x_ref) | copy-start | bytes 98308
  78.3 0.6 copy-start.10
  78.3 0.7 copy-start.15
  82.1 8.4 %collective-permute-start.18 = (f32[64,256]{1,0:T(8,128)}, f32[64,256]{1,0:T(8,128)S(1)}, u32[]{:S(2)}, u32[]{:S(2)}) collective-permute-start(f32[64,256]{1,0:T(8,128)} %get-tuple-element.59), channel_id=1, source_target_pairs={{0,1},{1,2},{2,3},{3,4},{4,5},{5,6},{6,7},{7,0},{8,9},{9,10},{10,1... | collective-permute-start | bytes 196616 | tf_op jit(solution)/shard_map/ppermute | solution.py:241
  82.1 8.4 %collective-permute-start.19 = (f32[64,256]{1,0:T(8,128)}, f32[64,256]{1,0:T(8,128)S(1)}, u32[]{:S(2)}, u32[]{:S(2)}) collective-permute-start(f32[64,256]{1,0:T(8,128)} %get-tuple-element.60), channel_id=1, source_target_pairs={{0,7},{1,0},{2,1},{3,2},{4,3},{5,4},{6,5},{7,6},{8,15},{9,8},{10,9... | collective-permute-start | bytes 196616 | tf_op jit(solution)/shard_map/ppermute | solution.py:242
  86.2 2.0 %collective-permute-start.16 = (f32[64,128]{1,0:T(8,128)}, f32[64,128]{1,0:T(8,128)S(1)}, u32[]{:S(2)}, u32[]{:S(2)}) collective-permute-start(f32[64,128]{1,0:T(8,128)} %get-tuple-element.57), channel_id=1, source_target_pairs={{0,8},{8,16},{16,24},{24,0},{1,9},{9,17},{17,25},{25,1},{2,10},{10... | collective-permute-start | bytes 98312 | tf_op jit(solution)/shard_map/ppermute | solution.py:237
  86.9 3.6 %collective-permute-start.17 = (f32[64,128]{1,0:T(8,128)}, f32[64,128]{1,0:T(8,128)S(1)}, u32[]{:S(2)}, u32[]{:S(2)}) collective-permute-start(f32[64,128]{1,0:T(8,128)} %get-tuple-element.58), channel_id=1, source_target_pairs={{0,24},{8,0},{16,8},{24,16},{1,25},{9,1},{17,9},{25,17},{2,26},{10... | collective-permute-start | bytes 98312 | tf_op jit(solution)/shard_map/ppermute | solution.py:238
  88.2 2.2 %copy-start.27 = (f32[64,128]{1,0:T(8,128)}, f32[64,128]{1,0:T(8,128)S(1)}, u32[]{:S(2)}) copy-start(f32[64,128]{1,0:T(8,128)S(1)} %collective-permute-done.16.lo_x_ref) | copy-start | bytes 98308
  90.5 0.6 copy-start.11
  90.5 0.7 copy-start.16
  94.2 8.4 %collective-permute-start.22 = (f32[64,256]{1,0:T(8,128)}, f32[64,256]{1,0:T(8,128)S(1)}, u32[]{:S(2)}, u32[]{:S(2)}) collective-permute-start(f32[64,256]{1,0:T(8,128)} %get-tuple-element.64), channel_id=1, source_target_pairs={{0,1},{1,2},{2,3},{3,4},{4,5},{5,6},{6,7},{7,0},{8,9},{9,10},{10,1... | collective-permute-start | bytes 196616 | tf_op jit(solution)/shard_map/ppermute | solution.py:241
  94.2 8.4 %collective-permute-start.23 = (f32[64,256]{1,0:T(8,128)}, f32[64,256]{1,0:T(8,128)S(1)}, u32[]{:S(2)}, u32[]{:S(2)}) collective-permute-start(f32[64,256]{1,0:T(8,128)} %get-tuple-element.65), channel_id=1, source_target_pairs={{0,7},{1,0},{2,1},{3,2},{4,3},{5,4},{6,5},{7,6},{8,15},{9,8},{10,9... | collective-permute-start | bytes 196616 | tf_op jit(solution)/shard_map/ppermute | solution.py:242
  98.4 2.0 %collective-permute-start.20 = (f32[64,128]{1,0:T(8,128)}, f32[64,128]{1,0:T(8,128)S(1)}, u32[]{:S(2)}, u32[]{:S(2)}) collective-permute-start(f32[64,128]{1,0:T(8,128)} %get-tuple-element.62), channel_id=1, source_target_pairs={{0,8},{8,16},{16,24},{24,0},{1,9},{9,17},{17,25},{25,1},{2,10},{10... | collective-permute-start | bytes 98312 | tf_op jit(solution)/shard_map/ppermute | solution.py:237
  99.0 3.6 %collective-permute-start.21 = (f32[64,128]{1,0:T(8,128)}, f32[64,128]{1,0:T(8,128)S(1)}, u32[]{:S(2)}, u32[]{:S(2)}) collective-permute-start(f32[64,128]{1,0:T(8,128)} %get-tuple-element.63), channel_id=1, source_target_pairs={{0,24},{8,0},{16,8},{24,16},{1,25},{9,1},{17,9},{25,17},{2,26},{10... | collective-permute-start | bytes 98312 | tf_op jit(solution)/shard_map/ppermute | solution.py:238
  100.4 2.2 %copy-start.28 = (f32[64,128]{1,0:T(8,128)}, f32[64,128]{1,0:T(8,128)S(1)}, u32[]{:S(2)}) copy-start(f32[64,128]{1,0:T(8,128)S(1)} %collective-permute-done.20.lo_x_ref) | copy-start | bytes 98308
  102.6 0.6 copy-start.12
  102.6 0.7 copy-start.17
  106.3 8.4 %collective-permute-start.26 = (f32[64,256]{1,0:T(8,128)}, f32[64,256]{1,0:T(8,128)S(1)}, u32[]{:S(2)}, u32[]{:S(2)}) collective-permute-start(f32[64,256]{1,0:T(8,128)} %get-tuple-element.69), channel_id=1, source_target_pairs={{0,1},{1,2},{2,3},{3,4},{4,5},{5,6},{6,7},{7,0},{8,9},{9,10},{10,1... | collective-permute-start | bytes 196616 | tf_op jit(solution)/shard_map/ppermute | solution.py:241
  106.3 8.4 %collective-permute-start.27 = (f32[64,256]{1,0:T(8,128)}, f32[64,256]{1,0:T(8,128)S(1)}, u32[]{:S(2)}, u32[]{:S(2)}) collective-permute-start(f32[64,256]{1,0:T(8,128)} %get-tuple-element.70), channel_id=1, source_target_pairs={{0,7},{1,0},{2,1},{3,2},{4,3},{5,4},{6,5},{7,6},{8,15},{9,8},{10,9... | collective-permute-start | bytes 196616 | tf_op jit(solution)/shard_map/ppermute | solution.py:242
  110.5 2.0 %collective-permute-start.24 = (f32[64,128]{1,0:T(8,128)}, f32[64,128]{1,0:T(8,128)S(1)}, u32[]{:S(2)}, u32[]{:S(2)}) collective-permute-start(f32[64,128]{1,0:T(8,128)} %get-tuple-element.67), channel_id=1, source_target_pairs={{0,8},{8,16},{16,24},{24,0},{1,9},{9,17},{17,25},{25,1},{2,10},{10... | collective-permute-start | bytes 98312 | tf_op jit(solution)/shard_map/ppermute | solution.py:237
  111.2 3.6 %collective-permute-start.25 = (f32[64,128]{1,0:T(8,128)}, f32[64,128]{1,0:T(8,128)S(1)}, u32[]{:S(2)}, u32[]{:S(2)}) collective-permute-start(f32[64,128]{1,0:T(8,128)} %get-tuple-element.68), channel_id=1, source_target_pairs={{0,24},{8,0},{16,8},{24,16},{1,25},{9,1},{17,9},{25,17},{2,26},{10... | collective-permute-start | bytes 98312 | tf_op jit(solution)/shard_map/ppermute | solution.py:238
  112.5 2.2 %copy-start.24 = (f32[64,128]{1,0:T(8,128)}, f32[64,128]{1,0:T(8,128)S(1)}, u32[]{:S(2)}) copy-start(f32[64,128]{1,0:T(8,128)S(1)} %collective-permute-done.24.lo_x_ref) | copy-start | bytes 98308
  114.7 0.6 copy-start.8
  114.7 0.7 copy-start.13
  118.4 8.4 %collective-permute-start.30 = (f32[64,256]{1,0:T(8,128)}, f32[64,256]{1,0:T(8,128)S(1)}, u32[]{:S(2)}, u32[]{:S(2)}) collective-permute-start(f32[64,256]{1,0:T(8,128)} %get-tuple-element.74), channel_id=1, source_target_pairs={{0,1},{1,2},{2,3},{3,4},{4,5},{5,6},{6,7},{7,0},{8,9},{9,10},{10,1... | collective-permute-start | bytes 196616 | tf_op jit(solution)/shard_map/ppermute | solution.py:241
  118.4 8.4 %collective-permute-start.31 = (f32[64,256]{1,0:T(8,128)}, f32[64,256]{1,0:T(8,128)S(1)}, u32[]{:S(2)}, u32[]{:S(2)}) collective-permute-start(f32[64,256]{1,0:T(8,128)} %get-tuple-element.75), channel_id=1, source_target_pairs={{0,7},{1,0},{2,1},{3,2},{4,3},{5,4},{6,5},{7,6},{8,15},{9,8},{10,9... | collective-permute-start | bytes 196616 | tf_op jit(solution)/shard_map/ppermute | solution.py:242
  122.6 2.0 %collective-permute-start.28 = (f32[64,128]{1,0:T(8,128)}, f32[64,128]{1,0:T(8,128)S(1)}, u32[]{:S(2)}, u32[]{:S(2)}) collective-permute-start(f32[64,128]{1,0:T(8,128)} %get-tuple-element.72), channel_id=1, source_target_pairs={{0,8},{8,16},{16,24},{24,0},{1,9},{9,17},{17,25},{25,1},{2,10},{10... | collective-permute-start | bytes 98312 | tf_op jit(solution)/shard_map/ppermute | solution.py:237
  123.3 3.6 %collective-permute-start.29 = (f32[64,128]{1,0:T(8,128)}, f32[64,128]{1,0:T(8,128)S(1)}, u32[]{:S(2)}, u32[]{:S(2)}) collective-permute-start(f32[64,128]{1,0:T(8,128)} %get-tuple-element.73), channel_id=1, source_target_pairs={{0,24},{8,0},{16,8},{24,16},{1,25},{9,1},{17,9},{25,17},{2,26},{10... | collective-permute-start | bytes 98312 | tf_op jit(solution)/shard_map/ppermute | solution.py:238
  124.6 2.2 %copy-start.22 = (f32[64,128]{1,0:T(8,128)}, f32[64,128]{1,0:T(8,128)S(1)}, u32[]{:S(2)}) copy-start(f32[64,128]{1,0:T(8,128)S(1)} %collective-permute-done.28.lo_x_ref) | copy-start | bytes 98308
  126.8 0.6 copy-start.6
  127.5 0.6 copy-start.7
  (6 other events, 3.6 us)

commit v2 on v1

--- a/solution.py
+++ b/solution.py
@@ -63,9 +63,10 @@
     lax.fori_loop(0, n, step, 0)
 
 
-def block_inverses(matrices):
+def block_inverses(matrices, lanes_out=False):
     nb, n, _ = matrices.shape
     if 128 % nb or (n * nb) % 128:
+        assert not lanes_out
         lower_factor = jnp.linalg.cholesky(matrices)
         identity = jnp.broadcast_to(jnp.eye(n, dtype=matrices.dtype), matrices.shape)
         solved = jax.scipy.linalg.solve_triangular(lower_factor, identity, lower=True)
@@ -80,6 +81,8 @@
             flops=2000 * n ** 3 * nb, transcendentals=0, bytes_accessed=8 * n * n * nb
         ),
     )(packed)
+    if lanes_out:
+        return jnp.transpose(inverted.reshape(n, n, nb), (0, 2, 1)).reshape(n, nb * n)
     return jnp.transpose(inverted.reshape(n, n, nb), (2, 0, 1))
 
 
@@ -118,7 +121,8 @@
         high = lax.index_in_dim(values, 1, axis=axis, keepdims=False)
         return jnp.where(mask, low, high)
 
-    member_inverse = [pick(inverse, paint).reshape(columns, P_SIZE, P_SIZE) for paint in (0, 1)]
+    member_inverse = [inverse[:, paint * columns * P_SIZE:(paint + 1) * columns * P_SIZE] for paint in (0, 1)]
+    face_row = jnp.transpose(face_blocks, (1, 0, 2)).reshape(P_SIZE, 6 * P_SIZE)
     member_target = [pick(forcing, paint).reshape(columns, P_SIZE, R) for paint in (0, 1)]
     member_weight = [pick(weight, paint, axis=3)[..., None] for paint in (0, 1)]
     state = [pick(initial, 0), pick(initial, 1)]
@@ -185,21 +189,19 @@
         other,
         other,
     ]
-    coupled = jnp.zeros_like(other)
-    for face in range(6):
-        product = jnp.dot(
-            face_ref[face], nearby[face], precision=highest, preferred_element_type=jnp.float32
-        )
-        coupled = coupled + weight_ref[face] * product
+    stacked = jnp.concatenate([weight_ref[face] * nearby[face] for face in range(6)], axis=0)
+    coupled = jnp.dot(face_ref[...], stacked, precision=highest, preferred_element_type=jnp.float32)
     rhs = target_ref[...] - coupled
     outs = []
     for x in range(span_x):
         part = rhs[:, x * tile:(x + 1) * tile]
-        first = jnp.dot(inverse_ref[2 * x], part, precision=highest, preferred_element_type=jnp.float32)
-        second = jnp.dot(
-            inverse_ref[2 * x + 1], part, precision=highest, preferred_element_type=jnp.float32
+        split = jnp.concatenate([jnp.where(low_half, part, 0.0), jnp.where(low_half, 0.0, part)], axis=0)
+        outs.append(
+            jnp.dot(
+                inverse_ref[:, x * tile:(x + 1) * tile], split, precision=highest,
+                preferred_element_type=jnp.float32,
+            )
         )
-        outs.append(jnp.where(low_half, first, second))
     out_ref[...] = jnp.concatenate(outs, axis=1)
     send_lo_x_ref[...] = outs[-1]
     send_hi_x_ref[...] = outs[0]
@@ -268,11 +270,11 @@
 
     start_state = to_lanes(pick(initial, 1))
     first_halos = trade(send_buffers(start_state, span_x))
-    inverse = block_inverses(blocks.reshape(count, P_SIZE, P_SIZE)).reshape(
-        span_x, span_y, span_z, P_SIZE, P_SIZE
-    )
+    by_colour = jnp.stack([pick(blocks, paint) for paint in (0, 1)]).reshape(count, P_SIZE, P_SIZE)
+    inverse = block_inverses(by_colour, lanes_out=True)
     weight = jnp.where(neighbours == empty_slot, 0.0, strength * strong.astype(jnp.float32))
-    member_inverse = [pick(inverse, paint).reshape(columns, P_SIZE, P_SIZE) for paint in (0, 1)]
+    member_inverse = [inverse[:, paint * columns * P_SIZE:(paint + 1) * columns * P_SIZE] for paint in (0, 1)]
+    face_row = jnp.transpose(face_blocks, (1, 0, 2)).reshape(P_SIZE, 6 * P_SIZE)
     member_target = [to_lanes(pick(forcing, paint)) for paint in (0, 1)]
     member_weight = [
         jnp.repeat(pick(weight, paint, axis=3).reshape(6, columns), R, axis=1).reshape(6, 1, columns * R)
@@ -286,7 +288,7 @@
             state[paint_now], *sends = half_sweep(
                 state[1 - paint_now],
                 halos,
-                face_blocks,
+                face_row,
                 member_weight[paint_now],
                 member_inverse[paint_now],
                 member_target[paint_now],

time: 134 us -> 133 us (level)
  Pallas kernels: 43.8 us -> 42 us
    pallas_call x8, Pallas kernels: 24.6 us -> 22.8 us  [half_sweep(): pl.pallas_call(functools.partial(_half_sweep_kernel, span_x=span_x), out_...]
    unnamed x74 -> x80, local copies, waits for them, and re-layouts: 7.93 us -> 6.75 us
  transfers between devices with their start and end apart: 32 -> 32, of which waited for: 13 -> 13; matrix products, arithmetic and copies ran while one was open for 5% -> 9% of each run, Pallas kernels for 0% -> 14%
where the time goes in v2:
time: 133 us
  starting transfers between devices  42.9 us (32%)
  Pallas kernels  42 us (32%)
  local copies, waits for them, and re-layouts  24.6 us (18%)
  waiting for transfers between devices  21.9 us (16%)
    ppermute x8, starting transfers between devices, trade(): lax.ppermute(sends[3], 'gy', shift_pairs('gy', -1))  32.2 us
    pallas_call x8, Pallas kernels, half_sweep(): pl.pallas_call(functools.partial(_half_sweep_kernel, span_x=span_x), out_...  22.8 us
    pallas_call x1, Pallas kernels, block_inverses(): pl.pallas_call(functools.partial(_gauss_jordan_kernel, n=n, nb=nb), out_s...  19.2 us
    ppermute x8, waiting for transfers between devices, trade(): lax.ppermute(sends[1], 'gx', shift_pairs('gx', -1))  15 us
    ppermute x8, starting transfers between devices, trade(): lax.ppermute(sends[0], 'gx', shift_pairs('gx', 1))  8.51 us
    ppermute x8, waiting for transfers between devices, trade(): lax.ppermute(sends[0], 'gx', shift_pairs('gx', 1))  6.81 us
    unnamed x80, local copies, waits for them, and re-layouts  6.75 us
    slice x3, local copies, waits for them, and re-layouts, pick(): high = lax.index_in_dim(values, 1, axis=axis, keepdims=False)  2.73 us
  transfers between devices with their start and end apart: 32, of which 13 were waited for; matrix products, arithmetic and copies ran while one was open for 9% of the time, Pallas kernels for 14%

profile of v2, /device:TPU:1, one launch (start us, length us, event | category | flops | bytes accessed | tf_op | source)
XLA Modules:
  0.0 132.9 jit_solution(12799146184214345720)
XLA Ops:
  0.0 0.7 slice-done
  1.1 1.9 %slice_reduce_fusion.2 = (f32[4,2,4096]{2,1,0:T(2,128)S(1)}, f32[4,2,4096]{2,1,0:T(2,128)S(1)}) fusion(f32[4,2,2,4096]{3,2,1,0:T(2,128)} %param.9), kind=kLoop, calls=%fused_computation.10 | loop fusion | bytes 524288 | tf_op jit(solution)/shard_map/slice | solution.py:265
  3.4 0.7 copy-done
  4.2 0.8 slice_reduce_fusion
  5.8 2.1 %collective-permute-start.2 = (f32[64,256]{1,0:T(8,128)S(1)}, f32[64,256]{1,0:T(8,128)S(1)}, u32[]{:S(2)}, u32[]{:S(2)}) collective-permute-start(f32[64,256]{1,0:T(8,128)S(1)} %reshape_squeeze.14), channel_id=1, source_target_pairs={{0,1},{1,2},{2,3},{3,4},{4,5},{5,6},{6,7},{7,0},{8,9},{9,10},{10,1... | collective-permute-start | bytes 196616 | tf_op jit(solution)/shard_map/ppermute | solution.py:243
  8.1 3.1 %collective-permute-start.3 = (f32[64,256]{1,0:T(8,128)S(1)}, f32[64,256]{1,0:T(8,128)S(1)}, u32[]{:S(2)}, u32[]{:S(2)}) collective-permute-start(f32[64,256]{1,0:T(8,128)S(1)} %reshape_squeeze.15), channel_id=1, source_target_pairs={{0,7},{1,0},{2,1},{3,2},{4,3},{5,4},{6,5},{7,6},{8,15},{9,8},{10,9... | collective-permute-start | bytes 196616 | tf_op jit(solution)/shard_map/ppermute | solution.py:244
  11.4 2.2 %collective-permute-start = (f32[64,128]{1,0:T(8,128)S(1)}, f32[64,128]{1,0:T(8,128)S(1)}, u32[]{:S(2)}, u32[]{:S(2)}) collective-permute-start(f32[64,128]{1,0:T(8,128)S(1)} %reshape_squeeze.12), channel_id=1, source_target_pairs={{0,8},{8,16},{16,24},{24,0},{1,9},{9,17},{17,25},{25,1},{2,10},{10... | collective-permute-start | bytes 98312 | tf_op jit(solution)/shard_map/ppermute | solution.py:239
  15.2 0.9 copy.65.a_ref
  16.1 19.2 %shard_map.82 = f32[64,1024]{1,0:T(8,128)} custom-call(f32[64,1024]{1,0:T(8,128)} %copy.65.a_ref), custom_call_target="tpu_custom_call" | custom-call | flops 8388608000 | bytes 524288 | tf_op jit(solution)/shard_map/pallas_call | solution.py:75
  35.2 1.1 copy.66
  36.4 0.4 copy.67
  37.0 0.7 fusion
  38.0 0.8 reshape.156.target_ref
  38.9 0.8 reshape.150.other_ref
  39.8 0.7 reshape_reshape.10.weight_ref
  40.7 0.7 reshape.151.face_ref
  41.5 0.5 copy-done.19
  42.1 2.8 %shard_map.83 = (f32[64,512]{1,0:T(8,128)}, f32[64,128]{1,0:T(8,128)}, f32[64,128]{1,0:T(8,128)}, f32[64,256]{1,0:T(8,128)}, f32[64,256]{1,0:T(8,128)}) custom-call(f32[64,512]{1,0:T(8,128)} %reshape.150.other_ref, f32[64,128]{1,0:T(8,128)} %copy-done.19, f32[64,128]{1,0:T(8,128)} %copy-done.20, f32[64,256]{1,0:T(8,128)} %copy-done.3, f32[64,256]{1,0:T(8,128)} %copy-done.4, ...), custom_call_target="tpu_custom_call" | custom-call | tf_op jit(solution)/shard_map/pallas_call | solution.py:219
  44.9 4.2 %collective-permute-start.7 = (f32[64,256]{1,0:T(8,128)}, f32[64,256]{1,0:T(8,128)S(1)}, u32[]{:S(2)}, u32[]{:S(2)}) collective-permute-start(f32[64,256]{1,0:T(8,128)} %get-tuple-element.45), channel_id=1, source_target_pairs={{0,7},{1,0},{2,1},{3,2},{4,3},{5,4},{6,5},{7,6},{8,15},{9,8},{10,9... | collective-permute-start | bytes 196616 | tf_op jit(solution)/shard_map/ppermute | solution.py:244
  49.1 2.3 %collective-permute-start.4 = (f32[64,128]{1,0:T(8,128)}, f32[64,128]{1,0:T(8,128)S(1)}, u32[]{:S(2)}, u32[]{:S(2)}) collective-permute-start(f32[64,128]{1,0:T(8,128)} %get-tuple-element.42), channel_id=1, source_target_pairs={{0,8},{8,16},{16,24},{24,0},{1,9},{9,17},{17,25},{25,1},{2,10},{10... | collective-permute-start | bytes 98312 | tf_op jit(solution)/shard_map/ppermute | solution.py:239
  51.5 0.8 reshape.157.target_ref
  52.5 0.7 reshape_reshape.11.weight_ref
  53.2 1.8 %collective-permute-done.5.hi_x_ref = f32[64,128]{1,0:T(8,128)S(1)} collective-permute-done((f32[64,128]{1,0:T(8,128)}, f32[64,128]{1,0:T(8,128)S(1)}, u32[]{:S(2)}, u32[]{:S(2)}) %collective-permute-start.5) | collective-permute-done | bytes 32800 | tf_op jit(solution)/shard_map/ppermute | solution.py:240
  55.0 0.6 copy-done.22
  55.6 2.8 %shard_map.84 = (f32[64,512]{1,0:T(8,128)}, f32[64,128]{1,0:T(8,128)}, f32[64,128]{1,0:T(8,128)}, f32[64,256]{1,0:T(8,128)}, f32[64,256]{1,0:T(8,128)}) custom-call(f32[64,512]{1,0:T(8,128)} %get-tuple-element.41.other_ref, f32[64,128]{1,0:T(8,128)} %copy-done.21, f32[64,128]{1,0:T(8,128)} %copy-done.22, f32[64,256]{1,0:T(8,128)} %copy-done.5, ...), custom_call_target="tpu_custom_call" | custom-call | tf_op jit(solution)/shard_map/pallas_call | solution.py:219
  58.4 4.2 %collective-permute-start.11 = (f32[64,256]{1,0:T(8,128)}, f32[64,256]{1,0:T(8,128)S(1)}, u32[]{:S(2)}, u32[]{:S(2)}) collective-permute-start(f32[64,256]{1,0:T(8,128)} %get-tuple-element.50), channel_id=1, source_target_pairs={{0,7},{1,0},{2,1},{3,2},{4,3},{5,4},{6,5},{7,6},{8,15},{9,8},{10,9... | collective-permute-start | bytes 196616 | tf_op jit(solution)/shard_map/ppermute | solution.py:244
  62.6 0.7 collective-permute-start.8
  63.3 1.3 %collective-permute-done.8.lo_x_ref = f32[64,128]{1,0:T(8,128)S(1)} collective-permute-done((f32[64,128]{1,0:T(8,128)}, f32[64,128]{1,0:T(8,128)S(1)}, u32[]{:S(2)}, u32[]{:S(2)}) %collective-permute-start.8) | collective-permute-done | bytes 32800 | tf_op jit(solution)/shard_map/ppermute | solution.py:239
  64.6 2.2 %collective-permute-done.9.hi_x_ref = f32[64,128]{1,0:T(8,128)S(1)} collective-permute-done((f32[64,128]{1,0:T(8,128)}, f32[64,128]{1,0:T(8,128)S(1)}, u32[]{:S(2)}, u32[]{:S(2)}) %collective-permute-start.9) | collective-permute-done | bytes 32800 | tf_op jit(solution)/shard_map/ppermute | solution.py:240
  66.9 0.6 copy-done.31
  67.5 2.9 %shard_map.85 = (f32[64,512]{1,0:T(8,128)}, f32[64,128]{1,0:T(8,128)}, f32[64,128]{1,0:T(8,128)}, f32[64,256]{1,0:T(8,128)}, f32[64,256]{1,0:T(8,128)}) custom-call(f32[64,512]{1,0:T(8,128)} %get-tuple-element.46.other_ref, f32[64,128]{1,0:T(8,128)} %copy-done.26, f32[64,128]{1,0:T(8,128)} %copy-done.31, f32[64,256]{1,0:T(8,128)} %copy-done.10, ...), custom_call_target="tpu_custom_call" | custom-call | tf_op jit(solution)/shard_map/pallas_call | solution.py:219
  70.4 4.2 %collective-permute-start.15 = (f32[64,256]{1,0:T(8,128)}, f32[64,256]{1,0:T(8,128)S(1)}, u32[]{:S(2)}, u32[]{:S(2)}) collective-permute-start(f32[64,256]{1,0:T(8,128)} %get-tuple-element.55), channel_id=1, source_target_pairs={{0,7},{1,0},{2,1},{3,2},{4,3},{5,4},{6,5},{7,6},{8,15},{9,8},{10,9... | collective-permute-start | bytes 196616 | tf_op jit(solution)/shard_map/ppermute | solution.py:244
  74.5 0.7 collective-permute-start.12
  75.2 1.3 %collective-permute-done.12.lo_x_ref = f32[64,128]{1,0:T(8,128)S(1)} collective-permute-done((f32[64,128]{1,0:T(8,128)}, f32[64,128]{1,0:T(8,128)S(1)}, u32[]{:S(2)}, u32[]{:S(2)}) %collective-permute-start.12) | collective-permute-done | bytes 32800 | tf_op jit(solution)/shard_map/ppermute | solution.py:239
  76.5 2.2 %collective-permute-done.13.hi_x_ref = f32[64,128]{1,0:T(8,128)S(1)} collective-permute-done((f32[64,128]{1,0:T(8,128)}, f32[64,128]{1,0:T(8,128)S(1)}, u32[]{:S(2)}, u32[]{:S(2)}) %collective-permute-start.13) | collective-permute-done | bytes 32800 | tf_op jit(solution)/shard_map/ppermute | solution.py:240
  78.8 0.6 copy-done.32
  79.4 2.8 %shard_map.86 = (f32[64,512]{1,0:T(8,128)}, f32[64,128]{1,0:T(8,128)}, f32[64,128]{1,0:T(8,128)}, f32[64,256]{1,0:T(8,128)}, f32[64,256]{1,0:T(8,128)}) custom-call(f32[64,512]{1,0:T(8,128)} %get-tuple-element.51.other_ref, f32[64,128]{1,0:T(8,128)} %copy-done.27, f32[64,128]{1,0:T(8,128)} %copy-done.32, f32[64,256]{1,0:T(8,128)} %copy-done.11, ...), custom_call_target="tpu_custom_call" | custom-call | tf_op jit(solution)/shard_map/pallas_call | solution.py:219
  82.2 4.2 %collective-permute-start.19 = (f32[64,256]{1,0:T(8,128)}, f32[64,256]{1,0:T(8,128)S(1)}, u32[]{:S(2)}, u32[]{:S(2)}) collective-permute-start(f32[64,256]{1,0:T(8,128)} %get-tuple-element.60), channel_id=1, source_target_pairs={{0,7},{1,0},{2,1},{3,2},{4,3},{5,4},{6,5},{7,6},{8,15},{9,8},{10,9... | collective-permute-start | bytes 196616 | tf_op jit(solution)/shard_map/ppermute | solution.py:244
  86.4 0.7 collective-permute-start.16
  87.1 1.3 %collective-permute-done.16.lo_x_ref = f32[64,128]{1,0:T(8,128)S(1)} collective-permute-done((f32[64,128]{1,0:T(8,128)}, f32[64,128]{1,0:T(8,128)S(1)}, u32[]{:S(2)}, u32[]{:S(2)}) %collective-permute-start.16) | collective-permute-done | bytes 32800 | tf_op jit(solution)/shard_map/ppermute | solution.py:239
  88.4 2.2 %collective-permute-done.17.hi_x_ref = f32[64,128]{1,0:T(8,128)S(1)} collective-permute-done((f32[64,128]{1,0:T(8,128)}, f32[64,128]{1,0:T(8,128)S(1)}, u32[]{:S(2)}, u32[]{:S(2)}) %collective-permute-start.17) | collective-permute-done | bytes 32800 | tf_op jit(solution)/shard_map/ppermute | solution.py:240
  90.7 0.6 copy-done.33
  91.3 2.9 %shard_map.87 = (f32[64,512]{1,0:T(8,128)}, f32[64,128]{1,0:T(8,128)}, f32[64,128]{1,0:T(8,128)}, f32[64,256]{1,0:T(8,128)}, f32[64,256]{1,0:T(8,128)}) custom-call(f32[64,512]{1,0:T(8,128)} %get-tuple-element.56.other_ref, f32[64,128]{1,0:T(8,128)} %copy-done.28, f32[64,128]{1,0:T(8,128)} %copy-done.33, f32[64,256]{1,0:T(8,128)} %copy-done.12, ...), custom_call_target="tpu_custom_call" | custom-call | tf_op jit(solution)/shard_map/pallas_call | solution.py:219
  94.2 4.2 %collective-permute-start.23 = (f32[64,256]{1,0:T(8,128)}, f32[64,256]{1,0:T(8,128)S(1)}, u32[]{:S(2)}, u32[]{:S(2)}) collective-permute-start(f32[64,256]{1,0:T(8,128)} %get-tuple-element.65), channel_id=1, source_target_pairs={{0,7},{1,0},{2,1},{3,2},{4,3},{5,4},{6,5},{7,6},{8,15},{9,8},{10,9... | collective-permute-start | bytes 196616 | tf_op jit(solution)/shard_map/ppermute | solution.py:244
  98.3 0.7 collective-permute-start.20
  99.0 1.3 %collective-permute-done.20.lo_x_ref = f32[64,128]{1,0:T(8,128)S(1)} collective-permute-done((f32[64,128]{1,0:T(8,128)}, f32[64,128]{1,0:T(8,128)S(1)}, u32[]{:S(2)}, u32[]{:S(2)}) %collective-permute-start.20) | collective-permute-done | bytes 32800 | tf_op jit(solution)/shard_map/ppermute | solution.py:239
  100.3 2.2 %collective-permute-done.21.hi_x_ref = f32[64,128]{1,0:T(8,128)S(1)} collective-permute-done((f32[64,128]{1,0:T(8,128)}, f32[64,128]{1,0:T(8,128)S(1)}, u32[]{:S(2)}, u32[]{:S(2)}) %collective-permute-start.21) | collective-permute-done | bytes 32800 | tf_op jit(solution)/shard_map/ppermute | solution.py:240
  102.6 0.6 copy-done.34
  103.2 2.8 %shard_map.88 = (f32[64,512]{1,0:T(8,128)}, f32[64,128]{1,0:T(8,128)}, f32[64,128]{1,0:T(8,128)}, f32[64,256]{1,0:T(8,128)}, f32[64,256]{1,0:T(8,128)}) custom-call(f32[64,512]{1,0:T(8,128)} %get-tuple-element.61.other_ref, f32[64,128]{1,0:T(8,128)} %copy-done.29, f32[64,128]{1,0:T(8,128)} %copy-done.34, f32[64,256]{1,0:T(8,128)} %copy-done.13, ...), custom_call_target="tpu_custom_call" | custom-call | tf_op jit(solution)/shard_map/pallas_call | solution.py:219
  106.0 4.2 %collective-permute-start.27 = (f32[64,256]{1,0:T(8,128)}, f32[64,256]{1,0:T(8,128)S(1)}, u32[]{:S(2)}, u32[]{:S(2)}) collective-permute-start(f32[64,256]{1,0:T(8,128)} %get-tuple-element.70), channel_id=1, source_target_pairs={{0,7},{1,0},{2,1},{3,2},{4,3},{5,4},{6,5},{7,6},{8,15},{9,8},{10,9... | collective-permute-start | bytes 196616 | tf_op jit(solution)/shard_map/ppermute | solution.py:244
  110.2 0.7 collective-permute-start.24
  110.9 1.3 %collective-permute-done.24.lo_x_ref = f32[64,128]{1,0:T(8,128)S(1)} collective-permute-done((f32[64,128]{1,0:T(8,128)}, f32[64,128]{1,0:T(8,128)S(1)}, u32[]{:S(2)}, u32[]{:S(2)}) %collective-permute-start.24) | collective-permute-done | bytes 32800 | tf_op jit(solution)/shard_map/ppermute | solution.py:239
  112.2 2.2 %collective-permute-done.25.hi_x_ref = f32[64,128]{1,0:T(8,128)S(1)} collective-permute-done((f32[64,128]{1,0:T(8,128)}, f32[64,128]{1,0:T(8,128)S(1)}, u32[]{:S(2)}, u32[]{:S(2)}) %collective-permute-start.25) | collective-permute-done | bytes 32800 | tf_op jit(solution)/shard_map/ppermute | solution.py:240
  114.5 0.6 copy-done.30
  115.1 2.9 %shard_map.89 = (f32[64,512]{1,0:T(8,128)}, f32[64,128]{1,0:T(8,128)}, f32[64,128]{1,0:T(8,128)}, f32[64,256]{1,0:T(8,128)}, f32[64,256]{1,0:T(8,128)}) custom-call(f32[64,512]{1,0:T(8,128)} %get-tuple-element.66.other_ref, f32[64,128]{1,0:T(8,128)} %copy-done.25, f32[64,128]{1,0:T(8,128)} %copy-done.30, f32[64,256]{1,0:T(8,128)} %copy-done.9, ...), custom_call_target="tpu_custom_call" | custom-call | tf_op jit(solution)/shard_map/pallas_call | solution.py:219
  118.0 4.2 %collective-permute-start.31 = (f32[64,256]{1,0:T(8,128)}, f32[64,256]{1,0:T(8,128)S(1)}, u32[]{:S(2)}, u32[]{:S(2)}) collective-permute-start(f32[64,256]{1,0:T(8,128)} %get-tuple-element.75), channel_id=1, source_target_pairs={{0,7},{1,0},{2,1},{3,2},{4,3},{5,4},{6,5},{7,6},{8,15},{9,8},{10,9... | collective-permute-start | bytes 196616 | tf_op jit(solution)/shard_map/ppermute | solution.py:244
  122.1 0.7 collective-permute-start.28
  122.8 1.0 reshape.158
  124.1 2.2 %collective-permute-done.29.hi_x_ref = f32[64,128]{1,0:T(8,128)S(1)} collective-permute-done((f32[64,128]{1,0:T(8,128)}, f32[64,128]{1,0:T(8,128)S(1)}, u32[]{:S(2)}, u32[]{:S(2)}) %collective-permute-start.29) | collective-permute-done | bytes 32800 | tf_op jit(solution)/shard_map/ppermute | solution.py:240
  126.4 0.6 copy-done.24
  127.0 0.6 copy-done.8
  127.6 2.8 %shard_map.90 = (f32[64,512]{1,0:T(8,128)}, f32[64,128]{1,0:T(8,128)}, f32[64,128]{1,0:T(8,128)}, f32[64,256]{1,0:T(8,128)}, f32[64,256]{1,0:T(8,128)}) custom-call(f32[64,512]{1,0:T(8,128)} %get-tuple-element.71.other_ref, f32[64,128]{1,0:T(8,128)} %copy-done.23, f32[64,128]{1,0:T(8,128)} %copy-done.24, f32[64,256]{1,0:T(8,128)} %copy-done.7, ...), custom_call_target="tpu_custom_call" | custom-call | tf_op jit(solution)/shard_map/pallas_call | solution.py:219
  130.4 1.0 reshape.160
  132.0 0.9 copy.73
  (145 shorter events, 6.2 us)
Async XLA Ops:
  0.0 0.7 slice-start
  3.2 1.0 copy-start
  5.8 35.7 %collective-permute-start.2 = (f32[64,256]{1,0:T(8,128)S(1)}, f32[64,256]{1,0:T(8,128)S(1)}, u32[]{:S(2)}, u32[]{:S(2)}) collective-permute-start(f32[64,256]{1,0:T(8,128)S(1)} %reshape_squeeze.14), channel_id=1, source_target_pairs={{0,1},{1,2},{2,3},{3,4},{4,5},{5,6},{6,7},{7,0},{8,9},{9,10},{10,1... | collective-permute-start | bytes 196616 | tf_op jit(solution)/shard_map/ppermute | solution.py:243
  8.1 33.3 %collective-permute-start.3 = (f32[64,256]{1,0:T(8,128)S(1)}, f32[64,256]{1,0:T(8,128)S(1)}, u32[]{:S(2)}, u32[]{:S(2)}) collective-permute-start(f32[64,256]{1,0:T(8,128)S(1)} %reshape_squeeze.15), channel_id=1, source_target_pairs={{0,7},{1,0},{2,1},{3,2},{4,3},{5,4},{6,5},{7,6},{8,15},{9,8},{10,9... | collective-permute-start | bytes 196616 | tf_op jit(solution)/shard_map/ppermute | solution.py:244
  11.2 2.6 %copy-start.1 = (f32[4,2,2,4096]{3,2,1,0:T(2,128)S(1)}, f32[4,2,2,4096]{3,2,1,0:T(2,128)}, u32[]{:S(2)}) copy-start(f32[4,2,2,4096]{3,2,1,0:T(2,128)} %param.10) | copy-start | bytes 786436
  11.4 30.0 %collective-permute-start = (f32[64,128]{1,0:T(8,128)S(1)}, f32[64,128]{1,0:T(8,128)S(1)}, u32[]{:S(2)}, u32[]{:S(2)}) collective-permute-start(f32[64,128]{1,0:T(8,128)S(1)} %reshape_squeeze.12), channel_id=1, source_target_pairs={{0,8},{8,16},{16,24},{24,0},{1,9},{9,17},{17,25},{25,1},{2,10},{10... | collective-permute-start | bytes 98312 | tf_op jit(solution)/shard_map/ppermute | solution.py:239
  13.7 27.7 %collective-permute-start.1 = (f32[64,128]{1,0:T(8,128)S(1)}, f32[64,128]{1,0:T(8,128)S(1)}, u32[]{:S(2)}, u32[]{:S(2)}) collective-permute-start(f32[64,128]{1,0:T(8,128)S(1)} %reshape_squeeze.13), channel_id=1, source_target_pairs={{0,24},{8,0},{16,8},{24,16},{1,25},{9,1},{17,9},{25,17},{2,26},{10... | collective-permute-start | bytes 98312 | tf_op jit(solution)/shard_map/ppermute | solution.py:240
  36.9 0.8 copy-start.35
  36.9 0.8 copy-start.36
  37.0 0.8 copy-start.37
  38.9 1.6 %copy-start.2 = (f32[6,64,64]{2,1,0:T(8,128)S(1)}, f32[6,64,64]{2,1,0:T(8,128)}, u32[]{:S(2)}) copy-start(f32[6,64,64]{2,1,0:T(8,128)} %param.11) | copy-start | bytes 294916
  41.4 0.6 copy-start.19
  41.4 0.6 copy-start.20
  41.4 0.6 copy-start.3
  41.5 0.6 copy-start.4
  44.9 10.0 %collective-permute-start.6 = (f32[64,256]{1,0:T(8,128)}, f32[64,256]{1,0:T(8,128)S(1)}, u32[]{:S(2)}, u32[]{:S(2)}) collective-permute-start(f32[64,256]{1,0:T(8,128)} %get-tuple-element.44), channel_id=1, source_target_pairs={{0,1},{1,2},{2,3},{3,4},{4,5},{5,6},{6,7},{7,0},{8,9},{9,10},{10,1... | collective-permute-start | bytes 196616 | tf_op jit(solution)/shard_map/ppermute | solution.py:243
  44.9 10.0 %collective-permute-start.7 = (f32[64,256]{1,0:T(8,128)}, f32[64,256]{1,0:T(8,128)S(1)}, u32[]{:S(2)}, u32[]{:S(2)}) collective-permute-start(f32[64,256]{1,0:T(8,128)} %get-tuple-element.45), channel_id=1, source_target_pairs={{0,7},{1,0},{2,1},{3,2},{4,3},{5,4},{6,5},{7,6},{8,15},{9,8},{10,9... | collective-permute-start | bytes 196616 | tf_op jit(solution)/shard_map/ppermute | solution.py:244
  49.1 4.1 %collective-permute-start.4 = (f32[64,128]{1,0:T(8,128)}, f32[64,128]{1,0:T(8,128)S(1)}, u32[]{:S(2)}, u32[]{:S(2)}) collective-permute-start(f32[64,128]{1,0:T(8,128)} %get-tuple-element.42), channel_id=1, source_target_pairs={{0,8},{8,16},{16,24},{24,0},{1,9},{9,17},{17,25},{25,1},{2,10},{10... | collective-permute-start | bytes 98312 | tf_op jit(solution)/shard_map/ppermute | solution.py:239
  51.4 3.6 %collective-permute-start.5 = (f32[64,128]{1,0:T(8,128)}, f32[64,128]{1,0:T(8,128)S(1)}, u32[]{:S(2)}, u32[]{:S(2)}) collective-permute-start(f32[64,128]{1,0:T(8,128)} %get-tuple-element.43), channel_id=1, source_target_pairs={{0,24},{8,0},{16,8},{24,16},{1,25},{9,1},{17,9},{25,17},{2,26},{10... | collective-permute-start | bytes 98312 | tf_op jit(solution)/shard_map/ppermute | solution.py:240
  53.2 1.8 %copy-start.21 = (f32[64,128]{1,0:T(8,128)}, f32[64,128]{1,0:T(8,128)S(1)}, u32[]{:S(2)}) copy-start(f32[64,128]{1,0:T(8,128)S(1)} %collective-permute-done.4.lo_x_ref) | copy-start | bytes 98308
  54.9 0.6 copy-start.5
  54.9 0.7 copy-start.6
  58.4 8.4 %collective-permute-start.10 = (f32[64,256]{1,0:T(8,128)}, f32[64,256]{1,0:T(8,128)S(1)}, u32[]{:S(2)}, u32[]{:S(2)}) collective-permute-start(f32[64,256]{1,0:T(8,128)} %get-tuple-element.49), channel_id=1, source_target_pairs={{0,1},{1,2},{2,3},{3,4},{4,5},{5,6},{6,7},{7,0},{8,9},{9,10},{10,1... | collective-permute-start | bytes 196616 | tf_op jit(solution)/shard_map/ppermute | solution.py:243
  58.4 8.4 %collective-permute-start.11 = (f32[64,256]{1,0:T(8,128)}, f32[64,256]{1,0:T(8,128)S(1)}, u32[]{:S(2)}, u32[]{:S(2)}) collective-permute-start(f32[64,256]{1,0:T(8,128)} %get-tuple-element.50), channel_id=1, source_target_pairs={{0,7},{1,0},{2,1},{3,2},{4,3},{5,4},{6,5},{7,6},{8,15},{9,8},{10,9... | collective-permute-start | bytes 196616 | tf_op jit(solution)/shard_map/ppermute | solution.py:244
  62.6 2.0 %collective-permute-start.8 = (f32[64,128]{1,0:T(8,128)}, f32[64,128]{1,0:T(8,128)S(1)}, u32[]{:S(2)}, u32[]{:S(2)}) collective-permute-start(f32[64,128]{1,0:T(8,128)} %get-tuple-element.47), channel_id=1, source_target_pairs={{0,8},{8,16},{16,24},{24,0},{1,9},{9,17},{17,25},{25,1},{2,10},{10... | collective-permute-start | bytes 98312 | tf_op jit(solution)/shard_map/ppermute | solution.py:239
  63.3 3.6 %collective-permute-start.9 = (f32[64,128]{1,0:T(8,128)}, f32[64,128]{1,0:T(8,128)S(1)}, u32[]{:S(2)}, u32[]{:S(2)}) collective-permute-start(f32[64,128]{1,0:T(8,128)} %get-tuple-element.48), channel_id=1, source_target_pairs={{0,24},{8,0},{16,8},{24,16},{1,25},{9,1},{17,9},{25,17},{2,26},{10... | collective-permute-start | bytes 98312 | tf_op jit(solution)/shard_map/ppermute | solution.py:240
  64.6 2.2 %copy-start.26 = (f32[64,128]{1,0:T(8,128)}, f32[64,128]{1,0:T(8,128)S(1)}, u32[]{:S(2)}) copy-start(f32[64,128]{1,0:T(8,128)S(1)} %collective-permute-done.8.lo_x_ref) | copy-start | bytes 98308
  66.8 0.6 copy-start.10
  66.8 0.7 copy-start.15
  70.3 8.4 %collective-permute-start.14 = (f32[64,256]{1,0:T(8,128)}, f32[64,256]{1,0:T(8,128)S(1)}, u32[]{:S(2)}, u32[]{:S(2)}) collective-permute-start(f32[64,256]{1,0:T(8,128)} %get-tuple-element.54), channel_id=1, source_target_pairs={{0,1},{1,2},{2,3},{3,4},{4,5},{5,6},{6,7},{7,0},{8,9},{9,10},{10,1... | collective-permute-start | bytes 196616 | tf_op jit(solution)/shard_map/ppermute | solution.py:243
  70.4 8.4 %collective-permute-start.15 = (f32[64,256]{1,0:T(8,128)}, f32[64,256]{1,0:T(8,128)S(1)}, u32[]{:S(2)}, u32[]{:S(2)}) collective-permute-start(f32[64,256]{1,0:T(8,128)} %get-tuple-element.55), channel_id=1, source_target_pairs={{0,7},{1,0},{2,1},{3,2},{4,3},{5,4},{6,5},{7,6},{8,15},{9,8},{10,9... | collective-permute-start | bytes 196616 | tf_op jit(solution)/shard_map/ppermute | solution.py:244
  74.5 2.0 %collective-permute-start.12 = (f32[64,128]{1,0:T(8,128)}, f32[64,128]{1,0:T(8,128)S(1)}, u32[]{:S(2)}, u32[]{:S(2)}) collective-permute-start(f32[64,128]{1,0:T(8,128)} %get-tuple-element.52), channel_id=1, source_target_pairs={{0,8},{8,16},{16,24},{24,0},{1,9},{9,17},{17,25},{25,1},{2,10},{10... | collective-permute-start | bytes 98312 | tf_op jit(solution)/shard_map/ppermute | solution.py:239
  75.2 3.6 %collective-permute-start.13 = (f32[64,128]{1,0:T(8,128)}, f32[64,128]{1,0:T(8,128)S(1)}, u32[]{:S(2)}, u32[]{:S(2)}) collective-permute-start(f32[64,128]{1,0:T(8,128)} %get-tuple-element.53), channel_id=1, source_target_pairs={{0,24},{8,0},{16,8},{24,16},{1,25},{9,1},{17,9},{25,17},{2,26},{10... | collective-permute-start | bytes 98312 | tf_op jit(solution)/shard_map/ppermute | solution.py:240
  76.5 2.2 %copy-start.27 = (f32[64,128]{1,0:T(8,128)}, f32[64,128]{1,0:T(8,128)S(1)}, u32[]{:S(2)}) copy-start(f32[64,128]{1,0:T(8,128)S(1)} %collective-permute-done.12.lo_x_ref) | copy-start | bytes 98308
  78.7 0.6 copy-start.11
  78.7 0.7 copy-start.16
  82.2 8.4 %collective-permute-start.18 = (f32[64,256]{1,0:T(8,128)}, f32[64,256]{1,0:T(8,128)S(1)}, u32[]{:S(2)}, u32[]{:S(2)}) collective-permute-start(f32[64,256]{1,0:T(8,128)} %get-tuple-element.59), channel_id=1, source_target_pairs={{0,1},{1,2},{2,3},{3,4},{4,5},{5,6},{6,7},{7,0},{8,9},{9,10},{10,1... | collective-permute-start | bytes 196616 | tf_op jit(solution)/shard_map/ppermute | solution.py:243
  82.2 8.4 %collective-permute-start.19 = (f32[64,256]{1,0:T(8,128)}, f32[64,256]{1,0:T(8,128)S(1)}, u32[]{:S(2)}, u32[]{:S(2)}) collective-permute-start(f32[64,256]{1,0:T(8,128)} %get-tuple-element.60), channel_id=1, source_target_pairs={{0,7},{1,0},{2,1},{3,2},{4,3},{5,4},{6,5},{7,6},{8,15},{9,8},{10,9... | collective-permute-start | bytes 196616 | tf_op jit(solution)/shard_map/ppermute | solution.py:244
  86.4 2.0 %collective-permute-start.16 = (f32[64,128]{1,0:T(8,128)}, f32[64,128]{1,0:T(8,128)S(1)}, u32[]{:S(2)}, u32[]{:S(2)}) collective-permute-start(f32[64,128]{1,0:T(8,128)} %get-tuple-element.57), channel_id=1, source_target_pairs={{0,8},{8,16},{16,24},{24,0},{1,9},{9,17},{17,25},{25,1},{2,10},{10... | collective-permute-start | bytes 98312 | tf_op jit(solution)/shard_map/ppermute | solution.py:239
  87.1 3.6 %collective-permute-start.17 = (f32[64,128]{1,0:T(8,128)}, f32[64,128]{1,0:T(8,128)S(1)}, u32[]{:S(2)}, u32[]{:S(2)}) collective-permute-start(f32[64,128]{1,0:T(8,128)} %get-tuple-element.58), channel_id=1, source_target_pairs={{0,24},{8,0},{16,8},{24,16},{1,25},{9,1},{17,9},{25,17},{2,26},{10... | collective-permute-start | bytes 98312 | tf_op jit(solution)/shard_map/ppermute | solution.py:240
  88.4 2.2 %copy-start.28 = (f32[64,128]{1,0:T(8,128)}, f32[64,128]{1,0:T(8,128)S(1)}, u32[]{:S(2)}) copy-start(f32[64,128]{1,0:T(8,128)S(1)} %collective-permute-done.16.lo_x_ref) | copy-start | bytes 98308
  90.6 0.6 copy-start.12
  90.6 0.7 copy-start.17
  94.2 8.4 %collective-permute-start.22 = (f32[64,256]{1,0:T(8,128)}, f32[64,256]{1,0:T(8,128)S(1)}, u32[]{:S(2)}, u32[]{:S(2)}) collective-permute-start(f32[64,256]{1,0:T(8,128)} %get-tuple-element.64), channel_id=1, source_target_pairs={{0,1},{1,2},{2,3},{3,4},{4,5},{5,6},{6,7},{7,0},{8,9},{9,10},{10,1... | collective-permute-start | bytes 196616 | tf_op jit(solution)/shard_map/ppermute | solution.py:243
  94.2 8.4 %collective-permute-start.23 = (f32[64,256]{1,0:T(8,128)}, f32[64,256]{1,0:T(8,128)S(1)}, u32[]{:S(2)}, u32[]{:S(2)}) collective-permute-start(f32[64,256]{1,0:T(8,128)} %get-tuple-element.65), channel_id=1, source_target_pairs={{0,7},{1,0},{2,1},{3,2},{4,3},{5,4},{6,5},{7,6},{8,15},{9,8},{10,9... | collective-permute-start | bytes 196616 | tf_op jit(solution)/shard_map/ppermute | solution.py:244
  98.3 2.0 %collective-permute-start.20 = (f32[64,128]{1,0:T(8,128)}, f32[64,128]{1,0:T(8,128)S(1)}, u32[]{:S(2)}, u32[]{:S(2)}) collective-permute-start(f32[64,128]{1,0:T(8,128)} %get-tuple-element.62), channel_id=1, source_target_pairs={{0,8},{8,16},{16,24},{24,0},{1,9},{9,17},{17,25},{25,1},{2,10},{10... | collective-permute-start | bytes 98312 | tf_op jit(solution)/shard_map/ppermute | solution.py:239
  99.0 3.6 %collective-permute-start.21 = (f32[64,128]{1,0:T(8,128)}, f32[64,128]{1,0:T(8,128)S(1)}, u32[]{:S(2)}, u32[]{:S(2)}) collective-permute-start(f32[64,128]{1,0:T(8,128)} %get-tuple-element.63), channel_id=1, source_target_pairs={{0,24},{8,0},{16,8},{24,16},{1,25},{9,1},{17,9},{25,17},{2,26},{10... | collective-permute-start | bytes 98312 | tf_op jit(solution)/shard_map/ppermute | solution.py:240
  100.3 2.2 %copy-start.29 = (f32[64,128]{1,0:T(8,128)}, f32[64,128]{1,0:T(8,128)S(1)}, u32[]{:S(2)}) copy-start(f32[64,128]{1,0:T(8,128)S(1)} %collective-permute-done.20.lo_x_ref) | copy-start | bytes 98308
  102.5 0.6 copy-start.13
  102.5 0.7 copy-start.18
  106.0 8.4 %collective-permute-start.26 = (f32[64,256]{1,0:T(8,128)}, f32[64,256]{1,0:T(8,128)S(1)}, u32[]{:S(2)}, u32[]{:S(2)}) collective-permute-start(f32[64,256]{1,0:T(8,128)} %get-tuple-element.69), channel_id=1, source_target_pairs={{0,1},{1,2},{2,3},{3,4},{4,5},{5,6},{6,7},{7,0},{8,9},{9,10},{10,1... | collective-permute-start | bytes 196616 | tf_op jit(solution)/shard_map/ppermute | solution.py:243
  106.0 8.4 %collective-permute-start.27 = (f32[64,256]{1,0:T(8,128)}, f32[64,256]{1,0:T(8,128)S(1)}, u32[]{:S(2)}, u32[]{:S(2)}) collective-permute-start(f32[64,256]{1,0:T(8,128)} %get-tuple-element.70), channel_id=1, source_target_pairs={{0,7},{1,0},{2,1},{3,2},{4,3},{5,4},{6,5},{7,6},{8,15},{9,8},{10,9... | collective-permute-start | bytes 196616 | tf_op jit(solution)/shard_map/ppermute | solution.py:244
  110.2 2.0 %collective-permute-start.24 = (f32[64,128]{1,0:T(8,128)}, f32[64,128]{1,0:T(8,128)S(1)}, u32[]{:S(2)}, u32[]{:S(2)}) collective-permute-start(f32[64,128]{1,0:T(8,128)} %get-tuple-element.67), channel_id=1, source_target_pairs={{0,8},{8,16},{16,24},{24,0},{1,9},{9,17},{17,25},{25,1},{2,10},{10... | collective-permute-start | bytes 98312 | tf_op jit(solution)/shard_map/ppermute | solution.py:239
  110.9 3.6 %collective-permute-start.25 = (f32[64,128]{1,0:T(8,128)}, f32[64,128]{1,0:T(8,128)S(1)}, u32[]{:S(2)}, u32[]{:S(2)}) collective-permute-start(f32[64,128]{1,0:T(8,128)} %get-tuple-element.68), channel_id=1, source_target_pairs={{0,24},{8,0},{16,8},{24,16},{1,25},{9,1},{17,9},{25,17},{2,26},{10... | collective-permute-start | bytes 98312 | tf_op jit(solution)/shard_map/ppermute | solution.py:240
  112.2 2.2 %copy-start.25 = (f32[64,128]{1,0:T(8,128)}, f32[64,128]{1,0:T(8,128)S(1)}, u32[]{:S(2)}) copy-start(f32[64,128]{1,0:T(8,128)S(1)} %collective-permute-done.24.lo_x_ref) | copy-start | bytes 98308
  114.4 0.6 copy-start.9
  114.4 0.7 copy-start.14
  118.0 8.4 %collective-permute-start.30 = (f32[64,256]{1,0:T(8,128)}, f32[64,256]{1,0:T(8,128)S(1)}, u32[]{:S(2)}, u32[]{:S(2)}) collective-permute-start(f32[64,256]{1,0:T(8,128)} %get-tuple-element.74), channel_id=1, source_target_pairs={{0,1},{1,2},{2,3},{3,4},{4,5},{5,6},{6,7},{7,0},{8,9},{9,10},{10,1... | collective-permute-start | bytes 196616 | tf_op jit(solution)/shard_map/ppermute | solution.py:243
  118.0 8.4 %collective-permute-start.31 = (f32[64,256]{1,0:T(8,128)}, f32[64,256]{1,0:T(8,128)S(1)}, u32[]{:S(2)}, u32[]{:S(2)}) collective-permute-start(f32[64,256]{1,0:T(8,128)} %get-tuple-element.75), channel_id=1, source_target_pairs={{0,7},{1,0},{2,1},{3,2},{4,3},{5,4},{6,5},{7,6},{8,15},{9,8},{10,9... | collective-permute-start | bytes 196616 | tf_op jit(solution)/shard_map/ppermute | solution.py:244
  122.1 2.0 %collective-permute-start.28 = (f32[64,128]{1,0:T(8,128)}, f32[64,128]{1,0:T(8,128)S(1)}, u32[]{:S(2)}, u32[]{:S(2)}) collective-permute-start(f32[64,128]{1,0:T(8,128)} %get-tuple-element.72), channel_id=1, source_target_pairs={{0,8},{8,16},{16,24},{24,0},{1,9},{9,17},{17,25},{25,1},{2,10},{10... | collective-permute-start | bytes 98312 | tf_op jit(solution)/shard_map/ppermute | solution.py:239
  122.8 3.6 %collective-permute-start.29 = (f32[64,128]{1,0:T(8,128)}, f32[64,128]{1,0:T(8,128)S(1)}, u32[]{:S(2)}, u32[]{:S(2)}) collective-permute-start(f32[64,128]{1,0:T(8,128)} %get-tuple-element.73), channel_id=1, source_target_pairs={{0,24},{8,0},{16,8},{24,16},{1,25},{9,1},{17,9},{25,17},{2,26},{10... | collective-permute-start | bytes 98312 | tf_op jit(solution)/shard_map/ppermute | solution.py:240
  124.1 2.2 %copy-start.23 = (f32[64,128]{1,0:T(8,128)}, f32[64,128]{1,0:T(8,128)S(1)}, u32[]{:S(2)}) copy-start(f32[64,128]{1,0:T(8,128)S(1)} %collective-permute-done.28.lo_x_ref) | copy-start | bytes 98308
  126.3 0.6 copy-start.7
  127.0 0.6 copy-start.8
  (7 other events, 4.2 us)

commit v3 on v2

--- a/solution.py
+++ b/solution.py
@@ -189,7 +189,9 @@
         other,
         other,
     ]
-    stacked = jnp.concatenate([weight_ref[face] * nearby[face] for face in range(6)], axis=0)
+    stacked = jnp.concatenate(
+        [weight_ref[face:face + 1, :] * nearby[face] for face in range(6)], axis=0
+    )
     coupled = jnp.dot(face_ref[...], stacked, precision=highest, preferred_element_type=jnp.float32)
     rhs = target_ref[...] - coupled
     outs = []
@@ -277,9 +279,12 @@
     face_row = jnp.transpose(face_blocks, (1, 0, 2)).reshape(P_SIZE, 6 * P_SIZE)
     member_target = [to_lanes(pick(forcing, paint)) for paint in (0, 1)]
     member_weight = [
-        jnp.repeat(pick(weight, paint, axis=3).reshape(6, columns), R, axis=1).reshape(6, 1, columns * R)
+        jnp.pad(jnp.repeat(pick(weight, paint, axis=3).reshape(6, columns), R, axis=1), ((0, 2), (0, 0)))
         for paint in (0, 1)
     ]
+    member_inverse, member_target, member_weight, face_row = lax.optimization_barrier(
+        (member_inverse, member_target, member_weight, face_row)
+    )
     state = [None, start_state]
     sends = None
     for sweep_index in range(SWEEPS):

time: 133 us -> 136 us (1.023)
  waiting for transfers between devices: 21.9 us -> 23.6 us
    another operation x2 -> x0, local copies, waits for them, and re-layouts: 1.37 us -> none  [lane_body(): jnp.repeat(pick(weight, paint, axis=3).reshape(6, columns), R, axis=1)]
  transfers between devices with their start and end apart: 32 -> 32, of which waited for: 13 -> 14; matrix products, arithmetic and copies ran while one was open for 9% -> 9% of each run, Pallas kernels for 14% -> 14%
where the time goes in v3:
time: 136 us; the launch traced here: 135 us
  starting transfers between devices  42.9 us (32%)
  Pallas kernels  41.9 us (31%)
  local copies, waits for them, and re-layouts  25.2 us (19%)
  waiting for transfers between devices  23.6 us (17%)
    ppermute x8, starting transfers between devices, trade(): lax.ppermute(sends[3], 'gy', shift_pairs('gy', -1))  32.2 us
    pallas_call x8, Pallas kernels, half_sweep(): pl.pallas_call(functools.partial(_half_sweep_kernel, span_x=span_x), out_...  22.7 us
    pallas_call x1, Pallas kernels, block_inverses(): pl.pallas_call(functools.partial(_gauss_jordan_kernel, n=n, nb=nb), out_s...  19.2 us
    ppermute x8, waiting for transfers between devices, trade(): lax.ppermute(sends[1], 'gx', shift_pairs('gx', -1))  15.5 us
    ppermute x8, starting transfers between devices, trade(): lax.ppermute(sends[0], 'gx', shift_pairs('gx', 1))  8.56 us
    ppermute x8, waiting for transfers between devices, trade(): lax.ppermute(sends[0], 'gx', shift_pairs('gx', 1))  8.15 us
    unnamed x80, local copies, waits for them, and re-layouts  7.35 us
    slice x3, local copies, waits for them, and re-layouts, pick(): high = lax.index_in_dim(values, 1, axis=axis, keepdims=False)  2.73 us
  transfers between devices with their start and end apart: 32, of which 14 were waited for; matrix products, arithmetic and copies ran while one was open for 9% of the time, Pallas kernels for 14%

profile of v3, /device:TPU:1, one launch (start us, length us, event | category | flops | bytes accessed | tf_op | source)
XLA Modules:
  0.0 135.2 jit_solution(16517529505733144584)
XLA Ops:
  0.0 0.7 slice-done
  1.1 1.9 %slice_reduce_fusion.2 = (f32[4,2,4096]{2,1,0:T(2,128)S(1)}, f32[4,2,4096]{2,1,0:T(2,128)S(1)}) fusion(f32[4,2,2,4096]{3,2,1,0:T(2,128)} %param.9), kind=kLoop, calls=%fused_computation.10 | loop fusion | bytes 524288 | tf_op jit(solution)/shard_map/slice | solution.py:267
  3.4 0.7 copy-done
  4.2 0.8 slice_reduce_fusion
  5.8 2.1 %collective-permute-start.2 = (f32[64,256]{1,0:T(8,128)S(1)}, f32[64,256]{1,0:T(8,128)S(1)}, u32[]{:S(2)}, u32[]{:S(2)}) collective-permute-start(f32[64,256]{1,0:T(8,128)S(1)} %reshape_squeeze.14), channel_id=1, source_target_pairs={{0,1},{1,2},{2,3},{3,4},{4,5},{5,6},{6,7},{7,0},{8,9},{9,10},{10,1... | collective-permute-start | bytes 196616 | tf_op jit(solution)/shard_map/ppermute | solution.py:245
  8.1 3.1 %collective-permute-start.3 = (f32[64,256]{1,0:T(8,128)S(1)}, f32[64,256]{1,0:T(8,128)S(1)}, u32[]{:S(2)}, u32[]{:S(2)}) collective-permute-start(f32[64,256]{1,0:T(8,128)S(1)} %reshape_squeeze.15), channel_id=1, source_target_pairs={{0,7},{1,0},{2,1},{3,2},{4,3},{5,4},{6,5},{7,6},{8,15},{9,8},{10,9... | collective-permute-start | bytes 196616 | tf_op jit(solution)/shard_map/ppermute | solution.py:246
  11.4 2.2 %collective-permute-start = (f32[64,128]{1,0:T(8,128)S(1)}, f32[64,128]{1,0:T(8,128)S(1)}, u32[]{:S(2)}, u32[]{:S(2)}) collective-permute-start(f32[64,128]{1,0:T(8,128)S(1)} %reshape_squeeze.12), channel_id=1, source_target_pairs={{0,8},{8,16},{16,24},{24,0},{1,9},{9,17},{17,25},{25,1},{2,10},{10... | collective-permute-start | bytes 98312 | tf_op jit(solution)/shard_map/ppermute | solution.py:241
  15.2 0.9 copy.62.a_ref
  16.1 19.2 %shard_map.82 = f32[64,1024]{1,0:T(8,128)} custom-call(f32[64,1024]{1,0:T(8,128)} %copy.62.a_ref), custom_call_target="tpu_custom_call" | custom-call | flops 8388608000 | bytes 524288 | tf_op jit(solution)/shard_map/pallas_call | solution.py:75
  35.2 1.1 copy.63
  37.0 0.7 fusion
  38.0 0.8 reshape.161.target_ref
  38.9 0.8 reshape.162.target_ref
  40.1 0.6 pad.7.weight_ref
  40.7 0.6 pad.8.weight_ref
  41.5 0.7 reshape.165.face_ref
  42.4 0.8 reshape.156.other_ref
  43.8 0.6 copy-done.4
  44.4 2.8 %shard_map.83 = (f32[64,512]{1,0:T(8,128)}, f32[64,128]{1,0:T(8,128)}, f32[64,128]{1,0:T(8,128)}, f32[64,256]{1,0:T(8,128)}, f32[64,256]{1,0:T(8,128)}) custom-call(f32[64,512]{1,0:T(8,128)} %reshape.156.other_ref, f32[64,128]{1,0:T(8,128)} %copy-done.19, f32[64,128]{1,0:T(8,128)} %copy-done.20, f32[64,256]{1,0:T(8,128)} %copy-done.3, f32[64,256]{1,0:T(8,128)} %copy-done.4, ...), custom_call_target="tpu_custom_call" | custom-call | tf_op jit(solution)/shard_map/pallas_call | solution.py:221
  47.3 4.2 %collective-permute-start.7 = (f32[64,256]{1,0:T(8,128)}, f32[64,256]{1,0:T(8,128)S(1)}, u32[]{:S(2)}, u32[]{:S(2)}) collective-permute-start(f32[64,256]{1,0:T(8,128)} %get-tuple-element.56), channel_id=1, source_target_pairs={{0,7},{1,0},{2,1},{3,2},{4,3},{5,4},{6,5},{7,6},{8,15},{9,8},{10,9... | collective-permute-start | bytes 196616 | tf_op jit(solution)/shard_map/ppermute | solution.py:246
  51.4 2.3 %collective-permute-start.4 = (f32[64,128]{1,0:T(8,128)}, f32[64,128]{1,0:T(8,128)S(1)}, u32[]{:S(2)}, u32[]{:S(2)}) collective-permute-start(f32[64,128]{1,0:T(8,128)} %get-tuple-element.53), channel_id=1, source_target_pairs={{0,8},{8,16},{16,24},{24,0},{1,9},{9,17},{17,25},{25,1},{2,10},{10... | collective-permute-start | bytes 98312 | tf_op jit(solution)/shard_map/ppermute | solution.py:241
  53.7 1.3 collective-permute-done.4.lo_x_ref
  55.0 2.2 %collective-permute-done.5.hi_x_ref = f32[64,128]{1,0:T(8,128)S(1)} collective-permute-done((f32[64,128]{1,0:T(8,128)}, f32[64,128]{1,0:T(8,128)S(1)}, u32[]{:S(2)}, u32[]{:S(2)}) %collective-permute-start.5) | collective-permute-done | bytes 32800 | tf_op jit(solution)/shard_map/ppermute | solution.py:242
  57.3 0.6 copy-done.30
  57.9 2.8 %shard_map.84 = (f32[64,512]{1,0:T(8,128)}, f32[64,128]{1,0:T(8,128)}, f32[64,128]{1,0:T(8,128)}, f32[64,256]{1,0:T(8,128)}, f32[64,256]{1,0:T(8,128)}) custom-call(f32[64,512]{1,0:T(8,128)} %get-tuple-element.52.other_ref, f32[64,128]{1,0:T(8,128)} %copy-done.24, f32[64,128]{1,0:T(8,128)} %copy-done.30, f32[64,256]{1,0:T(8,128)} %copy-done.8, ...), custom_call_target="tpu_custom_call" | custom-call | tf_op jit(solution)/shard_map/pallas_call | solution.py:221
  60.8 4.2 %collective-permute-start.11 = (f32[64,256]{1,0:T(8,128)}, f32[64,256]{1,0:T(8,128)S(1)}, u32[]{:S(2)}, u32[]{:S(2)}) collective-permute-start(f32[64,256]{1,0:T(8,128)} %get-tuple-element.64), channel_id=1, source_target_pairs={{0,7},{1,0},{2,1},{3,2},{4,3},{5,4},{6,5},{7,6},{8,15},{9,8},{10,9... | collective-permute-start | bytes 196616 | tf_op jit(solution)/shard_map/ppermute | solution.py:246
  64.9 0.7 collective-permute-start.8
  65.6 1.3 collective-permute-done.8.lo_x_ref
  67.0 2.2 %collective-permute-done.9.hi_x_ref = f32[64,128]{1,0:T(8,128)S(1)} collective-permute-done((f32[64,128]{1,0:T(8,128)}, f32[64,128]{1,0:T(8,128)S(1)}, u32[]{:S(2)}, u32[]{:S(2)}) %collective-permute-start.9) | collective-permute-done | bytes 32800 | tf_op jit(solution)/shard_map/ppermute | solution.py:242
  69.2 0.6 copy-done.31
  69.8 2.8 %shard_map.85 = (f32[64,512]{1,0:T(8,128)}, f32[64,128]{1,0:T(8,128)}, f32[64,128]{1,0:T(8,128)}, f32[64,256]{1,0:T(8,128)}, f32[64,256]{1,0:T(8,128)}) custom-call(f32[64,512]{1,0:T(8,128)} %get-tuple-element.60.other_ref, f32[64,128]{1,0:T(8,128)} %copy-done.25, f32[64,128]{1,0:T(8,128)} %copy-done.31, f32[64,256]{1,0:T(8,128)} %copy-done.9, ...), custom_call_target="tpu_custom_call" | custom-call | tf_op jit(solution)/shard_map/pallas_call | solution.py:221
  72.7 4.2 %collective-permute-start.15 = (f32[64,256]{1,0:T(8,128)}, f32[64,256]{1,0:T(8,128)S(1)}, u32[]{:S(2)}, u32[]{:S(2)}) collective-permute-start(f32[64,256]{1,0:T(8,128)} %get-tuple-element.69), channel_id=1, source_target_pairs={{0,7},{1,0},{2,1},{3,2},{4,3},{5,4},{6,5},{7,6},{8,15},{9,8},{10,9... | collective-permute-start | bytes 196616 | tf_op jit(solution)/shard_map/ppermute | solution.py:246
  76.8 0.7 collective-permute-start.12
  77.5 1.3 collective-permute-done.12.lo_x_ref
  78.9 2.2 %collective-permute-done.13.hi_x_ref = f32[64,128]{1,0:T(8,128)S(1)} collective-permute-done((f32[64,128]{1,0:T(8,128)}, f32[64,128]{1,0:T(8,128)S(1)}, u32[]{:S(2)}, u32[]{:S(2)}) %collective-permute-start.13) | collective-permute-done | bytes 32800 | tf_op jit(solution)/shard_map/ppermute | solution.py:242
  81.1 0.6 copy-done.32
  81.7 2.8 %shard_map.86 = (f32[64,512]{1,0:T(8,128)}, f32[64,128]{1,0:T(8,128)}, f32[64,128]{1,0:T(8,128)}, f32[64,256]{1,0:T(8,128)}, f32[64,256]{1,0:T(8,128)}) custom-call(f32[64,512]{1,0:T(8,128)} %get-tuple-element.65.other_ref, f32[64,128]{1,0:T(8,128)} %copy-done.26, f32[64,128]{1,0:T(8,128)} %copy-done.32, f32[64,256]{1,0:T(8,128)} %copy-done.10, ...), custom_call_target="tpu_custom_call" | custom-call | tf_op jit(solution)/shard_map/pallas_call | solution.py:221
  84.6 4.2 %collective-permute-start.19 = (f32[64,256]{1,0:T(8,128)}, f32[64,256]{1,0:T(8,128)S(1)}, u32[]{:S(2)}, u32[]{:S(2)}) collective-permute-start(f32[64,256]{1,0:T(8,128)} %get-tuple-element.74), channel_id=1, source_target_pairs={{0,7},{1,0},{2,1},{3,2},{4,3},{5,4},{6,5},{7,6},{8,15},{9,8},{10,9... | collective-permute-start | bytes 196616 | tf_op jit(solution)/shard_map/ppermute | solution.py:246
  88.7 0.7 collective-permute-start.16
  89.4 1.3 collective-permute-done.16.lo_x_ref
  90.8 2.2 %collective-permute-done.17.hi_x_ref = f32[64,128]{1,0:T(8,128)S(1)} collective-permute-done((f32[64,128]{1,0:T(8,128)}, f32[64,128]{1,0:T(8,128)S(1)}, u32[]{:S(2)}, u32[]{:S(2)}) %collective-permute-start.17) | collective-permute-done | bytes 32800 | tf_op jit(solution)/shard_map/ppermute | solution.py:242
  93.0 0.6 copy-done.33
  93.6 2.8 %shard_map.87 = (f32[64,512]{1,0:T(8,128)}, f32[64,128]{1,0:T(8,128)}, f32[64,128]{1,0:T(8,128)}, f32[64,256]{1,0:T(8,128)}, f32[64,256]{1,0:T(8,128)}) custom-call(f32[64,512]{1,0:T(8,128)} %get-tuple-element.70.other_ref, f32[64,128]{1,0:T(8,128)} %copy-done.27, f32[64,128]{1,0:T(8,128)} %copy-done.33, f32[64,256]{1,0:T(8,128)} %copy-done.11, ...), custom_call_target="tpu_custom_call" | custom-call | tf_op jit(solution)/shard_map/pallas_call | solution.py:221
  96.5 4.2 %collective-permute-start.23 = (f32[64,256]{1,0:T(8,128)}, f32[64,256]{1,0:T(8,128)S(1)}, u32[]{:S(2)}, u32[]{:S(2)}) collective-permute-start(f32[64,256]{1,0:T(8,128)} %get-tuple-element.79), channel_id=1, source_target_pairs={{0,7},{1,0},{2,1},{3,2},{4,3},{5,4},{6,5},{7,6},{8,15},{9,8},{10,9... | collective-permute-start | bytes 196616 | tf_op jit(solution)/shard_map/ppermute | solution.py:246
  100.6 0.7 collective-permute-start.20
  101.3 1.3 collective-permute-done.20.lo_x_ref
  102.6 2.2 %collective-permute-done.21.hi_x_ref = f32[64,128]{1,0:T(8,128)S(1)} collective-permute-done((f32[64,128]{1,0:T(8,128)}, f32[64,128]{1,0:T(8,128)S(1)}, u32[]{:S(2)}, u32[]{:S(2)}) %collective-permute-start.21) | collective-permute-done | bytes 32800 | tf_op jit(solution)/shard_map/ppermute | solution.py:242
  104.9 0.6 copy-done.34
  105.5 2.8 %shard_map.88 = (f32[64,512]{1,0:T(8,128)}, f32[64,128]{1,0:T(8,128)}, f32[64,128]{1,0:T(8,128)}, f32[64,256]{1,0:T(8,128)}, f32[64,256]{1,0:T(8,128)}) custom-call(f32[64,512]{1,0:T(8,128)} %get-tuple-element.75.other_ref, f32[64,128]{1,0:T(8,128)} %copy-done.28, f32[64,128]{1,0:T(8,128)} %copy-done.34, f32[64,256]{1,0:T(8,128)} %copy-done.12, ...), custom_call_target="tpu_custom_call" | custom-call | tf_op jit(solution)/shard_map/pallas_call | solution.py:221
  108.4 4.2 %collective-permute-start.27 = (f32[64,256]{1,0:T(8,128)}, f32[64,256]{1,0:T(8,128)S(1)}, u32[]{:S(2)}, u32[]{:S(2)}) collective-permute-start(f32[64,256]{1,0:T(8,128)} %get-tuple-element.84), channel_id=1, source_target_pairs={{0,7},{1,0},{2,1},{3,2},{4,3},{5,4},{6,5},{7,6},{8,15},{9,8},{10,9... | collective-permute-start | bytes 196616 | tf_op jit(solution)/shard_map/ppermute | solution.py:246
  112.5 0.7 collective-permute-start.24
  113.2 1.3 collective-permute-done.24.lo_x_ref
  114.5 2.2 %collective-permute-done.25.hi_x_ref = f32[64,128]{1,0:T(8,128)S(1)} collective-permute-done((f32[64,128]{1,0:T(8,128)}, f32[64,128]{1,0:T(8,128)S(1)}, u32[]{:S(2)}, u32[]{:S(2)}) %collective-permute-start.25) | collective-permute-done | bytes 32800 | tf_op jit(solution)/shard_map/ppermute | solution.py:242
  116.8 0.6 copy-done.29
  117.4 2.8 %shard_map.89 = (f32[64,512]{1,0:T(8,128)}, f32[64,128]{1,0:T(8,128)}, f32[64,128]{1,0:T(8,128)}, f32[64,256]{1,0:T(8,128)}, f32[64,256]{1,0:T(8,128)}) custom-call(f32[64,512]{1,0:T(8,128)} %get-tuple-element.80.other_ref, f32[64,128]{1,0:T(8,128)} %copy-done.23, f32[64,128]{1,0:T(8,128)} %copy-done.29, f32[64,256]{1,0:T(8,128)} %copy-done.7, ...), custom_call_target="tpu_custom_call" | custom-call | tf_op jit(solution)/shard_map/pallas_call | solution.py:221
  120.3 4.2 %collective-permute-start.31 = (f32[64,256]{1,0:T(8,128)}, f32[64,256]{1,0:T(8,128)S(1)}, u32[]{:S(2)}, u32[]{:S(2)}) collective-permute-start(f32[64,256]{1,0:T(8,128)} %get-tuple-element.89), channel_id=1, source_target_pairs={{0,7},{1,0},{2,1},{3,2},{4,3},{5,4},{6,5},{7,6},{8,15},{9,8},{10,9... | collective-permute-start | bytes 196616 | tf_op jit(solution)/shard_map/ppermute | solution.py:246
  124.4 0.7 collective-permute-start.28
  125.1 1.0 reshape.166
  126.4 2.2 %collective-permute-done.29.hi_x_ref = f32[64,128]{1,0:T(8,128)S(1)} collective-permute-done((f32[64,128]{1,0:T(8,128)}, f32[64,128]{1,0:T(8,128)S(1)}, u32[]{:S(2)}, u32[]{:S(2)}) %collective-permute-start.29) | collective-permute-done | bytes 32800 | tf_op jit(solution)/shard_map/ppermute | solution.py:242
  128.7 0.6 copy-done.22
  129.3 0.6 copy-done.6
  129.9 2.8 %shard_map.90 = (f32[64,512]{1,0:T(8,128)}, f32[64,128]{1,0:T(8,128)}, f32[64,128]{1,0:T(8,128)}, f32[64,256]{1,0:T(8,128)}, f32[64,256]{1,0:T(8,128)}) custom-call(f32[64,512]{1,0:T(8,128)} %get-tuple-element.85.other_ref, f32[64,128]{1,0:T(8,128)} %copy-done.21, f32[64,128]{1,0:T(8,128)} %copy-done.22, f32[64,256]{1,0:T(8,128)} %copy-done.5, ...), custom_call_target="tpu_custom_call" | custom-call | tf_op jit(solution)/shard_map/pallas_call | solution.py:221
  132.7 1.0 reshape.168
  134.2 0.9 copy.73
  (147 shorter events, 7.2 us)
Async XLA Ops:
  0.0 0.7 slice-start
  3.2 1.0 copy-start
  5.8 37.4 %collective-permute-start.2 = (f32[64,256]{1,0:T(8,128)S(1)}, f32[64,256]{1,0:T(8,128)S(1)}, u32[]{:S(2)}, u32[]{:S(2)}) collective-permute-start(f32[64,256]{1,0:T(8,128)S(1)} %reshape_squeeze.14), channel_id=1, source_target_pairs={{0,1},{1,2},{2,3},{3,4},{4,5},{5,6},{6,7},{7,0},{8,9},{9,10},{10,1... | collective-permute-start | bytes 196616 | tf_op jit(solution)/shard_map/ppermute | solution.py:245
  8.1 35.1 %collective-permute-start.3 = (f32[64,256]{1,0:T(8,128)S(1)}, f32[64,256]{1,0:T(8,128)S(1)}, u32[]{:S(2)}, u32[]{:S(2)}) collective-permute-start(f32[64,256]{1,0:T(8,128)S(1)} %reshape_squeeze.15), channel_id=1, source_target_pairs={{0,7},{1,0},{2,1},{3,2},{4,3},{5,4},{6,5},{7,6},{8,15},{9,8},{10,9... | collective-permute-start | bytes 196616 | tf_op jit(solution)/shard_map/ppermute | solution.py:246
  11.2 2.6 %copy-start.1 = (f32[4,2,2,4096]{3,2,1,0:T(2,128)S(1)}, f32[4,2,2,4096]{3,2,1,0:T(2,128)}, u32[]{:S(2)}) copy-start(f32[4,2,2,4096]{3,2,1,0:T(2,128)} %param.10) | copy-start | bytes 786436
  11.4 31.8 %collective-permute-start = (f32[64,128]{1,0:T(8,128)S(1)}, f32[64,128]{1,0:T(8,128)S(1)}, u32[]{:S(2)}, u32[]{:S(2)}) collective-permute-start(f32[64,128]{1,0:T(8,128)S(1)} %reshape_squeeze.12), channel_id=1, source_target_pairs={{0,8},{8,16},{16,24},{24,0},{1,9},{9,17},{17,25},{25,1},{2,10},{10... | collective-permute-start | bytes 98312 | tf_op jit(solution)/shard_map/ppermute | solution.py:241
  13.7 29.4 %collective-permute-start.1 = (f32[64,128]{1,0:T(8,128)S(1)}, f32[64,128]{1,0:T(8,128)S(1)}, u32[]{:S(2)}, u32[]{:S(2)}) collective-permute-start(f32[64,128]{1,0:T(8,128)S(1)} %reshape_squeeze.13), channel_id=1, source_target_pairs={{0,24},{8,0},{16,8},{24,16},{1,25},{9,1},{17,9},{25,17},{2,26},{10... | collective-permute-start | bytes 98312 | tf_op jit(solution)/shard_map/ppermute | solution.py:242
  36.9 0.7 copy-start.35
  36.9 0.7 copy-start.36
  37.0 0.7 copy-start.37
  39.7 1.7 %copy-start.2 = (f32[6,64,64]{2,1,0:T(8,128)S(1)}, f32[6,64,64]{2,1,0:T(8,128)}, u32[]{:S(2)}) copy-start(f32[6,64,64]{2,1,0:T(8,128)} %param.11) | copy-start | bytes 294916
  43.1 0.6 copy-start.19
  43.1 0.6 copy-start.20
  43.2 0.6 copy-start.3
  43.8 0.6 copy-start.4
  47.2 10.0 %collective-permute-start.6 = (f32[64,256]{1,0:T(8,128)}, f32[64,256]{1,0:T(8,128)S(1)}, u32[]{:S(2)}, u32[]{:S(2)}) collective-permute-start(f32[64,256]{1,0:T(8,128)} %get-tuple-element.55), channel_id=1, source_target_pairs={{0,1},{1,2},{2,3},{3,4},{4,5},{5,6},{6,7},{7,0},{8,9},{9,10},{10,1... | collective-permute-start | bytes 196616 | tf_op jit(solution)/shard_map/ppermute | solution.py:245
  47.3 10.0 %collective-permute-start.7 = (f32[64,256]{1,0:T(8,128)}, f32[64,256]{1,0:T(8,128)S(1)}, u32[]{:S(2)}, u32[]{:S(2)}) collective-permute-start(f32[64,256]{1,0:T(8,128)} %get-tuple-element.56), channel_id=1, source_target_pairs={{0,7},{1,0},{2,1},{3,2},{4,3},{5,4},{6,5},{7,6},{8,15},{9,8},{10,9... | collective-permute-start | bytes 196616 | tf_op jit(solution)/shard_map/ppermute | solution.py:246
  51.4 3.6 %collective-permute-start.4 = (f32[64,128]{1,0:T(8,128)}, f32[64,128]{1,0:T(8,128)S(1)}, u32[]{:S(2)}, u32[]{:S(2)}) collective-permute-start(f32[64,128]{1,0:T(8,128)} %get-tuple-element.53), channel_id=1, source_target_pairs={{0,8},{8,16},{16,24},{24,0},{1,9},{9,17},{17,25},{25,1},{2,10},{10... | collective-permute-start | bytes 98312 | tf_op jit(solution)/shard_map/ppermute | solution.py:241
  53.7 3.6 %collective-permute-start.5 = (f32[64,128]{1,0:T(8,128)}, f32[64,128]{1,0:T(8,128)S(1)}, u32[]{:S(2)}, u32[]{:S(2)}) collective-permute-start(f32[64,128]{1,0:T(8,128)} %get-tuple-element.54), channel_id=1, source_target_pairs={{0,24},{8,0},{16,8},{24,16},{1,25},{9,1},{17,9},{25,17},{2,26},{10... | collective-permute-start | bytes 98312 | tf_op jit(solution)/shard_map/ppermute | solution.py:242
  55.0 2.2 %copy-start.24 = (f32[64,128]{1,0:T(8,128)}, f32[64,128]{1,0:T(8,128)S(1)}, u32[]{:S(2)}) copy-start(f32[64,128]{1,0:T(8,128)S(1)} %collective-permute-done.4.lo_x_ref) | copy-start | bytes 98308
  57.3 0.6 copy-start.8
  57.3 0.7 copy-start.14
  60.8 8.4 %collective-permute-start.10 = (f32[64,256]{1,0:T(8,128)}, f32[64,256]{1,0:T(8,128)S(1)}, u32[]{:S(2)}, u32[]{:S(2)}) collective-permute-start(f32[64,256]{1,0:T(8,128)} %get-tuple-element.63), channel_id=1, source_target_pairs={{0,1},{1,2},{2,3},{3,4},{4,5},{5,6},{6,7},{7,0},{8,9},{9,10},{10,1... | collective-permute-start | bytes 196616 | tf_op jit(solution)/shard_map/ppermute | solution.py:245
  60.8 8.4 %collective-permute-start.11 = (f32[64,256]{1,0:T(8,128)}, f32[64,256]{1,0:T(8,128)S(1)}, u32[]{:S(2)}, u32[]{:S(2)}) collective-permute-start(f32[64,256]{1,0:T(8,128)} %get-tuple-element.64), channel_id=1, source_target_pairs={{0,7},{1,0},{2,1},{3,2},{4,3},{5,4},{6,5},{7,6},{8,15},{9,8},{10,9... | collective-permute-start | bytes 196616 | tf_op jit(solution)/shard_map/ppermute | solution.py:246
  64.9 2.0 %collective-permute-start.8 = (f32[64,128]{1,0:T(8,128)}, f32[64,128]{1,0:T(8,128)S(1)}, u32[]{:S(2)}, u32[]{:S(2)}) collective-permute-start(f32[64,128]{1,0:T(8,128)} %get-tuple-element.61), channel_id=1, source_target_pairs={{0,8},{8,16},{16,24},{24,0},{1,9},{9,17},{17,25},{25,1},{2,10},{10... | collective-permute-start | bytes 98312 | tf_op jit(solution)/shard_map/ppermute | solution.py:241
  65.6 3.6 %collective-permute-start.9 = (f32[64,128]{1,0:T(8,128)}, f32[64,128]{1,0:T(8,128)S(1)}, u32[]{:S(2)}, u32[]{:S(2)}) collective-permute-start(f32[64,128]{1,0:T(8,128)} %get-tuple-element.62), channel_id=1, source_target_pairs={{0,24},{8,0},{16,8},{24,16},{1,25},{9,1},{17,9},{25,17},{2,26},{10... | collective-permute-start | bytes 98312 | tf_op jit(solution)/shard_map/ppermute | solution.py:242
  67.0 2.2 %copy-start.25 = (f32[64,128]{1,0:T(8,128)}, f32[64,128]{1,0:T(8,128)S(1)}, u32[]{:S(2)}) copy-start(f32[64,128]{1,0:T(8,128)S(1)} %collective-permute-done.8.lo_x_ref) | copy-start | bytes 98308
  69.2 0.6 copy-start.9
  69.2 0.7 copy-start.15
  72.7 8.4 %collective-permute-start.14 = (f32[64,256]{1,0:T(8,128)}, f32[64,256]{1,0:T(8,128)S(1)}, u32[]{:S(2)}, u32[]{:S(2)}) collective-permute-start(f32[64,256]{1,0:T(8,128)} %get-tuple-element.68), channel_id=1, source_target_pairs={{0,1},{1,2},{2,3},{3,4},{4,5},{5,6},{6,7},{7,0},{8,9},{9,10},{10,1... | collective-permute-start | bytes 196616 | tf_op jit(solution)/shard_map/ppermute | solution.py:245
  72.7 8.4 %collective-permute-start.15 = (f32[64,256]{1,0:T(8,128)}, f32[64,256]{1,0:T(8,128)S(1)}, u32[]{:S(2)}, u32[]{:S(2)}) collective-permute-start(f32[64,256]{1,0:T(8,128)} %get-tuple-element.69), channel_id=1, source_target_pairs={{0,7},{1,0},{2,1},{3,2},{4,3},{5,4},{6,5},{7,6},{8,15},{9,8},{10,9... | collective-permute-start | bytes 196616 | tf_op jit(solution)/shard_map/ppermute | solution.py:246
  76.8 2.0 %collective-permute-start.12 = (f32[64,128]{1,0:T(8,128)}, f32[64,128]{1,0:T(8,128)S(1)}, u32[]{:S(2)}, u32[]{:S(2)}) collective-permute-start(f32[64,128]{1,0:T(8,128)} %get-tuple-element.66), channel_id=1, source_target_pairs={{0,8},{8,16},{16,24},{24,0},{1,9},{9,17},{17,25},{25,1},{2,10},{10... | collective-permute-start | bytes 98312 | tf_op jit(solution)/shard_map/ppermute | solution.py:241
  77.5 3.6 %collective-permute-start.13 = (f32[64,128]{1,0:T(8,128)}, f32[64,128]{1,0:T(8,128)S(1)}, u32[]{:S(2)}, u32[]{:S(2)}) collective-permute-start(f32[64,128]{1,0:T(8,128)} %get-tuple-element.67), channel_id=1, source_target_pairs={{0,24},{8,0},{16,8},{24,16},{1,25},{9,1},{17,9},{25,17},{2,26},{10... | collective-permute-start | bytes 98312 | tf_op jit(solution)/shard_map/ppermute | solution.py:242
  78.9 2.2 %copy-start.26 = (f32[64,128]{1,0:T(8,128)}, f32[64,128]{1,0:T(8,128)S(1)}, u32[]{:S(2)}) copy-start(f32[64,128]{1,0:T(8,128)S(1)} %collective-permute-done.12.lo_x_ref) | copy-start | bytes 98308
  81.1 0.6 copy-start.10
  81.1 0.7 copy-start.16
  84.6 8.4 %collective-permute-start.18 = (f32[64,256]{1,0:T(8,128)}, f32[64,256]{1,0:T(8,128)S(1)}, u32[]{:S(2)}, u32[]{:S(2)}) collective-permute-start(f32[64,256]{1,0:T(8,128)} %get-tuple-element.73), channel_id=1, source_target_pairs={{0,1},{1,2},{2,3},{3,4},{4,5},{5,6},{6,7},{7,0},{8,9},{9,10},{10,1... | collective-permute-start | bytes 196616 | tf_op jit(solution)/shard_map/ppermute | solution.py:245
  84.6 8.4 %collective-permute-start.19 = (f32[64,256]{1,0:T(8,128)}, f32[64,256]{1,0:T(8,128)S(1)}, u32[]{:S(2)}, u32[]{:S(2)}) collective-permute-start(f32[64,256]{1,0:T(8,128)} %get-tuple-element.74), channel_id=1, source_target_pairs={{0,7},{1,0},{2,1},{3,2},{4,3},{5,4},{6,5},{7,6},{8,15},{9,8},{10,9... | collective-permute-start | bytes 196616 | tf_op jit(solution)/shard_map/ppermute | solution.py:246
  88.7 2.0 %collective-permute-start.16 = (f32[64,128]{1,0:T(8,128)}, f32[64,128]{1,0:T(8,128)S(1)}, u32[]{:S(2)}, u32[]{:S(2)}) collective-permute-start(f32[64,128]{1,0:T(8,128)} %get-tuple-element.71), channel_id=1, source_target_pairs={{0,8},{8,16},{16,24},{24,0},{1,9},{9,17},{17,25},{25,1},{2,10},{10... | collective-permute-start | bytes 98312 | tf_op jit(solution)/shard_map/ppermute | solution.py:241
  89.4 3.6 %collective-permute-start.17 = (f32[64,128]{1,0:T(8,128)}, f32[64,128]{1,0:T(8,128)S(1)}, u32[]{:S(2)}, u32[]{:S(2)}) collective-permute-start(f32[64,128]{1,0:T(8,128)} %get-tuple-element.72), channel_id=1, source_target_pairs={{0,24},{8,0},{16,8},{24,16},{1,25},{9,1},{17,9},{25,17},{2,26},{10... | collective-permute-start | bytes 98312 | tf_op jit(solution)/shard_map/ppermute | solution.py:242
  90.8 2.2 %copy-start.27 = (f32[64,128]{1,0:T(8,128)}, f32[64,128]{1,0:T(8,128)S(1)}, u32[]{:S(2)}) copy-start(f32[64,128]{1,0:T(8,128)S(1)} %collective-permute-done.16.lo_x_ref) | copy-start | bytes 98308
  93.0 0.6 copy-start.11
  93.0 0.7 copy-start.17
  96.5 8.4 %collective-permute-start.22 = (f32[64,256]{1,0:T(8,128)}, f32[64,256]{1,0:T(8,128)S(1)}, u32[]{:S(2)}, u32[]{:S(2)}) collective-permute-start(f32[64,256]{1,0:T(8,128)} %get-tuple-element.78), channel_id=1, source_target_pairs={{0,1},{1,2},{2,3},{3,4},{4,5},{5,6},{6,7},{7,0},{8,9},{9,10},{10,1... | collective-permute-start | bytes 196616 | tf_op jit(solution)/shard_map/ppermute | solution.py:245
  96.5 8.4 %collective-permute-start.23 = (f32[64,256]{1,0:T(8,128)}, f32[64,256]{1,0:T(8,128)S(1)}, u32[]{:S(2)}, u32[]{:S(2)}) collective-permute-start(f32[64,256]{1,0:T(8,128)} %get-tuple-element.79), channel_id=1, source_target_pairs={{0,7},{1,0},{2,1},{3,2},{4,3},{5,4},{6,5},{7,6},{8,15},{9,8},{10,9... | collective-permute-start | bytes 196616 | tf_op jit(solution)/shard_map/ppermute | solution.py:246
  100.6 2.0 %collective-permute-start.20 = (f32[64,128]{1,0:T(8,128)}, f32[64,128]{1,0:T(8,128)S(1)}, u32[]{:S(2)}, u32[]{:S(2)}) collective-permute-start(f32[64,128]{1,0:T(8,128)} %get-tuple-element.76), channel_id=1, source_target_pairs={{0,8},{8,16},{16,24},{24,0},{1,9},{9,17},{17,25},{25,1},{2,10},{10... | collective-permute-start | bytes 98312 | tf_op jit(solution)/shard_map/ppermute | solution.py:241
  101.3 3.6 %collective-permute-start.21 = (f32[64,128]{1,0:T(8,128)}, f32[64,128]{1,0:T(8,128)S(1)}, u32[]{:S(2)}, u32[]{:S(2)}) collective-permute-start(f32[64,128]{1,0:T(8,128)} %get-tuple-element.77), channel_id=1, source_target_pairs={{0,24},{8,0},{16,8},{24,16},{1,25},{9,1},{17,9},{25,17},{2,26},{10... | collective-permute-start | bytes 98312 | tf_op jit(solution)/shard_map/ppermute | solution.py:242
  102.6 2.2 %copy-start.28 = (f32[64,128]{1,0:T(8,128)}, f32[64,128]{1,0:T(8,128)S(1)}, u32[]{:S(2)}) copy-start(f32[64,128]{1,0:T(8,128)S(1)} %collective-permute-done.20.lo_x_ref) | copy-start | bytes 98308
  104.9 0.6 copy-start.12
  104.9 0.7 copy-start.18
  108.4 8.4 %collective-permute-start.26 = (f32[64,256]{1,0:T(8,128)}, f32[64,256]{1,0:T(8,128)S(1)}, u32[]{:S(2)}, u32[]{:S(2)}) collective-permute-start(f32[64,256]{1,0:T(8,128)} %get-tuple-element.83), channel_id=1, source_target_pairs={{0,1},{1,2},{2,3},{3,4},{4,5},{5,6},{6,7},{7,0},{8,9},{9,10},{10,1... | collective-permute-start | bytes 196616 | tf_op jit(solution)/shard_map/ppermute | solution.py:245
  108.4 8.4 %collective-permute-start.27 = (f32[64,256]{1,0:T(8,128)}, f32[64,256]{1,0:T(8,128)S(1)}, u32[]{:S(2)}, u32[]{:S(2)}) collective-permute-start(f32[64,256]{1,0:T(8,128)} %get-tuple-element.84), channel_id=1, source_target_pairs={{0,7},{1,0},{2,1},{3,2},{4,3},{5,4},{6,5},{7,6},{8,15},{9,8},{10,9... | collective-permute-start | bytes 196616 | tf_op jit(solution)/shard_map/ppermute | solution.py:246
  112.5 2.0 %collective-permute-start.24 = (f32[64,128]{1,0:T(8,128)}, f32[64,128]{1,0:T(8,128)S(1)}, u32[]{:S(2)}, u32[]{:S(2)}) collective-permute-start(f32[64,128]{1,0:T(8,128)} %get-tuple-element.81), channel_id=1, source_target_pairs={{0,8},{8,16},{16,24},{24,0},{1,9},{9,17},{17,25},{25,1},{2,10},{10... | collective-permute-start | bytes 98312 | tf_op jit(solution)/shard_map/ppermute | solution.py:241
  113.2 3.6 %collective-permute-start.25 = (f32[64,128]{1,0:T(8,128)}, f32[64,128]{1,0:T(8,128)S(1)}, u32[]{:S(2)}, u32[]{:S(2)}) collective-permute-start(f32[64,128]{1,0:T(8,128)} %get-tuple-element.82), channel_id=1, source_target_pairs={{0,24},{8,0},{16,8},{24,16},{1,25},{9,1},{17,9},{25,17},{2,26},{10... | collective-permute-start | bytes 98312 | tf_op jit(solution)/shard_map/ppermute | solution.py:242
  114.5 2.2 %copy-start.23 = (f32[64,128]{1,0:T(8,128)}, f32[64,128]{1,0:T(8,128)S(1)}, u32[]{:S(2)}) copy-start(f32[64,128]{1,0:T(8,128)S(1)} %collective-permute-done.24.lo_x_ref) | copy-start | bytes 98308
  116.8 0.6 copy-start.7
  116.8 0.7 copy-start.13
  120.3 8.4 %collective-permute-start.30 = (f32[64,256]{1,0:T(8,128)}, f32[64,256]{1,0:T(8,128)S(1)}, u32[]{:S(2)}, u32[]{:S(2)}) collective-permute-start(f32[64,256]{1,0:T(8,128)} %get-tuple-element.88), channel_id=1, source_target_pairs={{0,1},{1,2},{2,3},{3,4},{4,5},{5,6},{6,7},{7,0},{8,9},{9,10},{10,1... | collective-permute-start | bytes 196616 | tf_op jit(solution)/shard_map/ppermute | solution.py:245
  120.3 8.4 %collective-permute-start.31 = (f32[64,256]{1,0:T(8,128)}, f32[64,256]{1,0:T(8,128)S(1)}, u32[]{:S(2)}, u32[]{:S(2)}) collective-permute-start(f32[64,256]{1,0:T(8,128)} %get-tuple-element.89), channel_id=1, source_target_pairs={{0,7},{1,0},{2,1},{3,2},{4,3},{5,4},{6,5},{7,6},{8,15},{9,8},{10,9... | collective-permute-start | bytes 196616 | tf_op jit(solution)/shard_map/ppermute | solution.py:246
  124.4 2.0 %collective-permute-start.28 = (f32[64,128]{1,0:T(8,128)}, f32[64,128]{1,0:T(8,128)S(1)}, u32[]{:S(2)}, u32[]{:S(2)}) collective-permute-start(f32[64,128]{1,0:T(8,128)} %get-tuple-element.86), channel_id=1, source_target_pairs={{0,8},{8,16},{16,24},{24,0},{1,9},{9,17},{17,25},{25,1},{2,10},{10... | collective-permute-start | bytes 98312 | tf_op jit(solution)/shard_map/ppermute | solution.py:241
  125.1 3.6 %collective-permute-start.29 = (f32[64,128]{1,0:T(8,128)}, f32[64,128]{1,0:T(8,128)S(1)}, u32[]{:S(2)}, u32[]{:S(2)}) collective-permute-start(f32[64,128]{1,0:T(8,128)} %get-tuple-element.87), channel_id=1, source_target_pairs={{0,24},{8,0},{16,8},{24,16},{1,25},{9,1},{17,9},{25,17},{2,26},{10... | collective-permute-start | bytes 98312 | tf_op jit(solution)/shard_map/ppermute | solution.py:242
  126.4 2.2 %copy-start.21 = (f32[64,128]{1,0:T(8,128)}, f32[64,128]{1,0:T(8,128)S(1)}, u32[]{:S(2)}) copy-start(f32[64,128]{1,0:T(8,128)S(1)} %collective-permute-done.28.lo_x_ref) | copy-start | bytes 98308
  128.6 0.6 copy-start.5
  129.3 0.6 copy-start.6
  (7 other events, 4.2 us)

commit v4 on v3

--- a/solution.py
+++ b/solution.py
@@ -223,7 +223,10 @@
         out_shape=(jax.ShapeDtypeStruct((P_SIZE, lanes), jnp.float32), x_shape, x_shape, y_shape, y_shape),
         in_specs=[vmem] * 9,
         out_specs=(vmem,) * 5,
-    )(other, *halos, face_blocks, weight, inverse, target)
+    )(*[
+        pltpu.with_memory_space_constraint(value, pltpu.VMEM)
+        for value in (other, *halos, face_blocks, weight, inverse, target)
+    ])
 
 
 def send_buffers(state, span_x):

time: 136 us -> 122 us (0.90)
  Pallas kernels: 41.9 us -> 32.4 us
  local copies, waits for them, and re-layouts: 25.2 us -> 20.9 us
    pallas_call x8, Pallas kernels: 22.7 us -> 13.2 us  [half_sweep(): pl.pallas_call(functools.partial(_half_sweep_kernel, span_x=span_x), out_...]
    reshape x3, local copies, waits for them, and re-layouts: 2.31 us -> 0.35 us  [to_lanes(): jnp.transpose(values.reshape(columns, P_SIZE, R), (1, 0, 2))]
    unnamed x80 -> x30, local copies, waits for them, and re-layouts: 7.35 us -> 7.58 us
  transfers between devices with their start and end apart: 32 -> 32, of which waited for: 14 -> 14; matrix products, arithmetic and copies ran while one was open for 9% -> 6% of each run, Pallas kernels for 14% -> 16%
where the time goes in v4:
time: 122 us; the launch traced here: 121 us
  starting transfers between devices  42.9 us (35%)
  Pallas kernels  32.4 us (27%)
  waiting for transfers between devices  23.6 us (19%)
  local copies, waits for them, and re-layouts  20.9 us (17%)
    ppermute x8, starting transfers between devices, trade(): lax.ppermute(sends[3], 'gy', shift_pairs('gy', -1))  32.2 us
    pallas_call x1, Pallas kernels, block_inverses(): pl.pallas_call(functools.partial(_gauss_jordan_kernel, n=n, nb=nb), out_s...  19.2 us
    ppermute x8, waiting for transfers between devices, trade(): lax.ppermute(sends[1], 'gx', shift_pairs('gx', -1))  15.5 us
    pallas_call x8, Pallas kernels, half_sweep(): pl.pallas_call(functools.partial(_half_sweep_kernel, span_x=span_x), out_...  13.2 us
    ppermute x8, starting transfers between devices, trade(): lax.ppermute(sends[0], 'gx', shift_pairs('gx', 1))  8.51 us
    ppermute x8, waiting for transfers between devices, trade(): lax.ppermute(sends[0], 'gx', shift_pairs('gx', 1))  8.13 us
    unnamed x30, local copies, waits for them, and re-layouts  7.58 us
    slice x3, local copies, waits for them, and re-layouts, pick(): high = lax.index_in_dim(values, 1, axis=axis, keepdims=False)  2.68 us
  transfers between devices with their start and end apart: 32, of which 14 were waited for; matrix products, arithmetic and copies ran while one was open for 6% of the time, Pallas kernels for 16%

profile of v4, /device:TPU:1, one launch (start us, length us, event | category | flops | bytes accessed | tf_op | source)
XLA Modules:
  0.0 121.2 jit_solution(16276839723579038561)
XLA Ops:
  0.0 0.7 slice-done
  1.1 1.9 %slice_reduce_fusion.2 = (f32[4,2,4096]{2,1,0:T(2,128)S(1)}, f32[4,2,4096]{2,1,0:T(2,128)S(1)}) fusion(f32[4,2,2,4096]{3,2,1,0:T(2,128)} %param.9), kind=kLoop, calls=%fused_computation.10 | loop fusion | bytes 524288 | tf_op jit(solution)/shard_map/slice | solution.py:270
  3.0 0.2 squeeze.32
  3.2 0.2 squeeze.33
  3.4 0.7 copy-done.7
  4.1 0.8 slice_reduce_fusion
  5.7 2.1 %collective-permute-start.2 = (f32[64,256]{1,0:T(8,128)S(1)}, f32[64,256]{1,0:T(8,128)S(1)}, u32[]{:S(2)}, u32[]{:S(2)}) collective-permute-start(f32[64,256]{1,0:T(8,128)S(1)} %reshape_squeeze.14), channel_id=1, source_target_pairs={{0,1},{1,2},{2,3},{3,4},{4,5},{5,6},{6,7},{7,0},{8,9},{9,10},{10,1... | collective-permute-start | bytes 196616 | tf_op jit(solution)/shard_map/ppermute | solution.py:248
  8.1 3.1 %collective-permute-start.3 = (f32[64,256]{1,0:T(8,128)S(1)}, f32[64,256]{1,0:T(8,128)S(1)}, u32[]{:S(2)}, u32[]{:S(2)}) collective-permute-start(f32[64,256]{1,0:T(8,128)S(1)} %reshape_squeeze.15), channel_id=1, source_target_pairs={{0,7},{1,0},{2,1},{3,2},{4,3},{5,4},{6,5},{7,6},{8,15},{9,8},{10,9... | collective-permute-start | bytes 196616 | tf_op jit(solution)/shard_map/ppermute | solution.py:249
  11.3 2.2 %collective-permute-start = (f32[64,128]{1,0:T(8,128)S(1)}, f32[64,128]{1,0:T(8,128)S(1)}, u32[]{:S(2)}, u32[]{:S(2)}) collective-permute-start(f32[64,128]{1,0:T(8,128)S(1)} %reshape_squeeze.12), channel_id=1, source_target_pairs={{0,8},{8,16},{16,24},{24,0},{1,9},{9,17},{17,25},{25,1},{2,10},{10... | collective-permute-start | bytes 98312 | tf_op jit(solution)/shard_map/ppermute | solution.py:244
  13.7 0.3 broadcast_select_fusion.1
  14.0 0.2 pad_maximum_fusion
  14.3 0.2 copy.60
  14.5 0.3 reshape.157
  14.8 0.3 copy.61
  15.1 0.9 copy.62.a_ref
  16.0 19.2 %shard_map.82 = f32[64,1024]{1,0:T(8,128)} custom-call(f32[64,1024]{1,0:T(8,128)} %copy.62.a_ref), custom_call_target="tpu_custom_call" | custom-call | flops 8388608000 | bytes 524288 | tf_op jit(solution)/shard_map/pallas_call | solution.py:75
  35.2 1.1 copy.63
  36.3 0.4 copy.64
  36.9 0.6 copy-done.10
  38.8 0.4 copy-done.9
  39.7 1.7 %shard_map.83 = (f32[64,512]{1,0:T(8,128)}, f32[64,128]{1,0:T(8,128)}, f32[64,128]{1,0:T(8,128)}, f32[64,256]{1,0:T(8,128)}, f32[64,256]{1,0:T(8,128)}) custom-call(f32[64,512]{1,0:T(8,128)S(1)} %reshape.156.other_ref, f32[64,128]{1,0:T(8,128)S(1)} %collective-permute-done.lo_x_ref, f32[64,128]{1,0:T(8,128)S(1)} %collective-permute-done.1.hi_x_ref, ...), custom_call_target="tpu_custom_call" | custom-call | tf_op jit(solution)/shard_map/pallas_call | solution.py:221
  41.4 4.2 %collective-permute-start.7 = (f32[64,256]{1,0:T(8,128)}, f32[64,256]{1,0:T(8,128)S(1)}, u32[]{:S(2)}, u32[]{:S(2)}) collective-permute-start(f32[64,256]{1,0:T(8,128)} %get-tuple-element.56), channel_id=1, source_target_pairs={{0,7},{1,0},{2,1},{3,2},{4,3},{5,4},{6,5},{7,6},{8,15},{9,8},{10,9... | collective-permute-start | bytes 196616 | tf_op jit(solution)/shard_map/ppermute | solution.py:249
  45.5 2.3 %collective-permute-start.4 = (f32[64,128]{1,0:T(8,128)}, f32[64,128]{1,0:T(8,128)S(1)}, u32[]{:S(2)}, u32[]{:S(2)}) collective-permute-start(f32[64,128]{1,0:T(8,128)} %get-tuple-element.53), channel_id=1, source_target_pairs={{0,8},{8,16},{16,24},{24,0},{1,9},{9,17},{17,25},{25,1},{2,10},{10... | collective-permute-start | bytes 98312 | tf_op jit(solution)/shard_map/ppermute | solution.py:244
  47.8 1.3 %collective-permute-done.4.lo_x_ref = f32[64,128]{1,0:T(8,128)S(1)} collective-permute-done((f32[64,128]{1,0:T(8,128)}, f32[64,128]{1,0:T(8,128)S(1)}, u32[]{:S(2)}, u32[]{:S(2)}) %collective-permute-start.4) | collective-permute-done | bytes 32800 | tf_op jit(solution)/shard_map/ppermute | solution.py:244
  49.2 2.2 %collective-permute-done.5.hi_x_ref = f32[64,128]{1,0:T(8,128)S(1)} collective-permute-done((f32[64,128]{1,0:T(8,128)}, f32[64,128]{1,0:T(8,128)S(1)}, u32[]{:S(2)}, u32[]{:S(2)}) %collective-permute-start.5) | collective-permute-done | bytes 32800 | tf_op jit(solution)/shard_map/ppermute | solution.py:245
  51.4 0.9 copy-done.2
  52.3 1.6 %shard_map.84 = (f32[64,512]{1,0:T(8,128)}, f32[64,128]{1,0:T(8,128)}, f32[64,128]{1,0:T(8,128)}, f32[64,256]{1,0:T(8,128)}, f32[64,256]{1,0:T(8,128)}) custom-call(f32[64,512]{1,0:T(8,128)S(1)} %copy-done.2, f32[64,128]{1,0:T(8,128)S(1)} %collective-permute-done.4.lo_x_ref, f32[64,128]{1,0:T(8,128)S(1)} %collective-permute-done.5.hi_x_ref, ...), custom_call_target="tpu_custom_call" | custom-call | tf_op jit(solution)/shard_map/pallas_call | solution.py:221
  53.9 4.2 %collective-permute-start.11 = (f32[64,256]{1,0:T(8,128)}, f32[64,256]{1,0:T(8,128)S(1)}, u32[]{:S(2)}, u32[]{:S(2)}) collective-permute-start(f32[64,256]{1,0:T(8,128)} %get-tuple-element.64), channel_id=1, source_target_pairs={{0,7},{1,0},{2,1},{3,2},{4,3},{5,4},{6,5},{7,6},{8,15},{9,8},{10,9... | collective-permute-start | bytes 196616 | tf_op jit(solution)/shard_map/ppermute | solution.py:249
  58.1 0.7 collective-permute-start.8
  58.8 1.3 %collective-permute-done.8.lo_x_ref = f32[64,128]{1,0:T(8,128)S(1)} collective-permute-done((f32[64,128]{1,0:T(8,128)}, f32[64,128]{1,0:T(8,128)S(1)}, u32[]{:S(2)}, u32[]{:S(2)}) %collective-permute-start.8) | collective-permute-done | bytes 32800 | tf_op jit(solution)/shard_map/ppermute | solution.py:244
  60.1 2.2 %collective-permute-done.9.hi_x_ref = f32[64,128]{1,0:T(8,128)S(1)} collective-permute-done((f32[64,128]{1,0:T(8,128)}, f32[64,128]{1,0:T(8,128)S(1)}, u32[]{:S(2)}, u32[]{:S(2)}) %collective-permute-start.9) | collective-permute-done | bytes 32800 | tf_op jit(solution)/shard_map/ppermute | solution.py:245
  62.3 0.9 copy-done.3
  63.2 1.6 %shard_map.85 = (f32[64,512]{1,0:T(8,128)}, f32[64,128]{1,0:T(8,128)}, f32[64,128]{1,0:T(8,128)}, f32[64,256]{1,0:T(8,128)}, f32[64,256]{1,0:T(8,128)}) custom-call(f32[64,512]{1,0:T(8,128)S(1)} %copy-done.3, f32[64,128]{1,0:T(8,128)S(1)} %collective-permute-done.8.lo_x_ref, f32[64,128]{1,0:T(8,128)S(1)} %collective-permute-done.9.hi_x_ref, ...), custom_call_target="tpu_custom_call" | custom-call | tf_op jit(solution)/shard_map/pallas_call | solution.py:221
  64.9 4.2 %collective-permute-start.15 = (f32[64,256]{1,0:T(8,128)}, f32[64,256]{1,0:T(8,128)S(1)}, u32[]{:S(2)}, u32[]{:S(2)}) collective-permute-start(f32[64,256]{1,0:T(8,128)} %get-tuple-element.69), channel_id=1, source_target_pairs={{0,7},{1,0},{2,1},{3,2},{4,3},{5,4},{6,5},{7,6},{8,15},{9,8},{10,9... | collective-permute-start | bytes 196616 | tf_op jit(solution)/shard_map/ppermute | solution.py:249
  69.1 0.7 collective-permute-start.12
  69.7 1.3 %collective-permute-done.12.lo_x_ref = f32[64,128]{1,0:T(8,128)S(1)} collective-permute-done((f32[64,128]{1,0:T(8,128)}, f32[64,128]{1,0:T(8,128)S(1)}, u32[]{:S(2)}, u32[]{:S(2)}) %collective-permute-start.12) | collective-permute-done | bytes 32800 | tf_op jit(solution)/shard_map/ppermute | solution.py:244
  71.1 2.2 %collective-permute-done.13.hi_x_ref = f32[64,128]{1,0:T(8,128)S(1)} collective-permute-done((f32[64,128]{1,0:T(8,128)}, f32[64,128]{1,0:T(8,128)S(1)}, u32[]{:S(2)}, u32[]{:S(2)}) %collective-permute-start.13) | collective-permute-done | bytes 32800 | tf_op jit(solution)/shard_map/ppermute | solution.py:245
  73.3 0.9 copy-done.4
  74.2 1.6 %shard_map.86 = (f32[64,512]{1,0:T(8,128)}, f32[64,128]{1,0:T(8,128)}, f32[64,128]{1,0:T(8,128)}, f32[64,256]{1,0:T(8,128)}, f32[64,256]{1,0:T(8,128)}) custom-call(f32[64,512]{1,0:T(8,128)S(1)} %copy-done.4, f32[64,128]{1,0:T(8,128)S(1)} %collective-permute-done.12.lo_x_ref, f32[64,128]{1,0:T(8,128)S(1)} %collective-permute-done.13.hi_x_ref, ...), custom_call_target="tpu_custom_call" | custom-call | tf_op jit(solution)/shard_map/pallas_call | solution.py:221
  75.8 4.2 %collective-permute-start.19 = (f32[64,256]{1,0:T(8,128)}, f32[64,256]{1,0:T(8,128)S(1)}, u32[]{:S(2)}, u32[]{:S(2)}) collective-permute-start(f32[64,256]{1,0:T(8,128)} %get-tuple-element.74), channel_id=1, source_target_pairs={{0,7},{1,0},{2,1},{3,2},{4,3},{5,4},{6,5},{7,6},{8,15},{9,8},{10,9... | collective-permute-start | bytes 196616 | tf_op jit(solution)/shard_map/ppermute | solution.py:249
  80.0 0.7 collective-permute-start.16
  80.7 1.3 %collective-permute-done.16.lo_x_ref = f32[64,128]{1,0:T(8,128)S(1)} collective-permute-done((f32[64,128]{1,0:T(8,128)}, f32[64,128]{1,0:T(8,128)S(1)}, u32[]{:S(2)}, u32[]{:S(2)}) %collective-permute-start.16) | collective-permute-done | bytes 32800 | tf_op jit(solution)/shard_map/ppermute | solution.py:244
  82.0 2.2 %collective-permute-done.17.hi_x_ref = f32[64,128]{1,0:T(8,128)S(1)} collective-permute-done((f32[64,128]{1,0:T(8,128)}, f32[64,128]{1,0:T(8,128)S(1)}, u32[]{:S(2)}, u32[]{:S(2)}) %collective-permute-start.17) | collective-permute-done | bytes 32800 | tf_op jit(solution)/shard_map/ppermute | solution.py:245
  84.2 0.9 copy-done.5
  85.1 1.6 %shard_map.87 = (f32[64,512]{1,0:T(8,128)}, f32[64,128]{1,0:T(8,128)}, f32[64,128]{1,0:T(8,128)}, f32[64,256]{1,0:T(8,128)}, f32[64,256]{1,0:T(8,128)}) custom-call(f32[64,512]{1,0:T(8,128)S(1)} %copy-done.5, f32[64,128]{1,0:T(8,128)S(1)} %collective-permute-done.16.lo_x_ref, f32[64,128]{1,0:T(8,128)S(1)} %collective-permute-done.17.hi_x_ref, ...), custom_call_target="tpu_custom_call" | custom-call | tf_op jit(solution)/shard_map/pallas_call | solution.py:221
  86.8 4.2 %collective-permute-start.23 = (f32[64,256]{1,0:T(8,128)}, f32[64,256]{1,0:T(8,128)S(1)}, u32[]{:S(2)}, u32[]{:S(2)}) collective-permute-start(f32[64,256]{1,0:T(8,128)} %get-tuple-element.79), channel_id=1, source_target_pairs={{0,7},{1,0},{2,1},{3,2},{4,3},{5,4},{6,5},{7,6},{8,15},{9,8},{10,9... | collective-permute-start | bytes 196616 | tf_op jit(solution)/shard_map/ppermute | solution.py:249
  90.9 0.7 collective-permute-start.20
  91.6 1.3 %collective-permute-done.20.lo_x_ref = f32[64,128]{1,0:T(8,128)S(1)} collective-permute-done((f32[64,128]{1,0:T(8,128)}, f32[64,128]{1,0:T(8,128)S(1)}, u32[]{:S(2)}, u32[]{:S(2)}) %collective-permute-start.20) | collective-permute-done | bytes 32800 | tf_op jit(solution)/shard_map/ppermute | solution.py:244
  93.0 2.2 %collective-permute-done.21.hi_x_ref = f32[64,128]{1,0:T(8,128)S(1)} collective-permute-done((f32[64,128]{1,0:T(8,128)}, f32[64,128]{1,0:T(8,128)S(1)}, u32[]{:S(2)}, u32[]{:S(2)}) %collective-permute-start.21) | collective-permute-done | bytes 32800 | tf_op jit(solution)/shard_map/ppermute | solution.py:245
  95.2 0.9 copy-done.6
  96.1 1.6 %shard_map.88 = (f32[64,512]{1,0:T(8,128)}, f32[64,128]{1,0:T(8,128)}, f32[64,128]{1,0:T(8,128)}, f32[64,256]{1,0:T(8,128)}, f32[64,256]{1,0:T(8,128)}) custom-call(f32[64,512]{1,0:T(8,128)S(1)} %copy-done.6, f32[64,128]{1,0:T(8,128)S(1)} %collective-permute-done.20.lo_x_ref, f32[64,128]{1,0:T(8,128)S(1)} %collective-permute-done.21.hi_x_ref, ...), custom_call_target="tpu_custom_call" | custom-call | tf_op jit(solution)/shard_map/pallas_call | solution.py:221
  97.7 4.2 %collective-permute-start.27 = (f32[64,256]{1,0:T(8,128)}, f32[64,256]{1,0:T(8,128)S(1)}, u32[]{:S(2)}, u32[]{:S(2)}) collective-permute-start(f32[64,256]{1,0:T(8,128)} %get-tuple-element.84), channel_id=1, source_target_pairs={{0,7},{1,0},{2,1},{3,2},{4,3},{5,4},{6,5},{7,6},{8,15},{9,8},{10,9... | collective-permute-start | bytes 196616 | tf_op jit(solution)/shard_map/ppermute | solution.py:249
  101.9 0.7 collective-permute-start.24
  102.6 1.3 %collective-permute-done.24.lo_x_ref = f32[64,128]{1,0:T(8,128)S(1)} collective-permute-done((f32[64,128]{1,0:T(8,128)}, f32[64,128]{1,0:T(8,128)S(1)}, u32[]{:S(2)}, u32[]{:S(2)}) %collective-permute-start.24) | collective-permute-done | bytes 32800 | tf_op jit(solution)/shard_map/ppermute | solution.py:244
  103.9 2.2 %collective-permute-done.25.hi_x_ref = f32[64,128]{1,0:T(8,128)S(1)} collective-permute-done((f32[64,128]{1,0:T(8,128)}, f32[64,128]{1,0:T(8,128)S(1)}, u32[]{:S(2)}, u32[]{:S(2)}) %collective-permute-start.25) | collective-permute-done | bytes 32800 | tf_op jit(solution)/shard_map/ppermute | solution.py:245
  106.1 0.9 copy-done.1
  107.0 1.6 %shard_map.89 = (f32[64,512]{1,0:T(8,128)}, f32[64,128]{1,0:T(8,128)}, f32[64,128]{1,0:T(8,128)}, f32[64,256]{1,0:T(8,128)}, f32[64,256]{1,0:T(8,128)}) custom-call(f32[64,512]{1,0:T(8,128)S(1)} %copy-done.1, f32[64,128]{1,0:T(8,128)S(1)} %collective-permute-done.24.lo_x_ref, f32[64,128]{1,0:T(8,128)S(1)} %collective-permute-done.25.hi_x_ref, ...), custom_call_target="tpu_custom_call" | custom-call | tf_op jit(solution)/shard_map/pallas_call | solution.py:221
  108.7 4.2 %collective-permute-start.31 = (f32[64,256]{1,0:T(8,128)}, f32[64,256]{1,0:T(8,128)S(1)}, u32[]{:S(2)}, u32[]{:S(2)}) collective-permute-start(f32[64,256]{1,0:T(8,128)} %get-tuple-element.89), channel_id=1, source_target_pairs={{0,7},{1,0},{2,1},{3,2},{4,3},{5,4},{6,5},{7,6},{8,15},{9,8},{10,9... | collective-permute-start | bytes 196616 | tf_op jit(solution)/shard_map/ppermute | solution.py:249
  112.8 0.7 collective-permute-start.28
  113.5 1.0 reshape.166
  114.9 2.2 %collective-permute-done.29.hi_x_ref = f32[64,128]{1,0:T(8,128)S(1)} collective-permute-done((f32[64,128]{1,0:T(8,128)}, f32[64,128]{1,0:T(8,128)S(1)}, u32[]{:S(2)}, u32[]{:S(2)}) %collective-permute-start.29) | collective-permute-done | bytes 32800 | tf_op jit(solution)/shard_map/ppermute | solution.py:245
  117.1 1.7 %shard_map.90 = (f32[64,512]{1,0:T(8,128)}, f32[64,128]{1,0:T(8,128)}, f32[64,128]{1,0:T(8,128)}, f32[64,256]{1,0:T(8,128)}, f32[64,256]{1,0:T(8,128)}) custom-call(f32[64,512]{1,0:T(8,128)S(1)} %copy-done, f32[64,128]{1,0:T(8,128)S(1)} %collective-permute-done.28.lo_x_ref, f32[64,128]{1,0:T(8,128)S(1)} %collective-permute-done.29.hi_x_ref, ...), custom_call_target="tpu_custom_call" | custom-call | tf_op jit(solution)/shard_map/pallas_call | solution.py:221
  118.7 1.0 reshape.168
  120.3 0.9 copy.73
  (97 shorter events, 4.5 us)
Async XLA Ops:
  0.0 0.7 slice-start
  3.2 1.0 copy-start.7
  5.7 34.0 %collective-permute-start.2 = (f32[64,256]{1,0:T(8,128)S(1)}, f32[64,256]{1,0:T(8,128)S(1)}, u32[]{:S(2)}, u32[]{:S(2)}) collective-permute-start(f32[64,256]{1,0:T(8,128)S(1)} %reshape_squeeze.14), channel_id=1, source_target_pairs={{0,1},{1,2},{2,3},{3,4},{4,5},{5,6},{6,7},{7,0},{8,9},{9,10},{10,1... | collective-permute-start | bytes 196616 | tf_op jit(solution)/shard_map/ppermute | solution.py:248
  8.1 31.7 %collective-permute-start.3 = (f32[64,256]{1,0:T(8,128)S(1)}, f32[64,256]{1,0:T(8,128)S(1)}, u32[]{:S(2)}, u32[]{:S(2)}) collective-permute-start(f32[64,256]{1,0:T(8,128)S(1)} %reshape_squeeze.15), channel_id=1, source_target_pairs={{0,7},{1,0},{2,1},{3,2},{4,3},{5,4},{6,5},{7,6},{8,15},{9,8},{10,9... | collective-permute-start | bytes 196616 | tf_op jit(solution)/shard_map/ppermute | solution.py:249
  11.2 2.6 %copy-start.8 = (f32[4,2,2,4096]{3,2,1,0:T(2,128)S(1)}, f32[4,2,2,4096]{3,2,1,0:T(2,128)}, u32[]{:S(2)}) copy-start(f32[4,2,2,4096]{3,2,1,0:T(2,128)} %param.10) | copy-start | bytes 786436
  11.3 28.4 %collective-permute-start = (f32[64,128]{1,0:T(8,128)S(1)}, f32[64,128]{1,0:T(8,128)S(1)}, u32[]{:S(2)}, u32[]{:S(2)}) collective-permute-start(f32[64,128]{1,0:T(8,128)S(1)} %reshape_squeeze.12), channel_id=1, source_target_pairs={{0,8},{8,16},{16,24},{24,0},{1,9},{9,17},{17,25},{25,1},{2,10},{10... | collective-permute-start | bytes 98312 | tf_op jit(solution)/shard_map/ppermute | solution.py:244
  13.7 26.0 %collective-permute-start.1 = (f32[64,128]{1,0:T(8,128)S(1)}, f32[64,128]{1,0:T(8,128)S(1)}, u32[]{:S(2)}, u32[]{:S(2)}) collective-permute-start(f32[64,128]{1,0:T(8,128)S(1)} %reshape_squeeze.13), channel_id=1, source_target_pairs={{0,24},{8,0},{16,8},{24,16},{1,25},{9,1},{17,9},{25,17},{2,26},{10... | collective-permute-start | bytes 98312 | tf_op jit(solution)/shard_map/ppermute | solution.py:245
  36.9 0.7 copy-start.10
  36.9 0.7 copy-start.11
  36.9 0.7 copy-start.12
  38.3 0.9 copy-start.9
  41.4 10.0 %collective-permute-start.6 = (f32[64,256]{1,0:T(8,128)}, f32[64,256]{1,0:T(8,128)S(1)}, u32[]{:S(2)}, u32[]{:S(2)}) collective-permute-start(f32[64,256]{1,0:T(8,128)} %get-tuple-element.55), channel_id=1, source_target_pairs={{0,1},{1,2},{2,3},{3,4},{4,5},{5,6},{6,7},{7,0},{8,9},{9,10},{10,1... | collective-permute-start | bytes 196616 | tf_op jit(solution)/shard_map/ppermute | solution.py:248
  41.4 10.0 %collective-permute-start.7 = (f32[64,256]{1,0:T(8,128)}, f32[64,256]{1,0:T(8,128)S(1)}, u32[]{:S(2)}, u32[]{:S(2)}) collective-permute-start(f32[64,256]{1,0:T(8,128)} %get-tuple-element.56), channel_id=1, source_target_pairs={{0,7},{1,0},{2,1},{3,2},{4,3},{5,4},{6,5},{7,6},{8,15},{9,8},{10,9... | collective-permute-start | bytes 196616 | tf_op jit(solution)/shard_map/ppermute | solution.py:249
  45.5 3.6 %collective-permute-start.4 = (f32[64,128]{1,0:T(8,128)}, f32[64,128]{1,0:T(8,128)S(1)}, u32[]{:S(2)}, u32[]{:S(2)}) collective-permute-start(f32[64,128]{1,0:T(8,128)} %get-tuple-element.53), channel_id=1, source_target_pairs={{0,8},{8,16},{16,24},{24,0},{1,9},{9,17},{17,25},{25,1},{2,10},{10... | collective-permute-start | bytes 98312 | tf_op jit(solution)/shard_map/ppermute | solution.py:244
  47.8 3.6 %collective-permute-start.5 = (f32[64,128]{1,0:T(8,128)}, f32[64,128]{1,0:T(8,128)S(1)}, u32[]{:S(2)}, u32[]{:S(2)}) collective-permute-start(f32[64,128]{1,0:T(8,128)} %get-tuple-element.54), channel_id=1, source_target_pairs={{0,24},{8,0},{16,8},{24,16},{1,25},{9,1},{17,9},{25,17},{2,26},{10... | collective-permute-start | bytes 98312 | tf_op jit(solution)/shard_map/ppermute | solution.py:245
  51.4 0.9 copy-start.2
  53.9 8.4 %collective-permute-start.10 = (f32[64,256]{1,0:T(8,128)}, f32[64,256]{1,0:T(8,128)S(1)}, u32[]{:S(2)}, u32[]{:S(2)}) collective-permute-start(f32[64,256]{1,0:T(8,128)} %get-tuple-element.63), channel_id=1, source_target_pairs={{0,1},{1,2},{2,3},{3,4},{4,5},{5,6},{6,7},{7,0},{8,9},{9,10},{10,1... | collective-permute-start | bytes 196616 | tf_op jit(solution)/shard_map/ppermute | solution.py:248
  53.9 8.4 %collective-permute-start.11 = (f32[64,256]{1,0:T(8,128)}, f32[64,256]{1,0:T(8,128)S(1)}, u32[]{:S(2)}, u32[]{:S(2)}) collective-permute-start(f32[64,256]{1,0:T(8,128)} %get-tuple-element.64), channel_id=1, source_target_pairs={{0,7},{1,0},{2,1},{3,2},{4,3},{5,4},{6,5},{7,6},{8,15},{9,8},{10,9... | collective-permute-start | bytes 196616 | tf_op jit(solution)/shard_map/ppermute | solution.py:249
  58.1 2.0 %collective-permute-start.8 = (f32[64,128]{1,0:T(8,128)}, f32[64,128]{1,0:T(8,128)S(1)}, u32[]{:S(2)}, u32[]{:S(2)}) collective-permute-start(f32[64,128]{1,0:T(8,128)} %get-tuple-element.61), channel_id=1, source_target_pairs={{0,8},{8,16},{16,24},{24,0},{1,9},{9,17},{17,25},{25,1},{2,10},{10... | collective-permute-start | bytes 98312 | tf_op jit(solution)/shard_map/ppermute | solution.py:244
  58.8 3.6 %collective-permute-start.9 = (f32[64,128]{1,0:T(8,128)}, f32[64,128]{1,0:T(8,128)S(1)}, u32[]{:S(2)}, u32[]{:S(2)}) collective-permute-start(f32[64,128]{1,0:T(8,128)} %get-tuple-element.62), channel_id=1, source_target_pairs={{0,24},{8,0},{16,8},{24,16},{1,25},{9,1},{17,9},{25,17},{2,26},{10... | collective-permute-start | bytes 98312 | tf_op jit(solution)/shard_map/ppermute | solution.py:245
  62.3 0.9 copy-start.3
  64.9 8.4 %collective-permute-start.14 = (f32[64,256]{1,0:T(8,128)}, f32[64,256]{1,0:T(8,128)S(1)}, u32[]{:S(2)}, u32[]{:S(2)}) collective-permute-start(f32[64,256]{1,0:T(8,128)} %get-tuple-element.68), channel_id=1, source_target_pairs={{0,1},{1,2},{2,3},{3,4},{4,5},{5,6},{6,7},{7,0},{8,9},{9,10},{10,1... | collective-permute-start | bytes 196616 | tf_op jit(solution)/shard_map/ppermute | solution.py:248
  64.9 8.4 %collective-permute-start.15 = (f32[64,256]{1,0:T(8,128)}, f32[64,256]{1,0:T(8,128)S(1)}, u32[]{:S(2)}, u32[]{:S(2)}) collective-permute-start(f32[64,256]{1,0:T(8,128)} %get-tuple-element.69), channel_id=1, source_target_pairs={{0,7},{1,0},{2,1},{3,2},{4,3},{5,4},{6,5},{7,6},{8,15},{9,8},{10,9... | collective-permute-start | bytes 196616 | tf_op jit(solution)/shard_map/ppermute | solution.py:249
  69.1 2.0 %collective-permute-start.12 = (f32[64,128]{1,0:T(8,128)}, f32[64,128]{1,0:T(8,128)S(1)}, u32[]{:S(2)}, u32[]{:S(2)}) collective-permute-start(f32[64,128]{1,0:T(8,128)} %get-tuple-element.66), channel_id=1, source_target_pairs={{0,8},{8,16},{16,24},{24,0},{1,9},{9,17},{17,25},{25,1},{2,10},{10... | collective-permute-start | bytes 98312 | tf_op jit(solution)/shard_map/ppermute | solution.py:244
  69.7 3.6 %collective-permute-start.13 = (f32[64,128]{1,0:T(8,128)}, f32[64,128]{1,0:T(8,128)S(1)}, u32[]{:S(2)}, u32[]{:S(2)}) collective-permute-start(f32[64,128]{1,0:T(8,128)} %get-tuple-element.67), channel_id=1, source_target_pairs={{0,24},{8,0},{16,8},{24,16},{1,25},{9,1},{17,9},{25,17},{2,26},{10... | collective-permute-start | bytes 98312 | tf_op jit(solution)/shard_map/ppermute | solution.py:245
  73.3 0.9 copy-start.4
  75.8 8.4 %collective-permute-start.18 = (f32[64,256]{1,0:T(8,128)}, f32[64,256]{1,0:T(8,128)S(1)}, u32[]{:S(2)}, u32[]{:S(2)}) collective-permute-start(f32[64,256]{1,0:T(8,128)} %get-tuple-element.73), channel_id=1, source_target_pairs={{0,1},{1,2},{2,3},{3,4},{4,5},{5,6},{6,7},{7,0},{8,9},{9,10},{10,1... | collective-permute-start | bytes 196616 | tf_op jit(solution)/shard_map/ppermute | solution.py:248
  75.8 8.4 %collective-permute-start.19 = (f32[64,256]{1,0:T(8,128)}, f32[64,256]{1,0:T(8,128)S(1)}, u32[]{:S(2)}, u32[]{:S(2)}) collective-permute-start(f32[64,256]{1,0:T(8,128)} %get-tuple-element.74), channel_id=1, source_target_pairs={{0,7},{1,0},{2,1},{3,2},{4,3},{5,4},{6,5},{7,6},{8,15},{9,8},{10,9... | collective-permute-start | bytes 196616 | tf_op jit(solution)/shard_map/ppermute | solution.py:249
  80.0 2.0 %collective-permute-start.16 = (f32[64,128]{1,0:T(8,128)}, f32[64,128]{1,0:T(8,128)S(1)}, u32[]{:S(2)}, u32[]{:S(2)}) collective-permute-start(f32[64,128]{1,0:T(8,128)} %get-tuple-element.71), channel_id=1, source_target_pairs={{0,8},{8,16},{16,24},{24,0},{1,9},{9,17},{17,25},{25,1},{2,10},{10... | collective-permute-start | bytes 98312 | tf_op jit(solution)/shard_map/ppermute | solution.py:244
  80.7 3.6 %collective-permute-start.17 = (f32[64,128]{1,0:T(8,128)}, f32[64,128]{1,0:T(8,128)S(1)}, u32[]{:S(2)}, u32[]{:S(2)}) collective-permute-start(f32[64,128]{1,0:T(8,128)} %get-tuple-element.72), channel_id=1, source_target_pairs={{0,24},{8,0},{16,8},{24,16},{1,25},{9,1},{17,9},{25,17},{2,26},{10... | collective-permute-start | bytes 98312 | tf_op jit(solution)/shard_map/ppermute | solution.py:245
  84.2 0.9 copy-start.5
  86.8 8.4 %collective-permute-start.22 = (f32[64,256]{1,0:T(8,128)}, f32[64,256]{1,0:T(8,128)S(1)}, u32[]{:S(2)}, u32[]{:S(2)}) collective-permute-start(f32[64,256]{1,0:T(8,128)} %get-tuple-element.78), channel_id=1, source_target_pairs={{0,1},{1,2},{2,3},{3,4},{4,5},{5,6},{6,7},{7,0},{8,9},{9,10},{10,1... | collective-permute-start | bytes 196616 | tf_op jit(solution)/shard_map/ppermute | solution.py:248
  86.8 8.4 %collective-permute-start.23 = (f32[64,256]{1,0:T(8,128)}, f32[64,256]{1,0:T(8,128)S(1)}, u32[]{:S(2)}, u32[]{:S(2)}) collective-permute-start(f32[64,256]{1,0:T(8,128)} %get-tuple-element.79), channel_id=1, source_target_pairs={{0,7},{1,0},{2,1},{3,2},{4,3},{5,4},{6,5},{7,6},{8,15},{9,8},{10,9... | collective-permute-start | bytes 196616 | tf_op jit(solution)/shard_map/ppermute | solution.py:249
  90.9 2.0 %collective-permute-start.20 = (f32[64,128]{1,0:T(8,128)}, f32[64,128]{1,0:T(8,128)S(1)}, u32[]{:S(2)}, u32[]{:S(2)}) collective-permute-start(f32[64,128]{1,0:T(8,128)} %get-tuple-element.76), channel_id=1, source_target_pairs={{0,8},{8,16},{16,24},{24,0},{1,9},{9,17},{17,25},{25,1},{2,10},{10... | collective-permute-start | bytes 98312 | tf_op jit(solution)/shard_map/ppermute | solution.py:244
  91.6 3.6 %collective-permute-start.21 = (f32[64,128]{1,0:T(8,128)}, f32[64,128]{1,0:T(8,128)S(1)}, u32[]{:S(2)}, u32[]{:S(2)}) collective-permute-start(f32[64,128]{1,0:T(8,128)} %get-tuple-element.77), channel_id=1, source_target_pairs={{0,24},{8,0},{16,8},{24,16},{1,25},{9,1},{17,9},{25,17},{2,26},{10... | collective-permute-start | bytes 98312 | tf_op jit(solution)/shard_map/ppermute | solution.py:245
  95.2 0.9 copy-start.6
  97.7 8.4 %collective-permute-start.26 = (f32[64,256]{1,0:T(8,128)}, f32[64,256]{1,0:T(8,128)S(1)}, u32[]{:S(2)}, u32[]{:S(2)}) collective-permute-start(f32[64,256]{1,0:T(8,128)} %get-tuple-element.83), channel_id=1, source_target_pairs={{0,1},{1,2},{2,3},{3,4},{4,5},{5,6},{6,7},{7,0},{8,9},{9,10},{10,1... | collective-permute-start | bytes 196616 | tf_op jit(solution)/shard_map/ppermute | solution.py:248
  97.7 8.4 %collective-permute-start.27 = (f32[64,256]{1,0:T(8,128)}, f32[64,256]{1,0:T(8,128)S(1)}, u32[]{:S(2)}, u32[]{:S(2)}) collective-permute-start(f32[64,256]{1,0:T(8,128)} %get-tuple-element.84), channel_id=1, source_target_pairs={{0,7},{1,0},{2,1},{3,2},{4,3},{5,4},{6,5},{7,6},{8,15},{9,8},{10,9... | collective-permute-start | bytes 196616 | tf_op jit(solution)/shard_map/ppermute | solution.py:249
  101.9 2.0 %collective-permute-start.24 = (f32[64,128]{1,0:T(8,128)}, f32[64,128]{1,0:T(8,128)S(1)}, u32[]{:S(2)}, u32[]{:S(2)}) collective-permute-start(f32[64,128]{1,0:T(8,128)} %get-tuple-element.81), channel_id=1, source_target_pairs={{0,8},{8,16},{16,24},{24,0},{1,9},{9,17},{17,25},{25,1},{2,10},{10... | collective-permute-start | bytes 98312 | tf_op jit(solution)/shard_map/ppermute | solution.py:244
  102.6 3.6 %collective-permute-start.25 = (f32[64,128]{1,0:T(8,128)}, f32[64,128]{1,0:T(8,128)S(1)}, u32[]{:S(2)}, u32[]{:S(2)}) collective-permute-start(f32[64,128]{1,0:T(8,128)} %get-tuple-element.82), channel_id=1, source_target_pairs={{0,24},{8,0},{16,8},{24,16},{1,25},{9,1},{17,9},{25,17},{2,26},{10... | collective-permute-start | bytes 98312 | tf_op jit(solution)/shard_map/ppermute | solution.py:245
  106.1 0.9 copy-start.1
  108.7 8.4 %collective-permute-start.30 = (f32[64,256]{1,0:T(8,128)}, f32[64,256]{1,0:T(8,128)S(1)}, u32[]{:S(2)}, u32[]{:S(2)}) collective-permute-start(f32[64,256]{1,0:T(8,128)} %get-tuple-element.88), channel_id=1, source_target_pairs={{0,1},{1,2},{2,3},{3,4},{4,5},{5,6},{6,7},{7,0},{8,9},{9,10},{10,1... | collective-permute-start | bytes 196616 | tf_op jit(solution)/shard_map/ppermute | solution.py:248
  108.7 8.4 %collective-permute-start.31 = (f32[64,256]{1,0:T(8,128)}, f32[64,256]{1,0:T(8,128)S(1)}, u32[]{:S(2)}, u32[]{:S(2)}) collective-permute-start(f32[64,256]{1,0:T(8,128)} %get-tuple-element.89), channel_id=1, source_target_pairs={{0,7},{1,0},{2,1},{3,2},{4,3},{5,4},{6,5},{7,6},{8,15},{9,8},{10,9... | collective-permute-start | bytes 196616 | tf_op jit(solution)/shard_map/ppermute | solution.py:249
  112.8 2.0 %collective-permute-start.28 = (f32[64,128]{1,0:T(8,128)}, f32[64,128]{1,0:T(8,128)S(1)}, u32[]{:S(2)}, u32[]{:S(2)}) collective-permute-start(f32[64,128]{1,0:T(8,128)} %get-tuple-element.86), channel_id=1, source_target_pairs={{0,8},{8,16},{16,24},{24,0},{1,9},{9,17},{17,25},{25,1},{2,10},{10... | collective-permute-start | bytes 98312 | tf_op jit(solution)/shard_map/ppermute | solution.py:244
  113.5 3.6 %collective-permute-start.29 = (f32[64,128]{1,0:T(8,128)}, f32[64,128]{1,0:T(8,128)S(1)}, u32[]{:S(2)}, u32[]{:S(2)}) collective-permute-start(f32[64,128]{1,0:T(8,128)} %get-tuple-element.87), channel_id=1, source_target_pairs={{0,24},{8,0},{16,8},{24,16},{1,25},{9,1},{17,9},{25,17},{2,26},{10... | collective-permute-start | bytes 98312 | tf_op jit(solution)/shard_map/ppermute | solution.py:245
  114.6 2.5 %copy-start = (f32[64,512]{1,0:T(8,128)S(1)}, f32[64,512]{1,0:T(8,128)}, u32[]{:S(2)}) copy-start(f32[64,512]{1,0:T(8,128)} %get-tuple-element.85.other_ref) | copy-start | bytes 393220

commit v5 on v4

--- a/solution.py
+++ b/solution.py
@@ -223,9 +223,9 @@
         out_shape=(jax.ShapeDtypeStruct((P_SIZE, lanes), jnp.float32), x_shape, x_shape, y_shape, y_shape),
         in_specs=[vmem] * 9,
         out_specs=(vmem,) * 5,
-    )(*[
+    )(other, *[
         pltpu.with_memory_space_constraint(value, pltpu.VMEM)
-        for value in (other, *halos, face_blocks, weight, inverse, target)
+        for value in (*halos, face_blocks, weight, inverse, target)
     ])
 
 

time: 122 us -> 124 us (1.016)
  Pallas kernels: 32.4 us -> 39.7 us
  local copies, waits for them, and re-layouts: 20.9 us -> 16.1 us
    pallas_call x8, Pallas kernels: 13.2 us -> 20.5 us  [half_sweep(): pl.pallas_call(functools.partial(_half_sweep_kernel, span_x=span_x), out_...]
    unnamed x30 -> x16, local copies, waits for them, and re-layouts: 7.58 us -> 2.15 us
where the time goes in v5:
time: 124 us
  starting transfers between devices  42.9 us (35%)
  Pallas kernels  39.7 us (32%)
  waiting for transfers between devices  23.7 us (19%)
  local copies, waits for them, and re-layouts  16.1 us (13%)
    ppermute x8, starting transfers between devices, trade(): lax.ppermute(sends[3], 'gy', shift_pairs('gy', -1))  32.2 us
    pallas_call x8, Pallas kernels, half_sweep(): pl.pallas_call(functools.partial(_half_sweep_kernel, span_x=span_x), out_...  20.5 us
    pallas_call x1, Pallas kernels, block_inverses(): pl.pallas_call(functools.partial(_gauss_jordan_kernel, n=n, nb=nb), out_s...  19.2 us
    ppermute x8, waiting for transfers between devices, trade(): lax.ppermute(sends[1], 'gx', shift_pairs('gx', -1))  15.5 us
    ppermute x8, starting transfers between devices, trade(): lax.ppermute(sends[0], 'gx', shift_pairs('gx', 1))  8.56 us
    ppermute x8, waiting for transfers between devices, trade(): lax.ppermute(sends[0], 'gx', shift_pairs('gx', 1))  8.15 us
    slice x3, local copies, waits for them, and re-layouts, pick(): high = lax.index_in_dim(values, 1, axis=axis, keepdims=False)  2.68 us
  transfers between devices with their start and end apart: 32, of which 14 were waited for; matrix products, arithmetic and copies ran while one was open for 6% of the time, Pallas kernels for 16%

profile of v5, /device:TPU:1, one launch (start us, length us, event | category | flops | bytes accessed | tf_op | source)
XLA Modules:
  0.0 123.7 jit_solution(5745670270364373243)
XLA Ops:
  0.0 0.7 slice-done
  1.1 1.9 %slice_reduce_fusion.2 = (f32[4,2,4096]{2,1,0:T(2,128)S(1)}, f32[4,2,4096]{2,1,0:T(2,128)S(1)}) fusion(f32[4,2,2,4096]{3,2,1,0:T(2,128)} %param.9), kind=kLoop, calls=%fused_computation.10 | loop fusion | bytes 524288 | tf_op jit(solution)/shard_map/slice | solution.py:270
  3.0 0.2 squeeze.32
  3.2 0.2 squeeze.33
  3.4 0.7 copy-done
  4.1 0.8 slice_reduce_fusion
  4.9 0.2 squeeze.36
  5.1 0.2 squeeze.37
  5.7 2.1 %collective-permute-start.2 = (f32[64,256]{1,0:T(8,128)S(1)}, f32[64,256]{1,0:T(8,128)S(1)}, u32[]{:S(2)}, u32[]{:S(2)}) collective-permute-start(f32[64,256]{1,0:T(8,128)S(1)} %reshape_squeeze.14), channel_id=1, source_target_pairs={{0,1},{1,2},{2,3},{3,4},{4,5},{5,6},{6,7},{7,0},{8,9},{9,10},{10,1... | collective-permute-start | bytes 196616 | tf_op jit(solution)/shard_map/ppermute | solution.py:248
  8.1 3.1 %collective-permute-start.3 = (f32[64,256]{1,0:T(8,128)S(1)}, f32[64,256]{1,0:T(8,128)S(1)}, u32[]{:S(2)}, u32[]{:S(2)}) collective-permute-start(f32[64,256]{1,0:T(8,128)S(1)} %reshape_squeeze.15), channel_id=1, source_target_pairs={{0,7},{1,0},{2,1},{3,2},{4,3},{5,4},{6,5},{7,6},{8,15},{9,8},{10,9... | collective-permute-start | bytes 196616 | tf_op jit(solution)/shard_map/ppermute | solution.py:249
  11.3 2.2 %collective-permute-start = (f32[64,128]{1,0:T(8,128)S(1)}, f32[64,128]{1,0:T(8,128)S(1)}, u32[]{:S(2)}, u32[]{:S(2)}) collective-permute-start(f32[64,128]{1,0:T(8,128)S(1)} %reshape_squeeze.12), channel_id=1, source_target_pairs={{0,8},{8,16},{16,24},{24,0},{1,9},{9,17},{17,25},{25,1},{2,10},{10... | collective-permute-start | bytes 98312 | tf_op jit(solution)/shard_map/ppermute | solution.py:244
  13.7 0.3 broadcast_select_fusion.1
  14.0 0.2 pad_maximum_fusion
  14.3 0.2 copy.60
  14.5 0.3 reshape.157
  14.8 0.3 copy.61
  15.1 0.9 copy.62.a_ref
  16.0 19.2 %shard_map.82 = f32[64,1024]{1,0:T(8,128)} custom-call(f32[64,1024]{1,0:T(8,128)} %copy.62.a_ref), custom_call_target="tpu_custom_call" | custom-call | flops 8388608000 | bytes 524288 | tf_op jit(solution)/shard_map/pallas_call | solution.py:75
  35.2 1.1 copy.63
  36.3 0.4 copy.64
  36.7 0.2 reshape.160
  37.0 0.6 copy-done.3
  37.7 0.2 copy.66
  38.8 0.4 copy-done.2
  39.6 0.8 reshape.156.other_ref
  40.4 2.6 %shard_map.83 = (f32[64,512]{1,0:T(8,128)}, f32[64,128]{1,0:T(8,128)}, f32[64,128]{1,0:T(8,128)}, f32[64,256]{1,0:T(8,128)}, f32[64,256]{1,0:T(8,128)}) custom-call(f32[64,512]{1,0:T(8,128)} %reshape.156.other_ref, f32[64,128]{1,0:T(8,128)S(1)} %collective-permute-done.lo_x_ref, f32[64,128]{1,0:T(8,128)S(1)} %collective-permute-done.1.hi_x_ref, ...), custom_call_target="tpu_custom_call" | custom-call | tf_op jit(solution)/shard_map/pallas_call | solution.py:221
  43.0 4.2 %collective-permute-start.7 = (f32[64,256]{1,0:T(8,128)}, f32[64,256]{1,0:T(8,128)S(1)}, u32[]{:S(2)}, u32[]{:S(2)}) collective-permute-start(f32[64,256]{1,0:T(8,128)} %get-tuple-element.56), channel_id=1, source_target_pairs={{0,7},{1,0},{2,1},{3,2},{4,3},{5,4},{6,5},{7,6},{8,15},{9,8},{10,9... | collective-permute-start | bytes 196616 | tf_op jit(solution)/shard_map/ppermute | solution.py:249
  47.1 2.3 %collective-permute-start.4 = (f32[64,128]{1,0:T(8,128)}, f32[64,128]{1,0:T(8,128)S(1)}, u32[]{:S(2)}, u32[]{:S(2)}) collective-permute-start(f32[64,128]{1,0:T(8,128)} %get-tuple-element.53), channel_id=1, source_target_pairs={{0,8},{8,16},{16,24},{24,0},{1,9},{9,17},{17,25},{25,1},{2,10},{10... | collective-permute-start | bytes 98312 | tf_op jit(solution)/shard_map/ppermute | solution.py:244
  49.4 1.3 %collective-permute-done.4.lo_x_ref = f32[64,128]{1,0:T(8,128)S(1)} collective-permute-done((f32[64,128]{1,0:T(8,128)}, f32[64,128]{1,0:T(8,128)S(1)}, u32[]{:S(2)}, u32[]{:S(2)}) %collective-permute-start.4) | collective-permute-done | bytes 32800 | tf_op jit(solution)/shard_map/ppermute | solution.py:244
  50.7 2.2 %collective-permute-done.5.hi_x_ref = f32[64,128]{1,0:T(8,128)S(1)} collective-permute-done((f32[64,128]{1,0:T(8,128)}, f32[64,128]{1,0:T(8,128)S(1)}, u32[]{:S(2)}, u32[]{:S(2)}) %collective-permute-start.5) | collective-permute-done | bytes 32800 | tf_op jit(solution)/shard_map/ppermute | solution.py:245
  53.0 2.6 %shard_map.84 = (f32[64,512]{1,0:T(8,128)}, f32[64,128]{1,0:T(8,128)}, f32[64,128]{1,0:T(8,128)}, f32[64,256]{1,0:T(8,128)}, f32[64,256]{1,0:T(8,128)}) custom-call(f32[64,512]{1,0:T(8,128)} %get-tuple-element.52.other_ref, f32[64,128]{1,0:T(8,128)S(1)} %collective-permute-done.4.lo_x_ref, f32[64,128]{1,0:T(8,128)S(1)} %collective-permute-done.5.hi_x_ref, ...), custom_call_target="tpu_custom_call" | custom-call | tf_op jit(solution)/shard_map/pallas_call | solution.py:221
  55.5 4.2 %collective-permute-start.11 = (f32[64,256]{1,0:T(8,128)}, f32[64,256]{1,0:T(8,128)S(1)}, u32[]{:S(2)}, u32[]{:S(2)}) collective-permute-start(f32[64,256]{1,0:T(8,128)} %get-tuple-element.64), channel_id=1, source_target_pairs={{0,7},{1,0},{2,1},{3,2},{4,3},{5,4},{6,5},{7,6},{8,15},{9,8},{10,9... | collective-permute-start | bytes 196616 | tf_op jit(solution)/shard_map/ppermute | solution.py:249
  59.7 0.7 collective-permute-start.8
  60.4 1.3 %collective-permute-done.8.lo_x_ref = f32[64,128]{1,0:T(8,128)S(1)} collective-permute-done((f32[64,128]{1,0:T(8,128)}, f32[64,128]{1,0:T(8,128)S(1)}, u32[]{:S(2)}, u32[]{:S(2)}) %collective-permute-start.8) | collective-permute-done | bytes 32800 | tf_op jit(solution)/shard_map/ppermute | solution.py:244
  61.7 2.2 %collective-permute-done.9.hi_x_ref = f32[64,128]{1,0:T(8,128)S(1)} collective-permute-done((f32[64,128]{1,0:T(8,128)}, f32[64,128]{1,0:T(8,128)S(1)}, u32[]{:S(2)}, u32[]{:S(2)}) %collective-permute-start.9) | collective-permute-done | bytes 32800 | tf_op jit(solution)/shard_map/ppermute | solution.py:245
  63.9 2.6 %shard_map.85 = (f32[64,512]{1,0:T(8,128)}, f32[64,128]{1,0:T(8,128)}, f32[64,128]{1,0:T(8,128)}, f32[64,256]{1,0:T(8,128)}, f32[64,256]{1,0:T(8,128)}) custom-call(f32[64,512]{1,0:T(8,128)} %get-tuple-element.60.other_ref, f32[64,128]{1,0:T(8,128)S(1)} %collective-permute-done.8.lo_x_ref, f32[64,128]{1,0:T(8,128)S(1)} %collective-permute-done.9.hi_x_ref, ...), custom_call_target="tpu_custom_call" | custom-call | tf_op jit(solution)/shard_map/pallas_call | solution.py:221
  66.5 4.2 %collective-permute-start.15 = (f32[64,256]{1,0:T(8,128)}, f32[64,256]{1,0:T(8,128)S(1)}, u32[]{:S(2)}, u32[]{:S(2)}) collective-permute-start(f32[64,256]{1,0:T(8,128)} %get-tuple-element.69), channel_id=1, source_target_pairs={{0,7},{1,0},{2,1},{3,2},{4,3},{5,4},{6,5},{7,6},{8,15},{9,8},{10,9... | collective-permute-start | bytes 196616 | tf_op jit(solution)/shard_map/ppermute | solution.py:249
  70.7 0.7 collective-permute-start.12
  71.4 1.3 %collective-permute-done.12.lo_x_ref = f32[64,128]{1,0:T(8,128)S(1)} collective-permute-done((f32[64,128]{1,0:T(8,128)}, f32[64,128]{1,0:T(8,128)S(1)}, u32[]{:S(2)}, u32[]{:S(2)}) %collective-permute-start.12) | collective-permute-done | bytes 32800 | tf_op jit(solution)/shard_map/ppermute | solution.py:244
  72.7 2.2 %collective-permute-done.13.hi_x_ref = f32[64,128]{1,0:T(8,128)S(1)} collective-permute-done((f32[64,128]{1,0:T(8,128)}, f32[64,128]{1,0:T(8,128)S(1)}, u32[]{:S(2)}, u32[]{:S(2)}) %collective-permute-start.13) | collective-permute-done | bytes 32800 | tf_op jit(solution)/shard_map/ppermute | solution.py:245
  74.9 2.6 %shard_map.86 = (f32[64,512]{1,0:T(8,128)}, f32[64,128]{1,0:T(8,128)}, f32[64,128]{1,0:T(8,128)}, f32[64,256]{1,0:T(8,128)}, f32[64,256]{1,0:T(8,128)}) custom-call(f32[64,512]{1,0:T(8,128)} %get-tuple-element.65.other_ref, f32[64,128]{1,0:T(8,128)S(1)} %collective-permute-done.12.lo_x_ref, f32[64,128]{1,0:T(8,128)S(1)} %collective-permute-done.13.hi_x_ref, ...), custom_call_target="tpu_custom_call" | custom-call | tf_op jit(solution)/shard_map/pallas_call | solution.py:221
  77.5 4.2 %collective-permute-start.19 = (f32[64,256]{1,0:T(8,128)}, f32[64,256]{1,0:T(8,128)S(1)}, u32[]{:S(2)}, u32[]{:S(2)}) collective-permute-start(f32[64,256]{1,0:T(8,128)} %get-tuple-element.74), channel_id=1, source_target_pairs={{0,7},{1,0},{2,1},{3,2},{4,3},{5,4},{6,5},{7,6},{8,15},{9,8},{10,9... | collective-permute-start | bytes 196616 | tf_op jit(solution)/shard_map/ppermute | solution.py:249
  81.6 0.7 collective-permute-start.16
  82.3 1.3 %collective-permute-done.16.lo_x_ref = f32[64,128]{1,0:T(8,128)S(1)} collective-permute-done((f32[64,128]{1,0:T(8,128)}, f32[64,128]{1,0:T(8,128)S(1)}, u32[]{:S(2)}, u32[]{:S(2)}) %collective-permute-start.16) | collective-permute-done | bytes 32800 | tf_op jit(solution)/shard_map/ppermute | solution.py:244
  83.6 2.2 %collective-permute-done.17.hi_x_ref = f32[64,128]{1,0:T(8,128)S(1)} collective-permute-done((f32[64,128]{1,0:T(8,128)}, f32[64,128]{1,0:T(8,128)S(1)}, u32[]{:S(2)}, u32[]{:S(2)}) %collective-permute-start.17) | collective-permute-done | bytes 32800 | tf_op jit(solution)/shard_map/ppermute | solution.py:245
  85.9 2.6 %shard_map.87 = (f32[64,512]{1,0:T(8,128)}, f32[64,128]{1,0:T(8,128)}, f32[64,128]{1,0:T(8,128)}, f32[64,256]{1,0:T(8,128)}, f32[64,256]{1,0:T(8,128)}) custom-call(f32[64,512]{1,0:T(8,128)} %get-tuple-element.70.other_ref, f32[64,128]{1,0:T(8,128)S(1)} %collective-permute-done.16.lo_x_ref, f32[64,128]{1,0:T(8,128)S(1)} %collective-permute-done.17.hi_x_ref, ...), custom_call_target="tpu_custom_call" | custom-call | tf_op jit(solution)/shard_map/pallas_call | solution.py:221
  88.4 4.2 %collective-permute-start.23 = (f32[64,256]{1,0:T(8,128)}, f32[64,256]{1,0:T(8,128)S(1)}, u32[]{:S(2)}, u32[]{:S(2)}) collective-permute-start(f32[64,256]{1,0:T(8,128)} %get-tuple-element.79), channel_id=1, source_target_pairs={{0,7},{1,0},{2,1},{3,2},{4,3},{5,4},{6,5},{7,6},{8,15},{9,8},{10,9... | collective-permute-start | bytes 196616 | tf_op jit(solution)/shard_map/ppermute | solution.py:249
  92.6 0.7 collective-permute-start.20
  93.3 1.3 %collective-permute-done.20.lo_x_ref = f32[64,128]{1,0:T(8,128)S(1)} collective-permute-done((f32[64,128]{1,0:T(8,128)}, f32[64,128]{1,0:T(8,128)S(1)}, u32[]{:S(2)}, u32[]{:S(2)}) %collective-permute-start.20) | collective-permute-done | bytes 32800 | tf_op jit(solution)/shard_map/ppermute | solution.py:244
  94.6 2.2 %collective-permute-done.21.hi_x_ref = f32[64,128]{1,0:T(8,128)S(1)} collective-permute-done((f32[64,128]{1,0:T(8,128)}, f32[64,128]{1,0:T(8,128)S(1)}, u32[]{:S(2)}, u32[]{:S(2)}) %collective-permute-start.21) | collective-permute-done | bytes 32800 | tf_op jit(solution)/shard_map/ppermute | solution.py:245
  96.8 2.6 %shard_map.88 = (f32[64,512]{1,0:T(8,128)}, f32[64,128]{1,0:T(8,128)}, f32[64,128]{1,0:T(8,128)}, f32[64,256]{1,0:T(8,128)}, f32[64,256]{1,0:T(8,128)}) custom-call(f32[64,512]{1,0:T(8,128)} %get-tuple-element.75.other_ref, f32[64,128]{1,0:T(8,128)S(1)} %collective-permute-done.20.lo_x_ref, f32[64,128]{1,0:T(8,128)S(1)} %collective-permute-done.21.hi_x_ref, ...), custom_call_target="tpu_custom_call" | custom-call | tf_op jit(solution)/shard_map/pallas_call | solution.py:221
  99.4 4.2 %collective-permute-start.27 = (f32[64,256]{1,0:T(8,128)}, f32[64,256]{1,0:T(8,128)S(1)}, u32[]{:S(2)}, u32[]{:S(2)}) collective-permute-start(f32[64,256]{1,0:T(8,128)} %get-tuple-element.84), channel_id=1, source_target_pairs={{0,7},{1,0},{2,1},{3,2},{4,3},{5,4},{6,5},{7,6},{8,15},{9,8},{10,9... | collective-permute-start | bytes 196616 | tf_op jit(solution)/shard_map/ppermute | solution.py:249
  103.5 0.7 collective-permute-start.24
  104.2 1.3 %collective-permute-done.24.lo_x_ref = f32[64,128]{1,0:T(8,128)S(1)} collective-permute-done((f32[64,128]{1,0:T(8,128)}, f32[64,128]{1,0:T(8,128)S(1)}, u32[]{:S(2)}, u32[]{:S(2)}) %collective-permute-start.24) | collective-permute-done | bytes 32800 | tf_op jit(solution)/shard_map/ppermute | solution.py:244
  105.5 2.2 %collective-permute-done.25.hi_x_ref = f32[64,128]{1,0:T(8,128)S(1)} collective-permute-done((f32[64,128]{1,0:T(8,128)}, f32[64,128]{1,0:T(8,128)S(1)}, u32[]{:S(2)}, u32[]{:S(2)}) %collective-permute-start.25) | collective-permute-done | bytes 32800 | tf_op jit(solution)/shard_map/ppermute | solution.py:245
  107.8 2.6 %shard_map.89 = (f32[64,512]{1,0:T(8,128)}, f32[64,128]{1,0:T(8,128)}, f32[64,128]{1,0:T(8,128)}, f32[64,256]{1,0:T(8,128)}, f32[64,256]{1,0:T(8,128)}) custom-call(f32[64,512]{1,0:T(8,128)} %get-tuple-element.80.other_ref, f32[64,128]{1,0:T(8,128)S(1)} %collective-permute-done.24.lo_x_ref, f32[64,128]{1,0:T(8,128)S(1)} %collective-permute-done.25.hi_x_ref, ...), custom_call_target="tpu_custom_call" | custom-call | tf_op jit(solution)/shard_map/pallas_call | solution.py:221
  110.3 4.2 %collective-permute-start.31 = (f32[64,256]{1,0:T(8,128)}, f32[64,256]{1,0:T(8,128)S(1)}, u32[]{:S(2)}, u32[]{:S(2)}) collective-permute-start(f32[64,256]{1,0:T(8,128)} %get-tuple-element.89), channel_id=1, source_target_pairs={{0,7},{1,0},{2,1},{3,2},{4,3},{5,4},{6,5},{7,6},{8,15},{9,8},{10,9... | collective-permute-start | bytes 196616 | tf_op jit(solution)/shard_map/ppermute | solution.py:249
  114.5 0.7 collective-permute-start.28
  115.2 1.0 reshape.166
  116.5 2.2 %collective-permute-done.29.hi_x_ref = f32[64,128]{1,0:T(8,128)S(1)} collective-permute-done((f32[64,128]{1,0:T(8,128)}, f32[64,128]{1,0:T(8,128)S(1)}, u32[]{:S(2)}, u32[]{:S(2)}) %collective-permute-start.29) | collective-permute-done | bytes 32800 | tf_op jit(solution)/shard_map/ppermute | solution.py:245
  118.7 2.6 %shard_map.90 = (f32[64,512]{1,0:T(8,128)}, f32[64,128]{1,0:T(8,128)}, f32[64,128]{1,0:T(8,128)}, f32[64,256]{1,0:T(8,128)}, f32[64,256]{1,0:T(8,128)}) custom-call(f32[64,512]{1,0:T(8,128)} %get-tuple-element.85.other_ref, f32[64,128]{1,0:T(8,128)S(1)} %collective-permute-done.28.lo_x_ref, f32[64,128]{1,0:T(8,128)S(1)} %collective-permute-done.29.hi_x_ref, ...), custom_call_target="tpu_custom_call" | custom-call | tf_op jit(solution)/shard_map/pallas_call | solution.py:221
  121.3 1.0 reshape.168
  122.5 0.2 broadcast_select_fusion.4
  122.8 0.9 copy.73
  (83 shorter events, 3.5 us)
Async XLA Ops:
  0.0 0.7 slice-start
  3.2 1.0 copy-start
  5.7 34.7 %collective-permute-start.2 = (f32[64,256]{1,0:T(8,128)S(1)}, f32[64,256]{1,0:T(8,128)S(1)}, u32[]{:S(2)}, u32[]{:S(2)}) collective-permute-start(f32[64,256]{1,0:T(8,128)S(1)} %reshape_squeeze.14), channel_id=1, source_target_pairs={{0,1},{1,2},{2,3},{3,4},{4,5},{5,6},{6,7},{7,0},{8,9},{9,10},{10,1... | collective-permute-start | bytes 196616 | tf_op jit(solution)/shard_map/ppermute | solution.py:248
  8.1 32.3 %collective-permute-start.3 = (f32[64,256]{1,0:T(8,128)S(1)}, f32[64,256]{1,0:T(8,128)S(1)}, u32[]{:S(2)}, u32[]{:S(2)}) collective-permute-start(f32[64,256]{1,0:T(8,128)S(1)} %reshape_squeeze.15), channel_id=1, source_target_pairs={{0,7},{1,0},{2,1},{3,2},{4,3},{5,4},{6,5},{7,6},{8,15},{9,8},{10,9... | collective-permute-start | bytes 196616 | tf_op jit(solution)/shard_map/ppermute | solution.py:249
  11.2 2.6 %copy-start.1 = (f32[4,2,2,4096]{3,2,1,0:T(2,128)S(1)}, f32[4,2,2,4096]{3,2,1,0:T(2,128)}, u32[]{:S(2)}) copy-start(f32[4,2,2,4096]{3,2,1,0:T(2,128)} %param.10) | copy-start | bytes 786436
  11.3 29.0 %collective-permute-start = (f32[64,128]{1,0:T(8,128)S(1)}, f32[64,128]{1,0:T(8,128)S(1)}, u32[]{:S(2)}, u32[]{:S(2)}) collective-permute-start(f32[64,128]{1,0:T(8,128)S(1)} %reshape_squeeze.12), channel_id=1, source_target_pairs={{0,8},{8,16},{16,24},{24,0},{1,9},{9,17},{17,25},{25,1},{2,10},{10... | collective-permute-start | bytes 98312 | tf_op jit(solution)/shard_map/ppermute | solution.py:244
  13.7 26.7 %collective-permute-start.1 = (f32[64,128]{1,0:T(8,128)S(1)}, f32[64,128]{1,0:T(8,128)S(1)}, u32[]{:S(2)}, u32[]{:S(2)}) collective-permute-start(f32[64,128]{1,0:T(8,128)S(1)} %reshape_squeeze.13), channel_id=1, source_target_pairs={{0,24},{8,0},{16,8},{24,16},{1,25},{9,1},{17,9},{25,17},{2,26},{10... | collective-permute-start | bytes 98312 | tf_op jit(solution)/shard_map/ppermute | solution.py:245
  36.9 0.7 copy-start.3
  36.9 0.7 copy-start.4
  36.9 0.7 copy-start.5
  38.3 0.9 copy-start.2
  43.0 10.0 %collective-permute-start.6 = (f32[64,256]{1,0:T(8,128)}, f32[64,256]{1,0:T(8,128)S(1)}, u32[]{:S(2)}, u32[]{:S(2)}) collective-permute-start(f32[64,256]{1,0:T(8,128)} %get-tuple-element.55), channel_id=1, source_target_pairs={{0,1},{1,2},{2,3},{3,4},{4,5},{5,6},{6,7},{7,0},{8,9},{9,10},{10,1... | collective-permute-start | bytes 196616 | tf_op jit(solution)/shard_map/ppermute | solution.py:248
  43.0 10.0 %collective-permute-start.7 = (f32[64,256]{1,0:T(8,128)}, f32[64,256]{1,0:T(8,128)S(1)}, u32[]{:S(2)}, u32[]{:S(2)}) collective-permute-start(f32[64,256]{1,0:T(8,128)} %get-tuple-element.56), channel_id=1, source_target_pairs={{0,7},{1,0},{2,1},{3,2},{4,3},{5,4},{6,5},{7,6},{8,15},{9,8},{10,9... | collective-permute-start | bytes 196616 | tf_op jit(solution)/shard_map/ppermute | solution.py:249
  47.1 3.6 %collective-permute-start.4 = (f32[64,128]{1,0:T(8,128)}, f32[64,128]{1,0:T(8,128)S(1)}, u32[]{:S(2)}, u32[]{:S(2)}) collective-permute-start(f32[64,128]{1,0:T(8,128)} %get-tuple-element.53), channel_id=1, source_target_pairs={{0,8},{8,16},{16,24},{24,0},{1,9},{9,17},{17,25},{25,1},{2,10},{10... | collective-permute-start | bytes 98312 | tf_op jit(solution)/shard_map/ppermute | solution.py:244
  49.4 3.6 %collective-permute-start.5 = (f32[64,128]{1,0:T(8,128)}, f32[64,128]{1,0:T(8,128)S(1)}, u32[]{:S(2)}, u32[]{:S(2)}) collective-permute-start(f32[64,128]{1,0:T(8,128)} %get-tuple-element.54), channel_id=1, source_target_pairs={{0,24},{8,0},{16,8},{24,16},{1,25},{9,1},{17,9},{25,17},{2,26},{10... | collective-permute-start | bytes 98312 | tf_op jit(solution)/shard_map/ppermute | solution.py:245
  55.5 8.4 %collective-permute-start.10 = (f32[64,256]{1,0:T(8,128)}, f32[64,256]{1,0:T(8,128)S(1)}, u32[]{:S(2)}, u32[]{:S(2)}) collective-permute-start(f32[64,256]{1,0:T(8,128)} %get-tuple-element.63), channel_id=1, source_target_pairs={{0,1},{1,2},{2,3},{3,4},{4,5},{5,6},{6,7},{7,0},{8,9},{9,10},{10,1... | collective-permute-start | bytes 196616 | tf_op jit(solution)/shard_map/ppermute | solution.py:248
  55.5 8.4 %collective-permute-start.11 = (f32[64,256]{1,0:T(8,128)}, f32[64,256]{1,0:T(8,128)S(1)}, u32[]{:S(2)}, u32[]{:S(2)}) collective-permute-start(f32[64,256]{1,0:T(8,128)} %get-tuple-element.64), channel_id=1, source_target_pairs={{0,7},{1,0},{2,1},{3,2},{4,3},{5,4},{6,5},{7,6},{8,15},{9,8},{10,9... | collective-permute-start | bytes 196616 | tf_op jit(solution)/shard_map/ppermute | solution.py:249
  59.7 2.0 %collective-permute-start.8 = (f32[64,128]{1,0:T(8,128)}, f32[64,128]{1,0:T(8,128)S(1)}, u32[]{:S(2)}, u32[]{:S(2)}) collective-permute-start(f32[64,128]{1,0:T(8,128)} %get-tuple-element.61), channel_id=1, source_target_pairs={{0,8},{8,16},{16,24},{24,0},{1,9},{9,17},{17,25},{25,1},{2,10},{10... | collective-permute-start | bytes 98312 | tf_op jit(solution)/shard_map/ppermute | solution.py:244
  60.4 3.6 %collective-permute-start.9 = (f32[64,128]{1,0:T(8,128)}, f32[64,128]{1,0:T(8,128)S(1)}, u32[]{:S(2)}, u32[]{:S(2)}) collective-permute-start(f32[64,128]{1,0:T(8,128)} %get-tuple-element.62), channel_id=1, source_target_pairs={{0,24},{8,0},{16,8},{24,16},{1,25},{9,1},{17,9},{25,17},{2,26},{10... | collective-permute-start | bytes 98312 | tf_op jit(solution)/shard_map/ppermute | solution.py:245
  66.5 8.4 %collective-permute-start.14 = (f32[64,256]{1,0:T(8,128)}, f32[64,256]{1,0:T(8,128)S(1)}, u32[]{:S(2)}, u32[]{:S(2)}) collective-permute-start(f32[64,256]{1,0:T(8,128)} %get-tuple-element.68), channel_id=1, source_target_pairs={{0,1},{1,2},{2,3},{3,4},{4,5},{5,6},{6,7},{7,0},{8,9},{9,10},{10,1... | collective-permute-start | bytes 196616 | tf_op jit(solution)/shard_map/ppermute | solution.py:248
  66.5 8.4 %collective-permute-start.15 = (f32[64,256]{1,0:T(8,128)}, f32[64,256]{1,0:T(8,128)S(1)}, u32[]{:S(2)}, u32[]{:S(2)}) collective-permute-start(f32[64,256]{1,0:T(8,128)} %get-tuple-element.69), channel_id=1, source_target_pairs={{0,7},{1,0},{2,1},{3,2},{4,3},{5,4},{6,5},{7,6},{8,15},{9,8},{10,9... | collective-permute-start | bytes 196616 | tf_op jit(solution)/shard_map/ppermute | solution.py:249
  70.7 2.0 %collective-permute-start.12 = (f32[64,128]{1,0:T(8,128)}, f32[64,128]{1,0:T(8,128)S(1)}, u32[]{:S(2)}, u32[]{:S(2)}) collective-permute-start(f32[64,128]{1,0:T(8,128)} %get-tuple-element.66), channel_id=1, source_target_pairs={{0,8},{8,16},{16,24},{24,0},{1,9},{9,17},{17,25},{25,1},{2,10},{10... | collective-permute-start | bytes 98312 | tf_op jit(solution)/shard_map/ppermute | solution.py:244
  71.4 3.6 %collective-permute-start.13 = (f32[64,128]{1,0:T(8,128)}, f32[64,128]{1,0:T(8,128)S(1)}, u32[]{:S(2)}, u32[]{:S(2)}) collective-permute-start(f32[64,128]{1,0:T(8,128)} %get-tuple-element.67), channel_id=1, source_target_pairs={{0,24},{8,0},{16,8},{24,16},{1,25},{9,1},{17,9},{25,17},{2,26},{10... | collective-permute-start | bytes 98312 | tf_op jit(solution)/shard_map/ppermute | solution.py:245
  77.5 8.4 %collective-permute-start.18 = (f32[64,256]{1,0:T(8,128)}, f32[64,256]{1,0:T(8,128)S(1)}, u32[]{:S(2)}, u32[]{:S(2)}) collective-permute-start(f32[64,256]{1,0:T(8,128)} %get-tuple-element.73), channel_id=1, source_target_pairs={{0,1},{1,2},{2,3},{3,4},{4,5},{5,6},{6,7},{7,0},{8,9},{9,10},{10,1... | collective-permute-start | bytes 196616 | tf_op jit(solution)/shard_map/ppermute | solution.py:248
  77.5 8.4 %collective-permute-start.19 = (f32[64,256]{1,0:T(8,128)}, f32[64,256]{1,0:T(8,128)S(1)}, u32[]{:S(2)}, u32[]{:S(2)}) collective-permute-start(f32[64,256]{1,0:T(8,128)} %get-tuple-element.74), channel_id=1, source_target_pairs={{0,7},{1,0},{2,1},{3,2},{4,3},{5,4},{6,5},{7,6},{8,15},{9,8},{10,9... | collective-permute-start | bytes 196616 | tf_op jit(solution)/shard_map/ppermute | solution.py:249
  81.6 2.0 %collective-permute-start.16 = (f32[64,128]{1,0:T(8,128)}, f32[64,128]{1,0:T(8,128)S(1)}, u32[]{:S(2)}, u32[]{:S(2)}) collective-permute-start(f32[64,128]{1,0:T(8,128)} %get-tuple-element.71), channel_id=1, source_target_pairs={{0,8},{8,16},{16,24},{24,0},{1,9},{9,17},{17,25},{25,1},{2,10},{10... | collective-permute-start | bytes 98312 | tf_op jit(solution)/shard_map/ppermute | solution.py:244
  82.3 3.6 %collective-permute-start.17 = (f32[64,128]{1,0:T(8,128)}, f32[64,128]{1,0:T(8,128)S(1)}, u32[]{:S(2)}, u32[]{:S(2)}) collective-permute-start(f32[64,128]{1,0:T(8,128)} %get-tuple-element.72), channel_id=1, source_target_pairs={{0,24},{8,0},{16,8},{24,16},{1,25},{9,1},{17,9},{25,17},{2,26},{10... | collective-permute-start | bytes 98312 | tf_op jit(solution)/shard_map/ppermute | solution.py:245
  88.4 8.4 %collective-permute-start.22 = (f32[64,256]{1,0:T(8,128)}, f32[64,256]{1,0:T(8,128)S(1)}, u32[]{:S(2)}, u32[]{:S(2)}) collective-permute-start(f32[64,256]{1,0:T(8,128)} %get-tuple-element.78), channel_id=1, source_target_pairs={{0,1},{1,2},{2,3},{3,4},{4,5},{5,6},{6,7},{7,0},{8,9},{9,10},{10,1... | collective-permute-start | bytes 196616 | tf_op jit(solution)/shard_map/ppermute | solution.py:248
  88.4 8.4 %collective-permute-start.23 = (f32[64,256]{1,0:T(8,128)}, f32[64,256]{1,0:T(8,128)S(1)}, u32[]{:S(2)}, u32[]{:S(2)}) collective-permute-start(f32[64,256]{1,0:T(8,128)} %get-tuple-element.79), channel_id=1, source_target_pairs={{0,7},{1,0},{2,1},{3,2},{4,3},{5,4},{6,5},{7,6},{8,15},{9,8},{10,9... | collective-permute-start | bytes 196616 | tf_op jit(solution)/shard_map/ppermute | solution.py:249
  92.6 2.0 %collective-permute-start.20 = (f32[64,128]{1,0:T(8,128)}, f32[64,128]{1,0:T(8,128)S(1)}, u32[]{:S(2)}, u32[]{:S(2)}) collective-permute-start(f32[64,128]{1,0:T(8,128)} %get-tuple-element.76), channel_id=1, source_target_pairs={{0,8},{8,16},{16,24},{24,0},{1,9},{9,17},{17,25},{25,1},{2,10},{10... | collective-permute-start | bytes 98312 | tf_op jit(solution)/shard_map/ppermute | solution.py:244
  93.3 3.6 %collective-permute-start.21 = (f32[64,128]{1,0:T(8,128)}, f32[64,128]{1,0:T(8,128)S(1)}, u32[]{:S(2)}, u32[]{:S(2)}) collective-permute-start(f32[64,128]{1,0:T(8,128)} %get-tuple-element.77), channel_id=1, source_target_pairs={{0,24},{8,0},{16,8},{24,16},{1,25},{9,1},{17,9},{25,17},{2,26},{10... | collective-permute-start | bytes 98312 | tf_op jit(solution)/shard_map/ppermute | solution.py:245
  99.4 8.4 %collective-permute-start.26 = (f32[64,256]{1,0:T(8,128)}, f32[64,256]{1,0:T(8,128)S(1)}, u32[]{:S(2)}, u32[]{:S(2)}) collective-permute-start(f32[64,256]{1,0:T(8,128)} %get-tuple-element.83), channel_id=1, source_target_pairs={{0,1},{1,2},{2,3},{3,4},{4,5},{5,6},{6,7},{7,0},{8,9},{9,10},{10,1... | collective-permute-start | bytes 196616 | tf_op jit(solution)/shard_map/ppermute | solution.py:248
  99.4 8.4 %collective-permute-start.27 = (f32[64,256]{1,0:T(8,128)}, f32[64,256]{1,0:T(8,128)S(1)}, u32[]{:S(2)}, u32[]{:S(2)}) collective-permute-start(f32[64,256]{1,0:T(8,128)} %get-tuple-element.84), channel_id=1, source_target_pairs={{0,7},{1,0},{2,1},{3,2},{4,3},{5,4},{6,5},{7,6},{8,15},{9,8},{10,9... | collective-permute-start | bytes 196616 | tf_op jit(solution)/shard_map/ppermute | solution.py:249
  103.5 2.0 %collective-permute-start.24 = (f32[64,128]{1,0:T(8,128)}, f32[64,128]{1,0:T(8,128)S(1)}, u32[]{:S(2)}, u32[]{:S(2)}) collective-permute-start(f32[64,128]{1,0:T(8,128)} %get-tuple-element.81), channel_id=1, source_target_pairs={{0,8},{8,16},{16,24},{24,0},{1,9},{9,17},{17,25},{25,1},{2,10},{10... | collective-permute-start | bytes 98312 | tf_op jit(solution)/shard_map/ppermute | solution.py:244
  104.2 3.6 %collective-permute-start.25 = (f32[64,128]{1,0:T(8,128)}, f32[64,128]{1,0:T(8,128)S(1)}, u32[]{:S(2)}, u32[]{:S(2)}) collective-permute-start(f32[64,128]{1,0:T(8,128)} %get-tuple-element.82), channel_id=1, source_target_pairs={{0,24},{8,0},{16,8},{24,16},{1,25},{9,1},{17,9},{25,17},{2,26},{10... | collective-permute-start | bytes 98312 | tf_op jit(solution)/shard_map/ppermute | solution.py:245
  110.3 8.4 %collective-permute-start.30 = (f32[64,256]{1,0:T(8,128)}, f32[64,256]{1,0:T(8,128)S(1)}, u32[]{:S(2)}, u32[]{:S(2)}) collective-permute-start(f32[64,256]{1,0:T(8,128)} %get-tuple-element.88), channel_id=1, source_target_pairs={{0,1},{1,2},{2,3},{3,4},{4,5},{5,6},{6,7},{7,0},{8,9},{9,10},{10,1... | collective-permute-start | bytes 196616 | tf_op jit(solution)/shard_map/ppermute | solution.py:248
  110.3 8.4 %collective-permute-start.31 = (f32[64,256]{1,0:T(8,128)}, f32[64,256]{1,0:T(8,128)S(1)}, u32[]{:S(2)}, u32[]{:S(2)}) collective-permute-start(f32[64,256]{1,0:T(8,128)} %get-tuple-element.89), channel_id=1, source_target_pairs={{0,7},{1,0},{2,1},{3,2},{4,3},{5,4},{6,5},{7,6},{8,15},{9,8},{10,9... | collective-permute-start | bytes 196616 | tf_op jit(solution)/shard_map/ppermute | solution.py:249
  114.5 2.0 %collective-permute-start.28 = (f32[64,128]{1,0:T(8,128)}, f32[64,128]{1,0:T(8,128)S(1)}, u32[]{:S(2)}, u32[]{:S(2)}) collective-permute-start(f32[64,128]{1,0:T(8,128)} %get-tuple-element.86), channel_id=1, source_target_pairs={{0,8},{8,16},{16,24},{24,0},{1,9},{9,17},{17,25},{25,1},{2,10},{10... | collective-permute-start | bytes 98312 | tf_op jit(solution)/shard_map/ppermute | solution.py:244
  115.2 3.6 %collective-permute-start.29 = (f32[64,128]{1,0:T(8,128)}, f32[64,128]{1,0:T(8,128)S(1)}, u32[]{:S(2)}, u32[]{:S(2)}) collective-permute-start(f32[64,128]{1,0:T(8,128)} %get-tuple-element.87), channel_id=1, source_target_pairs={{0,24},{8,0},{16,8},{24,16},{1,25},{9,1},{17,9},{25,17},{2,26},{10... | collective-permute-start | bytes 98312 | tf_op jit(solution)/shard_map/ppermute | solution.py:245

commit v6 on v4

--- a/solution.py
+++ b/solution.py
@@ -160,7 +160,7 @@
 
 def _half_sweep_kernel(
     other_ref, lo_x_ref, hi_x_ref, lo_y_ref, hi_y_ref, face_ref, weight_ref, inverse_ref,
-    target_ref, out_ref, send_lo_x_ref, send_hi_x_ref, send_lo_y_ref, send_hi_y_ref, *, span_x
+    target_ref, previous_ref, out_ref, send_lo_x_ref, send_hi_x_ref, send_lo_y_ref, send_hi_y_ref, *, span_x
 ):
     tile = 2 * R
     highest = lax.Precision.HIGHEST
@@ -213,7 +213,7 @@
         send_hi_y_ref[:, t * tile:(t + 1) * tile] = jnp.where(low_half, even, pltpu.roll(odd, R, 1))
 
 
-def half_sweep(other, halos, face_blocks, weight, inverse, target, span_x):
+def half_sweep(other, halos, face_blocks, weight, inverse, target, previous, span_x):
     lanes = other.shape[1]
     x_shape = jax.ShapeDtypeStruct((P_SIZE, 2 * R), jnp.float32)
     y_shape = jax.ShapeDtypeStruct((P_SIZE, span_x * R), jnp.float32)
@@ -221,11 +221,12 @@
     return pl.pallas_call(
         functools.partial(_half_sweep_kernel, span_x=span_x),
         out_shape=(jax.ShapeDtypeStruct((P_SIZE, lanes), jnp.float32), x_shape, x_shape, y_shape, y_shape),
-        in_specs=[vmem] * 9,
+        in_specs=[vmem] * 10,
         out_specs=(vmem,) * 5,
+        input_output_aliases={9: 0},
     )(*[
         pltpu.with_memory_space_constraint(value, pltpu.VMEM)
-        for value in (other, *halos, face_blocks, weight, inverse, target)
+        for value in (other, *halos, face_blocks, weight, inverse, target, previous)
     ])
 
 
@@ -288,7 +289,7 @@
     member_inverse, member_target, member_weight, face_row = lax.optimization_barrier(
         (member_inverse, member_target, member_weight, face_row)
     )
-    state = [None, start_state]
+    state = [jnp.zeros_like(start_state), start_state]
     sends = None
     for sweep_index in range(SWEEPS):
         for paint_now in (0, 1):
@@ -300,6 +301,7 @@
                 member_weight[paint_now],
                 member_inverse[paint_now],
                 member_target[paint_now],
+                state[paint_now],
                 span_x,
             )
     first = first_is[0][..., None]

time: 122 us -> 115 us (0.943)
  local copies, waits for them, and re-layouts: 20.9 us -> 13.7 us
    unnamed x30 -> x16, local copies, waits for them, and re-layouts: 7.58 us -> 2.15 us
    reshape x4, local copies, waits for them, and re-layouts: 2.12 us -> 0.31 us  [lane_body(): part.reshape(P_SIZE, columns, R)]
  transfers between devices with their start and end apart: 32 -> 32, of which waited for: 14 -> 14; matrix products, arithmetic and copies ran while one was open for 6% -> 6% of each run, Pallas kernels for 16% -> 17%
where the time goes in v6:
time: 115 us
  starting transfers between devices  42.9 us (37%)
  Pallas kernels  32.2 us (28%)
  waiting for transfers between devices  24.6 us (21%)
  local copies, waits for them, and re-layouts  13.7 us (12%)
    ppermute x8, starting transfers between devices, trade(): lax.ppermute(sends[3], 'gy', shift_pairs('gy', -1))  32.2 us
    pallas_call x1, Pallas kernels, block_inverses(): pl.pallas_call(functools.partial(_gauss_jordan_kernel, n=n, nb=nb), out_s...  19.2 us
    ppermute x8, waiting for transfers between devices, trade(): lax.ppermute(sends[1], 'gx', shift_pairs('gx', -1))  15.5 us
    pallas_call x8, Pallas kernels, half_sweep(): pl.pallas_call(functools.partial(_half_sweep_kernel, span_x=span_x), out_...  13.1 us
    ppermute x8, waiting for transfers between devices, trade(): lax.ppermute(sends[0], 'gx', shift_pairs('gx', 1))  9.05 us
    ppermute x8, starting transfers between devices, trade(): lax.ppermute(sends[0], 'gx', shift_pairs('gx', 1))  8.56 us
    slice x3, local copies, waits for them, and re-layouts, pick(): high = lax.index_in_dim(values, 1, axis=axis, keepdims=False)  2.68 us
  transfers between devices with their start and end apart: 32, of which 14 were waited for; matrix products, arithmetic and copies ran while one was open for 6% of the time, Pallas kernels for 17%

profile of v6, /device:TPU:1, one launch (start us, length us, event | category | flops | bytes accessed | tf_op | source)
XLA Modules:
  0.0 114.8 jit_solution(4895196984524900725)
XLA Ops:
  0.0 0.7 slice-done
  1.1 1.9 %slice_reduce_fusion.2 = (f32[4,2,4096]{2,1,0:T(2,128)S(1)}, f32[4,2,4096]{2,1,0:T(2,128)S(1)}) fusion(f32[4,2,2,4096]{3,2,1,0:T(2,128)} %param.9), kind=kLoop, calls=%fused_computation.10 | loop fusion | bytes 524288 | tf_op jit(solution)/shard_map/slice | solution.py:271
  3.0 0.2 squeeze.32
  3.2 0.2 squeeze.33
  3.4 0.7 copy-done
  4.1 0.8 slice_reduce_fusion
  4.9 0.2 squeeze.36
  5.1 0.2 squeeze.37
  5.7 2.1 %collective-permute-start.2 = (f32[64,256]{1,0:T(8,128)S(1)}, f32[64,256]{1,0:T(8,128)S(1)}, u32[]{:S(2)}, u32[]{:S(2)}) collective-permute-start(f32[64,256]{1,0:T(8,128)S(1)} %reshape_squeeze.14), channel_id=1, source_target_pairs={{0,1},{1,2},{2,3},{3,4},{4,5},{5,6},{6,7},{7,0},{8,9},{9,10},{10,1... | collective-permute-start | bytes 196616 | tf_op jit(solution)/shard_map/ppermute | solution.py:249
  8.1 3.1 %collective-permute-start.3 = (f32[64,256]{1,0:T(8,128)S(1)}, f32[64,256]{1,0:T(8,128)S(1)}, u32[]{:S(2)}, u32[]{:S(2)}) collective-permute-start(f32[64,256]{1,0:T(8,128)S(1)} %reshape_squeeze.15), channel_id=1, source_target_pairs={{0,7},{1,0},{2,1},{3,2},{4,3},{5,4},{6,5},{7,6},{8,15},{9,8},{10,9... | collective-permute-start | bytes 196616 | tf_op jit(solution)/shard_map/ppermute | solution.py:250
  11.3 2.2 %collective-permute-start = (f32[64,128]{1,0:T(8,128)S(1)}, f32[64,128]{1,0:T(8,128)S(1)}, u32[]{:S(2)}, u32[]{:S(2)}) collective-permute-start(f32[64,128]{1,0:T(8,128)S(1)} %reshape_squeeze.12), channel_id=1, source_target_pairs={{0,8},{8,16},{16,24},{24,0},{1,9},{9,17},{17,25},{25,1},{2,10},{10... | collective-permute-start | bytes 98312 | tf_op jit(solution)/shard_map/ppermute | solution.py:245
  13.7 0.3 broadcast_select_fusion.1
  14.0 0.2 pad_maximum_fusion
  14.3 0.2 copy.68
  14.5 0.3 reshape.157
  14.8 0.3 copy.69
  15.1 0.9 copy.70.a_ref
  16.0 19.2 %shard_map.82 = f32[64,1024]{1,0:T(8,128)} custom-call(f32[64,1024]{1,0:T(8,128)} %copy.70.a_ref), custom_call_target="tpu_custom_call" | custom-call | flops 8388608000 | bytes 524288 | tf_op jit(solution)/shard_map/pallas_call | solution.py:75
  35.2 1.1 copy.71
  36.3 0.4 copy.72
  36.7 0.2 reshape.160
  37.0 0.6 copy-done.3
  37.7 0.2 copy.74
  38.0 0.2 copy.75
  38.8 0.4 copy-done.2
  39.4 0.2 copy.62
  39.8 1.6 %shard_map.83 = (f32[64,512]{1,0:T(8,128)S(1)}, f32[64,128]{1,0:T(8,128)}, f32[64,128]{1,0:T(8,128)}, f32[64,256]{1,0:T(8,128)}, f32[64,256]{1,0:T(8,128)}) custom-call(f32[64,512]{1,0:T(8,128)S(1)} %reshape.156.other_ref.previous_ref, f32[64,128]{1,0:T(8,128)S(1)} %collective-permute-done.lo_x_ref, ...), custom_call_target="tpu_custom_call", output_to_operand_aliasing={{0}: (9, {})} | custom-call | tf_op jit(solution)/shard_map/pallas_call | solution.py:221
  41.4 4.2 %collective-permute-start.7 = (f32[64,256]{1,0:T(8,128)}, f32[64,256]{1,0:T(8,128)S(1)}, u32[]{:S(2)}, u32[]{:S(2)}) collective-permute-start(f32[64,256]{1,0:T(8,128)} %get-tuple-element.56), channel_id=1, source_target_pairs={{0,7},{1,0},{2,1},{3,2},{4,3},{5,4},{6,5},{7,6},{8,15},{9,8},{10,9... | collective-permute-start | bytes 196616 | tf_op jit(solution)/shard_map/ppermute | solution.py:250
  45.6 2.3 %collective-permute-start.4 = (f32[64,128]{1,0:T(8,128)}, f32[64,128]{1,0:T(8,128)S(1)}, u32[]{:S(2)}, u32[]{:S(2)}) collective-permute-start(f32[64,128]{1,0:T(8,128)} %get-tuple-element.53), channel_id=1, source_target_pairs={{0,8},{8,16},{16,24},{24,0},{1,9},{9,17},{17,25},{25,1},{2,10},{10... | collective-permute-start | bytes 98312 | tf_op jit(solution)/shard_map/ppermute | solution.py:245
  47.8 1.3 %collective-permute-done.4.lo_x_ref = f32[64,128]{1,0:T(8,128)S(1)} collective-permute-done((f32[64,128]{1,0:T(8,128)}, f32[64,128]{1,0:T(8,128)S(1)}, u32[]{:S(2)}, u32[]{:S(2)}) %collective-permute-start.4) | collective-permute-done | bytes 32800 | tf_op jit(solution)/shard_map/ppermute | solution.py:245
  49.2 2.2 %collective-permute-done.5.hi_x_ref = f32[64,128]{1,0:T(8,128)S(1)} collective-permute-done((f32[64,128]{1,0:T(8,128)}, f32[64,128]{1,0:T(8,128)S(1)}, u32[]{:S(2)}, u32[]{:S(2)}) %collective-permute-start.5) | collective-permute-done | bytes 32800 | tf_op jit(solution)/shard_map/ppermute | solution.py:246
  51.4 1.6 %shard_map.84 = (f32[64,512]{1,0:T(8,128)S(1)}, f32[64,128]{1,0:T(8,128)}, f32[64,128]{1,0:T(8,128)}, f32[64,256]{1,0:T(8,128)}, f32[64,256]{1,0:T(8,128)}) custom-call(f32[64,512]{1,0:T(8,128)S(1)} %get-tuple-element.52.other_ref.previous_ref, f32[64,128]{1,0:T(8,128)S(1)} %collective-permute-done.4.lo_x_ref, ...), custom_call_target="tpu_custom_call", output_to_operand_aliasing={{0}: (9, {})} | custom-call | tf_op jit(solution)/shard_map/pallas_call | solution.py:221
  53.0 4.2 %collective-permute-start.11 = (f32[64,256]{1,0:T(8,128)}, f32[64,256]{1,0:T(8,128)S(1)}, u32[]{:S(2)}, u32[]{:S(2)}) collective-permute-start(f32[64,256]{1,0:T(8,128)} %get-tuple-element.64), channel_id=1, source_target_pairs={{0,7},{1,0},{2,1},{3,2},{4,3},{5,4},{6,5},{7,6},{8,15},{9,8},{10,9... | collective-permute-start | bytes 196616 | tf_op jit(solution)/shard_map/ppermute | solution.py:250
  57.2 0.7 collective-permute-start.8
  57.9 1.3 %collective-permute-done.8.lo_x_ref = f32[64,128]{1,0:T(8,128)S(1)} collective-permute-done((f32[64,128]{1,0:T(8,128)}, f32[64,128]{1,0:T(8,128)S(1)}, u32[]{:S(2)}, u32[]{:S(2)}) %collective-permute-start.8) | collective-permute-done | bytes 32800 | tf_op jit(solution)/shard_map/ppermute | solution.py:245
  59.2 2.2 %collective-permute-done.9.hi_x_ref = f32[64,128]{1,0:T(8,128)S(1)} collective-permute-done((f32[64,128]{1,0:T(8,128)}, f32[64,128]{1,0:T(8,128)S(1)}, u32[]{:S(2)}, u32[]{:S(2)}) %collective-permute-start.9) | collective-permute-done | bytes 32800 | tf_op jit(solution)/shard_map/ppermute | solution.py:246
  61.5 1.6 %shard_map.85 = (f32[64,512]{1,0:T(8,128)S(1)}, f32[64,128]{1,0:T(8,128)}, f32[64,128]{1,0:T(8,128)}, f32[64,256]{1,0:T(8,128)}, f32[64,256]{1,0:T(8,128)}) custom-call(f32[64,512]{1,0:T(8,128)S(1)} %get-tuple-element.60.other_ref.previous_ref, f32[64,128]{1,0:T(8,128)S(1)} %collective-permute-done.8.lo_x_ref, ...), custom_call_target="tpu_custom_call", output_to_operand_aliasing={{0}: (9, {})} | custom-call | tf_op jit(solution)/shard_map/pallas_call | solution.py:221
  63.1 4.2 %collective-permute-start.15 = (f32[64,256]{1,0:T(8,128)}, f32[64,256]{1,0:T(8,128)S(1)}, u32[]{:S(2)}, u32[]{:S(2)}) collective-permute-start(f32[64,256]{1,0:T(8,128)} %get-tuple-element.69), channel_id=1, source_target_pairs={{0,7},{1,0},{2,1},{3,2},{4,3},{5,4},{6,5},{7,6},{8,15},{9,8},{10,9... | collective-permute-start | bytes 196616 | tf_op jit(solution)/shard_map/ppermute | solution.py:250
  67.3 0.7 collective-permute-start.12
  67.9 1.3 %collective-permute-done.12.lo_x_ref = f32[64,128]{1,0:T(8,128)S(1)} collective-permute-done((f32[64,128]{1,0:T(8,128)}, f32[64,128]{1,0:T(8,128)S(1)}, u32[]{:S(2)}, u32[]{:S(2)}) %collective-permute-start.12) | collective-permute-done | bytes 32800 | tf_op jit(solution)/shard_map/ppermute | solution.py:245
  69.3 2.2 %collective-permute-done.13.hi_x_ref = f32[64,128]{1,0:T(8,128)S(1)} collective-permute-done((f32[64,128]{1,0:T(8,128)}, f32[64,128]{1,0:T(8,128)S(1)}, u32[]{:S(2)}, u32[]{:S(2)}) %collective-permute-start.13) | collective-permute-done | bytes 32800 | tf_op jit(solution)/shard_map/ppermute | solution.py:246
  71.5 1.6 %shard_map.86 = (f32[64,512]{1,0:T(8,128)S(1)}, f32[64,128]{1,0:T(8,128)}, f32[64,128]{1,0:T(8,128)}, f32[64,256]{1,0:T(8,128)}, f32[64,256]{1,0:T(8,128)}) custom-call(f32[64,512]{1,0:T(8,128)S(1)} %get-tuple-element.65.other_ref.previous_ref, f32[64,128]{1,0:T(8,128)S(1)} %collective-permute-done.12.lo_x_ref, ...), custom_call_target="tpu_custom_call", output_to_operand_aliasing={{0}: (9, {})} | custom-call | tf_op jit(solution)/shard_map/pallas_call | solution.py:221
  73.1 4.2 %collective-permute-start.19 = (f32[64,256]{1,0:T(8,128)}, f32[64,256]{1,0:T(8,128)S(1)}, u32[]{:S(2)}, u32[]{:S(2)}) collective-permute-start(f32[64,256]{1,0:T(8,128)} %get-tuple-element.74), channel_id=1, source_target_pairs={{0,7},{1,0},{2,1},{3,2},{4,3},{5,4},{6,5},{7,6},{8,15},{9,8},{10,9... | collective-permute-start | bytes 196616 | tf_op jit(solution)/shard_map/ppermute | solution.py:250
  77.3 0.7 collective-permute-start.16
  78.0 1.3 %collective-permute-done.16.lo_x_ref = f32[64,128]{1,0:T(8,128)S(1)} collective-permute-done((f32[64,128]{1,0:T(8,128)}, f32[64,128]{1,0:T(8,128)S(1)}, u32[]{:S(2)}, u32[]{:S(2)}) %collective-permute-start.16) | collective-permute-done | bytes 32800 | tf_op jit(solution)/shard_map/ppermute | solution.py:245
  79.3 2.2 %collective-permute-done.17.hi_x_ref = f32[64,128]{1,0:T(8,128)S(1)} collective-permute-done((f32[64,128]{1,0:T(8,128)}, f32[64,128]{1,0:T(8,128)S(1)}, u32[]{:S(2)}, u32[]{:S(2)}) %collective-permute-start.17) | collective-permute-done | bytes 32800 | tf_op jit(solution)/shard_map/ppermute | solution.py:246
  81.5 1.6 %shard_map.87 = (f32[64,512]{1,0:T(8,128)S(1)}, f32[64,128]{1,0:T(8,128)}, f32[64,128]{1,0:T(8,128)}, f32[64,256]{1,0:T(8,128)}, f32[64,256]{1,0:T(8,128)}) custom-call(f32[64,512]{1,0:T(8,128)S(1)} %get-tuple-element.70.other_ref.previous_ref, f32[64,128]{1,0:T(8,128)S(1)} %collective-permute-done.16.lo_x_ref, ...), custom_call_target="tpu_custom_call", output_to_operand_aliasing={{0}: (9, {})} | custom-call | tf_op jit(solution)/shard_map/pallas_call | solution.py:221
  83.2 4.2 %collective-permute-start.23 = (f32[64,256]{1,0:T(8,128)}, f32[64,256]{1,0:T(8,128)S(1)}, u32[]{:S(2)}, u32[]{:S(2)}) collective-permute-start(f32[64,256]{1,0:T(8,128)} %get-tuple-element.79), channel_id=1, source_target_pairs={{0,7},{1,0},{2,1},{3,2},{4,3},{5,4},{6,5},{7,6},{8,15},{9,8},{10,9... | collective-permute-start | bytes 196616 | tf_op jit(solution)/shard_map/ppermute | solution.py:250
  87.3 0.7 collective-permute-start.20
  88.0 1.3 %collective-permute-done.20.lo_x_ref = f32[64,128]{1,0:T(8,128)S(1)} collective-permute-done((f32[64,128]{1,0:T(8,128)}, f32[64,128]{1,0:T(8,128)S(1)}, u32[]{:S(2)}, u32[]{:S(2)}) %collective-permute-start.20) | collective-permute-done | bytes 32800 | tf_op jit(solution)/shard_map/ppermute | solution.py:245
  89.3 2.2 %collective-permute-done.21.hi_x_ref = f32[64,128]{1,0:T(8,128)S(1)} collective-permute-done((f32[64,128]{1,0:T(8,128)}, f32[64,128]{1,0:T(8,128)S(1)}, u32[]{:S(2)}, u32[]{:S(2)}) %collective-permute-start.21) | collective-permute-done | bytes 32800 | tf_op jit(solution)/shard_map/ppermute | solution.py:246
  91.5 1.6 %shard_map.88 = (f32[64,512]{1,0:T(8,128)S(1)}, f32[64,128]{1,0:T(8,128)}, f32[64,128]{1,0:T(8,128)}, f32[64,256]{1,0:T(8,128)}, f32[64,256]{1,0:T(8,128)}) custom-call(f32[64,512]{1,0:T(8,128)S(1)} %get-tuple-element.75.other_ref.previous_ref, f32[64,128]{1,0:T(8,128)S(1)} %collective-permute-done.20.lo_x_ref, ...), custom_call_target="tpu_custom_call", output_to_operand_aliasing={{0}: (9, {})} | custom-call | tf_op jit(solution)/shard_map/pallas_call | solution.py:221
  93.2 4.2 %collective-permute-start.27 = (f32[64,256]{1,0:T(8,128)}, f32[64,256]{1,0:T(8,128)S(1)}, u32[]{:S(2)}, u32[]{:S(2)}) collective-permute-start(f32[64,256]{1,0:T(8,128)} %get-tuple-element.84), channel_id=1, source_target_pairs={{0,7},{1,0},{2,1},{3,2},{4,3},{5,4},{6,5},{7,6},{8,15},{9,8},{10,9... | collective-permute-start | bytes 196616 | tf_op jit(solution)/shard_map/ppermute | solution.py:250
  97.3 0.7 collective-permute-start.24
  98.0 1.3 %collective-permute-done.24.lo_x_ref = f32[64,128]{1,0:T(8,128)S(1)} collective-permute-done((f32[64,128]{1,0:T(8,128)}, f32[64,128]{1,0:T(8,128)S(1)}, u32[]{:S(2)}, u32[]{:S(2)}) %collective-permute-start.24) | collective-permute-done | bytes 32800 | tf_op jit(solution)/shard_map/ppermute | solution.py:245
  99.4 2.2 %collective-permute-done.25.hi_x_ref = f32[64,128]{1,0:T(8,128)S(1)} collective-permute-done((f32[64,128]{1,0:T(8,128)}, f32[64,128]{1,0:T(8,128)S(1)}, u32[]{:S(2)}, u32[]{:S(2)}) %collective-permute-start.25) | collective-permute-done | bytes 32800 | tf_op jit(solution)/shard_map/ppermute | solution.py:246
  101.6 1.6 %shard_map.89 = (f32[64,512]{1,0:T(8,128)S(1)}, f32[64,128]{1,0:T(8,128)}, f32[64,128]{1,0:T(8,128)}, f32[64,256]{1,0:T(8,128)}, f32[64,256]{1,0:T(8,128)}) custom-call(f32[64,512]{1,0:T(8,128)S(1)} %get-tuple-element.80.other_ref.previous_ref, f32[64,128]{1,0:T(8,128)S(1)} %collective-permute-done.24.lo_x_ref, ...), custom_call_target="tpu_custom_call", output_to_operand_aliasing={{0}: (9, {})} | custom-call | tf_op jit(solution)/shard_map/pallas_call | solution.py:221
  103.2 4.2 %collective-permute-start.31 = (f32[64,256]{1,0:T(8,128)}, f32[64,256]{1,0:T(8,128)S(1)}, u32[]{:S(2)}, u32[]{:S(2)}) collective-permute-start(f32[64,256]{1,0:T(8,128)} %get-tuple-element.89), channel_id=1, source_target_pairs={{0,7},{1,0},{2,1},{3,2},{4,3},{5,4},{6,5},{7,6},{8,15},{9,8},{10,9... | collective-permute-start | bytes 196616 | tf_op jit(solution)/shard_map/ppermute | solution.py:250
  107.4 0.7 collective-permute-start.28
  108.3 1.0 collective-permute-done.28.lo_x_ref
  109.4 2.2 %collective-permute-done.29.hi_x_ref = f32[64,128]{1,0:T(8,128)S(1)} collective-permute-done((f32[64,128]{1,0:T(8,128)}, f32[64,128]{1,0:T(8,128)S(1)}, u32[]{:S(2)}, u32[]{:S(2)}) %collective-permute-start.29) | collective-permute-done | bytes 32800 | tf_op jit(solution)/shard_map/ppermute | solution.py:246
  111.6 1.6 %shard_map.90 = (f32[64,512]{1,0:T(8,128)S(1)}, f32[64,128]{1,0:T(8,128)}, f32[64,128]{1,0:T(8,128)}, f32[64,256]{1,0:T(8,128)}, f32[64,256]{1,0:T(8,128)}) custom-call(f32[64,512]{1,0:T(8,128)S(1)} %get-tuple-element.85.other_ref, f32[64,128]{1,0:T(8,128)S(1)} %collective-permute-done.28.lo_x_ref, ...), custom_call_target="tpu_custom_call", output_to_operand_aliasing={{0}: (9, {})} | custom-call | tf_op jit(solution)/shard_map/pallas_call | solution.py:221
  113.5 0.2 broadcast_select_fusion.4
  113.8 0.9 copy.81
  (84 shorter events, 3.4 us)
Async XLA Ops:
  0.0 0.7 slice-start
  3.2 1.0 copy-start
  5.7 34.0 %collective-permute-start.2 = (f32[64,256]{1,0:T(8,128)S(1)}, f32[64,256]{1,0:T(8,128)S(1)}, u32[]{:S(2)}, u32[]{:S(2)}) collective-permute-start(f32[64,256]{1,0:T(8,128)S(1)} %reshape_squeeze.14), channel_id=1, source_target_pairs={{0,1},{1,2},{2,3},{3,4},{4,5},{5,6},{6,7},{7,0},{8,9},{9,10},{10,1... | collective-permute-start | bytes 196616 | tf_op jit(solution)/shard_map/ppermute | solution.py:249
  8.1 31.7 %collective-permute-start.3 = (f32[64,256]{1,0:T(8,128)S(1)}, f32[64,256]{1,0:T(8,128)S(1)}, u32[]{:S(2)}, u32[]{:S(2)}) collective-permute-start(f32[64,256]{1,0:T(8,128)S(1)} %reshape_squeeze.15), channel_id=1, source_target_pairs={{0,7},{1,0},{2,1},{3,2},{4,3},{5,4},{6,5},{7,6},{8,15},{9,8},{10,9... | collective-permute-start | bytes 196616 | tf_op jit(solution)/shard_map/ppermute | solution.py:250
  11.2 2.6 %copy-start.1 = (f32[4,2,2,4096]{3,2,1,0:T(2,128)S(1)}, f32[4,2,2,4096]{3,2,1,0:T(2,128)}, u32[]{:S(2)}) copy-start(f32[4,2,2,4096]{3,2,1,0:T(2,128)} %param.10) | copy-start | bytes 786436
  11.3 28.4 %collective-permute-start = (f32[64,128]{1,0:T(8,128)S(1)}, f32[64,128]{1,0:T(8,128)S(1)}, u32[]{:S(2)}, u32[]{:S(2)}) collective-permute-start(f32[64,128]{1,0:T(8,128)S(1)} %reshape_squeeze.12), channel_id=1, source_target_pairs={{0,8},{8,16},{16,24},{24,0},{1,9},{9,17},{17,25},{25,1},{2,10},{10... | collective-permute-start | bytes 98312 | tf_op jit(solution)/shard_map/ppermute | solution.py:245
  13.7 26.0 %collective-permute-start.1 = (f32[64,128]{1,0:T(8,128)S(1)}, f32[64,128]{1,0:T(8,128)S(1)}, u32[]{:S(2)}, u32[]{:S(2)}) collective-permute-start(f32[64,128]{1,0:T(8,128)S(1)} %reshape_squeeze.13), channel_id=1, source_target_pairs={{0,24},{8,0},{16,8},{24,16},{1,25},{9,1},{17,9},{25,17},{2,26},{10... | collective-permute-start | bytes 98312 | tf_op jit(solution)/shard_map/ppermute | solution.py:246
  36.9 0.7 copy-start.3
  36.9 0.7 copy-start.4
  36.9 0.7 copy-start.5
  38.3 0.9 copy-start.2
  41.4 10.0 %collective-permute-start.6 = (f32[64,256]{1,0:T(8,128)}, f32[64,256]{1,0:T(8,128)S(1)}, u32[]{:S(2)}, u32[]{:S(2)}) collective-permute-start(f32[64,256]{1,0:T(8,128)} %get-tuple-element.55), channel_id=1, source_target_pairs={{0,1},{1,2},{2,3},{3,4},{4,5},{5,6},{6,7},{7,0},{8,9},{9,10},{10,1... | collective-permute-start | bytes 196616 | tf_op jit(solution)/shard_map/ppermute | solution.py:249
  41.4 10.0 %collective-permute-start.7 = (f32[64,256]{1,0:T(8,128)}, f32[64,256]{1,0:T(8,128)S(1)}, u32[]{:S(2)}, u32[]{:S(2)}) collective-permute-start(f32[64,256]{1,0:T(8,128)} %get-tuple-element.56), channel_id=1, source_target_pairs={{0,7},{1,0},{2,1},{3,2},{4,3},{5,4},{6,5},{7,6},{8,15},{9,8},{10,9... | collective-permute-start | bytes 196616 | tf_op jit(solution)/shard_map/ppermute | solution.py:250
  45.6 3.6 %collective-permute-start.4 = (f32[64,128]{1,0:T(8,128)}, f32[64,128]{1,0:T(8,128)S(1)}, u32[]{:S(2)}, u32[]{:S(2)}) collective-permute-start(f32[64,128]{1,0:T(8,128)} %get-tuple-element.53), channel_id=1, source_target_pairs={{0,8},{8,16},{16,24},{24,0},{1,9},{9,17},{17,25},{25,1},{2,10},{10... | collective-permute-start | bytes 98312 | tf_op jit(solution)/shard_map/ppermute | solution.py:245
  47.8 3.6 %collective-permute-start.5 = (f32[64,128]{1,0:T(8,128)}, f32[64,128]{1,0:T(8,128)S(1)}, u32[]{:S(2)}, u32[]{:S(2)}) collective-permute-start(f32[64,128]{1,0:T(8,128)} %get-tuple-element.54), channel_id=1, source_target_pairs={{0,24},{8,0},{16,8},{24,16},{1,25},{9,1},{17,9},{25,17},{2,26},{10... | collective-permute-start | bytes 98312 | tf_op jit(solution)/shard_map/ppermute | solution.py:246
  53.0 8.4 %collective-permute-start.10 = (f32[64,256]{1,0:T(8,128)}, f32[64,256]{1,0:T(8,128)S(1)}, u32[]{:S(2)}, u32[]{:S(2)}) collective-permute-start(f32[64,256]{1,0:T(8,128)} %get-tuple-element.63), channel_id=1, source_target_pairs={{0,1},{1,2},{2,3},{3,4},{4,5},{5,6},{6,7},{7,0},{8,9},{9,10},{10,1... | collective-permute-start | bytes 196616 | tf_op jit(solution)/shard_map/ppermute | solution.py:249
  53.0 8.4 %collective-permute-start.11 = (f32[64,256]{1,0:T(8,128)}, f32[64,256]{1,0:T(8,128)S(1)}, u32[]{:S(2)}, u32[]{:S(2)}) collective-permute-start(f32[64,256]{1,0:T(8,128)} %get-tuple-element.64), channel_id=1, source_target_pairs={{0,7},{1,0},{2,1},{3,2},{4,3},{5,4},{6,5},{7,6},{8,15},{9,8},{10,9... | collective-permute-start | bytes 196616 | tf_op jit(solution)/shard_map/ppermute | solution.py:250
  57.2 2.0 %collective-permute-start.8 = (f32[64,128]{1,0:T(8,128)}, f32[64,128]{1,0:T(8,128)S(1)}, u32[]{:S(2)}, u32[]{:S(2)}) collective-permute-start(f32[64,128]{1,0:T(8,128)} %get-tuple-element.61), channel_id=1, source_target_pairs={{0,8},{8,16},{16,24},{24,0},{1,9},{9,17},{17,25},{25,1},{2,10},{10... | collective-permute-start | bytes 98312 | tf_op jit(solution)/shard_map/ppermute | solution.py:245
  57.9 3.6 %collective-permute-start.9 = (f32[64,128]{1,0:T(8,128)}, f32[64,128]{1,0:T(8,128)S(1)}, u32[]{:S(2)}, u32[]{:S(2)}) collective-permute-start(f32[64,128]{1,0:T(8,128)} %get-tuple-element.62), channel_id=1, source_target_pairs={{0,24},{8,0},{16,8},{24,16},{1,25},{9,1},{17,9},{25,17},{2,26},{10... | collective-permute-start | bytes 98312 | tf_op jit(solution)/shard_map/ppermute | solution.py:246
  63.1 8.4 %collective-permute-start.14 = (f32[64,256]{1,0:T(8,128)}, f32[64,256]{1,0:T(8,128)S(1)}, u32[]{:S(2)}, u32[]{:S(2)}) collective-permute-start(f32[64,256]{1,0:T(8,128)} %get-tuple-element.68), channel_id=1, source_target_pairs={{0,1},{1,2},{2,3},{3,4},{4,5},{5,6},{6,7},{7,0},{8,9},{9,10},{10,1... | collective-permute-start | bytes 196616 | tf_op jit(solution)/shard_map/ppermute | solution.py:249
  63.1 8.4 %collective-permute-start.15 = (f32[64,256]{1,0:T(8,128)}, f32[64,256]{1,0:T(8,128)S(1)}, u32[]{:S(2)}, u32[]{:S(2)}) collective-permute-start(f32[64,256]{1,0:T(8,128)} %get-tuple-element.69), channel_id=1, source_target_pairs={{0,7},{1,0},{2,1},{3,2},{4,3},{5,4},{6,5},{7,6},{8,15},{9,8},{10,9... | collective-permute-start | bytes 196616 | tf_op jit(solution)/shard_map/ppermute | solution.py:250
  67.3 2.0 %collective-permute-start.12 = (f32[64,128]{1,0:T(8,128)}, f32[64,128]{1,0:T(8,128)S(1)}, u32[]{:S(2)}, u32[]{:S(2)}) collective-permute-start(f32[64,128]{1,0:T(8,128)} %get-tuple-element.66), channel_id=1, source_target_pairs={{0,8},{8,16},{16,24},{24,0},{1,9},{9,17},{17,25},{25,1},{2,10},{10... | collective-permute-start | bytes 98312 | tf_op jit(solution)/shard_map/ppermute | solution.py:245
  67.9 3.6 %collective-permute-start.13 = (f32[64,128]{1,0:T(8,128)}, f32[64,128]{1,0:T(8,128)S(1)}, u32[]{:S(2)}, u32[]{:S(2)}) collective-permute-start(f32[64,128]{1,0:T(8,128)} %get-tuple-element.67), channel_id=1, source_target_pairs={{0,24},{8,0},{16,8},{24,16},{1,25},{9,1},{17,9},{25,17},{2,26},{10... | collective-permute-start | bytes 98312 | tf_op jit(solution)/shard_map/ppermute | solution.py:246
  73.1 8.4 %collective-permute-start.18 = (f32[64,256]{1,0:T(8,128)}, f32[64,256]{1,0:T(8,128)S(1)}, u32[]{:S(2)}, u32[]{:S(2)}) collective-permute-start(f32[64,256]{1,0:T(8,128)} %get-tuple-element.73), channel_id=1, source_target_pairs={{0,1},{1,2},{2,3},{3,4},{4,5},{5,6},{6,7},{7,0},{8,9},{9,10},{10,1... | collective-permute-start | bytes 196616 | tf_op jit(solution)/shard_map/ppermute | solution.py:249
  73.1 8.4 %collective-permute-start.19 = (f32[64,256]{1,0:T(8,128)}, f32[64,256]{1,0:T(8,128)S(1)}, u32[]{:S(2)}, u32[]{:S(2)}) collective-permute-start(f32[64,256]{1,0:T(8,128)} %get-tuple-element.74), channel_id=1, source_target_pairs={{0,7},{1,0},{2,1},{3,2},{4,3},{5,4},{6,5},{7,6},{8,15},{9,8},{10,9... | collective-permute-start | bytes 196616 | tf_op jit(solution)/shard_map/ppermute | solution.py:250
  77.3 2.0 %collective-permute-start.16 = (f32[64,128]{1,0:T(8,128)}, f32[64,128]{1,0:T(8,128)S(1)}, u32[]{:S(2)}, u32[]{:S(2)}) collective-permute-start(f32[64,128]{1,0:T(8,128)} %get-tuple-element.71), channel_id=1, source_target_pairs={{0,8},{8,16},{16,24},{24,0},{1,9},{9,17},{17,25},{25,1},{2,10},{10... | collective-permute-start | bytes 98312 | tf_op jit(solution)/shard_map/ppermute | solution.py:245
  78.0 3.6 %collective-permute-start.17 = (f32[64,128]{1,0:T(8,128)}, f32[64,128]{1,0:T(8,128)S(1)}, u32[]{:S(2)}, u32[]{:S(2)}) collective-permute-start(f32[64,128]{1,0:T(8,128)} %get-tuple-element.72), channel_id=1, source_target_pairs={{0,24},{8,0},{16,8},{24,16},{1,25},{9,1},{17,9},{25,17},{2,26},{10... | collective-permute-start | bytes 98312 | tf_op jit(solution)/shard_map/ppermute | solution.py:246
  83.2 8.4 %collective-permute-start.22 = (f32[64,256]{1,0:T(8,128)}, f32[64,256]{1,0:T(8,128)S(1)}, u32[]{:S(2)}, u32[]{:S(2)}) collective-permute-start(f32[64,256]{1,0:T(8,128)} %get-tuple-element.78), channel_id=1, source_target_pairs={{0,1},{1,2},{2,3},{3,4},{4,5},{5,6},{6,7},{7,0},{8,9},{9,10},{10,1... | collective-permute-start | bytes 196616 | tf_op jit(solution)/shard_map/ppermute | solution.py:249
  83.2 8.4 %collective-permute-start.23 = (f32[64,256]{1,0:T(8,128)}, f32[64,256]{1,0:T(8,128)S(1)}, u32[]{:S(2)}, u32[]{:S(2)}) collective-permute-start(f32[64,256]{1,0:T(8,128)} %get-tuple-element.79), channel_id=1, source_target_pairs={{0,7},{1,0},{2,1},{3,2},{4,3},{5,4},{6,5},{7,6},{8,15},{9,8},{10,9... | collective-permute-start | bytes 196616 | tf_op jit(solution)/shard_map/ppermute | solution.py:250
  87.3 2.0 %collective-permute-start.20 = (f32[64,128]{1,0:T(8,128)}, f32[64,128]{1,0:T(8,128)S(1)}, u32[]{:S(2)}, u32[]{:S(2)}) collective-permute-start(f32[64,128]{1,0:T(8,128)} %get-tuple-element.76), channel_id=1, source_target_pairs={{0,8},{8,16},{16,24},{24,0},{1,9},{9,17},{17,25},{25,1},{2,10},{10... | collective-permute-start | bytes 98312 | tf_op jit(solution)/shard_map/ppermute | solution.py:245
  88.0 3.6 %collective-permute-start.21 = (f32[64,128]{1,0:T(8,128)}, f32[64,128]{1,0:T(8,128)S(1)}, u32[]{:S(2)}, u32[]{:S(2)}) collective-permute-start(f32[64,128]{1,0:T(8,128)} %get-tuple-element.77), channel_id=1, source_target_pairs={{0,24},{8,0},{16,8},{24,16},{1,25},{9,1},{17,9},{25,17},{2,26},{10... | collective-permute-start | bytes 98312 | tf_op jit(solution)/shard_map/ppermute | solution.py:246
  93.2 8.4 %collective-permute-start.26 = (f32[64,256]{1,0:T(8,128)}, f32[64,256]{1,0:T(8,128)S(1)}, u32[]{:S(2)}, u32[]{:S(2)}) collective-permute-start(f32[64,256]{1,0:T(8,128)} %get-tuple-element.83), channel_id=1, source_target_pairs={{0,1},{1,2},{2,3},{3,4},{4,5},{5,6},{6,7},{7,0},{8,9},{9,10},{10,1... | collective-permute-start | bytes 196616 | tf_op jit(solution)/shard_map/ppermute | solution.py:249
  93.2 8.4 %collective-permute-start.27 = (f32[64,256]{1,0:T(8,128)}, f32[64,256]{1,0:T(8,128)S(1)}, u32[]{:S(2)}, u32[]{:S(2)}) collective-permute-start(f32[64,256]{1,0:T(8,128)} %get-tuple-element.84), channel_id=1, source_target_pairs={{0,7},{1,0},{2,1},{3,2},{4,3},{5,4},{6,5},{7,6},{8,15},{9,8},{10,9... | collective-permute-start | bytes 196616 | tf_op jit(solution)/shard_map/ppermute | solution.py:250
  97.3 2.0 %collective-permute-start.24 = (f32[64,128]{1,0:T(8,128)}, f32[64,128]{1,0:T(8,128)S(1)}, u32[]{:S(2)}, u32[]{:S(2)}) collective-permute-start(f32[64,128]{1,0:T(8,128)} %get-tuple-element.81), channel_id=1, source_target_pairs={{0,8},{8,16},{16,24},{24,0},{1,9},{9,17},{17,25},{25,1},{2,10},{10... | collective-permute-start | bytes 98312 | tf_op jit(solution)/shard_map/ppermute | solution.py:245
  98.0 3.6 %collective-permute-start.25 = (f32[64,128]{1,0:T(8,128)}, f32[64,128]{1,0:T(8,128)S(1)}, u32[]{:S(2)}, u32[]{:S(2)}) collective-permute-start(f32[64,128]{1,0:T(8,128)} %get-tuple-element.82), channel_id=1, source_target_pairs={{0,24},{8,0},{16,8},{24,16},{1,25},{9,1},{17,9},{25,17},{2,26},{10... | collective-permute-start | bytes 98312 | tf_op jit(solution)/shard_map/ppermute | solution.py:246
  103.2 8.4 %collective-permute-start.30 = (f32[64,256]{1,0:T(8,128)}, f32[64,256]{1,0:T(8,128)S(1)}, u32[]{:S(2)}, u32[]{:S(2)}) collective-permute-start(f32[64,256]{1,0:T(8,128)} %get-tuple-element.88), channel_id=1, source_target_pairs={{0,1},{1,2},{2,3},{3,4},{4,5},{5,6},{6,7},{7,0},{8,9},{9,10},{10,1... | collective-permute-start | bytes 196616 | tf_op jit(solution)/shard_map/ppermute | solution.py:249
  103.2 8.4 %collective-permute-start.31 = (f32[64,256]{1,0:T(8,128)}, f32[64,256]{1,0:T(8,128)S(1)}, u32[]{:S(2)}, u32[]{:S(2)}) collective-permute-start(f32[64,256]{1,0:T(8,128)} %get-tuple-element.89), channel_id=1, source_target_pairs={{0,7},{1,0},{2,1},{3,2},{4,3},{5,4},{6,5},{7,6},{8,15},{9,8},{10,9... | collective-permute-start | bytes 196616 | tf_op jit(solution)/shard_map/ppermute | solution.py:250
  107.4 2.0 %collective-permute-start.28 = (f32[64,128]{1,0:T(8,128)}, f32[64,128]{1,0:T(8,128)S(1)}, u32[]{:S(2)}, u32[]{:S(2)}) collective-permute-start(f32[64,128]{1,0:T(8,128)} %get-tuple-element.86), channel_id=1, source_target_pairs={{0,8},{8,16},{16,24},{24,0},{1,9},{9,17},{17,25},{25,1},{2,10},{10... | collective-permute-start | bytes 98312 | tf_op jit(solution)/shard_map/ppermute | solution.py:245
  108.0 3.6 %collective-permute-start.29 = (f32[64,128]{1,0:T(8,128)}, f32[64,128]{1,0:T(8,128)S(1)}, u32[]{:S(2)}, u32[]{:S(2)}) collective-permute-start(f32[64,128]{1,0:T(8,128)} %get-tuple-element.87), channel_id=1, source_target_pairs={{0,24},{8,0},{16,8},{24,16},{1,25},{9,1},{17,9},{25,17},{2,26},{10... | collective-permute-start | bytes 98312 | tf_op jit(solution)/shard_map/ppermute | solution.py:246

commit v7 on v6

--- a/solution.py
+++ b/solution.py
@@ -160,7 +160,7 @@
 
 def _half_sweep_kernel(
     other_ref, lo_x_ref, hi_x_ref, lo_y_ref, hi_y_ref, face_ref, weight_ref, inverse_ref,
-    target_ref, previous_ref, out_ref, send_lo_x_ref, send_hi_x_ref, send_lo_y_ref, send_hi_y_ref, *, span_x
+    target_ref, previous_ref, old_lo_x, old_hi_x, old_lo_y, old_hi_y, out_ref, send_lo_x_ref, send_hi_x_ref, send_lo_y_ref, send_hi_y_ref, *, span_x
 ):
     tile = 2 * R
     highest = lax.Precision.HIGHEST
@@ -213,7 +213,7 @@
         send_hi_y_ref[:, t * tile:(t + 1) * tile] = jnp.where(low_half, even, pltpu.roll(odd, R, 1))
 
 
-def half_sweep(other, halos, face_blocks, weight, inverse, target, previous, span_x):
+def half_sweep(other, halos, face_blocks, weight, inverse, target, previous, old_sends, span_x):
     lanes = other.shape[1]
     x_shape = jax.ShapeDtypeStruct((P_SIZE, 2 * R), jnp.float32)
     y_shape = jax.ShapeDtypeStruct((P_SIZE, span_x * R), jnp.float32)
@@ -221,12 +221,12 @@
     return pl.pallas_call(
         functools.partial(_half_sweep_kernel, span_x=span_x),
         out_shape=(jax.ShapeDtypeStruct((P_SIZE, lanes), jnp.float32), x_shape, x_shape, y_shape, y_shape),
-        in_specs=[vmem] * 10,
+        in_specs=[vmem] * 14,
         out_specs=(vmem,) * 5,
-        input_output_aliases={9: 0},
+        input_output_aliases={9: 0, 10: 1, 11: 2, 12: 3, 13: 4},
     )(*[
         pltpu.with_memory_space_constraint(value, pltpu.VMEM)
-        for value in (other, *halos, face_blocks, weight, inverse, target, previous)
+        for value in (other, *halos, face_blocks, weight, inverse, target, previous, *old_sends)
     ])
 
 
@@ -275,7 +275,8 @@
         return jnp.transpose(values.reshape(columns, P_SIZE, R), (1, 0, 2)).reshape(P_SIZE, columns * R)
 
     start_state = to_lanes(pick(initial, 1))
-    first_halos = trade(send_buffers(start_state, span_x))
+    first_sends = send_buffers(start_state, span_x)
+    first_halos = trade(first_sends)
     by_colour = jnp.stack([pick(blocks, paint) for paint in (0, 1)]).reshape(count, P_SIZE, P_SIZE)
     inverse = block_inverses(by_colour, lanes_out=True)
     weight = jnp.where(neighbours == empty_slot, 0.0, strength * strong.astype(jnp.float32))
@@ -302,6 +303,7 @@
                 member_inverse[paint_now],
                 member_target[paint_now],
                 state[paint_now],
+                first_sends if sends is None else sends,
                 span_x,
             )
     first = first_is[0][..., None]

time: 115 us -> 108 us (0.939)
  Pallas kernels: 32.2 us -> 27.2 us
  waiting for transfers between devices: 24.6 us -> 23.1 us
    pallas_call x8, Pallas kernels: 13.1 us -> 7.98 us  [half_sweep(): pl.pallas_call(functools.partial(_half_sweep_kernel, span_x=span_x), out_...]
    ppermute x8, waiting for transfers between devices: 9.05 us -> 6.84 us  [trade(): lax.ppermute(sends[0], 'gx', shift_pairs('gx', 1))]
  transfers between devices with their start and end apart: 32 -> 32, of which waited for: 14 -> 14; matrix products, arithmetic and copies ran while one was open for 6% -> 6% of each run, Pallas kernels for 17% -> 18%
where the time goes in v7:
time: 108 us
  starting transfers between devices  42.6 us (39%)
  Pallas kernels  27.2 us (25%)
  waiting for transfers between devices  23.1 us (21%)
  local copies, waits for them, and re-layouts  13.7 us (13%)
    ppermute x8, starting transfers between devices, trade(): lax.ppermute(sends[3], 'gy', shift_pairs('gy', -1))  32.1 us
    pallas_call x1, Pallas kernels, block_inverses(): pl.pallas_call(functools.partial(_gauss_jordan_kernel, n=n, nb=nb), out_s...  19.2 us
    ppermute x8, waiting for transfers between devices, trade(): lax.ppermute(sends[1], 'gx', shift_pairs('gx', -1))  16.2 us
    pallas_call x8, Pallas kernels, half_sweep(): pl.pallas_call(functools.partial(_half_sweep_kernel, span_x=span_x), out_...  7.98 us
    ppermute x8, starting transfers between devices, trade(): lax.ppermute(sends[0], 'gx', shift_pairs('gx', 1))  7.91 us
    ppermute x8, waiting for transfers between devices, trade(): lax.ppermute(sends[0], 'gx', shift_pairs('gx', 1))  6.84 us
    slice x3, local copies, waits for them, and re-layouts, pick(): high = lax.index_in_dim(values, 1, axis=axis, keepdims=False)  2.68 us
    ppermute x8, starting transfers between devices, trade(): lax.ppermute(sends[2], 'gy', shift_pairs('gy', 1))  2.51 us
  transfers between devices with their start and end apart: 32, of which 14 were waited for; matrix products, arithmetic and copies ran while one was open for 6% of the time, Pallas kernels for 18%

profile of v7, /device:TPU:1, one launch (start us, length us, event | category | flops | bytes accessed | tf_op | source)
XLA Modules:
  0.0 108.0 jit_solution(13873013020585139609)
XLA Ops:
  0.0 0.7 slice-done
  1.1 1.9 %slice_reduce_fusion.2 = (f32[4,2,4096]{2,1,0:T(2,128)S(1)}, f32[4,2,4096]{2,1,0:T(2,128)S(1)}) fusion(f32[4,2,2,4096]{3,2,1,0:T(2,128)} %param.9), kind=kLoop, calls=%fused_computation.10 | loop fusion | bytes 524288 | tf_op jit(solution)/shard_map/slice | solution.py:271
  3.0 0.2 squeeze.32
  3.2 0.2 squeeze.33
  3.4 0.7 copy-done
  4.1 0.8 slice_reduce_fusion
  4.9 0.2 squeeze.36
  5.1 0.2 squeeze.37
  5.7 2.1 %collective-permute-start.2 = (f32[64,256]{1,0:T(8,128)S(1)}, f32[64,256]{1,0:T(8,128)S(1)}, u32[]{:S(2)}, u32[]{:S(2)}) collective-permute-start(f32[64,256]{1,0:T(8,128)S(1)} %reshape_squeeze.14.old_lo_y), channel_id=1, source_target_pairs={{0,1},{1,2},{2,3},{3,4},{4,5},{5,6},{6,7},{7,0},{8,9},{9,10},{10,1... | collective-permute-start | bytes 196616 | tf_op jit(solution)/shard_map/ppermute | solution.py:249
  8.1 3.1 %collective-permute-start.3 = (f32[64,256]{1,0:T(8,128)S(1)}, f32[64,256]{1,0:T(8,128)S(1)}, u32[]{:S(2)}, u32[]{:S(2)}) collective-permute-start(f32[64,256]{1,0:T(8,128)S(1)} %reshape_squeeze.15.old_hi_y), channel_id=1, source_target_pairs={{0,7},{1,0},{2,1},{3,2},{4,3},{5,4},{6,5},{7,6},{8,15},{9,8},{10,9... | collective-permute-start | bytes 196616 | tf_op jit(solution)/shard_map/ppermute | solution.py:250
  11.3 2.2 %collective-permute-start = (f32[64,128]{1,0:T(8,128)S(1)}, f32[64,128]{1,0:T(8,128)S(1)}, u32[]{:S(2)}, u32[]{:S(2)}) collective-permute-start(f32[64,128]{1,0:T(8,128)S(1)} %reshape_squeeze.12.old_lo_x), channel_id=1, source_target_pairs={{0,8},{8,16},{16,24},{24,0},{1,9},{9,17},{17,25},{25,1},{2,10},{10... | collective-permute-start | bytes 98312 | tf_op jit(solution)/shard_map/ppermute | solution.py:245
  13.7 0.3 broadcast_select_fusion.1
  14.0 0.2 pad_maximum_fusion
  14.3 0.2 copy.100
  14.5 0.3 reshape.157
  14.8 0.3 copy.101
  15.1 0.9 copy.102.a_ref
  16.0 19.2 %shard_map.82 = f32[64,1024]{1,0:T(8,128)} custom-call(f32[64,1024]{1,0:T(8,128)} %copy.102.a_ref), custom_call_target="tpu_custom_call" | custom-call | flops 8388608000 | bytes 524288 | tf_op jit(solution)/shard_map/pallas_call | solution.py:75
  35.2 1.1 %copy.103 = f32[64,1024]{0,1:T(8,128)S(1)} copy(f32[64,1024]{1,0:T(8,128)} %shard_map.82) | data formatting | bytes 524288 | tf_op jit(solution)/shard_map/pallas_call | solution.py:75
  36.3 0.4 copy.104
  36.7 0.2 reshape.160
  37.0 0.6 copy-done.3
  37.7 0.2 copy.106
  38.0 0.2 copy.107
  38.8 0.4 copy-done.2
  39.4 0.2 copy.94
  39.8 1.0 shard_map.83
  40.8 4.1 %collective-permute-start.7 = (f32[64,256]{1,0:T(8,128)S(1)}, f32[64,256]{1,0:T(8,128)S(1)}, u32[]{:S(2)}, u32[]{:S(2)}) collective-permute-start(f32[64,256]{1,0:T(8,128)S(1)} %get-tuple-element.56.old_hi_y), channel_id=1, source_target_pairs={{0,7},{1,0},{2,1},{3,2},{4,3},{5,4},{6,5},{7,6},{8,15},{9,8},{10,9... | collective-permute-start | bytes 196616 | tf_op jit(solution)/shard_map/ppermute | solution.py:250
  45.0 2.3 %collective-permute-start.4 = (f32[64,128]{1,0:T(8,128)S(1)}, f32[64,128]{1,0:T(8,128)S(1)}, u32[]{:S(2)}, u32[]{:S(2)}) collective-permute-start(f32[64,128]{1,0:T(8,128)S(1)} %get-tuple-element.53.old_lo_x), channel_id=1, source_target_pairs={{0,8},{8,16},{16,24},{24,0},{1,9},{9,17},{17,25},{25,1},{2,10},{10... | collective-permute-start | bytes 98312 | tf_op jit(solution)/shard_map/ppermute | solution.py:245
  47.3 1.0 collective-permute-done.4.lo_x_ref
  48.3 2.3 %collective-permute-done.5.hi_x_ref = f32[64,128]{1,0:T(8,128)S(1)} collective-permute-done((f32[64,128]{1,0:T(8,128)S(1)}, f32[64,128]{1,0:T(8,128)S(1)}, u32[]{:S(2)}, u32[]{:S(2)}) %collective-permute-start.5) | collective-permute-done | bytes 32800 | tf_op jit(solution)/shard_map/ppermute | solution.py:246
  50.6 1.0 shard_map.84
  51.7 4.1 %collective-permute-start.11 = (f32[64,256]{1,0:T(8,128)S(1)}, f32[64,256]{1,0:T(8,128)S(1)}, u32[]{:S(2)}, u32[]{:S(2)}) collective-permute-start(f32[64,256]{1,0:T(8,128)S(1)} %get-tuple-element.64.old_hi_y), channel_id=1, source_target_pairs={{0,7},{1,0},{2,1},{3,2},{4,3},{5,4},{6,5},{7,6},{8,15},{9,8},{10,9... | collective-permute-start | bytes 196616 | tf_op jit(solution)/shard_map/ppermute | solution.py:250
  55.8 0.6 collective-permute-start.8
  56.4 1.0 collective-permute-done.8.lo_x_ref
  57.4 2.3 %collective-permute-done.9.hi_x_ref = f32[64,128]{1,0:T(8,128)S(1)} collective-permute-done((f32[64,128]{1,0:T(8,128)S(1)}, f32[64,128]{1,0:T(8,128)S(1)}, u32[]{:S(2)}, u32[]{:S(2)}) %collective-permute-start.9) | collective-permute-done | bytes 32800 | tf_op jit(solution)/shard_map/ppermute | solution.py:246
  59.8 1.0 shard_map.85
  60.8 4.1 %collective-permute-start.15 = (f32[64,256]{1,0:T(8,128)S(1)}, f32[64,256]{1,0:T(8,128)S(1)}, u32[]{:S(2)}, u32[]{:S(2)}) collective-permute-start(f32[64,256]{1,0:T(8,128)S(1)} %get-tuple-element.69.old_hi_y), channel_id=1, source_target_pairs={{0,7},{1,0},{2,1},{3,2},{4,3},{5,4},{6,5},{7,6},{8,15},{9,8},{10,9... | collective-permute-start | bytes 196616 | tf_op jit(solution)/shard_map/ppermute | solution.py:250
  65.0 0.6 collective-permute-start.12
  65.5 1.0 collective-permute-done.12.lo_x_ref
  66.6 2.3 %collective-permute-done.13.hi_x_ref = f32[64,128]{1,0:T(8,128)S(1)} collective-permute-done((f32[64,128]{1,0:T(8,128)S(1)}, f32[64,128]{1,0:T(8,128)S(1)}, u32[]{:S(2)}, u32[]{:S(2)}) %collective-permute-start.13) | collective-permute-done | bytes 32800 | tf_op jit(solution)/shard_map/ppermute | solution.py:246
  68.9 1.0 shard_map.86
  70.0 4.1 %collective-permute-start.19 = (f32[64,256]{1,0:T(8,128)S(1)}, f32[64,256]{1,0:T(8,128)S(1)}, u32[]{:S(2)}, u32[]{:S(2)}) collective-permute-start(f32[64,256]{1,0:T(8,128)S(1)} %get-tuple-element.74.old_hi_y), channel_id=1, source_target_pairs={{0,7},{1,0},{2,1},{3,2},{4,3},{5,4},{6,5},{7,6},{8,15},{9,8},{10,9... | collective-permute-start | bytes 196616 | tf_op jit(solution)/shard_map/ppermute | solution.py:250
  74.1 0.6 collective-permute-start.16
  74.7 1.0 collective-permute-done.16.lo_x_ref
  75.7 2.3 %collective-permute-done.17.hi_x_ref = f32[64,128]{1,0:T(8,128)S(1)} collective-permute-done((f32[64,128]{1,0:T(8,128)S(1)}, f32[64,128]{1,0:T(8,128)S(1)}, u32[]{:S(2)}, u32[]{:S(2)}) %collective-permute-start.17) | collective-permute-done | bytes 32800 | tf_op jit(solution)/shard_map/ppermute | solution.py:246
  78.0 1.0 shard_map.87
  79.1 4.1 %collective-permute-start.23 = (f32[64,256]{1,0:T(8,128)S(1)}, f32[64,256]{1,0:T(8,128)S(1)}, u32[]{:S(2)}, u32[]{:S(2)}) collective-permute-start(f32[64,256]{1,0:T(8,128)S(1)} %get-tuple-element.79.old_hi_y), channel_id=1, source_target_pairs={{0,7},{1,0},{2,1},{3,2},{4,3},{5,4},{6,5},{7,6},{8,15},{9,8},{10,9... | collective-permute-start | bytes 196616 | tf_op jit(solution)/shard_map/ppermute | solution.py:250
  83.3 0.6 collective-permute-start.20
  83.8 1.0 collective-permute-done.20.lo_x_ref
  84.8 2.3 %collective-permute-done.21.hi_x_ref = f32[64,128]{1,0:T(8,128)S(1)} collective-permute-done((f32[64,128]{1,0:T(8,128)S(1)}, f32[64,128]{1,0:T(8,128)S(1)}, u32[]{:S(2)}, u32[]{:S(2)}) %collective-permute-start.21) | collective-permute-done | bytes 32800 | tf_op jit(solution)/shard_map/ppermute | solution.py:246
  87.2 1.0 shard_map.88
  88.2 4.1 %collective-permute-start.27 = (f32[64,256]{1,0:T(8,128)S(1)}, f32[64,256]{1,0:T(8,128)S(1)}, u32[]{:S(2)}, u32[]{:S(2)}) collective-permute-start(f32[64,256]{1,0:T(8,128)S(1)} %get-tuple-element.84.old_hi_y), channel_id=1, source_target_pairs={{0,7},{1,0},{2,1},{3,2},{4,3},{5,4},{6,5},{7,6},{8,15},{9,8},{10,9... | collective-permute-start | bytes 196616 | tf_op jit(solution)/shard_map/ppermute | solution.py:250
  92.4 0.6 collective-permute-start.24
  93.0 1.0 collective-permute-done.24.lo_x_ref
  94.0 2.3 %collective-permute-done.25.hi_x_ref = f32[64,128]{1,0:T(8,128)S(1)} collective-permute-done((f32[64,128]{1,0:T(8,128)S(1)}, f32[64,128]{1,0:T(8,128)S(1)}, u32[]{:S(2)}, u32[]{:S(2)}) %collective-permute-start.25) | collective-permute-done | bytes 32800 | tf_op jit(solution)/shard_map/ppermute | solution.py:246
  96.3 1.0 shard_map.89
  97.4 4.1 %collective-permute-start.31 = (f32[64,256]{1,0:T(8,128)S(1)}, f32[64,256]{1,0:T(8,128)S(1)}, u32[]{:S(2)}, u32[]{:S(2)}) collective-permute-start(f32[64,256]{1,0:T(8,128)S(1)} %get-tuple-element.89.old_hi_y), channel_id=1, source_target_pairs={{0,7},{1,0},{2,1},{3,2},{4,3},{5,4},{6,5},{7,6},{8,15},{9,8},{10,9... | collective-permute-start | bytes 196616 | tf_op jit(solution)/shard_map/ppermute | solution.py:250
  101.5 0.6 collective-permute-start.28
  102.4 0.7 collective-permute-done.28.lo_x_ref
  103.1 2.3 %collective-permute-done.29.hi_x_ref = f32[64,128]{1,0:T(8,128)S(1)} collective-permute-done((f32[64,128]{1,0:T(8,128)S(1)}, f32[64,128]{1,0:T(8,128)S(1)}, u32[]{:S(2)}, u32[]{:S(2)}) %collective-permute-start.29) | collective-permute-done | bytes 32800 | tf_op jit(solution)/shard_map/ppermute | solution.py:246
  105.4 1.0 shard_map.90
  106.8 0.2 broadcast_select_fusion.4
  107.1 0.9 copy.113
  (84 shorter events, 3.8 us)
Async XLA Ops:
  0.0 0.7 slice-start
  3.2 1.0 copy-start
  5.7 34.0 %collective-permute-start.2 = (f32[64,256]{1,0:T(8,128)S(1)}, f32[64,256]{1,0:T(8,128)S(1)}, u32[]{:S(2)}, u32[]{:S(2)}) collective-permute-start(f32[64,256]{1,0:T(8,128)S(1)} %reshape_squeeze.14.old_lo_y), channel_id=1, source_target_pairs={{0,1},{1,2},{2,3},{3,4},{4,5},{5,6},{6,7},{7,0},{8,9},{9,10},{10,1... | collective-permute-start | bytes 196616 | tf_op jit(solution)/shard_map/ppermute | solution.py:249
  8.1 31.7 %collective-permute-start.3 = (f32[64,256]{1,0:T(8,128)S(1)}, f32[64,256]{1,0:T(8,128)S(1)}, u32[]{:S(2)}, u32[]{:S(2)}) collective-permute-start(f32[64,256]{1,0:T(8,128)S(1)} %reshape_squeeze.15.old_hi_y), channel_id=1, source_target_pairs={{0,7},{1,0},{2,1},{3,2},{4,3},{5,4},{6,5},{7,6},{8,15},{9,8},{10,9... | collective-permute-start | bytes 196616 | tf_op jit(solution)/shard_map/ppermute | solution.py:250
  11.2 2.6 %copy-start.1 = (f32[4,2,2,4096]{3,2,1,0:T(2,128)S(1)}, f32[4,2,2,4096]{3,2,1,0:T(2,128)}, u32[]{:S(2)}) copy-start(f32[4,2,2,4096]{3,2,1,0:T(2,128)} %param.10) | copy-start | bytes 786436
  11.3 28.4 %collective-permute-start = (f32[64,128]{1,0:T(8,128)S(1)}, f32[64,128]{1,0:T(8,128)S(1)}, u32[]{:S(2)}, u32[]{:S(2)}) collective-permute-start(f32[64,128]{1,0:T(8,128)S(1)} %reshape_squeeze.12.old_lo_x), channel_id=1, source_target_pairs={{0,8},{8,16},{16,24},{24,0},{1,9},{9,17},{17,25},{25,1},{2,10},{10... | collective-permute-start | bytes 98312 | tf_op jit(solution)/shard_map/ppermute | solution.py:245
  13.7 26.0 %collective-permute-start.1 = (f32[64,128]{1,0:T(8,128)S(1)}, f32[64,128]{1,0:T(8,128)S(1)}, u32[]{:S(2)}, u32[]{:S(2)}) collective-permute-start(f32[64,128]{1,0:T(8,128)S(1)} %reshape_squeeze.13.old_hi_x), channel_id=1, source_target_pairs={{0,24},{8,0},{16,8},{24,16},{1,25},{9,1},{17,9},{25,17},{2,26},{10... | collective-permute-start | bytes 98312 | tf_op jit(solution)/shard_map/ppermute | solution.py:246
  36.9 0.7 copy-start.3
  36.9 0.7 copy-start.4
  36.9 0.7 copy-start.5
  38.3 0.9 copy-start.2
  40.8 9.8 %collective-permute-start.6 = (f32[64,256]{1,0:T(8,128)S(1)}, f32[64,256]{1,0:T(8,128)S(1)}, u32[]{:S(2)}, u32[]{:S(2)}) collective-permute-start(f32[64,256]{1,0:T(8,128)S(1)} %get-tuple-element.55.old_lo_y), channel_id=1, source_target_pairs={{0,1},{1,2},{2,3},{3,4},{4,5},{5,6},{6,7},{7,0},{8,9},{9,10},{10,1... | collective-permute-start | bytes 196616 | tf_op jit(solution)/shard_map/ppermute | solution.py:249
  40.8 9.8 %collective-permute-start.7 = (f32[64,256]{1,0:T(8,128)S(1)}, f32[64,256]{1,0:T(8,128)S(1)}, u32[]{:S(2)}, u32[]{:S(2)}) collective-permute-start(f32[64,256]{1,0:T(8,128)S(1)} %get-tuple-element.56.old_hi_y), channel_id=1, source_target_pairs={{0,7},{1,0},{2,1},{3,2},{4,3},{5,4},{6,5},{7,6},{8,15},{9,8},{10,9... | collective-permute-start | bytes 196616 | tf_op jit(solution)/shard_map/ppermute | solution.py:250
  45.0 3.3 %collective-permute-start.4 = (f32[64,128]{1,0:T(8,128)S(1)}, f32[64,128]{1,0:T(8,128)S(1)}, u32[]{:S(2)}, u32[]{:S(2)}) collective-permute-start(f32[64,128]{1,0:T(8,128)S(1)} %get-tuple-element.53.old_lo_x), channel_id=1, source_target_pairs={{0,8},{8,16},{16,24},{24,0},{1,9},{9,17},{17,25},{25,1},{2,10},{10... | collective-permute-start | bytes 98312 | tf_op jit(solution)/shard_map/ppermute | solution.py:245
  47.3 3.3 %collective-permute-start.5 = (f32[64,128]{1,0:T(8,128)S(1)}, f32[64,128]{1,0:T(8,128)S(1)}, u32[]{:S(2)}, u32[]{:S(2)}) collective-permute-start(f32[64,128]{1,0:T(8,128)S(1)} %get-tuple-element.54.old_hi_x), channel_id=1, source_target_pairs={{0,24},{8,0},{16,8},{24,16},{1,25},{9,1},{17,9},{25,17},{2,26},{10... | collective-permute-start | bytes 98312 | tf_op jit(solution)/shard_map/ppermute | solution.py:246
  51.6 8.1 %collective-permute-start.10 = (f32[64,256]{1,0:T(8,128)S(1)}, f32[64,256]{1,0:T(8,128)S(1)}, u32[]{:S(2)}, u32[]{:S(2)}) collective-permute-start(f32[64,256]{1,0:T(8,128)S(1)} %get-tuple-element.63.old_lo_y), channel_id=1, source_target_pairs={{0,1},{1,2},{2,3},{3,4},{4,5},{5,6},{6,7},{7,0},{8,9},{9,10},{10,1... | collective-permute-start | bytes 196616 | tf_op jit(solution)/shard_map/ppermute | solution.py:249
  51.7 8.1 %collective-permute-start.11 = (f32[64,256]{1,0:T(8,128)S(1)}, f32[64,256]{1,0:T(8,128)S(1)}, u32[]{:S(2)}, u32[]{:S(2)}) collective-permute-start(f32[64,256]{1,0:T(8,128)S(1)} %get-tuple-element.64.old_hi_y), channel_id=1, source_target_pairs={{0,7},{1,0},{2,1},{3,2},{4,3},{5,4},{6,5},{7,6},{8,15},{9,8},{10,9... | collective-permute-start | bytes 196616 | tf_op jit(solution)/shard_map/ppermute | solution.py:250
  55.8 1.6 %collective-permute-start.8 = (f32[64,128]{1,0:T(8,128)S(1)}, f32[64,128]{1,0:T(8,128)S(1)}, u32[]{:S(2)}, u32[]{:S(2)}) collective-permute-start(f32[64,128]{1,0:T(8,128)S(1)} %get-tuple-element.61.old_lo_x), channel_id=1, source_target_pairs={{0,8},{8,16},{16,24},{24,0},{1,9},{9,17},{17,25},{25,1},{2,10},{10... | collective-permute-start | bytes 98312 | tf_op jit(solution)/shard_map/ppermute | solution.py:245
  56.4 3.3 %collective-permute-start.9 = (f32[64,128]{1,0:T(8,128)S(1)}, f32[64,128]{1,0:T(8,128)S(1)}, u32[]{:S(2)}, u32[]{:S(2)}) collective-permute-start(f32[64,128]{1,0:T(8,128)S(1)} %get-tuple-element.62.old_hi_x), channel_id=1, source_target_pairs={{0,24},{8,0},{16,8},{24,16},{1,25},{9,1},{17,9},{25,17},{2,26},{10... | collective-permute-start | bytes 98312 | tf_op jit(solution)/shard_map/ppermute | solution.py:246
  60.8 8.1 %collective-permute-start.14 = (f32[64,256]{1,0:T(8,128)S(1)}, f32[64,256]{1,0:T(8,128)S(1)}, u32[]{:S(2)}, u32[]{:S(2)}) collective-permute-start(f32[64,256]{1,0:T(8,128)S(1)} %get-tuple-element.68.old_lo_y), channel_id=1, source_target_pairs={{0,1},{1,2},{2,3},{3,4},{4,5},{5,6},{6,7},{7,0},{8,9},{9,10},{10,1... | collective-permute-start | bytes 196616 | tf_op jit(solution)/shard_map/ppermute | solution.py:249
  60.8 8.1 %collective-permute-start.15 = (f32[64,256]{1,0:T(8,128)S(1)}, f32[64,256]{1,0:T(8,128)S(1)}, u32[]{:S(2)}, u32[]{:S(2)}) collective-permute-start(f32[64,256]{1,0:T(8,128)S(1)} %get-tuple-element.69.old_hi_y), channel_id=1, source_target_pairs={{0,7},{1,0},{2,1},{3,2},{4,3},{5,4},{6,5},{7,6},{8,15},{9,8},{10,9... | collective-permute-start | bytes 196616 | tf_op jit(solution)/shard_map/ppermute | solution.py:250
  65.0 1.6 %collective-permute-start.12 = (f32[64,128]{1,0:T(8,128)S(1)}, f32[64,128]{1,0:T(8,128)S(1)}, u32[]{:S(2)}, u32[]{:S(2)}) collective-permute-start(f32[64,128]{1,0:T(8,128)S(1)} %get-tuple-element.66.old_lo_x), channel_id=1, source_target_pairs={{0,8},{8,16},{16,24},{24,0},{1,9},{9,17},{17,25},{25,1},{2,10},{10... | collective-permute-start | bytes 98312 | tf_op jit(solution)/shard_map/ppermute | solution.py:245
  65.5 3.3 %collective-permute-start.13 = (f32[64,128]{1,0:T(8,128)S(1)}, f32[64,128]{1,0:T(8,128)S(1)}, u32[]{:S(2)}, u32[]{:S(2)}) collective-permute-start(f32[64,128]{1,0:T(8,128)S(1)} %get-tuple-element.67.old_hi_x), channel_id=1, source_target_pairs={{0,24},{8,0},{16,8},{24,16},{1,25},{9,1},{17,9},{25,17},{2,26},{10... | collective-permute-start | bytes 98312 | tf_op jit(solution)/shard_map/ppermute | solution.py:246
  69.9 8.1 %collective-permute-start.18 = (f32[64,256]{1,0:T(8,128)S(1)}, f32[64,256]{1,0:T(8,128)S(1)}, u32[]{:S(2)}, u32[]{:S(2)}) collective-permute-start(f32[64,256]{1,0:T(8,128)S(1)} %get-tuple-element.73.old_lo_y), channel_id=1, source_target_pairs={{0,1},{1,2},{2,3},{3,4},{4,5},{5,6},{6,7},{7,0},{8,9},{9,10},{10,1... | collective-permute-start | bytes 196616 | tf_op jit(solution)/shard_map/ppermute | solution.py:249
  70.0 8.1 %collective-permute-start.19 = (f32[64,256]{1,0:T(8,128)S(1)}, f32[64,256]{1,0:T(8,128)S(1)}, u32[]{:S(2)}, u32[]{:S(2)}) collective-permute-start(f32[64,256]{1,0:T(8,128)S(1)} %get-tuple-element.74.old_hi_y), channel_id=1, source_target_pairs={{0,7},{1,0},{2,1},{3,2},{4,3},{5,4},{6,5},{7,6},{8,15},{9,8},{10,9... | collective-permute-start | bytes 196616 | tf_op jit(solution)/shard_map/ppermute | solution.py:250
  74.1 1.6 %collective-permute-start.16 = (f32[64,128]{1,0:T(8,128)S(1)}, f32[64,128]{1,0:T(8,128)S(1)}, u32[]{:S(2)}, u32[]{:S(2)}) collective-permute-start(f32[64,128]{1,0:T(8,128)S(1)} %get-tuple-element.71.old_lo_x), channel_id=1, source_target_pairs={{0,8},{8,16},{16,24},{24,0},{1,9},{9,17},{17,25},{25,1},{2,10},{10... | collective-permute-start | bytes 98312 | tf_op jit(solution)/shard_map/ppermute | solution.py:245
  74.7 3.3 %collective-permute-start.17 = (f32[64,128]{1,0:T(8,128)S(1)}, f32[64,128]{1,0:T(8,128)S(1)}, u32[]{:S(2)}, u32[]{:S(2)}) collective-permute-start(f32[64,128]{1,0:T(8,128)S(1)} %get-tuple-element.72.old_hi_x), channel_id=1, source_target_pairs={{0,24},{8,0},{16,8},{24,16},{1,25},{9,1},{17,9},{25,17},{2,26},{10... | collective-permute-start | bytes 98312 | tf_op jit(solution)/shard_map/ppermute | solution.py:246
  79.0 8.1 %collective-permute-start.22 = (f32[64,256]{1,0:T(8,128)S(1)}, f32[64,256]{1,0:T(8,128)S(1)}, u32[]{:S(2)}, u32[]{:S(2)}) collective-permute-start(f32[64,256]{1,0:T(8,128)S(1)} %get-tuple-element.78.old_lo_y), channel_id=1, source_target_pairs={{0,1},{1,2},{2,3},{3,4},{4,5},{5,6},{6,7},{7,0},{8,9},{9,10},{10,1... | collective-permute-start | bytes 196616 | tf_op jit(solution)/shard_map/ppermute | solution.py:249
  79.1 8.1 %collective-permute-start.23 = (f32[64,256]{1,0:T(8,128)S(1)}, f32[64,256]{1,0:T(8,128)S(1)}, u32[]{:S(2)}, u32[]{:S(2)}) collective-permute-start(f32[64,256]{1,0:T(8,128)S(1)} %get-tuple-element.79.old_hi_y), channel_id=1, source_target_pairs={{0,7},{1,0},{2,1},{3,2},{4,3},{5,4},{6,5},{7,6},{8,15},{9,8},{10,9... | collective-permute-start | bytes 196616 | tf_op jit(solution)/shard_map/ppermute | solution.py:250
  83.3 1.6 %collective-permute-start.20 = (f32[64,128]{1,0:T(8,128)S(1)}, f32[64,128]{1,0:T(8,128)S(1)}, u32[]{:S(2)}, u32[]{:S(2)}) collective-permute-start(f32[64,128]{1,0:T(8,128)S(1)} %get-tuple-element.76.old_lo_x), channel_id=1, source_target_pairs={{0,8},{8,16},{16,24},{24,0},{1,9},{9,17},{17,25},{25,1},{2,10},{10... | collective-permute-start | bytes 98312 | tf_op jit(solution)/shard_map/ppermute | solution.py:245
  83.8 3.3 %collective-permute-start.21 = (f32[64,128]{1,0:T(8,128)S(1)}, f32[64,128]{1,0:T(8,128)S(1)}, u32[]{:S(2)}, u32[]{:S(2)}) collective-permute-start(f32[64,128]{1,0:T(8,128)S(1)} %get-tuple-element.77.old_hi_x), channel_id=1, source_target_pairs={{0,24},{8,0},{16,8},{24,16},{1,25},{9,1},{17,9},{25,17},{2,26},{10... | collective-permute-start | bytes 98312 | tf_op jit(solution)/shard_map/ppermute | solution.py:246
  88.2 8.1 %collective-permute-start.26 = (f32[64,256]{1,0:T(8,128)S(1)}, f32[64,256]{1,0:T(8,128)S(1)}, u32[]{:S(2)}, u32[]{:S(2)}) collective-permute-start(f32[64,256]{1,0:T(8,128)S(1)} %get-tuple-element.83.old_lo_y), channel_id=1, source_target_pairs={{0,1},{1,2},{2,3},{3,4},{4,5},{5,6},{6,7},{7,0},{8,9},{9,10},{10,1... | collective-permute-start | bytes 196616 | tf_op jit(solution)/shard_map/ppermute | solution.py:249
  88.2 8.1 %collective-permute-start.27 = (f32[64,256]{1,0:T(8,128)S(1)}, f32[64,256]{1,0:T(8,128)S(1)}, u32[]{:S(2)}, u32[]{:S(2)}) collective-permute-start(f32[64,256]{1,0:T(8,128)S(1)} %get-tuple-element.84.old_hi_y), channel_id=1, source_target_pairs={{0,7},{1,0},{2,1},{3,2},{4,3},{5,4},{6,5},{7,6},{8,15},{9,8},{10,9... | collective-permute-start | bytes 196616 | tf_op jit(solution)/shard_map/ppermute | solution.py:250
  92.4 1.6 %collective-permute-start.24 = (f32[64,128]{1,0:T(8,128)S(1)}, f32[64,128]{1,0:T(8,128)S(1)}, u32[]{:S(2)}, u32[]{:S(2)}) collective-permute-start(f32[64,128]{1,0:T(8,128)S(1)} %get-tuple-element.81.old_lo_x), channel_id=1, source_target_pairs={{0,8},{8,16},{16,24},{24,0},{1,9},{9,17},{17,25},{25,1},{2,10},{10... | collective-permute-start | bytes 98312 | tf_op jit(solution)/shard_map/ppermute | solution.py:245
  93.0 3.3 %collective-permute-start.25 = (f32[64,128]{1,0:T(8,128)S(1)}, f32[64,128]{1,0:T(8,128)S(1)}, u32[]{:S(2)}, u32[]{:S(2)}) collective-permute-start(f32[64,128]{1,0:T(8,128)S(1)} %get-tuple-element.82.old_hi_x), channel_id=1, source_target_pairs={{0,24},{8,0},{16,8},{24,16},{1,25},{9,1},{17,9},{25,17},{2,26},{10... | collective-permute-start | bytes 98312 | tf_op jit(solution)/shard_map/ppermute | solution.py:246
  97.3 8.1 %collective-permute-start.30 = (f32[64,256]{1,0:T(8,128)S(1)}, f32[64,256]{1,0:T(8,128)S(1)}, u32[]{:S(2)}, u32[]{:S(2)}) collective-permute-start(f32[64,256]{1,0:T(8,128)S(1)} %get-tuple-element.88.old_lo_y), channel_id=1, source_target_pairs={{0,1},{1,2},{2,3},{3,4},{4,5},{5,6},{6,7},{7,0},{8,9},{9,10},{10,1... | collective-permute-start | bytes 196616 | tf_op jit(solution)/shard_map/ppermute | solution.py:249
  97.4 8.1 %collective-permute-start.31 = (f32[64,256]{1,0:T(8,128)S(1)}, f32[64,256]{1,0:T(8,128)S(1)}, u32[]{:S(2)}, u32[]{:S(2)}) collective-permute-start(f32[64,256]{1,0:T(8,128)S(1)} %get-tuple-element.89.old_hi_y), channel_id=1, source_target_pairs={{0,7},{1,0},{2,1},{3,2},{4,3},{5,4},{6,5},{7,6},{8,15},{9,8},{10,9... | collective-permute-start | bytes 196616 | tf_op jit(solution)/shard_map/ppermute | solution.py:250
  101.5 1.6 %collective-permute-start.28 = (f32[64,128]{1,0:T(8,128)S(1)}, f32[64,128]{1,0:T(8,128)S(1)}, u32[]{:S(2)}, u32[]{:S(2)}) collective-permute-start(f32[64,128]{1,0:T(8,128)S(1)} %get-tuple-element.86.old_lo_x), channel_id=1, source_target_pairs={{0,8},{8,16},{16,24},{24,0},{1,9},{9,17},{17,25},{25,1},{2,10},{10... | collective-permute-start | bytes 98312 | tf_op jit(solution)/shard_map/ppermute | solution.py:245
  102.1 3.3 %collective-permute-start.29 = (f32[64,128]{1,0:T(8,128)S(1)}, f32[64,128]{1,0:T(8,128)S(1)}, u32[]{:S(2)}, u32[]{:S(2)}) collective-permute-start(f32[64,128]{1,0:T(8,128)S(1)} %get-tuple-element.87.old_hi_x), channel_id=1, source_target_pairs={{0,24},{8,0},{16,8},{24,16},{1,25},{9,1},{17,9},{25,17},{2,26},{10... | collective-permute-start | bytes 98312 | tf_op jit(solution)/shard_map/ppermute | solution.py:246

commit v8 on v7

--- a/solution.py
+++ b/solution.py
@@ -28,7 +28,7 @@
 def _gauss_jordan_kernel(a_ref, o_ref, *, n, nb):
     lanes = n * nb
     tiles = lanes // 128
-    o_ref[...] = a_ref[...]
+    del a_ref
     lane_t = lax.broadcasted_iota(jnp.int32, (n, 128), 1)
     lane_r = lax.broadcasted_iota(jnp.int32, (1, 128), 1)
     row_i = lax.broadcasted_iota(jnp.int32, (n, 128), 0)
@@ -77,10 +77,11 @@
         out_shape=jax.ShapeDtypeStruct((n, n * nb), jnp.float32),
         in_specs=[pl.BlockSpec(memory_space=pltpu.VMEM)],
         out_specs=pl.BlockSpec(memory_space=pltpu.VMEM),
+        input_output_aliases={0: 0},
         cost_estimate=pl.CostEstimate(
             flops=2000 * n ** 3 * nb, transcendentals=0, bytes_accessed=8 * n * n * nb
         ),
-    )(packed)
+    )(pltpu.with_memory_space_constraint(packed, pltpu.VMEM))
     if lanes_out:
         return jnp.transpose(inverted.reshape(n, n, nb), (0, 2, 1)).reshape(n, nb * n)
     return jnp.transpose(inverted.reshape(n, n, nb), (2, 0, 1))

time: 108 us -> 105 us (0.972)
  Pallas kernels: 27.2 us -> 25.5 us
  local copies, waits for them, and re-layouts: 13.7 us -> 12 us
    pallas_call x1, Pallas kernels: 19.2 us -> 17.5 us  [block_inverses(): pl.pallas_call(functools.partial(_gauss_jordan_kernel, n=n, nb=nb), out_s...]
  transfers between devices with their start and end apart: 32 -> 32, of which waited for: 14 -> 14; matrix products, arithmetic and copies ran while one was open for 6% -> 5% of each run, Pallas kernels for 18% -> 17%
where the time goes in v8:
time: 105 us
  starting transfers between devices  42.6 us (41%)
  Pallas kernels  25.5 us (24%)
  waiting for transfers between devices  23.1 us (22%)
  local copies, waits for them, and re-layouts  12 us (11%)
    ppermute x8, starting transfers between devices, trade(): lax.ppermute(sends[3], 'gy', shift_pairs('gy', -1))  32.1 us
    pallas_call x1, Pallas kernels, block_inverses(): pl.pallas_call(functools.partial(_gauss_jordan_kernel, n=n, nb=nb), out_s...  17.5 us
    ppermute x8, waiting for transfers between devices, trade(): lax.ppermute(sends[1], 'gx', shift_pairs('gx', -1))  16.2 us
    pallas_call x8, Pallas kernels, half_sweep(): pl.pallas_call(functools.partial(_half_sweep_kernel, span_x=span_x), out_...  7.99 us
    ppermute x8, starting transfers between devices, trade(): lax.ppermute(sends[0], 'gx', shift_pairs('gx', 1))  7.91 us
    ppermute x8, waiting for transfers between devices, trade(): lax.ppermute(sends[0], 'gx', shift_pairs('gx', 1))  6.84 us
    slice x3, local copies, waits for them, and re-layouts, pick(): high = lax.index_in_dim(values, 1, axis=axis, keepdims=False)  2.68 us
    ppermute x8, starting transfers between devices, trade(): lax.ppermute(sends[2], 'gy', shift_pairs('gy', 1))  2.51 us
  transfers between devices with their start and end apart: 32, of which 14 were waited for; matrix products, arithmetic and copies ran while one was open for 5% of the time, Pallas kernels for 17%

profile of v8, /device:TPU:1, one launch (start us, length us, event | category | flops | bytes accessed | tf_op | source)
XLA Modules:
  0.0 104.7 jit_solution(4646943258067925712)
XLA Ops:
  0.0 0.7 slice-done
  1.1 1.9 %slice_reduce_fusion.2 = (f32[4,2,4096]{2,1,0:T(2,128)S(1)}, f32[4,2,4096]{2,1,0:T(2,128)S(1)}) fusion(f32[4,2,2,4096]{3,2,1,0:T(2,128)} %param.9), kind=kLoop, calls=%fused_computation.10 | loop fusion | bytes 524288 | tf_op jit(solution)/shard_map/slice | solution.py:272
  3.0 0.2 squeeze.32
  3.2 0.2 squeeze.33
  3.4 0.7 copy-done
  4.1 0.8 slice_reduce_fusion
  4.9 0.2 squeeze.36
  5.1 0.2 squeeze.37
  5.7 2.1 %collective-permute-start.2 = (f32[64,256]{1,0:T(8,128)S(1)}, f32[64,256]{1,0:T(8,128)S(1)}, u32[]{:S(2)}, u32[]{:S(2)}) collective-permute-start(f32[64,256]{1,0:T(8,128)S(1)} %reshape_squeeze.14.old_lo_y), channel_id=1, source_target_pairs={{0,1},{1,2},{2,3},{3,4},{4,5},{5,6},{6,7},{7,0},{8,9},{9,10},{10,1... | collective-permute-start | bytes 196616 | tf_op jit(solution)/shard_map/ppermute | solution.py:250
  8.1 3.1 %collective-permute-start.3 = (f32[64,256]{1,0:T(8,128)S(1)}, f32[64,256]{1,0:T(8,128)S(1)}, u32[]{:S(2)}, u32[]{:S(2)}) collective-permute-start(f32[64,256]{1,0:T(8,128)S(1)} %reshape_squeeze.15.old_hi_y), channel_id=1, source_target_pairs={{0,7},{1,0},{2,1},{3,2},{4,3},{5,4},{6,5},{7,6},{8,15},{9,8},{10,9... | collective-permute-start | bytes 196616 | tf_op jit(solution)/shard_map/ppermute | solution.py:251
  11.3 2.2 %collective-permute-start = (f32[64,128]{1,0:T(8,128)S(1)}, f32[64,128]{1,0:T(8,128)S(1)}, u32[]{:S(2)}, u32[]{:S(2)}) collective-permute-start(f32[64,128]{1,0:T(8,128)S(1)} %reshape_squeeze.12.old_lo_x), channel_id=1, source_target_pairs={{0,8},{8,16},{16,24},{24,0},{1,9},{9,17},{17,25},{25,1},{2,10},{10... | collective-permute-start | bytes 98312 | tf_op jit(solution)/shard_map/ppermute | solution.py:246
  13.7 0.3 broadcast_select_fusion.1
  14.0 0.2 pad_maximum_fusion
  14.3 0.2 copy.101
  14.5 0.3 reshape.157
  14.8 0.3 copy.102
  15.1 0.2 copy.103.a_ref
  15.3 17.5 %shard_map.82 = f32[64,1024]{1,0:T(8,128)S(1)} custom-call(f32[64,1024]{1,0:T(8,128)S(1)} %copy.103.a_ref), custom_call_target="tpu_custom_call", output_to_operand_aliasing={{}: (0, {})} | custom-call | flops 8388608000 | bytes 524288 | tf_op jit(solution)/shard_map/pallas_call | solution.py:75
  32.8 0.2 copy.104
  33.0 0.4 copy.105
  33.4 0.2 reshape.160
  33.6 0.6 copy-done.3
  34.4 0.2 copy.107
  34.7 0.2 copy.108
  35.5 0.4 copy-done.2
  36.1 0.2 copy.95
  36.4 1.0 shard_map.83
  37.5 4.1 %collective-permute-start.7 = (f32[64,256]{1,0:T(8,128)S(1)}, f32[64,256]{1,0:T(8,128)S(1)}, u32[]{:S(2)}, u32[]{:S(2)}) collective-permute-start(f32[64,256]{1,0:T(8,128)S(1)} %get-tuple-element.56.old_hi_y), channel_id=1, source_target_pairs={{0,7},{1,0},{2,1},{3,2},{4,3},{5,4},{6,5},{7,6},{8,15},{9,8},{10,9... | collective-permute-start | bytes 196616 | tf_op jit(solution)/shard_map/ppermute | solution.py:251
  41.7 2.3 %collective-permute-start.4 = (f32[64,128]{1,0:T(8,128)S(1)}, f32[64,128]{1,0:T(8,128)S(1)}, u32[]{:S(2)}, u32[]{:S(2)}) collective-permute-start(f32[64,128]{1,0:T(8,128)S(1)} %get-tuple-element.53.old_lo_x), channel_id=1, source_target_pairs={{0,8},{8,16},{16,24},{24,0},{1,9},{9,17},{17,25},{25,1},{2,10},{10... | collective-permute-start | bytes 98312 | tf_op jit(solution)/shard_map/ppermute | solution.py:246
  44.0 1.0 collective-permute-done.4.lo_x_ref
  45.0 2.3 %collective-permute-done.5.hi_x_ref = f32[64,128]{1,0:T(8,128)S(1)} collective-permute-done((f32[64,128]{1,0:T(8,128)S(1)}, f32[64,128]{1,0:T(8,128)S(1)}, u32[]{:S(2)}, u32[]{:S(2)}) %collective-permute-start.5) | collective-permute-done | bytes 32800 | tf_op jit(solution)/shard_map/ppermute | solution.py:247
  47.3 1.0 shard_map.84
  48.4 4.1 %collective-permute-start.11 = (f32[64,256]{1,0:T(8,128)S(1)}, f32[64,256]{1,0:T(8,128)S(1)}, u32[]{:S(2)}, u32[]{:S(2)}) collective-permute-start(f32[64,256]{1,0:T(8,128)S(1)} %get-tuple-element.64.old_hi_y), channel_id=1, source_target_pairs={{0,7},{1,0},{2,1},{3,2},{4,3},{5,4},{6,5},{7,6},{8,15},{9,8},{10,9... | collective-permute-start | bytes 196616 | tf_op jit(solution)/shard_map/ppermute | solution.py:251
  52.5 0.6 collective-permute-start.8
  53.1 1.0 collective-permute-done.8.lo_x_ref
  54.1 2.3 %collective-permute-done.9.hi_x_ref = f32[64,128]{1,0:T(8,128)S(1)} collective-permute-done((f32[64,128]{1,0:T(8,128)S(1)}, f32[64,128]{1,0:T(8,128)S(1)}, u32[]{:S(2)}, u32[]{:S(2)}) %collective-permute-start.9) | collective-permute-done | bytes 32800 | tf_op jit(solution)/shard_map/ppermute | solution.py:247
  56.4 1.0 shard_map.85
  57.5 4.1 %collective-permute-start.15 = (f32[64,256]{1,0:T(8,128)S(1)}, f32[64,256]{1,0:T(8,128)S(1)}, u32[]{:S(2)}, u32[]{:S(2)}) collective-permute-start(f32[64,256]{1,0:T(8,128)S(1)} %get-tuple-element.69.old_hi_y), channel_id=1, source_target_pairs={{0,7},{1,0},{2,1},{3,2},{4,3},{5,4},{6,5},{7,6},{8,15},{9,8},{10,9... | collective-permute-start | bytes 196616 | tf_op jit(solution)/shard_map/ppermute | solution.py:251
  61.7 0.6 collective-permute-start.12
  62.2 1.0 collective-permute-done.12.lo_x_ref
  63.3 2.3 %collective-permute-done.13.hi_x_ref = f32[64,128]{1,0:T(8,128)S(1)} collective-permute-done((f32[64,128]{1,0:T(8,128)S(1)}, f32[64,128]{1,0:T(8,128)S(1)}, u32[]{:S(2)}, u32[]{:S(2)}) %collective-permute-start.13) | collective-permute-done | bytes 32800 | tf_op jit(solution)/shard_map/ppermute | solution.py:247
  65.6 1.0 shard_map.86
  66.7 4.1 %collective-permute-start.19 = (f32[64,256]{1,0:T(8,128)S(1)}, f32[64,256]{1,0:T(8,128)S(1)}, u32[]{:S(2)}, u32[]{:S(2)}) collective-permute-start(f32[64,256]{1,0:T(8,128)S(1)} %get-tuple-element.74.old_hi_y), channel_id=1, source_target_pairs={{0,7},{1,0},{2,1},{3,2},{4,3},{5,4},{6,5},{7,6},{8,15},{9,8},{10,9... | collective-permute-start | bytes 196616 | tf_op jit(solution)/shard_map/ppermute | solution.py:251
  70.8 0.6 collective-permute-start.16
  71.4 1.0 collective-permute-done.16.lo_x_ref
  72.4 2.3 %collective-permute-done.17.hi_x_ref = f32[64,128]{1,0:T(8,128)S(1)} collective-permute-done((f32[64,128]{1,0:T(8,128)S(1)}, f32[64,128]{1,0:T(8,128)S(1)}, u32[]{:S(2)}, u32[]{:S(2)}) %collective-permute-start.17) | collective-permute-done | bytes 32800 | tf_op jit(solution)/shard_map/ppermute | solution.py:247
  74.7 1.0 shard_map.87
  75.8 4.1 %collective-permute-start.23 = (f32[64,256]{1,0:T(8,128)S(1)}, f32[64,256]{1,0:T(8,128)S(1)}, u32[]{:S(2)}, u32[]{:S(2)}) collective-permute-start(f32[64,256]{1,0:T(8,128)S(1)} %get-tuple-element.79.old_hi_y), channel_id=1, source_target_pairs={{0,7},{1,0},{2,1},{3,2},{4,3},{5,4},{6,5},{7,6},{8,15},{9,8},{10,9... | collective-permute-start | bytes 196616 | tf_op jit(solution)/shard_map/ppermute | solution.py:251
  79.9 0.6 collective-permute-start.20
  80.5 1.0 collective-permute-done.20.lo_x_ref
  81.5 2.3 %collective-permute-done.21.hi_x_ref = f32[64,128]{1,0:T(8,128)S(1)} collective-permute-done((f32[64,128]{1,0:T(8,128)S(1)}, f32[64,128]{1,0:T(8,128)S(1)}, u32[]{:S(2)}, u32[]{:S(2)}) %collective-permute-start.21) | collective-permute-done | bytes 32800 | tf_op jit(solution)/shard_map/ppermute | solution.py:247
  83.9 1.0 shard_map.88
  84.9 4.1 %collective-permute-start.27 = (f32[64,256]{1,0:T(8,128)S(1)}, f32[64,256]{1,0:T(8,128)S(1)}, u32[]{:S(2)}, u32[]{:S(2)}) collective-permute-start(f32[64,256]{1,0:T(8,128)S(1)} %get-tuple-element.84.old_hi_y), channel_id=1, source_target_pairs={{0,7},{1,0},{2,1},{3,2},{4,3},{5,4},{6,5},{7,6},{8,15},{9,8},{10,9... | collective-permute-start | bytes 196616 | tf_op jit(solution)/shard_map/ppermute | solution.py:251
  89.1 0.6 collective-permute-start.24
  89.7 1.0 collective-permute-done.24.lo_x_ref
  90.7 2.3 %collective-permute-done.25.hi_x_ref = f32[64,128]{1,0:T(8,128)S(1)} collective-permute-done((f32[64,128]{1,0:T(8,128)S(1)}, f32[64,128]{1,0:T(8,128)S(1)}, u32[]{:S(2)}, u32[]{:S(2)}) %collective-permute-start.25) | collective-permute-done | bytes 32800 | tf_op jit(solution)/shard_map/ppermute | solution.py:247
  93.0 1.0 shard_map.89
  94.1 4.1 %collective-permute-start.31 = (f32[64,256]{1,0:T(8,128)S(1)}, f32[64,256]{1,0:T(8,128)S(1)}, u32[]{:S(2)}, u32[]{:S(2)}) collective-permute-start(f32[64,256]{1,0:T(8,128)S(1)} %get-tuple-element.89.old_hi_y), channel_id=1, source_target_pairs={{0,7},{1,0},{2,1},{3,2},{4,3},{5,4},{6,5},{7,6},{8,15},{9,8},{10,9... | collective-permute-start | bytes 196616 | tf_op jit(solution)/shard_map/ppermute | solution.py:251
  98.2 0.6 collective-permute-start.28
  99.1 0.7 collective-permute-done.28.lo_x_ref
  99.8 2.3 %collective-permute-done.29.hi_x_ref = f32[64,128]{1,0:T(8,128)S(1)} collective-permute-done((f32[64,128]{1,0:T(8,128)S(1)}, f32[64,128]{1,0:T(8,128)S(1)}, u32[]{:S(2)}, u32[]{:S(2)}) %collective-permute-start.29) | collective-permute-done | bytes 32800 | tf_op jit(solution)/shard_map/ppermute | solution.py:247
  102.1 1.0 shard_map.90
  103.5 0.2 broadcast_select_fusion.4
  103.8 0.9 copy.114
  (84 shorter events, 3.8 us)
Async XLA Ops:
  0.0 0.7 slice-start
  3.2 1.0 copy-start
  5.7 30.7 %collective-permute-start.2 = (f32[64,256]{1,0:T(8,128)S(1)}, f32[64,256]{1,0:T(8,128)S(1)}, u32[]{:S(2)}, u32[]{:S(2)}) collective-permute-start(f32[64,256]{1,0:T(8,128)S(1)} %reshape_squeeze.14.old_lo_y), channel_id=1, source_target_pairs={{0,1},{1,2},{2,3},{3,4},{4,5},{5,6},{6,7},{7,0},{8,9},{9,10},{10,1... | collective-permute-start | bytes 196616 | tf_op jit(solution)/shard_map/ppermute | solution.py:250
  8.1 28.4 %collective-permute-start.3 = (f32[64,256]{1,0:T(8,128)S(1)}, f32[64,256]{1,0:T(8,128)S(1)}, u32[]{:S(2)}, u32[]{:S(2)}) collective-permute-start(f32[64,256]{1,0:T(8,128)S(1)} %reshape_squeeze.15.old_hi_y), channel_id=1, source_target_pairs={{0,7},{1,0},{2,1},{3,2},{4,3},{5,4},{6,5},{7,6},{8,15},{9,8},{10,9... | collective-permute-start | bytes 196616 | tf_op jit(solution)/shard_map/ppermute | solution.py:251
  11.2 2.6 %copy-start.1 = (f32[4,2,2,4096]{3,2,1,0:T(2,128)S(1)}, f32[4,2,2,4096]{3,2,1,0:T(2,128)}, u32[]{:S(2)}) copy-start(f32[4,2,2,4096]{3,2,1,0:T(2,128)} %param.10) | copy-start | bytes 786436
  11.3 25.1 %collective-permute-start = (f32[64,128]{1,0:T(8,128)S(1)}, f32[64,128]{1,0:T(8,128)S(1)}, u32[]{:S(2)}, u32[]{:S(2)}) collective-permute-start(f32[64,128]{1,0:T(8,128)S(1)} %reshape_squeeze.12.old_lo_x), channel_id=1, source_target_pairs={{0,8},{8,16},{16,24},{24,0},{1,9},{9,17},{17,25},{25,1},{2,10},{10... | collective-permute-start | bytes 98312 | tf_op jit(solution)/shard_map/ppermute | solution.py:246
  13.7 22.7 %collective-permute-start.1 = (f32[64,128]{1,0:T(8,128)S(1)}, f32[64,128]{1,0:T(8,128)S(1)}, u32[]{:S(2)}, u32[]{:S(2)}) collective-permute-start(f32[64,128]{1,0:T(8,128)S(1)} %reshape_squeeze.13.old_hi_x), channel_id=1, source_target_pairs={{0,24},{8,0},{16,8},{24,16},{1,25},{9,1},{17,9},{25,17},{2,26},{10... | collective-permute-start | bytes 98312 | tf_op jit(solution)/shard_map/ppermute | solution.py:247
  33.6 0.7 copy-start.3
  33.6 0.7 copy-start.4
  33.6 0.7 copy-start.5
  35.0 0.9 copy-start.2
  37.5 9.8 %collective-permute-start.6 = (f32[64,256]{1,0:T(8,128)S(1)}, f32[64,256]{1,0:T(8,128)S(1)}, u32[]{:S(2)}, u32[]{:S(2)}) collective-permute-start(f32[64,256]{1,0:T(8,128)S(1)} %get-tuple-element.55.old_lo_y), channel_id=1, source_target_pairs={{0,1},{1,2},{2,3},{3,4},{4,5},{5,6},{6,7},{7,0},{8,9},{9,10},{10,1... | collective-permute-start | bytes 196616 | tf_op jit(solution)/shard_map/ppermute | solution.py:250
  37.5 9.8 %collective-permute-start.7 = (f32[64,256]{1,0:T(8,128)S(1)}, f32[64,256]{1,0:T(8,128)S(1)}, u32[]{:S(2)}, u32[]{:S(2)}) collective-permute-start(f32[64,256]{1,0:T(8,128)S(1)} %get-tuple-element.56.old_hi_y), channel_id=1, source_target_pairs={{0,7},{1,0},{2,1},{3,2},{4,3},{5,4},{6,5},{7,6},{8,15},{9,8},{10,9... | collective-permute-start | bytes 196616 | tf_op jit(solution)/shard_map/ppermute | solution.py:251
  41.7 3.3 %collective-permute-start.4 = (f32[64,128]{1,0:T(8,128)S(1)}, f32[64,128]{1,0:T(8,128)S(1)}, u32[]{:S(2)}, u32[]{:S(2)}) collective-permute-start(f32[64,128]{1,0:T(8,128)S(1)} %get-tuple-element.53.old_lo_x), channel_id=1, source_target_pairs={{0,8},{8,16},{16,24},{24,0},{1,9},{9,17},{17,25},{25,1},{2,10},{10... | collective-permute-start | bytes 98312 | tf_op jit(solution)/shard_map/ppermute | solution.py:246
  44.0 3.3 %collective-permute-start.5 = (f32[64,128]{1,0:T(8,128)S(1)}, f32[64,128]{1,0:T(8,128)S(1)}, u32[]{:S(2)}, u32[]{:S(2)}) collective-permute-start(f32[64,128]{1,0:T(8,128)S(1)} %get-tuple-element.54.old_hi_x), channel_id=1, source_target_pairs={{0,24},{8,0},{16,8},{24,16},{1,25},{9,1},{17,9},{25,17},{2,26},{10... | collective-permute-start | bytes 98312 | tf_op jit(solution)/shard_map/ppermute | solution.py:247
  48.3 8.1 %collective-permute-start.10 = (f32[64,256]{1,0:T(8,128)S(1)}, f32[64,256]{1,0:T(8,128)S(1)}, u32[]{:S(2)}, u32[]{:S(2)}) collective-permute-start(f32[64,256]{1,0:T(8,128)S(1)} %get-tuple-element.63.old_lo_y), channel_id=1, source_target_pairs={{0,1},{1,2},{2,3},{3,4},{4,5},{5,6},{6,7},{7,0},{8,9},{9,10},{10,1... | collective-permute-start | bytes 196616 | tf_op jit(solution)/shard_map/ppermute | solution.py:250
  48.4 8.1 %collective-permute-start.11 = (f32[64,256]{1,0:T(8,128)S(1)}, f32[64,256]{1,0:T(8,128)S(1)}, u32[]{:S(2)}, u32[]{:S(2)}) collective-permute-start(f32[64,256]{1,0:T(8,128)S(1)} %get-tuple-element.64.old_hi_y), channel_id=1, source_target_pairs={{0,7},{1,0},{2,1},{3,2},{4,3},{5,4},{6,5},{7,6},{8,15},{9,8},{10,9... | collective-permute-start | bytes 196616 | tf_op jit(solution)/shard_map/ppermute | solution.py:251
  52.5 1.6 %collective-permute-start.8 = (f32[64,128]{1,0:T(8,128)S(1)}, f32[64,128]{1,0:T(8,128)S(1)}, u32[]{:S(2)}, u32[]{:S(2)}) collective-permute-start(f32[64,128]{1,0:T(8,128)S(1)} %get-tuple-element.61.old_lo_x), channel_id=1, source_target_pairs={{0,8},{8,16},{16,24},{24,0},{1,9},{9,17},{17,25},{25,1},{2,10},{10... | collective-permute-start | bytes 98312 | tf_op jit(solution)/shard_map/ppermute | solution.py:246
  53.1 3.3 %collective-permute-start.9 = (f32[64,128]{1,0:T(8,128)S(1)}, f32[64,128]{1,0:T(8,128)S(1)}, u32[]{:S(2)}, u32[]{:S(2)}) collective-permute-start(f32[64,128]{1,0:T(8,128)S(1)} %get-tuple-element.62.old_hi_x), channel_id=1, source_target_pairs={{0,24},{8,0},{16,8},{24,16},{1,25},{9,1},{17,9},{25,17},{2,26},{10... | collective-permute-start | bytes 98312 | tf_op jit(solution)/shard_map/ppermute | solution.py:247
  57.4 8.1 %collective-permute-start.14 = (f32[64,256]{1,0:T(8,128)S(1)}, f32[64,256]{1,0:T(8,128)S(1)}, u32[]{:S(2)}, u32[]{:S(2)}) collective-permute-start(f32[64,256]{1,0:T(8,128)S(1)} %get-tuple-element.68.old_lo_y), channel_id=1, source_target_pairs={{0,1},{1,2},{2,3},{3,4},{4,5},{5,6},{6,7},{7,0},{8,9},{9,10},{10,1... | collective-permute-start | bytes 196616 | tf_op jit(solution)/shard_map/ppermute | solution.py:250
  57.5 8.1 %collective-permute-start.15 = (f32[64,256]{1,0:T(8,128)S(1)}, f32[64,256]{1,0:T(8,128)S(1)}, u32[]{:S(2)}, u32[]{:S(2)}) collective-permute-start(f32[64,256]{1,0:T(8,128)S(1)} %get-tuple-element.69.old_hi_y), channel_id=1, source_target_pairs={{0,7},{1,0},{2,1},{3,2},{4,3},{5,4},{6,5},{7,6},{8,15},{9,8},{10,9... | collective-permute-start | bytes 196616 | tf_op jit(solution)/shard_map/ppermute | solution.py:251
  61.7 1.6 %collective-permute-start.12 = (f32[64,128]{1,0:T(8,128)S(1)}, f32[64,128]{1,0:T(8,128)S(1)}, u32[]{:S(2)}, u32[]{:S(2)}) collective-permute-start(f32[64,128]{1,0:T(8,128)S(1)} %get-tuple-element.66.old_lo_x), channel_id=1, source_target_pairs={{0,8},{8,16},{16,24},{24,0},{1,9},{9,17},{17,25},{25,1},{2,10},{10... | collective-permute-start | bytes 98312 | tf_op jit(solution)/shard_map/ppermute | solution.py:246
  62.2 3.3 %collective-permute-start.13 = (f32[64,128]{1,0:T(8,128)S(1)}, f32[64,128]{1,0:T(8,128)S(1)}, u32[]{:S(2)}, u32[]{:S(2)}) collective-permute-start(f32[64,128]{1,0:T(8,128)S(1)} %get-tuple-element.67.old_hi_x), channel_id=1, source_target_pairs={{0,24},{8,0},{16,8},{24,16},{1,25},{9,1},{17,9},{25,17},{2,26},{10... | collective-permute-start | bytes 98312 | tf_op jit(solution)/shard_map/ppermute | solution.py:247
  66.6 8.1 %collective-permute-start.18 = (f32[64,256]{1,0:T(8,128)S(1)}, f32[64,256]{1,0:T(8,128)S(1)}, u32[]{:S(2)}, u32[]{:S(2)}) collective-permute-start(f32[64,256]{1,0:T(8,128)S(1)} %get-tuple-element.73.old_lo_y), channel_id=1, source_target_pairs={{0,1},{1,2},{2,3},{3,4},{4,5},{5,6},{6,7},{7,0},{8,9},{9,10},{10,1... | collective-permute-start | bytes 196616 | tf_op jit(solution)/shard_map/ppermute | solution.py:250
  66.7 8.1 %collective-permute-start.19 = (f32[64,256]{1,0:T(8,128)S(1)}, f32[64,256]{1,0:T(8,128)S(1)}, u32[]{:S(2)}, u32[]{:S(2)}) collective-permute-start(f32[64,256]{1,0:T(8,128)S(1)} %get-tuple-element.74.old_hi_y), channel_id=1, source_target_pairs={{0,7},{1,0},{2,1},{3,2},{4,3},{5,4},{6,5},{7,6},{8,15},{9,8},{10,9... | collective-permute-start | bytes 196616 | tf_op jit(solution)/shard_map/ppermute | solution.py:251
  70.8 1.6 %collective-permute-start.16 = (f32[64,128]{1,0:T(8,128)S(1)}, f32[64,128]{1,0:T(8,128)S(1)}, u32[]{:S(2)}, u32[]{:S(2)}) collective-permute-start(f32[64,128]{1,0:T(8,128)S(1)} %get-tuple-element.71.old_lo_x), channel_id=1, source_target_pairs={{0,8},{8,16},{16,24},{24,0},{1,9},{9,17},{17,25},{25,1},{2,10},{10... | collective-permute-start | bytes 98312 | tf_op jit(solution)/shard_map/ppermute | solution.py:246
  71.4 3.3 %collective-permute-start.17 = (f32[64,128]{1,0:T(8,128)S(1)}, f32[64,128]{1,0:T(8,128)S(1)}, u32[]{:S(2)}, u32[]{:S(2)}) collective-permute-start(f32[64,128]{1,0:T(8,128)S(1)} %get-tuple-element.72.old_hi_x), channel_id=1, source_target_pairs={{0,24},{8,0},{16,8},{24,16},{1,25},{9,1},{17,9},{25,17},{2,26},{10... | collective-permute-start | bytes 98312 | tf_op jit(solution)/shard_map/ppermute | solution.py:247
  75.7 8.1 %collective-permute-start.22 = (f32[64,256]{1,0:T(8,128)S(1)}, f32[64,256]{1,0:T(8,128)S(1)}, u32[]{:S(2)}, u32[]{:S(2)}) collective-permute-start(f32[64,256]{1,0:T(8,128)S(1)} %get-tuple-element.78.old_lo_y), channel_id=1, source_target_pairs={{0,1},{1,2},{2,3},{3,4},{4,5},{5,6},{6,7},{7,0},{8,9},{9,10},{10,1... | collective-permute-start | bytes 196616 | tf_op jit(solution)/shard_map/ppermute | solution.py:250
  75.8 8.1 %collective-permute-start.23 = (f32[64,256]{1,0:T(8,128)S(1)}, f32[64,256]{1,0:T(8,128)S(1)}, u32[]{:S(2)}, u32[]{:S(2)}) collective-permute-start(f32[64,256]{1,0:T(8,128)S(1)} %get-tuple-element.79.old_hi_y), channel_id=1, source_target_pairs={{0,7},{1,0},{2,1},{3,2},{4,3},{5,4},{6,5},{7,6},{8,15},{9,8},{10,9... | collective-permute-start | bytes 196616 | tf_op jit(solution)/shard_map/ppermute | solution.py:251
  79.9 1.6 %collective-permute-start.20 = (f32[64,128]{1,0:T(8,128)S(1)}, f32[64,128]{1,0:T(8,128)S(1)}, u32[]{:S(2)}, u32[]{:S(2)}) collective-permute-start(f32[64,128]{1,0:T(8,128)S(1)} %get-tuple-element.76.old_lo_x), channel_id=1, source_target_pairs={{0,8},{8,16},{16,24},{24,0},{1,9},{9,17},{17,25},{25,1},{2,10},{10... | collective-permute-start | bytes 98312 | tf_op jit(solution)/shard_map/ppermute | solution.py:246
  80.5 3.3 %collective-permute-start.21 = (f32[64,128]{1,0:T(8,128)S(1)}, f32[64,128]{1,0:T(8,128)S(1)}, u32[]{:S(2)}, u32[]{:S(2)}) collective-permute-start(f32[64,128]{1,0:T(8,128)S(1)} %get-tuple-element.77.old_hi_x), channel_id=1, source_target_pairs={{0,24},{8,0},{16,8},{24,16},{1,25},{9,1},{17,9},{25,17},{2,26},{10... | collective-permute-start | bytes 98312 | tf_op jit(solution)/shard_map/ppermute | solution.py:247
  84.9 8.1 %collective-permute-start.26 = (f32[64,256]{1,0:T(8,128)S(1)}, f32[64,256]{1,0:T(8,128)S(1)}, u32[]{:S(2)}, u32[]{:S(2)}) collective-permute-start(f32[64,256]{1,0:T(8,128)S(1)} %get-tuple-element.83.old_lo_y), channel_id=1, source_target_pairs={{0,1},{1,2},{2,3},{3,4},{4,5},{5,6},{6,7},{7,0},{8,9},{9,10},{10,1... | collective-permute-start | bytes 196616 | tf_op jit(solution)/shard_map/ppermute | solution.py:250
  84.9 8.1 %collective-permute-start.27 = (f32[64,256]{1,0:T(8,128)S(1)}, f32[64,256]{1,0:T(8,128)S(1)}, u32[]{:S(2)}, u32[]{:S(2)}) collective-permute-start(f32[64,256]{1,0:T(8,128)S(1)} %get-tuple-element.84.old_hi_y), channel_id=1, source_target_pairs={{0,7},{1,0},{2,1},{3,2},{4,3},{5,4},{6,5},{7,6},{8,15},{9,8},{10,9... | collective-permute-start | bytes 196616 | tf_op jit(solution)/shard_map/ppermute | solution.py:251
  89.1 1.6 %collective-permute-start.24 = (f32[64,128]{1,0:T(8,128)S(1)}, f32[64,128]{1,0:T(8,128)S(1)}, u32[]{:S(2)}, u32[]{:S(2)}) collective-permute-start(f32[64,128]{1,0:T(8,128)S(1)} %get-tuple-element.81.old_lo_x), channel_id=1, source_target_pairs={{0,8},{8,16},{16,24},{24,0},{1,9},{9,17},{17,25},{25,1},{2,10},{10... | collective-permute-start | bytes 98312 | tf_op jit(solution)/shard_map/ppermute | solution.py:246
  89.6 3.3 %collective-permute-start.25 = (f32[64,128]{1,0:T(8,128)S(1)}, f32[64,128]{1,0:T(8,128)S(1)}, u32[]{:S(2)}, u32[]{:S(2)}) collective-permute-start(f32[64,128]{1,0:T(8,128)S(1)} %get-tuple-element.82.old_hi_x), channel_id=1, source_target_pairs={{0,24},{8,0},{16,8},{24,16},{1,25},{9,1},{17,9},{25,17},{2,26},{10... | collective-permute-start | bytes 98312 | tf_op jit(solution)/shard_map/ppermute | solution.py:247
  94.0 8.1 %collective-permute-start.30 = (f32[64,256]{1,0:T(8,128)S(1)}, f32[64,256]{1,0:T(8,128)S(1)}, u32[]{:S(2)}, u32[]{:S(2)}) collective-permute-start(f32[64,256]{1,0:T(8,128)S(1)} %get-tuple-element.88.old_lo_y), channel_id=1, source_target_pairs={{0,1},{1,2},{2,3},{3,4},{4,5},{5,6},{6,7},{7,0},{8,9},{9,10},{10,1... | collective-permute-start | bytes 196616 | tf_op jit(solution)/shard_map/ppermute | solution.py:250
  94.1 8.1 %collective-permute-start.31 = (f32[64,256]{1,0:T(8,128)S(1)}, f32[64,256]{1,0:T(8,128)S(1)}, u32[]{:S(2)}, u32[]{:S(2)}) collective-permute-start(f32[64,256]{1,0:T(8,128)S(1)} %get-tuple-element.89.old_hi_y), channel_id=1, source_target_pairs={{0,7},{1,0},{2,1},{3,2},{4,3},{5,4},{6,5},{7,6},{8,15},{9,8},{10,9... | collective-permute-start | bytes 196616 | tf_op jit(solution)/shard_map/ppermute | solution.py:251
  98.2 1.6 %collective-permute-start.28 = (f32[64,128]{1,0:T(8,128)S(1)}, f32[64,128]{1,0:T(8,128)S(1)}, u32[]{:S(2)}, u32[]{:S(2)}) collective-permute-start(f32[64,128]{1,0:T(8,128)S(1)} %get-tuple-element.86.old_lo_x), channel_id=1, source_target_pairs={{0,8},{8,16},{16,24},{24,0},{1,9},{9,17},{17,25},{25,1},{2,10},{10... | collective-permute-start | bytes 98312 | tf_op jit(solution)/shard_map/ppermute | solution.py:246
  98.8 3.3 %collective-permute-start.29 = (f32[64,128]{1,0:T(8,128)S(1)}, f32[64,128]{1,0:T(8,128)S(1)}, u32[]{:S(2)}, u32[]{:S(2)}) collective-permute-start(f32[64,128]{1,0:T(8,128)S(1)} %get-tuple-element.87.old_hi_x), channel_id=1, source_target_pairs={{0,24},{8,0},{16,8},{24,16},{1,25},{9,1},{17,9},{25,17},{2,26},{10... | collective-permute-start | bytes 98312 | tf_op jit(solution)/shard_map/ppermute | solution.py:247

commit v9 on v8

--- a/solution.py
+++ b/solution.py
@@ -307,14 +307,11 @@
                 first_sends if sends is None else sends,
                 span_x,
             )
-    first = first_is[0][..., None]
     whole = [
-        jnp.transpose(part.reshape(P_SIZE, columns, R), (1, 0, 2)).reshape(span_x, span_y, width)
+        jnp.transpose(part.reshape(P_SIZE, columns, R), (1, 0, 2)).reshape(span_x, span_y, 1, width)
         for part in state
     ]
-    return jnp.stack(
-        [jnp.where(first, whole[0], whole[1]), jnp.where(first, whole[1], whole[0])], axis=2
-    )
+    return jnp.where((colour == 0)[..., None], whole[0], whole[1])
 
 
 def dispatch(forcing, *rest):

time: 105 us -> 105 us (level)
    unnamed x16 -> x18, local copies, waits for them, and re-layouts: 2.15 us -> 2.16 us
where the time goes in v9:
time: 105 us; the launch traced here: 104 us
  starting transfers between devices  42.6 us (41%)
  Pallas kernels  25.5 us (24%)
  waiting for transfers between devices  23 us (22%)
  local copies, waits for them, and re-layouts  11.2 us (11%)
  other arithmetic  1.65 us (2%)
    ppermute x8, starting transfers between devices, trade(): lax.ppermute(sends[3], 'gy', shift_pairs('gy', -1))  32.1 us
    pallas_call x1, Pallas kernels, block_inverses(): pl.pallas_call(functools.partial(_gauss_jordan_kernel, n=n, nb=nb), out_s...  17.5 us
    ppermute x8, waiting for transfers between devices, trade(): lax.ppermute(sends[1], 'gx', shift_pairs('gx', -1))  16.2 us
    pallas_call x8, Pallas kernels, half_sweep(): pl.pallas_call(functools.partial(_half_sweep_kernel, span_x=span_x), out_...  7.98 us
    ppermute x8, starting transfers between devices, trade(): lax.ppermute(sends[0], 'gx', shift_pairs('gx', 1))  7.91 us
    ppermute x8, waiting for transfers between devices, trade(): lax.ppermute(sends[0], 'gx', shift_pairs('gx', 1))  6.7 us
    slice x3, local copies, waits for them, and re-layouts, pick(): high = lax.index_in_dim(values, 1, axis=axis, keepdims=False)  2.68 us
    ppermute x8, starting transfers between devices, trade(): lax.ppermute(sends[2], 'gy', shift_pairs('gy', 1))  2.51 us
  transfers between devices with their start and end apart: 32, of which 14 were waited for; matrix products, arithmetic and copies ran while one was open for 5% of the time, Pallas kernels for 17%

profile of v9, /device:TPU:1, one launch (start us, length us, event | category | flops | bytes accessed | tf_op | source)
XLA Modules:
  0.0 104.4 jit_solution(7588474021357118795)
XLA Ops:
  0.0 0.7 slice-done
  1.1 1.9 %slice_reduce_fusion.2 = (f32[4,2,4096]{2,1,0:T(2,128)S(1)}, f32[4,2,4096]{2,1,0:T(2,128)S(1)}) fusion(f32[4,2,2,4096]{3,2,1,0:T(2,128)} %param.9), kind=kLoop, calls=%fused_computation.10 | loop fusion | bytes 524288 | tf_op jit(solution)/shard_map/slice | solution.py:272
  3.0 0.2 squeeze.32
  3.2 0.2 squeeze.33
  3.4 0.7 copy-done
  4.1 0.8 slice_reduce_fusion
  4.9 0.2 squeeze.36
  5.1 0.2 squeeze.37
  5.7 2.1 %collective-permute-start.2 = (f32[64,256]{1,0:T(8,128)S(1)}, f32[64,256]{1,0:T(8,128)S(1)}, u32[]{:S(2)}, u32[]{:S(2)}) collective-permute-start(f32[64,256]{1,0:T(8,128)S(1)} %reshape_squeeze.14.old_lo_y), channel_id=1, source_target_pairs={{0,1},{1,2},{2,3},{3,4},{4,5},{5,6},{6,7},{7,0},{8,9},{9,10},{10,1... | collective-permute-start | bytes 196616 | tf_op jit(solution)/shard_map/ppermute | solution.py:250
  8.1 3.1 %collective-permute-start.3 = (f32[64,256]{1,0:T(8,128)S(1)}, f32[64,256]{1,0:T(8,128)S(1)}, u32[]{:S(2)}, u32[]{:S(2)}) collective-permute-start(f32[64,256]{1,0:T(8,128)S(1)} %reshape_squeeze.15.old_hi_y), channel_id=1, source_target_pairs={{0,7},{1,0},{2,1},{3,2},{4,3},{5,4},{6,5},{7,6},{8,15},{9,8},{10,9... | collective-permute-start | bytes 196616 | tf_op jit(solution)/shard_map/ppermute | solution.py:251
  11.3 2.2 %collective-permute-start = (f32[64,128]{1,0:T(8,128)S(1)}, f32[64,128]{1,0:T(8,128)S(1)}, u32[]{:S(2)}, u32[]{:S(2)}) collective-permute-start(f32[64,128]{1,0:T(8,128)S(1)} %reshape_squeeze.12.old_lo_x), channel_id=1, source_target_pairs={{0,8},{8,16},{16,24},{24,0},{1,9},{9,17},{17,25},{25,1},{2,10},{10... | collective-permute-start | bytes 98312 | tf_op jit(solution)/shard_map/ppermute | solution.py:246
  13.7 0.3 broadcast_select_fusion.1
  14.1 0.2 pad_maximum_fusion
  14.3 0.2 copy.101
  14.5 0.3 reshape.122
  14.8 0.3 copy.102
  15.1 0.2 copy.103.a_ref
  15.3 17.5 %shard_map.82 = f32[64,1024]{1,0:T(8,128)S(1)} custom-call(f32[64,1024]{1,0:T(8,128)S(1)} %copy.103.a_ref), custom_call_target="tpu_custom_call", output_to_operand_aliasing={{}: (0, {})} | custom-call | flops 8388608000 | bytes 524288 | tf_op jit(solution)/shard_map/pallas_call | solution.py:75
  32.8 0.2 copy.104
  33.0 0.4 copy.105
  33.4 0.2 reshape.125
  33.6 0.6 copy-done.3
  34.4 0.2 copy.107
  34.7 0.2 copy.108
  35.5 0.4 copy-done.2
  36.1 0.2 copy.94
  36.4 1.0 shard_map.83
  37.5 4.1 %collective-permute-start.7 = (f32[64,256]{1,0:T(8,128)S(1)}, f32[64,256]{1,0:T(8,128)S(1)}, u32[]{:S(2)}, u32[]{:S(2)}) collective-permute-start(f32[64,256]{1,0:T(8,128)S(1)} %get-tuple-element.56.old_hi_y), channel_id=1, source_target_pairs={{0,7},{1,0},{2,1},{3,2},{4,3},{5,4},{6,5},{7,6},{8,15},{9,8},{10,9... | collective-permute-start | bytes 196616 | tf_op jit(solution)/shard_map/ppermute | solution.py:251
  41.7 2.3 %collective-permute-start.4 = (f32[64,128]{1,0:T(8,128)S(1)}, f32[64,128]{1,0:T(8,128)S(1)}, u32[]{:S(2)}, u32[]{:S(2)}) collective-permute-start(f32[64,128]{1,0:T(8,128)S(1)} %get-tuple-element.53.old_lo_x), channel_id=1, source_target_pairs={{0,8},{8,16},{16,24},{24,0},{1,9},{9,17},{17,25},{25,1},{2,10},{10... | collective-permute-start | bytes 98312 | tf_op jit(solution)/shard_map/ppermute | solution.py:246
  44.0 1.0 collective-permute-done.4.lo_x_ref
  45.0 2.3 %collective-permute-done.5.hi_x_ref = f32[64,128]{1,0:T(8,128)S(1)} collective-permute-done((f32[64,128]{1,0:T(8,128)S(1)}, f32[64,128]{1,0:T(8,128)S(1)}, u32[]{:S(2)}, u32[]{:S(2)}) %collective-permute-start.5) | collective-permute-done | bytes 32800 | tf_op jit(solution)/shard_map/ppermute | solution.py:247
  47.3 1.0 shard_map.84
  48.4 4.1 %collective-permute-start.11 = (f32[64,256]{1,0:T(8,128)S(1)}, f32[64,256]{1,0:T(8,128)S(1)}, u32[]{:S(2)}, u32[]{:S(2)}) collective-permute-start(f32[64,256]{1,0:T(8,128)S(1)} %get-tuple-element.64.old_hi_y), channel_id=1, source_target_pairs={{0,7},{1,0},{2,1},{3,2},{4,3},{5,4},{6,5},{7,6},{8,15},{9,8},{10,9... | collective-permute-start | bytes 196616 | tf_op jit(solution)/shard_map/ppermute | solution.py:251
  52.5 0.6 collective-permute-start.8
  53.1 1.0 collective-permute-done.8.lo_x_ref
  54.1 2.3 %collective-permute-done.9.hi_x_ref = f32[64,128]{1,0:T(8,128)S(1)} collective-permute-done((f32[64,128]{1,0:T(8,128)S(1)}, f32[64,128]{1,0:T(8,128)S(1)}, u32[]{:S(2)}, u32[]{:S(2)}) %collective-permute-start.9) | collective-permute-done | bytes 32800 | tf_op jit(solution)/shard_map/ppermute | solution.py:247
  56.4 1.0 shard_map.85
  57.5 4.1 %collective-permute-start.15 = (f32[64,256]{1,0:T(8,128)S(1)}, f32[64,256]{1,0:T(8,128)S(1)}, u32[]{:S(2)}, u32[]{:S(2)}) collective-permute-start(f32[64,256]{1,0:T(8,128)S(1)} %get-tuple-element.69.old_hi_y), channel_id=1, source_target_pairs={{0,7},{1,0},{2,1},{3,2},{4,3},{5,4},{6,5},{7,6},{8,15},{9,8},{10,9... | collective-permute-start | bytes 196616 | tf_op jit(solution)/shard_map/ppermute | solution.py:251
  61.7 0.6 collective-permute-start.12
  62.2 1.0 collective-permute-done.12.lo_x_ref
  63.3 2.3 %collective-permute-done.13.hi_x_ref = f32[64,128]{1,0:T(8,128)S(1)} collective-permute-done((f32[64,128]{1,0:T(8,128)S(1)}, f32[64,128]{1,0:T(8,128)S(1)}, u32[]{:S(2)}, u32[]{:S(2)}) %collective-permute-start.13) | collective-permute-done | bytes 32800 | tf_op jit(solution)/shard_map/ppermute | solution.py:247
  65.6 1.0 shard_map.86
  66.7 4.1 %collective-permute-start.19 = (f32[64,256]{1,0:T(8,128)S(1)}, f32[64,256]{1,0:T(8,128)S(1)}, u32[]{:S(2)}, u32[]{:S(2)}) collective-permute-start(f32[64,256]{1,0:T(8,128)S(1)} %get-tuple-element.74.old_hi_y), channel_id=1, source_target_pairs={{0,7},{1,0},{2,1},{3,2},{4,3},{5,4},{6,5},{7,6},{8,15},{9,8},{10,9... | collective-permute-start | bytes 196616 | tf_op jit(solution)/shard_map/ppermute | solution.py:251
  70.8 0.6 collective-permute-start.16
  71.4 1.0 collective-permute-done.16.lo_x_ref
  72.4 2.3 %collective-permute-done.17.hi_x_ref = f32[64,128]{1,0:T(8,128)S(1)} collective-permute-done((f32[64,128]{1,0:T(8,128)S(1)}, f32[64,128]{1,0:T(8,128)S(1)}, u32[]{:S(2)}, u32[]{:S(2)}) %collective-permute-start.17) | collective-permute-done | bytes 32800 | tf_op jit(solution)/shard_map/ppermute | solution.py:247
  74.7 1.0 shard_map.87
  75.8 4.1 %collective-permute-start.23 = (f32[64,256]{1,0:T(8,128)S(1)}, f32[64,256]{1,0:T(8,128)S(1)}, u32[]{:S(2)}, u32[]{:S(2)}) collective-permute-start(f32[64,256]{1,0:T(8,128)S(1)} %get-tuple-element.79.old_hi_y), channel_id=1, source_target_pairs={{0,7},{1,0},{2,1},{3,2},{4,3},{5,4},{6,5},{7,6},{8,15},{9,8},{10,9... | collective-permute-start | bytes 196616 | tf_op jit(solution)/shard_map/ppermute | solution.py:251
  79.9 0.6 collective-permute-start.20
  80.5 1.0 collective-permute-done.20.lo_x_ref
  81.5 2.3 %collective-permute-done.21.hi_x_ref = f32[64,128]{1,0:T(8,128)S(1)} collective-permute-done((f32[64,128]{1,0:T(8,128)S(1)}, f32[64,128]{1,0:T(8,128)S(1)}, u32[]{:S(2)}, u32[]{:S(2)}) %collective-permute-start.21) | collective-permute-done | bytes 32800 | tf_op jit(solution)/shard_map/ppermute | solution.py:247
  83.9 1.0 shard_map.88
  84.9 4.1 %collective-permute-start.27 = (f32[64,256]{1,0:T(8,128)S(1)}, f32[64,256]{1,0:T(8,128)S(1)}, u32[]{:S(2)}, u32[]{:S(2)}) collective-permute-start(f32[64,256]{1,0:T(8,128)S(1)} %get-tuple-element.84.old_hi_y), channel_id=1, source_target_pairs={{0,7},{1,0},{2,1},{3,2},{4,3},{5,4},{6,5},{7,6},{8,15},{9,8},{10,9... | collective-permute-start | bytes 196616 | tf_op jit(solution)/shard_map/ppermute | solution.py:251
  89.1 0.6 collective-permute-start.24
  89.7 1.0 collective-permute-done.24.lo_x_ref
  90.7 2.3 %collective-permute-done.25.hi_x_ref = f32[64,128]{1,0:T(8,128)S(1)} collective-permute-done((f32[64,128]{1,0:T(8,128)S(1)}, f32[64,128]{1,0:T(8,128)S(1)}, u32[]{:S(2)}, u32[]{:S(2)}) %collective-permute-start.25) | collective-permute-done | bytes 32800 | tf_op jit(solution)/shard_map/ppermute | solution.py:247
  93.0 1.0 shard_map.89
  94.1 4.1 %collective-permute-start.31 = (f32[64,256]{1,0:T(8,128)S(1)}, f32[64,256]{1,0:T(8,128)S(1)}, u32[]{:S(2)}, u32[]{:S(2)}) collective-permute-start(f32[64,256]{1,0:T(8,128)S(1)} %get-tuple-element.89.old_hi_y), channel_id=1, source_target_pairs={{0,7},{1,0},{2,1},{3,2},{4,3},{5,4},{6,5},{7,6},{8,15},{9,8},{10,9... | collective-permute-start | bytes 196616 | tf_op jit(solution)/shard_map/ppermute | solution.py:251
  98.2 0.6 collective-permute-start.28
  99.1 0.1 broadcast_in_dim.104
  99.2 0.6 collective-permute-done.28.lo_x_ref
  99.8 2.3 %collective-permute-done.29.hi_x_ref = f32[64,128]{1,0:T(8,128)S(1)} collective-permute-done((f32[64,128]{1,0:T(8,128)S(1)}, f32[64,128]{1,0:T(8,128)S(1)}, u32[]{:S(2)}, u32[]{:S(2)}) %collective-permute-start.29) | collective-permute-done | bytes 32800 | tf_op jit(solution)/shard_map/ppermute | solution.py:247
  102.1 1.0 shard_map.90
  103.5 0.9 broadcast_select_fusion.2
  (86 shorter events, 3.6 us)
Async XLA Ops:
  0.0 0.7 slice-start
  3.2 1.0 copy-start
  5.7 30.7 %collective-permute-start.2 = (f32[64,256]{1,0:T(8,128)S(1)}, f32[64,256]{1,0:T(8,128)S(1)}, u32[]{:S(2)}, u32[]{:S(2)}) collective-permute-start(f32[64,256]{1,0:T(8,128)S(1)} %reshape_squeeze.14.old_lo_y), channel_id=1, source_target_pairs={{0,1},{1,2},{2,3},{3,4},{4,5},{5,6},{6,7},{7,0},{8,9},{9,10},{10,1... | collective-permute-start | bytes 196616 | tf_op jit(solution)/shard_map/ppermute | solution.py:250
  8.1 28.4 %collective-permute-start.3 = (f32[64,256]{1,0:T(8,128)S(1)}, f32[64,256]{1,0:T(8,128)S(1)}, u32[]{:S(2)}, u32[]{:S(2)}) collective-permute-start(f32[64,256]{1,0:T(8,128)S(1)} %reshape_squeeze.15.old_hi_y), channel_id=1, source_target_pairs={{0,7},{1,0},{2,1},{3,2},{4,3},{5,4},{6,5},{7,6},{8,15},{9,8},{10,9... | collective-permute-start | bytes 196616 | tf_op jit(solution)/shard_map/ppermute | solution.py:251
  11.2 2.6 %copy-start.1 = (f32[4,2,2,4096]{3,2,1,0:T(2,128)S(1)}, f32[4,2,2,4096]{3,2,1,0:T(2,128)}, u32[]{:S(2)}) copy-start(f32[4,2,2,4096]{3,2,1,0:T(2,128)} %param.10) | copy-start | bytes 786436
  11.3 25.1 %collective-permute-start = (f32[64,128]{1,0:T(8,128)S(1)}, f32[64,128]{1,0:T(8,128)S(1)}, u32[]{:S(2)}, u32[]{:S(2)}) collective-permute-start(f32[64,128]{1,0:T(8,128)S(1)} %reshape_squeeze.12.old_lo_x), channel_id=1, source_target_pairs={{0,8},{8,16},{16,24},{24,0},{1,9},{9,17},{17,25},{25,1},{2,10},{10... | collective-permute-start | bytes 98312 | tf_op jit(solution)/shard_map/ppermute | solution.py:246
  13.7 22.7 %collective-permute-start.1 = (f32[64,128]{1,0:T(8,128)S(1)}, f32[64,128]{1,0:T(8,128)S(1)}, u32[]{:S(2)}, u32[]{:S(2)}) collective-permute-start(f32[64,128]{1,0:T(8,128)S(1)} %reshape_squeeze.13.old_hi_x), channel_id=1, source_target_pairs={{0,24},{8,0},{16,8},{24,16},{1,25},{9,1},{17,9},{25,17},{2,26},{10... | collective-permute-start | bytes 98312 | tf_op jit(solution)/shard_map/ppermute | solution.py:247
  33.6 0.7 copy-start.3
  33.6 0.7 copy-start.4
  33.6 0.7 copy-start.5
  35.0 0.9 copy-start.2
  37.5 9.8 %collective-permute-start.6 = (f32[64,256]{1,0:T(8,128)S(1)}, f32[64,256]{1,0:T(8,128)S(1)}, u32[]{:S(2)}, u32[]{:S(2)}) collective-permute-start(f32[64,256]{1,0:T(8,128)S(1)} %get-tuple-element.55.old_lo_y), channel_id=1, source_target_pairs={{0,1},{1,2},{2,3},{3,4},{4,5},{5,6},{6,7},{7,0},{8,9},{9,10},{10,1... | collective-permute-start | bytes 196616 | tf_op jit(solution)/shard_map/ppermute | solution.py:250
  37.5 9.8 %collective-permute-start.7 = (f32[64,256]{1,0:T(8,128)S(1)}, f32[64,256]{1,0:T(8,128)S(1)}, u32[]{:S(2)}, u32[]{:S(2)}) collective-permute-start(f32[64,256]{1,0:T(8,128)S(1)} %get-tuple-element.56.old_hi_y), channel_id=1, source_target_pairs={{0,7},{1,0},{2,1},{3,2},{4,3},{5,4},{6,5},{7,6},{8,15},{9,8},{10,9... | collective-permute-start | bytes 196616 | tf_op jit(solution)/shard_map/ppermute | solution.py:251
  41.7 3.3 %collective-permute-start.4 = (f32[64,128]{1,0:T(8,128)S(1)}, f32[64,128]{1,0:T(8,128)S(1)}, u32[]{:S(2)}, u32[]{:S(2)}) collective-permute-start(f32[64,128]{1,0:T(8,128)S(1)} %get-tuple-element.53.old_lo_x), channel_id=1, source_target_pairs={{0,8},{8,16},{16,24},{24,0},{1,9},{9,17},{17,25},{25,1},{2,10},{10... | collective-permute-start | bytes 98312 | tf_op jit(solution)/shard_map/ppermute | solution.py:246
  44.0 3.3 %collective-permute-start.5 = (f32[64,128]{1,0:T(8,128)S(1)}, f32[64,128]{1,0:T(8,128)S(1)}, u32[]{:S(2)}, u32[]{:S(2)}) collective-permute-start(f32[64,128]{1,0:T(8,128)S(1)} %get-tuple-element.54.old_hi_x), channel_id=1, source_target_pairs={{0,24},{8,0},{16,8},{24,16},{1,25},{9,1},{17,9},{25,17},{2,26},{10... | collective-permute-start | bytes 98312 | tf_op jit(solution)/shard_map/ppermute | solution.py:247
  48.3 8.1 %collective-permute-start.10 = (f32[64,256]{1,0:T(8,128)S(1)}, f32[64,256]{1,0:T(8,128)S(1)}, u32[]{:S(2)}, u32[]{:S(2)}) collective-permute-start(f32[64,256]{1,0:T(8,128)S(1)} %get-tuple-element.63.old_lo_y), channel_id=1, source_target_pairs={{0,1},{1,2},{2,3},{3,4},{4,5},{5,6},{6,7},{7,0},{8,9},{9,10},{10,1... | collective-permute-start | bytes 196616 | tf_op jit(solution)/shard_map/ppermute | solution.py:250
  48.4 8.1 %collective-permute-start.11 = (f32[64,256]{1,0:T(8,128)S(1)}, f32[64,256]{1,0:T(8,128)S(1)}, u32[]{:S(2)}, u32[]{:S(2)}) collective-permute-start(f32[64,256]{1,0:T(8,128)S(1)} %get-tuple-element.64.old_hi_y), channel_id=1, source_target_pairs={{0,7},{1,0},{2,1},{3,2},{4,3},{5,4},{6,5},{7,6},{8,15},{9,8},{10,9... | collective-permute-start | bytes 196616 | tf_op jit(solution)/shard_map/ppermute | solution.py:251
  52.5 1.6 %collective-permute-start.8 = (f32[64,128]{1,0:T(8,128)S(1)}, f32[64,128]{1,0:T(8,128)S(1)}, u32[]{:S(2)}, u32[]{:S(2)}) collective-permute-start(f32[64,128]{1,0:T(8,128)S(1)} %get-tuple-element.61.old_lo_x), channel_id=1, source_target_pairs={{0,8},{8,16},{16,24},{24,0},{1,9},{9,17},{17,25},{25,1},{2,10},{10... | collective-permute-start | bytes 98312 | tf_op jit(solution)/shard_map/ppermute | solution.py:246
  53.1 3.3 %collective-permute-start.9 = (f32[64,128]{1,0:T(8,128)S(1)}, f32[64,128]{1,0:T(8,128)S(1)}, u32[]{:S(2)}, u32[]{:S(2)}) collective-permute-start(f32[64,128]{1,0:T(8,128)S(1)} %get-tuple-element.62.old_hi_x), channel_id=1, source_target_pairs={{0,24},{8,0},{16,8},{24,16},{1,25},{9,1},{17,9},{25,17},{2,26},{10... | collective-permute-start | bytes 98312 | tf_op jit(solution)/shard_map/ppermute | solution.py:247
  57.4 8.1 %collective-permute-start.14 = (f32[64,256]{1,0:T(8,128)S(1)}, f32[64,256]{1,0:T(8,128)S(1)}, u32[]{:S(2)}, u32[]{:S(2)}) collective-permute-start(f32[64,256]{1,0:T(8,128)S(1)} %get-tuple-element.68.old_lo_y), channel_id=1, source_target_pairs={{0,1},{1,2},{2,3},{3,4},{4,5},{5,6},{6,7},{7,0},{8,9},{9,10},{10,1... | collective-permute-start | bytes 196616 | tf_op jit(solution)/shard_map/ppermute | solution.py:250
  57.5 8.1 %collective-permute-start.15 = (f32[64,256]{1,0:T(8,128)S(1)}, f32[64,256]{1,0:T(8,128)S(1)}, u32[]{:S(2)}, u32[]{:S(2)}) collective-permute-start(f32[64,256]{1,0:T(8,128)S(1)} %get-tuple-element.69.old_hi_y), channel_id=1, source_target_pairs={{0,7},{1,0},{2,1},{3,2},{4,3},{5,4},{6,5},{7,6},{8,15},{9,8},{10,9... | collective-permute-start | bytes 196616 | tf_op jit(solution)/shard_map/ppermute | solution.py:251
  61.7 1.6 %collective-permute-start.12 = (f32[64,128]{1,0:T(8,128)S(1)}, f32[64,128]{1,0:T(8,128)S(1)}, u32[]{:S(2)}, u32[]{:S(2)}) collective-permute-start(f32[64,128]{1,0:T(8,128)S(1)} %get-tuple-element.66.old_lo_x), channel_id=1, source_target_pairs={{0,8},{8,16},{16,24},{24,0},{1,9},{9,17},{17,25},{25,1},{2,10},{10... | collective-permute-start | bytes 98312 | tf_op jit(solution)/shard_map/ppermute | solution.py:246
  62.2 3.3 %collective-permute-start.13 = (f32[64,128]{1,0:T(8,128)S(1)}, f32[64,128]{1,0:T(8,128)S(1)}, u32[]{:S(2)}, u32[]{:S(2)}) collective-permute-start(f32[64,128]{1,0:T(8,128)S(1)} %get-tuple-element.67.old_hi_x), channel_id=1, source_target_pairs={{0,24},{8,0},{16,8},{24,16},{1,25},{9,1},{17,9},{25,17},{2,26},{10... | collective-permute-start | bytes 98312 | tf_op jit(solution)/shard_map/ppermute | solution.py:247
  66.6 8.1 %collective-permute-start.18 = (f32[64,256]{1,0:T(8,128)S(1)}, f32[64,256]{1,0:T(8,128)S(1)}, u32[]{:S(2)}, u32[]{:S(2)}) collective-permute-start(f32[64,256]{1,0:T(8,128)S(1)} %get-tuple-element.73.old_lo_y), channel_id=1, source_target_pairs={{0,1},{1,2},{2,3},{3,4},{4,5},{5,6},{6,7},{7,0},{8,9},{9,10},{10,1... | collective-permute-start | bytes 196616 | tf_op jit(solution)/shard_map/ppermute | solution.py:250
  66.7 8.1 %collective-permute-start.19 = (f32[64,256]{1,0:T(8,128)S(1)}, f32[64,256]{1,0:T(8,128)S(1)}, u32[]{:S(2)}, u32[]{:S(2)}) collective-permute-start(f32[64,256]{1,0:T(8,128)S(1)} %get-tuple-element.74.old_hi_y), channel_id=1, source_target_pairs={{0,7},{1,0},{2,1},{3,2},{4,3},{5,4},{6,5},{7,6},{8,15},{9,8},{10,9... | collective-permute-start | bytes 196616 | tf_op jit(solution)/shard_map/ppermute | solution.py:251
  70.8 1.6 %collective-permute-start.16 = (f32[64,128]{1,0:T(8,128)S(1)}, f32[64,128]{1,0:T(8,128)S(1)}, u32[]{:S(2)}, u32[]{:S(2)}) collective-permute-start(f32[64,128]{1,0:T(8,128)S(1)} %get-tuple-element.71.old_lo_x), channel_id=1, source_target_pairs={{0,8},{8,16},{16,24},{24,0},{1,9},{9,17},{17,25},{25,1},{2,10},{10... | collective-permute-start | bytes 98312 | tf_op jit(solution)/shard_map/ppermute | solution.py:246
  71.4 3.3 %collective-permute-start.17 = (f32[64,128]{1,0:T(8,128)S(1)}, f32[64,128]{1,0:T(8,128)S(1)}, u32[]{:S(2)}, u32[]{:S(2)}) collective-permute-start(f32[64,128]{1,0:T(8,128)S(1)} %get-tuple-element.72.old_hi_x), channel_id=1, source_target_pairs={{0,24},{8,0},{16,8},{24,16},{1,25},{9,1},{17,9},{25,17},{2,26},{10... | collective-permute-start | bytes 98312 | tf_op jit(solution)/shard_map/ppermute | solution.py:247
  75.7 8.1 %collective-permute-start.22 = (f32[64,256]{1,0:T(8,128)S(1)}, f32[64,256]{1,0:T(8,128)S(1)}, u32[]{:S(2)}, u32[]{:S(2)}) collective-permute-start(f32[64,256]{1,0:T(8,128)S(1)} %get-tuple-element.78.old_lo_y), channel_id=1, source_target_pairs={{0,1},{1,2},{2,3},{3,4},{4,5},{5,6},{6,7},{7,0},{8,9},{9,10},{10,1... | collective-permute-start | bytes 196616 | tf_op jit(solution)/shard_map/ppermute | solution.py:250
  75.8 8.1 %collective-permute-start.23 = (f32[64,256]{1,0:T(8,128)S(1)}, f32[64,256]{1,0:T(8,128)S(1)}, u32[]{:S(2)}, u32[]{:S(2)}) collective-permute-start(f32[64,256]{1,0:T(8,128)S(1)} %get-tuple-element.79.old_hi_y), channel_id=1, source_target_pairs={{0,7},{1,0},{2,1},{3,2},{4,3},{5,4},{6,5},{7,6},{8,15},{9,8},{10,9... | collective-permute-start | bytes 196616 | tf_op jit(solution)/shard_map/ppermute | solution.py:251
  79.9 1.6 %collective-permute-start.20 = (f32[64,128]{1,0:T(8,128)S(1)}, f32[64,128]{1,0:T(8,128)S(1)}, u32[]{:S(2)}, u32[]{:S(2)}) collective-permute-start(f32[64,128]{1,0:T(8,128)S(1)} %get-tuple-element.76.old_lo_x), channel_id=1, source_target_pairs={{0,8},{8,16},{16,24},{24,0},{1,9},{9,17},{17,25},{25,1},{2,10},{10... | collective-permute-start | bytes 98312 | tf_op jit(solution)/shard_map/ppermute | solution.py:246
  80.5 3.3 %collective-permute-start.21 = (f32[64,128]{1,0:T(8,128)S(1)}, f32[64,128]{1,0:T(8,128)S(1)}, u32[]{:S(2)}, u32[]{:S(2)}) collective-permute-start(f32[64,128]{1,0:T(8,128)S(1)} %get-tuple-element.77.old_hi_x), channel_id=1, source_target_pairs={{0,24},{8,0},{16,8},{24,16},{1,25},{9,1},{17,9},{25,17},{2,26},{10... | collective-permute-start | bytes 98312 | tf_op jit(solution)/shard_map/ppermute | solution.py:247
  84.9 8.1 %collective-permute-start.26 = (f32[64,256]{1,0:T(8,128)S(1)}, f32[64,256]{1,0:T(8,128)S(1)}, u32[]{:S(2)}, u32[]{:S(2)}) collective-permute-start(f32[64,256]{1,0:T(8,128)S(1)} %get-tuple-element.83.old_lo_y), channel_id=1, source_target_pairs={{0,1},{1,2},{2,3},{3,4},{4,5},{5,6},{6,7},{7,0},{8,9},{9,10},{10,1... | collective-permute-start | bytes 196616 | tf_op jit(solution)/shard_map/ppermute | solution.py:250
  84.9 8.1 %collective-permute-start.27 = (f32[64,256]{1,0:T(8,128)S(1)}, f32[64,256]{1,0:T(8,128)S(1)}, u32[]{:S(2)}, u32[]{:S(2)}) collective-permute-start(f32[64,256]{1,0:T(8,128)S(1)} %get-tuple-element.84.old_hi_y), channel_id=1, source_target_pairs={{0,7},{1,0},{2,1},{3,2},{4,3},{5,4},{6,5},{7,6},{8,15},{9,8},{10,9... | collective-permute-start | bytes 196616 | tf_op jit(solution)/shard_map/ppermute | solution.py:251
  89.1 1.6 %collective-permute-start.24 = (f32[64,128]{1,0:T(8,128)S(1)}, f32[64,128]{1,0:T(8,128)S(1)}, u32[]{:S(2)}, u32[]{:S(2)}) collective-permute-start(f32[64,128]{1,0:T(8,128)S(1)} %get-tuple-element.81.old_lo_x), channel_id=1, source_target_pairs={{0,8},{8,16},{16,24},{24,0},{1,9},{9,17},{17,25},{25,1},{2,10},{10... | collective-permute-start | bytes 98312 | tf_op jit(solution)/shard_map/ppermute | solution.py:246
  89.7 3.3 %collective-permute-start.25 = (f32[64,128]{1,0:T(8,128)S(1)}, f32[64,128]{1,0:T(8,128)S(1)}, u32[]{:S(2)}, u32[]{:S(2)}) collective-permute-start(f32[64,128]{1,0:T(8,128)S(1)} %get-tuple-element.82.old_hi_x), channel_id=1, source_target_pairs={{0,24},{8,0},{16,8},{24,16},{1,25},{9,1},{17,9},{25,17},{2,26},{10... | collective-permute-start | bytes 98312 | tf_op jit(solution)/shard_map/ppermute | solution.py:247
  94.0 8.1 %collective-permute-start.30 = (f32[64,256]{1,0:T(8,128)S(1)}, f32[64,256]{1,0:T(8,128)S(1)}, u32[]{:S(2)}, u32[]{:S(2)}) collective-permute-start(f32[64,256]{1,0:T(8,128)S(1)} %get-tuple-element.88.old_lo_y), channel_id=1, source_target_pairs={{0,1},{1,2},{2,3},{3,4},{4,5},{5,6},{6,7},{7,0},{8,9},{9,10},{10,1... | collective-permute-start | bytes 196616 | tf_op jit(solution)/shard_map/ppermute | solution.py:250
  94.1 4.7 %copy-start.6 = (s32[4,2,2]{0,2,1:T(2,128)S(1)}, s32[4,2,2]{0,2,1:T(2,128)}, u32[]{:S(2)}) copy-start(s32[4,2,2]{0,2,1:T(2,128)} %param.14) | copy-start | bytes 196
  94.1 8.1 %collective-permute-start.31 = (f32[64,256]{1,0:T(8,128)S(1)}, f32[64,256]{1,0:T(8,128)S(1)}, u32[]{:S(2)}, u32[]{:S(2)}) collective-permute-start(f32[64,256]{1,0:T(8,128)S(1)} %get-tuple-element.89.old_hi_y), channel_id=1, source_target_pairs={{0,7},{1,0},{2,1},{3,2},{4,3},{5,4},{6,5},{7,6},{8,15},{9,8},{10,9... | collective-permute-start | bytes 196616 | tf_op jit(solution)/shard_map/ppermute | solution.py:251
  98.2 1.6 %collective-permute-start.28 = (f32[64,128]{1,0:T(8,128)S(1)}, f32[64,128]{1,0:T(8,128)S(1)}, u32[]{:S(2)}, u32[]{:S(2)}) collective-permute-start(f32[64,128]{1,0:T(8,128)S(1)} %get-tuple-element.86.old_lo_x), channel_id=1, source_target_pairs={{0,8},{8,16},{16,24},{24,0},{1,9},{9,17},{17,25},{25,1},{2,10},{10... | collective-permute-start | bytes 98312 | tf_op jit(solution)/shard_map/ppermute | solution.py:246
  98.8 3.3 %collective-permute-start.29 = (f32[64,128]{1,0:T(8,128)S(1)}, f32[64,128]{1,0:T(8,128)S(1)}, u32[]{:S(2)}, u32[]{:S(2)}) collective-permute-start(f32[64,128]{1,0:T(8,128)S(1)} %get-tuple-element.87.old_hi_x), channel_id=1, source_target_pairs={{0,24},{8,0},{16,8},{24,16},{1,25},{9,1},{17,9},{25,17},{2,26},{10... | collective-permute-start | bytes 98312 | tf_op jit(solution)/shard_map/ppermute | solution.py:247

commit v10 on v9

--- a/solution.py
+++ b/solution.py
@@ -288,9 +288,11 @@
         jnp.pad(jnp.repeat(pick(weight, paint, axis=3).reshape(6, columns), R, axis=1), ((0, 2), (0, 0)))
         for paint in (0, 1)
     ]
-    member_inverse, member_target, member_weight, face_row = lax.optimization_barrier(
-        (member_inverse, member_target, member_weight, face_row)
-    )
+    constants = [
+        lax.optimization_barrier((member_inverse[paint], member_target[paint], member_weight[paint]))
+        for paint in (0, 1)
+    ]
+    member_inverse, member_target, member_weight = (list(group) for group in zip(*constants))
     state = [jnp.zeros_like(start_state), start_state]
     sends = None
     for sweep_index in range(SWEEPS):

time: 105 us -> 103 us (0.981); the launches traced: 104 us -> 101 us
  waiting for transfers between devices: 23 us -> 20.7 us
  starting transfers between devices: 42.6 us -> 41.2 us
    ppermute x8, waiting for transfers between devices: 16.2 us -> 13.9 us  [trade(): lax.ppermute(sends[1], 'gx', shift_pairs('gx', -1))]
    ppermute x8, starting transfers between devices: 2.51 us -> 0.39 us  [trade(): lax.ppermute(sends[2], 'gy', shift_pairs('gy', 1))]
    ppermute x8, starting transfers between devices: 32.1 us -> 33.4 us  [trade(): lax.ppermute(sends[3], 'gy', shift_pairs('gy', -1))]
    ppermute x8, waiting for transfers between devices: 0.02 us -> 1.2 us  [trade(): lax.ppermute(sends[2], 'gy', shift_pairs('gy', 1))]
    ppermute x8, starting transfers between devices: 7.91 us -> 6.78 us  [trade(): lax.ppermute(sends[0], 'gx', shift_pairs('gx', 1))]
    ppermute x8, waiting for transfers between devices: 6.7 us -> 5.61 us  [trade(): lax.ppermute(sends[0], 'gx', shift_pairs('gx', 1))]
  transfers between devices with their start and end apart: 32 -> 32, of which waited for: 14 -> 13; matrix products, arithmetic and copies ran while one was open for 5% -> 5% of each run, Pallas kernels for 17% -> 17%
where the time goes in v10:
time: 103 us; the launch traced here: 101 us
  starting transfers between devices  41.2 us (40%)
  Pallas kernels  25.5 us (25%)
  waiting for transfers between devices  20.7 us (20%)
  local copies, waits for them, and re-layouts  11.2 us (11%)
  other arithmetic  1.65 us (2%)
    ppermute x8, starting transfers between devices, trade(): lax.ppermute(sends[3], 'gy', shift_pairs('gy', -1))  33.4 us
    pallas_call x1, Pallas kernels, block_inverses(): pl.pallas_call(functools.partial(_gauss_jordan_kernel, n=n, nb=nb), out_s...  17.5 us
    ppermute x8, waiting for transfers between devices, trade(): lax.ppermute(sends[1], 'gx', shift_pairs('gx', -1))  13.9 us
    pallas_call x8, Pallas kernels, half_sweep(): pl.pallas_call(functools.partial(_half_sweep_kernel, span_x=span_x), out_...  7.98 us
    ppermute x8, starting transfers between devices, trade(): lax.ppermute(sends[0], 'gx', shift_pairs('gx', 1))  6.78 us
    ppermute x8, waiting for transfers between devices, trade(): lax.ppermute(sends[0], 'gx', shift_pairs('gx', 1))  5.61 us
    slice x3, local copies, waits for them, and re-layouts, pick(): high = lax.index_in_dim(values, 1, axis=axis, keepdims=False)  2.68 us
    unnamed x18, local copies, waits for them, and re-layouts  2.14 us
  transfers between devices with their start and end apart: 32, of which 13 were waited for; matrix products, arithmetic and copies ran while one was open for 5% of the time, Pallas kernels for 17%

profile of v10, /device:TPU:1, one launch (start us, length us, event | category | flops | bytes accessed | tf_op | source)
XLA Modules:
  0.0 100.7 jit_solution(13003489690592898779)
XLA Ops:
  0.0 0.7 slice-done
  1.1 1.9 %slice_reduce_fusion = (f32[4,2,4096]{2,1,0:T(2,128)S(1)}, f32[4,2,4096]{2,1,0:T(2,128)S(1)}) fusion(f32[4,2,2,4096]{3,2,1,0:T(2,128)} %param.8), kind=kLoop, calls=%fused_computation.8 | loop fusion | bytes 524288 | tf_op jit(solution)/shard_map/slice | solution.py:272
  3.0 0.2 squeeze.37
  3.2 0.2 squeeze.36
  3.4 0.7 copy-done
  4.1 0.8 slice_reduce_fusion.2
  4.9 0.2 squeeze.33
  5.1 0.2 squeeze.32
  5.9 2.6 %collective-permute-start = (f32[64,128]{1,0:T(8,128)S(1)}, f32[64,128]{1,0:T(8,128)S(1)}, u32[]{:S(2)}, u32[]{:S(2)}) collective-permute-start(f32[64,128]{1,0:T(8,128)S(1)} %reshape_squeeze.12.old_lo_x), channel_id=1, source_target_pairs={{0,8},{8,16},{16,24},{24,0},{1,9},{9,17},{17,25},{25,1},{2,10},{10... | collective-permute-start | bytes 98312 | tf_op jit(solution)/shard_map/ppermute | solution.py:246
  8.7 4.3 %collective-permute-start.3 = (f32[64,256]{1,0:T(8,128)S(1)}, f32[64,256]{1,0:T(8,128)S(1)}, u32[]{:S(2)}, u32[]{:S(2)}) collective-permute-start(f32[64,256]{1,0:T(8,128)S(1)} %reshape_squeeze.15.old_hi_y), channel_id=1, source_target_pairs={{0,7},{1,0},{2,1},{3,2},{4,3},{5,4},{6,5},{7,6},{8,15},{9,8},{10,9... | collective-permute-start | bytes 196616 | tf_op jit(solution)/shard_map/ppermute | solution.py:251
  13.2 0.1 reshape_squeeze.14.old_lo_y
  13.4 0.5 copy-done.3
  13.9 0.3 broadcast_select_fusion.1
  14.2 0.2 pad_maximum_fusion
  14.4 0.2 copy.102
  14.7 0.3 reshape.123
  15.0 0.3 copy.103
  15.3 0.2 copy.104.a_ref
  15.5 17.5 %shard_map.82 = f32[64,1024]{1,0:T(8,128)S(1)} custom-call(f32[64,1024]{1,0:T(8,128)S(1)} %copy.104.a_ref), custom_call_target="tpu_custom_call", output_to_operand_aliasing={{}: (0, {})} | custom-call | flops 8388608000 | bytes 524288 | tf_op jit(solution)/shard_map/pallas_call | solution.py:75
  33.0 0.2 copy.105
  33.2 0.4 copy.106
  33.6 0.2 reshape.126
  34.1 0.6 copy-done.2
  34.9 0.2 copy.108
  35.2 0.2 copy.94
  35.5 1.0 shard_map.83
  36.6 4.2 %collective-permute-start.7 = (f32[64,256]{1,0:T(8,128)S(1)}, f32[64,256]{1,0:T(8,128)S(1)}, u32[]{:S(2)}, u32[]{:S(2)}) collective-permute-start(f32[64,256]{1,0:T(8,128)S(1)} %get-tuple-element.54.old_hi_y), channel_id=1, source_target_pairs={{0,7},{1,0},{2,1},{3,2},{4,3},{5,4},{6,5},{7,6},{8,15},{9,8},{10,9... | collective-permute-start | bytes 196616 | tf_op jit(solution)/shard_map/ppermute | solution.py:251
  40.8 1.3 %collective-permute-start.4 = (f32[64,128]{1,0:T(8,128)S(1)}, f32[64,128]{1,0:T(8,128)S(1)}, u32[]{:S(2)}, u32[]{:S(2)}) collective-permute-start(f32[64,128]{1,0:T(8,128)S(1)} %get-tuple-element.51.old_lo_x), channel_id=1, source_target_pairs={{0,8},{8,16},{16,24},{24,0},{1,9},{9,17},{17,25},{25,1},{2,10},{10... | collective-permute-start | bytes 98312 | tf_op jit(solution)/shard_map/ppermute | solution.py:246
  42.3 0.2 copy.110
  42.6 0.5 collective-permute-done.4.lo_x_ref
  43.1 2.3 %collective-permute-done.5.hi_x_ref = f32[64,128]{1,0:T(8,128)S(1)} collective-permute-done((f32[64,128]{1,0:T(8,128)S(1)}, f32[64,128]{1,0:T(8,128)S(1)}, u32[]{:S(2)}, u32[]{:S(2)}) %collective-permute-start.5) | collective-permute-done | bytes 32800 | tf_op jit(solution)/shard_map/ppermute | solution.py:247
  45.4 1.0 shard_map.84
  46.5 4.1 %collective-permute-start.11 = (f32[64,256]{1,0:T(8,128)S(1)}, f32[64,256]{1,0:T(8,128)S(1)}, u32[]{:S(2)}, u32[]{:S(2)}) collective-permute-start(f32[64,256]{1,0:T(8,128)S(1)} %get-tuple-element.62.old_hi_y), channel_id=1, source_target_pairs={{0,7},{1,0},{2,1},{3,2},{4,3},{5,4},{6,5},{7,6},{8,15},{9,8},{10,9... | collective-permute-start | bytes 196616 | tf_op jit(solution)/shard_map/ppermute | solution.py:251
  50.6 0.6 collective-permute-start.8
  51.2 1.0 %collective-permute-done.8.lo_x_ref = f32[64,128]{1,0:T(8,128)S(1)} collective-permute-done((f32[64,128]{1,0:T(8,128)S(1)}, f32[64,128]{1,0:T(8,128)S(1)}, u32[]{:S(2)}, u32[]{:S(2)}) %collective-permute-start.8) | collective-permute-done | bytes 32800 | tf_op jit(solution)/shard_map/ppermute | solution.py:246
  52.2 2.3 %collective-permute-done.9.hi_x_ref = f32[64,128]{1,0:T(8,128)S(1)} collective-permute-done((f32[64,128]{1,0:T(8,128)S(1)}, f32[64,128]{1,0:T(8,128)S(1)}, u32[]{:S(2)}, u32[]{:S(2)}) %collective-permute-start.9) | collective-permute-done | bytes 32800 | tf_op jit(solution)/shard_map/ppermute | solution.py:247
  54.5 1.0 shard_map.85
  55.6 4.1 %collective-permute-start.15 = (f32[64,256]{1,0:T(8,128)S(1)}, f32[64,256]{1,0:T(8,128)S(1)}, u32[]{:S(2)}, u32[]{:S(2)}) collective-permute-start(f32[64,256]{1,0:T(8,128)S(1)} %get-tuple-element.67.old_hi_y), channel_id=1, source_target_pairs={{0,7},{1,0},{2,1},{3,2},{4,3},{5,4},{6,5},{7,6},{8,15},{9,8},{10,9... | collective-permute-start | bytes 196616 | tf_op jit(solution)/shard_map/ppermute | solution.py:251
  59.8 0.6 collective-permute-start.12
  60.3 1.0 %collective-permute-done.12.lo_x_ref = f32[64,128]{1,0:T(8,128)S(1)} collective-permute-done((f32[64,128]{1,0:T(8,128)S(1)}, f32[64,128]{1,0:T(8,128)S(1)}, u32[]{:S(2)}, u32[]{:S(2)}) %collective-permute-start.12) | collective-permute-done | bytes 32800 | tf_op jit(solution)/shard_map/ppermute | solution.py:246
  61.4 2.3 %collective-permute-done.13.hi_x_ref = f32[64,128]{1,0:T(8,128)S(1)} collective-permute-done((f32[64,128]{1,0:T(8,128)S(1)}, f32[64,128]{1,0:T(8,128)S(1)}, u32[]{:S(2)}, u32[]{:S(2)}) %collective-permute-start.13) | collective-permute-done | bytes 32800 | tf_op jit(solution)/shard_map/ppermute | solution.py:247
  63.7 1.0 shard_map.86
  64.7 4.1 %collective-permute-start.19 = (f32[64,256]{1,0:T(8,128)S(1)}, f32[64,256]{1,0:T(8,128)S(1)}, u32[]{:S(2)}, u32[]{:S(2)}) collective-permute-start(f32[64,256]{1,0:T(8,128)S(1)} %get-tuple-element.72.old_hi_y), channel_id=1, source_target_pairs={{0,7},{1,0},{2,1},{3,2},{4,3},{5,4},{6,5},{7,6},{8,15},{9,8},{10,9... | collective-permute-start | bytes 196616 | tf_op jit(solution)/shard_map/ppermute | solution.py:251
  68.9 0.6 collective-permute-start.16
  69.5 1.0 %collective-permute-done.16.lo_x_ref = f32[64,128]{1,0:T(8,128)S(1)} collective-permute-done((f32[64,128]{1,0:T(8,128)S(1)}, f32[64,128]{1,0:T(8,128)S(1)}, u32[]{:S(2)}, u32[]{:S(2)}) %collective-permute-start.16) | collective-permute-done | bytes 32800 | tf_op jit(solution)/shard_map/ppermute | solution.py:246
  70.5 2.3 %collective-permute-done.17.hi_x_ref = f32[64,128]{1,0:T(8,128)S(1)} collective-permute-done((f32[64,128]{1,0:T(8,128)S(1)}, f32[64,128]{1,0:T(8,128)S(1)}, u32[]{:S(2)}, u32[]{:S(2)}) %collective-permute-start.17) | collective-permute-done | bytes 32800 | tf_op jit(solution)/shard_map/ppermute | solution.py:247
  72.8 1.0 shard_map.87
  73.9 4.1 %collective-permute-start.23 = (f32[64,256]{1,0:T(8,128)S(1)}, f32[64,256]{1,0:T(8,128)S(1)}, u32[]{:S(2)}, u32[]{:S(2)}) collective-permute-start(f32[64,256]{1,0:T(8,128)S(1)} %get-tuple-element.77.old_hi_y), channel_id=1, source_target_pairs={{0,7},{1,0},{2,1},{3,2},{4,3},{5,4},{6,5},{7,6},{8,15},{9,8},{10,9... | collective-permute-start | bytes 196616 | tf_op jit(solution)/shard_map/ppermute | solution.py:251
  78.0 0.6 collective-permute-start.20
  78.6 1.0 %collective-permute-done.20.lo_x_ref = f32[64,128]{1,0:T(8,128)S(1)} collective-permute-done((f32[64,128]{1,0:T(8,128)S(1)}, f32[64,128]{1,0:T(8,128)S(1)}, u32[]{:S(2)}, u32[]{:S(2)}) %collective-permute-start.20) | collective-permute-done | bytes 32800 | tf_op jit(solution)/shard_map/ppermute | solution.py:246
  79.6 2.3 %collective-permute-done.21.hi_x_ref = f32[64,128]{1,0:T(8,128)S(1)} collective-permute-done((f32[64,128]{1,0:T(8,128)S(1)}, f32[64,128]{1,0:T(8,128)S(1)}, u32[]{:S(2)}, u32[]{:S(2)}) %collective-permute-start.21) | collective-permute-done | bytes 32800 | tf_op jit(solution)/shard_map/ppermute | solution.py:247
  82.0 1.0 shard_map.88
  83.0 4.1 %collective-permute-start.27 = (f32[64,256]{1,0:T(8,128)S(1)}, f32[64,256]{1,0:T(8,128)S(1)}, u32[]{:S(2)}, u32[]{:S(2)}) collective-permute-start(f32[64,256]{1,0:T(8,128)S(1)} %get-tuple-element.82.old_hi_y), channel_id=1, source_target_pairs={{0,7},{1,0},{2,1},{3,2},{4,3},{5,4},{6,5},{7,6},{8,15},{9,8},{10,9... | collective-permute-start | bytes 196616 | tf_op jit(solution)/shard_map/ppermute | solution.py:251
  87.2 0.6 collective-permute-start.24
  87.8 1.0 %collective-permute-done.24.lo_x_ref = f32[64,128]{1,0:T(8,128)S(1)} collective-permute-done((f32[64,128]{1,0:T(8,128)S(1)}, f32[64,128]{1,0:T(8,128)S(1)}, u32[]{:S(2)}, u32[]{:S(2)}) %collective-permute-start.24) | collective-permute-done | bytes 32800 | tf_op jit(solution)/shard_map/ppermute | solution.py:246
  88.8 2.3 %collective-permute-done.25.hi_x_ref = f32[64,128]{1,0:T(8,128)S(1)} collective-permute-done((f32[64,128]{1,0:T(8,128)S(1)}, f32[64,128]{1,0:T(8,128)S(1)}, u32[]{:S(2)}, u32[]{:S(2)}) %collective-permute-start.25) | collective-permute-done | bytes 32800 | tf_op jit(solution)/shard_map/ppermute | solution.py:247
  91.1 1.0 shard_map.89
  92.2 0.5 collective-permute-start.29
  92.7 4.2 %collective-permute-start.31 = (f32[64,256]{1,0:T(8,128)S(1)}, f32[64,256]{1,0:T(8,128)S(1)}, u32[]{:S(2)}, u32[]{:S(2)}) collective-permute-start(f32[64,256]{1,0:T(8,128)S(1)} %get-tuple-element.87.old_hi_y), channel_id=1, source_target_pairs={{0,7},{1,0},{2,1},{3,2},{4,3},{5,4},{6,5},{7,6},{8,15},{9,8},{10,9... | collective-permute-start | bytes 196616 | tf_op jit(solution)/shard_map/ppermute | solution.py:251
  97.1 0.1 broadcast_in_dim.104
  97.3 1.2 %collective-permute-done.30.lo_y_ref = f32[64,256]{1,0:T(8,128)S(1)} collective-permute-done((f32[64,256]{1,0:T(8,128)S(1)}, f32[64,256]{1,0:T(8,128)S(1)}, u32[]{:S(2)}, u32[]{:S(2)}) %collective-permute-start.30) | collective-permute-done | bytes 65568 | tf_op jit(solution)/shard_map/ppermute | solution.py:250
  98.5 1.0 shard_map.90
  99.6 0.1 broadcast_in_dim.106
  99.8 0.9 broadcast_select_fusion.2
  (86 shorter events, 3.4 us)
Async XLA Ops:
  0.0 0.7 slice-start
  3.2 1.0 copy-start
  5.6 29.8 %collective-permute-start.1 = (f32[64,128]{1,0:T(8,128)S(1)}, f32[64,128]{1,0:T(8,128)S(1)}, u32[]{:S(2)}, u32[]{:S(2)}) collective-permute-start(f32[64,128]{1,0:T(8,128)S(1)} %reshape_squeeze.13.old_hi_x), channel_id=1, source_target_pairs={{0,24},{8,0},{16,8},{24,16},{1,25},{9,1},{17,9},{25,17},{2,26},{10... | collective-permute-start | bytes 98312 | tf_op jit(solution)/shard_map/ppermute | solution.py:247
  5.9 29.6 %collective-permute-start = (f32[64,128]{1,0:T(8,128)S(1)}, f32[64,128]{1,0:T(8,128)S(1)}, u32[]{:S(2)}, u32[]{:S(2)}) collective-permute-start(f32[64,128]{1,0:T(8,128)S(1)} %reshape_squeeze.12.old_lo_x), channel_id=1, source_target_pairs={{0,8},{8,16},{16,24},{24,0},{1,9},{9,17},{17,25},{25,1},{2,10},{10... | collective-permute-start | bytes 98312 | tf_op jit(solution)/shard_map/ppermute | solution.py:246
  8.7 5.2 %copy-start.1 = (f32[4,2,2,4096]{3,2,1,0:T(2,128)S(1)}, f32[4,2,2,4096]{3,2,1,0:T(2,128)}, u32[]{:S(2)}) copy-start(f32[4,2,2,4096]{3,2,1,0:T(2,128)} %param.10) | copy-start | bytes 786436
  8.7 26.8 %collective-permute-start.3 = (f32[64,256]{1,0:T(8,128)S(1)}, f32[64,256]{1,0:T(8,128)S(1)}, u32[]{:S(2)}, u32[]{:S(2)}) collective-permute-start(f32[64,256]{1,0:T(8,128)S(1)} %reshape_squeeze.15.old_hi_y), channel_id=1, source_target_pairs={{0,7},{1,0},{2,1},{3,2},{4,3},{5,4},{6,5},{7,6},{8,15},{9,8},{10,9... | collective-permute-start | bytes 196616 | tf_op jit(solution)/shard_map/ppermute | solution.py:251
  13.1 0.7 copy-start.3
  13.1 0.7 copy-start.4
  13.2 0.7 copy-start.5
  13.3 22.2 %collective-permute-start.2 = (f32[64,256]{1,0:T(8,128)S(1)}, f32[64,256]{1,0:T(8,128)S(1)}, u32[]{:S(2)}, u32[]{:S(2)}) collective-permute-start(f32[64,256]{1,0:T(8,128)S(1)} %reshape_squeeze.14.old_lo_y), channel_id=1, source_target_pairs={{0,1},{1,2},{2,3},{3,4},{4,5},{5,6},{6,7},{7,0},{8,9},{9,10},{10,1... | collective-permute-start | bytes 196616 | tf_op jit(solution)/shard_map/ppermute | solution.py:250
  33.7 0.9 copy-start.2
  36.5 8.9 %collective-permute-start.6 = (f32[64,256]{1,0:T(8,128)S(1)}, f32[64,256]{1,0:T(8,128)S(1)}, u32[]{:S(2)}, u32[]{:S(2)}) collective-permute-start(f32[64,256]{1,0:T(8,128)S(1)} %get-tuple-element.53.old_lo_y), channel_id=1, source_target_pairs={{0,1},{1,2},{2,3},{3,4},{4,5},{5,6},{6,7},{7,0},{8,9},{9,10},{10,1... | collective-permute-start | bytes 196616 | tf_op jit(solution)/shard_map/ppermute | solution.py:250
  36.6 8.8 %collective-permute-start.7 = (f32[64,256]{1,0:T(8,128)S(1)}, f32[64,256]{1,0:T(8,128)S(1)}, u32[]{:S(2)}, u32[]{:S(2)}) collective-permute-start(f32[64,256]{1,0:T(8,128)S(1)} %get-tuple-element.54.old_hi_y), channel_id=1, source_target_pairs={{0,7},{1,0},{2,1},{3,2},{4,3},{5,4},{6,5},{7,6},{8,15},{9,8},{10,9... | collective-permute-start | bytes 196616 | tf_op jit(solution)/shard_map/ppermute | solution.py:251
  40.8 2.3 %collective-permute-start.4 = (f32[64,128]{1,0:T(8,128)S(1)}, f32[64,128]{1,0:T(8,128)S(1)}, u32[]{:S(2)}, u32[]{:S(2)}) collective-permute-start(f32[64,128]{1,0:T(8,128)S(1)} %get-tuple-element.51.old_lo_x), channel_id=1, source_target_pairs={{0,8},{8,16},{16,24},{24,0},{1,9},{9,17},{17,25},{25,1},{2,10},{10... | collective-permute-start | bytes 98312 | tf_op jit(solution)/shard_map/ppermute | solution.py:246
  42.1 3.3 %collective-permute-start.5 = (f32[64,128]{1,0:T(8,128)S(1)}, f32[64,128]{1,0:T(8,128)S(1)}, u32[]{:S(2)}, u32[]{:S(2)}) collective-permute-start(f32[64,128]{1,0:T(8,128)S(1)} %get-tuple-element.52.old_hi_x), channel_id=1, source_target_pairs={{0,24},{8,0},{16,8},{24,16},{1,25},{9,1},{17,9},{25,17},{2,26},{10... | collective-permute-start | bytes 98312 | tf_op jit(solution)/shard_map/ppermute | solution.py:247
  46.4 8.1 %collective-permute-start.10 = (f32[64,256]{1,0:T(8,128)S(1)}, f32[64,256]{1,0:T(8,128)S(1)}, u32[]{:S(2)}, u32[]{:S(2)}) collective-permute-start(f32[64,256]{1,0:T(8,128)S(1)} %get-tuple-element.61.old_lo_y), channel_id=1, source_target_pairs={{0,1},{1,2},{2,3},{3,4},{4,5},{5,6},{6,7},{7,0},{8,9},{9,10},{10,1... | collective-permute-start | bytes 196616 | tf_op jit(solution)/shard_map/ppermute | solution.py:250
  46.5 8.1 %collective-permute-start.11 = (f32[64,256]{1,0:T(8,128)S(1)}, f32[64,256]{1,0:T(8,128)S(1)}, u32[]{:S(2)}, u32[]{:S(2)}) collective-permute-start(f32[64,256]{1,0:T(8,128)S(1)} %get-tuple-element.62.old_hi_y), channel_id=1, source_target_pairs={{0,7},{1,0},{2,1},{3,2},{4,3},{5,4},{6,5},{7,6},{8,15},{9,8},{10,9... | collective-permute-start | bytes 196616 | tf_op jit(solution)/shard_map/ppermute | solution.py:251
  50.6 1.6 %collective-permute-start.8 = (f32[64,128]{1,0:T(8,128)S(1)}, f32[64,128]{1,0:T(8,128)S(1)}, u32[]{:S(2)}, u32[]{:S(2)}) collective-permute-start(f32[64,128]{1,0:T(8,128)S(1)} %get-tuple-element.59.old_lo_x), channel_id=1, source_target_pairs={{0,8},{8,16},{16,24},{24,0},{1,9},{9,17},{17,25},{25,1},{2,10},{10... | collective-permute-start | bytes 98312 | tf_op jit(solution)/shard_map/ppermute | solution.py:246
  51.2 3.3 %collective-permute-start.9 = (f32[64,128]{1,0:T(8,128)S(1)}, f32[64,128]{1,0:T(8,128)S(1)}, u32[]{:S(2)}, u32[]{:S(2)}) collective-permute-start(f32[64,128]{1,0:T(8,128)S(1)} %get-tuple-element.60.old_hi_x), channel_id=1, source_target_pairs={{0,24},{8,0},{16,8},{24,16},{1,25},{9,1},{17,9},{25,17},{2,26},{10... | collective-permute-start | bytes 98312 | tf_op jit(solution)/shard_map/ppermute | solution.py:247
  55.5 8.1 %collective-permute-start.14 = (f32[64,256]{1,0:T(8,128)S(1)}, f32[64,256]{1,0:T(8,128)S(1)}, u32[]{:S(2)}, u32[]{:S(2)}) collective-permute-start(f32[64,256]{1,0:T(8,128)S(1)} %get-tuple-element.66.old_lo_y), channel_id=1, source_target_pairs={{0,1},{1,2},{2,3},{3,4},{4,5},{5,6},{6,7},{7,0},{8,9},{9,10},{10,1... | collective-permute-start | bytes 196616 | tf_op jit(solution)/shard_map/ppermute | solution.py:250
  55.6 8.1 %collective-permute-start.15 = (f32[64,256]{1,0:T(8,128)S(1)}, f32[64,256]{1,0:T(8,128)S(1)}, u32[]{:S(2)}, u32[]{:S(2)}) collective-permute-start(f32[64,256]{1,0:T(8,128)S(1)} %get-tuple-element.67.old_hi_y), channel_id=1, source_target_pairs={{0,7},{1,0},{2,1},{3,2},{4,3},{5,4},{6,5},{7,6},{8,15},{9,8},{10,9... | collective-permute-start | bytes 196616 | tf_op jit(solution)/shard_map/ppermute | solution.py:251
  59.8 1.6 %collective-permute-start.12 = (f32[64,128]{1,0:T(8,128)S(1)}, f32[64,128]{1,0:T(8,128)S(1)}, u32[]{:S(2)}, u32[]{:S(2)}) collective-permute-start(f32[64,128]{1,0:T(8,128)S(1)} %get-tuple-element.64.old_lo_x), channel_id=1, source_target_pairs={{0,8},{8,16},{16,24},{24,0},{1,9},{9,17},{17,25},{25,1},{2,10},{10... | collective-permute-start | bytes 98312 | tf_op jit(solution)/shard_map/ppermute | solution.py:246
  60.3 3.3 %collective-permute-start.13 = (f32[64,128]{1,0:T(8,128)S(1)}, f32[64,128]{1,0:T(8,128)S(1)}, u32[]{:S(2)}, u32[]{:S(2)}) collective-permute-start(f32[64,128]{1,0:T(8,128)S(1)} %get-tuple-element.65.old_hi_x), channel_id=1, source_target_pairs={{0,24},{8,0},{16,8},{24,16},{1,25},{9,1},{17,9},{25,17},{2,26},{10... | collective-permute-start | bytes 98312 | tf_op jit(solution)/shard_map/ppermute | solution.py:247
  64.7 8.1 %collective-permute-start.18 = (f32[64,256]{1,0:T(8,128)S(1)}, f32[64,256]{1,0:T(8,128)S(1)}, u32[]{:S(2)}, u32[]{:S(2)}) collective-permute-start(f32[64,256]{1,0:T(8,128)S(1)} %get-tuple-element.71.old_lo_y), channel_id=1, source_target_pairs={{0,1},{1,2},{2,3},{3,4},{4,5},{5,6},{6,7},{7,0},{8,9},{9,10},{10,1... | collective-permute-start | bytes 196616 | tf_op jit(solution)/shard_map/ppermute | solution.py:250
  64.7 8.1 %collective-permute-start.19 = (f32[64,256]{1,0:T(8,128)S(1)}, f32[64,256]{1,0:T(8,128)S(1)}, u32[]{:S(2)}, u32[]{:S(2)}) collective-permute-start(f32[64,256]{1,0:T(8,128)S(1)} %get-tuple-element.72.old_hi_y), channel_id=1, source_target_pairs={{0,7},{1,0},{2,1},{3,2},{4,3},{5,4},{6,5},{7,6},{8,15},{9,8},{10,9... | collective-permute-start | bytes 196616 | tf_op jit(solution)/shard_map/ppermute | solution.py:251
  68.9 1.6 %collective-permute-start.16 = (f32[64,128]{1,0:T(8,128)S(1)}, f32[64,128]{1,0:T(8,128)S(1)}, u32[]{:S(2)}, u32[]{:S(2)}) collective-permute-start(f32[64,128]{1,0:T(8,128)S(1)} %get-tuple-element.69.old_lo_x), channel_id=1, source_target_pairs={{0,8},{8,16},{16,24},{24,0},{1,9},{9,17},{17,25},{25,1},{2,10},{10... | collective-permute-start | bytes 98312 | tf_op jit(solution)/shard_map/ppermute | solution.py:246
  69.5 3.3 %collective-permute-start.17 = (f32[64,128]{1,0:T(8,128)S(1)}, f32[64,128]{1,0:T(8,128)S(1)}, u32[]{:S(2)}, u32[]{:S(2)}) collective-permute-start(f32[64,128]{1,0:T(8,128)S(1)} %get-tuple-element.70.old_hi_x), channel_id=1, source_target_pairs={{0,24},{8,0},{16,8},{24,16},{1,25},{9,1},{17,9},{25,17},{2,26},{10... | collective-permute-start | bytes 98312 | tf_op jit(solution)/shard_map/ppermute | solution.py:247
  73.8 8.1 %collective-permute-start.22 = (f32[64,256]{1,0:T(8,128)S(1)}, f32[64,256]{1,0:T(8,128)S(1)}, u32[]{:S(2)}, u32[]{:S(2)}) collective-permute-start(f32[64,256]{1,0:T(8,128)S(1)} %get-tuple-element.76.old_lo_y), channel_id=1, source_target_pairs={{0,1},{1,2},{2,3},{3,4},{4,5},{5,6},{6,7},{7,0},{8,9},{9,10},{10,1... | collective-permute-start | bytes 196616 | tf_op jit(solution)/shard_map/ppermute | solution.py:250
  73.9 8.1 %collective-permute-start.23 = (f32[64,256]{1,0:T(8,128)S(1)}, f32[64,256]{1,0:T(8,128)S(1)}, u32[]{:S(2)}, u32[]{:S(2)}) collective-permute-start(f32[64,256]{1,0:T(8,128)S(1)} %get-tuple-element.77.old_hi_y), channel_id=1, source_target_pairs={{0,7},{1,0},{2,1},{3,2},{4,3},{5,4},{6,5},{7,6},{8,15},{9,8},{10,9... | collective-permute-start | bytes 196616 | tf_op jit(solution)/shard_map/ppermute | solution.py:251
  78.0 1.6 %collective-permute-start.20 = (f32[64,128]{1,0:T(8,128)S(1)}, f32[64,128]{1,0:T(8,128)S(1)}, u32[]{:S(2)}, u32[]{:S(2)}) collective-permute-start(f32[64,128]{1,0:T(8,128)S(1)} %get-tuple-element.74.old_lo_x), channel_id=1, source_target_pairs={{0,8},{8,16},{16,24},{24,0},{1,9},{9,17},{17,25},{25,1},{2,10},{10... | collective-permute-start | bytes 98312 | tf_op jit(solution)/shard_map/ppermute | solution.py:246
  78.6 3.3 %collective-permute-start.21 = (f32[64,128]{1,0:T(8,128)S(1)}, f32[64,128]{1,0:T(8,128)S(1)}, u32[]{:S(2)}, u32[]{:S(2)}) collective-permute-start(f32[64,128]{1,0:T(8,128)S(1)} %get-tuple-element.75.old_hi_x), channel_id=1, source_target_pairs={{0,24},{8,0},{16,8},{24,16},{1,25},{9,1},{17,9},{25,17},{2,26},{10... | collective-permute-start | bytes 98312 | tf_op jit(solution)/shard_map/ppermute | solution.py:247
  83.0 8.1 %collective-permute-start.26 = (f32[64,256]{1,0:T(8,128)S(1)}, f32[64,256]{1,0:T(8,128)S(1)}, u32[]{:S(2)}, u32[]{:S(2)}) collective-permute-start(f32[64,256]{1,0:T(8,128)S(1)} %get-tuple-element.81.old_lo_y), channel_id=1, source_target_pairs={{0,1},{1,2},{2,3},{3,4},{4,5},{5,6},{6,7},{7,0},{8,9},{9,10},{10,1... | collective-permute-start | bytes 196616 | tf_op jit(solution)/shard_map/ppermute | solution.py:250
  83.0 8.1 %collective-permute-start.27 = (f32[64,256]{1,0:T(8,128)S(1)}, f32[64,256]{1,0:T(8,128)S(1)}, u32[]{:S(2)}, u32[]{:S(2)}) collective-permute-start(f32[64,256]{1,0:T(8,128)S(1)} %get-tuple-element.82.old_hi_y), channel_id=1, source_target_pairs={{0,7},{1,0},{2,1},{3,2},{4,3},{5,4},{6,5},{7,6},{8,15},{9,8},{10,9... | collective-permute-start | bytes 196616 | tf_op jit(solution)/shard_map/ppermute | solution.py:251
  87.2 1.6 %collective-permute-start.24 = (f32[64,128]{1,0:T(8,128)S(1)}, f32[64,128]{1,0:T(8,128)S(1)}, u32[]{:S(2)}, u32[]{:S(2)}) collective-permute-start(f32[64,128]{1,0:T(8,128)S(1)} %get-tuple-element.79.old_lo_x), channel_id=1, source_target_pairs={{0,8},{8,16},{16,24},{24,0},{1,9},{9,17},{17,25},{25,1},{2,10},{10... | collective-permute-start | bytes 98312 | tf_op jit(solution)/shard_map/ppermute | solution.py:246
  87.7 3.3 %collective-permute-start.25 = (f32[64,128]{1,0:T(8,128)S(1)}, f32[64,128]{1,0:T(8,128)S(1)}, u32[]{:S(2)}, u32[]{:S(2)}) collective-permute-start(f32[64,128]{1,0:T(8,128)S(1)} %get-tuple-element.80.old_hi_x), channel_id=1, source_target_pairs={{0,24},{8,0},{16,8},{24,16},{1,25},{9,1},{17,9},{25,17},{2,26},{10... | collective-permute-start | bytes 98312 | tf_op jit(solution)/shard_map/ppermute | solution.py:247
  92.1 5.2 %collective-permute-start.28 = (f32[64,128]{1,0:T(8,128)S(1)}, f32[64,128]{1,0:T(8,128)S(1)}, u32[]{:S(2)}, u32[]{:S(2)}) collective-permute-start(f32[64,128]{1,0:T(8,128)S(1)} %get-tuple-element.84.old_lo_x), channel_id=1, source_target_pairs={{0,8},{8,16},{16,24},{24,0},{1,9},{9,17},{17,25},{25,1},{2,10},{10... | collective-permute-start | bytes 98312 | tf_op jit(solution)/shard_map/ppermute | solution.py:246
  92.2 4.7 %copy-start.6 = (s32[4,2,2]{0,2,1:T(2,128)S(1)}, s32[4,2,2]{0,2,1:T(2,128)}, u32[]{:S(2)}) copy-start(s32[4,2,2]{0,2,1:T(2,128)} %param.14) | copy-start | bytes 196
  92.2 5.1 %collective-permute-start.29 = (f32[64,128]{1,0:T(8,128)S(1)}, f32[64,128]{1,0:T(8,128)S(1)}, u32[]{:S(2)}, u32[]{:S(2)}) collective-permute-start(f32[64,128]{1,0:T(8,128)S(1)} %get-tuple-element.85.old_hi_x), channel_id=1, source_target_pairs={{0,24},{8,0},{16,8},{24,16},{1,25},{9,1},{17,9},{25,17},{2,26},{10... | collective-permute-start | bytes 98312 | tf_op jit(solution)/shard_map/ppermute | solution.py:247
  92.7 5.8 %collective-permute-start.30 = (f32[64,256]{1,0:T(8,128)S(1)}, f32[64,256]{1,0:T(8,128)S(1)}, u32[]{:S(2)}, u32[]{:S(2)}) collective-permute-start(f32[64,256]{1,0:T(8,128)S(1)} %get-tuple-element.86.old_lo_y), channel_id=1, source_target_pairs={{0,1},{1,2},{2,3},{3,4},{4,5},{5,6},{6,7},{7,0},{8,9},{9,10},{10,1... | collective-permute-start | bytes 196616 | tf_op jit(solution)/shard_map/ppermute | solution.py:250
  92.7 5.8 %collective-permute-start.31 = (f32[64,256]{1,0:T(8,128)S(1)}, f32[64,256]{1,0:T(8,128)S(1)}, u32[]{:S(2)}, u32[]{:S(2)}) collective-permute-start(f32[64,256]{1,0:T(8,128)S(1)} %get-tuple-element.87.old_hi_y), channel_id=1, source_target_pairs={{0,7},{1,0},{2,1},{3,2},{4,3},{5,4},{6,5},{7,6},{8,15},{9,8},{10,9... | collective-permute-start | bytes 196616 | tf_op jit(solution)/shard_map/ppermute | solution.py:251

commit v11 on v10

--- a/solution.py
+++ b/solution.py
@@ -159,17 +159,51 @@
     )
 
 
-def _half_sweep_kernel(
-    other_ref, lo_x_ref, hi_x_ref, lo_y_ref, hi_y_ref, face_ref, weight_ref, inverse_ref,
-    target_ref, previous_ref, old_lo_x, old_hi_x, old_lo_y, old_hi_y, out_ref, send_lo_x_ref, send_hi_x_ref, send_lo_y_ref, send_hi_y_ref, *, span_x
-):
+def _local_kernel(other_ref, face_ref, weight_ref, previous_ref, out_ref, *, span_x):
     tile = 2 * R
-    highest = lax.Precision.HIGHEST
     other = other_ref[...]
     lanes = other.shape[1]
     lane = lax.broadcasted_iota(jnp.int32, (P_SIZE, tile), 1)
     low_half = lane < R
-    tiles = [other[:, t * tile:(t + 1) * tile] for t in range(span_x)]
+    rolled = [pltpu.roll(other[:, t * tile:(t + 1) * tile], R, 1) for t in range(span_x)]
+    empty = jnp.zeros((P_SIZE, tile), jnp.float32)
+    nearby = [
+        jnp.concatenate([empty, other[:, :lanes - tile]], axis=1),
+        jnp.concatenate([other[:, tile:], empty], axis=1),
+        jnp.concatenate([jnp.where(low_half, 0.0, part) for part in rolled], axis=1),
+        jnp.concatenate([jnp.where(low_half, part, 0.0) for part in rolled], axis=1),
+        other,
+        other,
+    ]
+    stacked = jnp.concatenate(
+        [weight_ref[face:face + 1, :] * nearby[face] for face in range(6)], axis=0
+    )
+    out_ref[...] = jnp.dot(
+        face_ref[...], stacked, precision=lax.Precision.HIGHEST, preferred_element_type=jnp.float32
+    )
+
+
+def local_part(other, face_blocks, weight, previous, span_x):
+    vmem = pl.BlockSpec(memory_space=pltpu.VMEM)
+    return pl.pallas_call(
+        functools.partial(_local_kernel, span_x=span_x),
+        out_shape=jax.ShapeDtypeStruct(other.shape, jnp.float32),
+        in_specs=[vmem] * 4,
+        out_specs=vmem,
+        input_output_aliases={3: 0},
+    )(*[pltpu.with_memory_space_constraint(v, pltpu.VMEM) for v in (other, face_blocks, weight, previous)])
+
+
+def _half_sweep_kernel(
+    local_ref, lo_x_ref, hi_x_ref, lo_y_ref, hi_y_ref, face_ref, weight_ref, inverse_ref,
+    target_ref, previous_ref, old_lo_x, old_hi_x, old_lo_y, old_hi_y, out_ref, send_lo_x_ref,
+    send_hi_x_ref, send_lo_y_ref, send_hi_y_ref, *, span_x
+):
+    tile = 2 * R
+    highest = lax.Precision.HIGHEST
+    lanes = local_ref.shape[1]
+    lane = lax.broadcasted_iota(jnp.int32, (P_SIZE, tile), 1)
+    low_half = lane < R
     lo_y = lo_y_ref[...]
     hi_y = hi_y_ref[...]
 
@@ -177,23 +211,21 @@
         held = packed[:, (x // 2) * tile:(x // 2 + 1) * tile]
         return held if x % 2 == 0 else pltpu.roll(held, R, 1)
 
-    below, above = [], []
-    for x in range(span_x):
-        rolled = pltpu.roll(tiles[x], R, 1)
-        below.append(jnp.where(low_half, y_block(lo_y, x), rolled))
-        above.append(jnp.where(low_half, rolled, pltpu.roll(y_block(hi_y, x), R, 1)))
+    empty = jnp.zeros((P_SIZE, lanes - tile), jnp.float32)
     nearby = [
-        jnp.concatenate([lo_x_ref[...], other[:, :lanes - tile]], axis=1),
-        jnp.concatenate([other[:, tile:], hi_x_ref[...]], axis=1),
-        jnp.concatenate(below, axis=1),
-        jnp.concatenate(above, axis=1),
-        other,
-        other,
+        jnp.concatenate([lo_x_ref[...], empty], axis=1),
+        jnp.concatenate([empty, hi_x_ref[...]], axis=1),
+        jnp.concatenate([jnp.where(low_half, y_block(lo_y, x), 0.0) for x in range(span_x)], axis=1),
+        jnp.concatenate(
+            [jnp.where(low_half, 0.0, pltpu.roll(y_block(hi_y, x), R, 1)) for x in range(span_x)], axis=1
+        ),
     ]
     stacked = jnp.concatenate(
-        [weight_ref[face:face + 1, :] * nearby[face] for face in range(6)], axis=0
-    )
-    coupled = jnp.dot(face_ref[...], stacked, precision=highest, preferred_element_type=jnp.float32)
+        [weight_ref[face:face + 1, :] * nearby[face] for face in range(4)], axis=0
+    )
+    coupled = local_ref[...] + jnp.dot(
+        face_ref[:, :4 * P_SIZE], stacked, precision=highest, preferred_element_type=jnp.float32
+    )
     rhs = target_ref[...] - coupled
     outs = []
     for x in range(span_x):
@@ -214,8 +246,8 @@
         send_hi_y_ref[:, t * tile:(t + 1) * tile] = jnp.where(low_half, even, pltpu.roll(odd, R, 1))
 
 
-def half_sweep(other, halos, face_blocks, weight, inverse, target, previous, old_sends, span_x):
-    lanes = other.shape[1]
+def half_sweep(local, halos, face_blocks, weight, inverse, target, previous, old_sends, span_x):
+    lanes = local.shape[1]
     x_shape = jax.ShapeDtypeStruct((P_SIZE, 2 * R), jnp.float32)
     y_shape = jax.ShapeDtypeStruct((P_SIZE, span_x * R), jnp.float32)
     vmem = pl.BlockSpec(memory_space=pltpu.VMEM)
@@ -227,7 +259,7 @@
         input_output_aliases={9: 0, 10: 1, 11: 2, 12: 3, 13: 4},
     )(*[
         pltpu.with_memory_space_constraint(value, pltpu.VMEM)
-        for value in (other, *halos, face_blocks, weight, inverse, target, previous, *old_sends)
+        for value in (local, *halos, face_blocks, weight, inverse, target, previous, *old_sends)
     ])
 
 
@@ -295,11 +327,15 @@
     member_inverse, member_target, member_weight = (list(group) for group in zip(*constants))
     state = [jnp.zeros_like(start_state), start_state]
     sends = None
+    local = jnp.zeros_like(start_state)
     for sweep_index in range(SWEEPS):
         for paint_now in (0, 1):
             halos = first_halos if sends is None else trade(sends)
+            local = local_part(
+                state[1 - paint_now], face_row, member_weight[paint_now], local, span_x
+            )
             state[paint_now], *sends = half_sweep(
-                state[1 - paint_now],
+                local,
                 halos,
                 face_row,
                 member_weight[paint_now],

time: 103 us -> 102 us (level)
  waiting for transfers between devices: 20.7 us -> 16.5 us
  Pallas kernels: 25.5 us -> 29.4 us
    pallas_call x0 -> x8, Pallas kernels: none -> 4.74 us  [local_part(): pl.pallas_call(functools.partial(_local_kernel, span_x=span_x), out_shape...]
    ppermute x8, waiting for transfers between devices: 5.61 us -> 2.12 us  [trade(): lax.ppermute(sends[0], 'gx', shift_pairs('gx', 1))]
  transfers between devices with their start and end apart: 32 -> 32, of which waited for: 13 -> 12; matrix products, arithmetic and copies ran while one was open for 5% -> 5% of each run, Pallas kernels for 17% -> 22%
where the time goes in v11:
time: 102 us; the launch traced here: 100 us
  starting transfers between devices  41.2 us (40%)
  Pallas kernels  29.4 us (29%)
  waiting for transfers between devices  16.5 us (16%)
  local copies, waits for them, and re-layouts  11.2 us (11%)
  other arithmetic  1.65 us (2%)
    ppermute x8, starting transfers between devices, trade(): lax.ppermute(sends[3], 'gy', shift_pairs('gy', -1))  33.4 us
    pallas_call x1, Pallas kernels, block_inverses(): pl.pallas_call(functools.partial(_gauss_jordan_kernel, n=n, nb=nb), out_s...  17.5 us
    ppermute x8, waiting for transfers between devices, trade(): lax.ppermute(sends[1], 'gx', shift_pairs('gx', -1))  13.8 us
    pallas_call x8, Pallas kernels, half_sweep(): pl.pallas_call(functools.partial(_half_sweep_kernel, span_x=span_x), out_...  7.18 us
    ppermute x8, starting transfers between devices, trade(): lax.ppermute(sends[0], 'gx', shift_pairs('gx', 1))  6.77 us
    pallas_call x8, Pallas kernels, local_part(): pl.pallas_call(functools.partial(_local_kernel, span_x=span_x), out_shape...  4.74 us
    slice x3, local copies, waits for them, and re-layouts, pick(): high = lax.index_in_dim(values, 1, axis=axis, keepdims=False)  2.68 us
    unnamed x18, local copies, waits for them, and re-layouts  2.14 us
  transfers between devices with their start and end apart: 32, of which 12 were waited for; matrix products, arithmetic and copies ran while one was open for 5% of the time, Pallas kernels for 22%

profile of v11, /device:TPU:1, one launch (start us, length us, event | category | flops | bytes accessed | tf_op | source)
XLA Modules:
  0.0 100.5 jit_solution(6547955382607072148)
XLA Ops:
  0.0 0.7 slice-done
  1.1 1.9 %slice_reduce_fusion = (f32[4,2,4096]{2,1,0:T(2,128)S(1)}, f32[4,2,4096]{2,1,0:T(2,128)S(1)}) fusion(f32[4,2,2,4096]{3,2,1,0:T(2,128)} %param.8), kind=kLoop, calls=%fused_computation.8 | loop fusion | bytes 524288 | tf_op jit(solution)/shard_map/slice | solution.py:304
  3.0 0.2 squeeze.37
  3.2 0.2 squeeze.36
  3.4 0.7 copy-done
  4.1 0.8 slice_reduce_fusion.2
  4.9 0.2 squeeze.33
  5.1 0.2 squeeze.32
  5.9 2.6 %collective-permute-start = (f32[64,128]{1,0:T(8,128)S(1)}, f32[64,128]{1,0:T(8,128)S(1)}, u32[]{:S(2)}, u32[]{:S(2)}) collective-permute-start(f32[64,128]{1,0:T(8,128)S(1)} %reshape_squeeze.12.old_lo_x), channel_id=1, source_target_pairs={{0,8},{8,16},{16,24},{24,0},{1,9},{9,17},{17,25},{25,1},{2,10},{10... | collective-permute-start | bytes 98312 | tf_op jit(solution)/shard_map/ppermute | solution.py:278
  8.7 4.3 %collective-permute-start.3 = (f32[64,256]{1,0:T(8,128)S(1)}, f32[64,256]{1,0:T(8,128)S(1)}, u32[]{:S(2)}, u32[]{:S(2)}) collective-permute-start(f32[64,256]{1,0:T(8,128)S(1)} %reshape_squeeze.15.old_hi_y), channel_id=1, source_target_pairs={{0,7},{1,0},{2,1},{3,2},{4,3},{5,4},{6,5},{7,6},{8,15},{9,8},{10,9... | collective-permute-start | bytes 196616 | tf_op jit(solution)/shard_map/ppermute | solution.py:283
  13.4 0.5 copy-done.3
  13.9 0.3 broadcast_select_fusion.1
  14.2 0.2 pad_maximum_fusion
  14.4 0.2 copy.106
  14.7 0.3 reshape.123
  15.0 0.3 copy.107
  15.3 0.2 copy.108.a_ref
  15.5 17.5 %shard_map.82 = f32[64,1024]{1,0:T(8,128)S(1)} custom-call(f32[64,1024]{1,0:T(8,128)S(1)} %copy.108.a_ref), custom_call_target="tpu_custom_call", output_to_operand_aliasing={{}: (0, {})} | custom-call | flops 8388608000 | bytes 524288 | tf_op jit(solution)/shard_map/pallas_call | solution.py:75
  33.0 0.2 copy.109
  33.2 0.4 copy.110
  34.1 0.6 copy-done.2
  35.5 0.6 shard_map.83.local_ref.previous_ref
  36.1 0.9 shard_map.84
  37.1 4.2 %collective-permute-start.7 = (f32[64,256]{1,0:T(8,128)S(1)}, f32[64,256]{1,0:T(8,128)S(1)}, u32[]{:S(2)}, u32[]{:S(2)}) collective-permute-start(f32[64,256]{1,0:T(8,128)S(1)} %get-tuple-element.55.old_hi_y), channel_id=1, source_target_pairs={{0,7},{1,0},{2,1},{3,2},{4,3},{5,4},{6,5},{7,6},{8,15},{9,8},{10,9... | collective-permute-start | bytes 196616 | tf_op jit(solution)/shard_map/ppermute | solution.py:283
  41.3 1.3 %collective-permute-start.4 = (f32[64,128]{1,0:T(8,128)S(1)}, f32[64,128]{1,0:T(8,128)S(1)}, u32[]{:S(2)}, u32[]{:S(2)}) collective-permute-start(f32[64,128]{1,0:T(8,128)S(1)} %get-tuple-element.52.old_lo_x), channel_id=1, source_target_pairs={{0,8},{8,16},{16,24},{24,0},{1,9},{9,17},{17,25},{25,1},{2,10},{10... | collective-permute-start | bytes 98312 | tf_op jit(solution)/shard_map/ppermute | solution.py:278
  43.1 0.6 shard_map.85.local_ref.previous_ref
  43.7 2.2 %collective-permute-done.5.hi_x_ref = f32[64,128]{1,0:T(8,128)S(1)} collective-permute-done((f32[64,128]{1,0:T(8,128)S(1)}, f32[64,128]{1,0:T(8,128)S(1)}, u32[]{:S(2)}, u32[]{:S(2)}) %collective-permute-start.5) | collective-permute-done | bytes 32800 | tf_op jit(solution)/shard_map/ppermute | solution.py:279
  45.9 0.9 shard_map.86
  46.9 4.1 %collective-permute-start.11 = (f32[64,256]{1,0:T(8,128)S(1)}, f32[64,256]{1,0:T(8,128)S(1)}, u32[]{:S(2)}, u32[]{:S(2)}) collective-permute-start(f32[64,256]{1,0:T(8,128)S(1)} %get-tuple-element.62.old_hi_y), channel_id=1, source_target_pairs={{0,7},{1,0},{2,1},{3,2},{4,3},{5,4},{6,5},{7,6},{8,15},{9,8},{10,9... | collective-permute-start | bytes 196616 | tf_op jit(solution)/shard_map/ppermute | solution.py:283
  51.0 0.6 collective-permute-start.8
  51.6 0.6 shard_map.87.local_ref.previous_ref
  52.2 0.4 collective-permute-done.8.lo_x_ref
  52.6 2.3 %collective-permute-done.9.hi_x_ref = f32[64,128]{1,0:T(8,128)S(1)} collective-permute-done((f32[64,128]{1,0:T(8,128)S(1)}, f32[64,128]{1,0:T(8,128)S(1)}, u32[]{:S(2)}, u32[]{:S(2)}) %collective-permute-start.9) | collective-permute-done | bytes 32800 | tf_op jit(solution)/shard_map/ppermute | solution.py:279
  55.0 0.9 shard_map.88
  55.9 4.1 %collective-permute-start.15 = (f32[64,256]{1,0:T(8,128)S(1)}, f32[64,256]{1,0:T(8,128)S(1)}, u32[]{:S(2)}, u32[]{:S(2)}) collective-permute-start(f32[64,256]{1,0:T(8,128)S(1)} %get-tuple-element.67.old_hi_y), channel_id=1, source_target_pairs={{0,7},{1,0},{2,1},{3,2},{4,3},{5,4},{6,5},{7,6},{8,15},{9,8},{10,9... | collective-permute-start | bytes 196616 | tf_op jit(solution)/shard_map/ppermute | solution.py:283
  60.1 0.6 collective-permute-start.12
  60.6 0.6 shard_map.89.local_ref.previous_ref
  61.2 0.4 collective-permute-done.12.lo_x_ref
  61.7 2.3 %collective-permute-done.13.hi_x_ref = f32[64,128]{1,0:T(8,128)S(1)} collective-permute-done((f32[64,128]{1,0:T(8,128)S(1)}, f32[64,128]{1,0:T(8,128)S(1)}, u32[]{:S(2)}, u32[]{:S(2)}) %collective-permute-start.13) | collective-permute-done | bytes 32800 | tf_op jit(solution)/shard_map/ppermute | solution.py:279
  64.0 0.9 shard_map.90
  65.0 4.1 %collective-permute-start.19 = (f32[64,256]{1,0:T(8,128)S(1)}, f32[64,256]{1,0:T(8,128)S(1)}, u32[]{:S(2)}, u32[]{:S(2)}) collective-permute-start(f32[64,256]{1,0:T(8,128)S(1)} %get-tuple-element.72.old_hi_y), channel_id=1, source_target_pairs={{0,7},{1,0},{2,1},{3,2},{4,3},{5,4},{6,5},{7,6},{8,15},{9,8},{10,9... | collective-permute-start | bytes 196616 | tf_op jit(solution)/shard_map/ppermute | solution.py:283
  69.1 0.6 collective-permute-start.16
  69.7 0.6 shard_map.91.local_ref.previous_ref
  70.3 0.4 collective-permute-done.16.lo_x_ref
  70.7 2.3 %collective-permute-done.17.hi_x_ref = f32[64,128]{1,0:T(8,128)S(1)} collective-permute-done((f32[64,128]{1,0:T(8,128)S(1)}, f32[64,128]{1,0:T(8,128)S(1)}, u32[]{:S(2)}, u32[]{:S(2)}) %collective-permute-start.17) | collective-permute-done | bytes 32800 | tf_op jit(solution)/shard_map/ppermute | solution.py:279
  73.0 0.9 shard_map.92
  74.0 4.1 %collective-permute-start.23 = (f32[64,256]{1,0:T(8,128)S(1)}, f32[64,256]{1,0:T(8,128)S(1)}, u32[]{:S(2)}, u32[]{:S(2)}) collective-permute-start(f32[64,256]{1,0:T(8,128)S(1)} %get-tuple-element.77.old_hi_y), channel_id=1, source_target_pairs={{0,7},{1,0},{2,1},{3,2},{4,3},{5,4},{6,5},{7,6},{8,15},{9,8},{10,9... | collective-permute-start | bytes 196616 | tf_op jit(solution)/shard_map/ppermute | solution.py:283
  78.1 0.6 collective-permute-start.20
  78.7 0.6 shard_map.93.local_ref.previous_ref
  79.3 0.4 collective-permute-done.20.lo_x_ref
  79.7 2.3 %collective-permute-done.21.hi_x_ref = f32[64,128]{1,0:T(8,128)S(1)} collective-permute-done((f32[64,128]{1,0:T(8,128)S(1)}, f32[64,128]{1,0:T(8,128)S(1)}, u32[]{:S(2)}, u32[]{:S(2)}) %collective-permute-start.21) | collective-permute-done | bytes 32800 | tf_op jit(solution)/shard_map/ppermute | solution.py:279
  82.1 0.9 shard_map.94
  83.0 4.1 %collective-permute-start.27 = (f32[64,256]{1,0:T(8,128)S(1)}, f32[64,256]{1,0:T(8,128)S(1)}, u32[]{:S(2)}, u32[]{:S(2)}) collective-permute-start(f32[64,256]{1,0:T(8,128)S(1)} %get-tuple-element.82.old_hi_y), channel_id=1, source_target_pairs={{0,7},{1,0},{2,1},{3,2},{4,3},{5,4},{6,5},{7,6},{8,15},{9,8},{10,9... | collective-permute-start | bytes 196616 | tf_op jit(solution)/shard_map/ppermute | solution.py:283
  87.2 0.6 collective-permute-start.24
  87.8 0.6 shard_map.95.local_ref.previous_ref
  88.4 0.4 collective-permute-done.24.lo_x_ref
  88.8 2.3 %collective-permute-done.25.hi_x_ref = f32[64,128]{1,0:T(8,128)S(1)} collective-permute-done((f32[64,128]{1,0:T(8,128)S(1)}, f32[64,128]{1,0:T(8,128)S(1)}, u32[]{:S(2)}, u32[]{:S(2)}) %collective-permute-start.25) | collective-permute-done | bytes 32800 | tf_op jit(solution)/shard_map/ppermute | solution.py:279
  91.1 0.9 shard_map.96
  92.1 0.5 collective-permute-start.29
  92.6 4.2 %collective-permute-start.31 = (f32[64,256]{1,0:T(8,128)S(1)}, f32[64,256]{1,0:T(8,128)S(1)}, u32[]{:S(2)}, u32[]{:S(2)}) collective-permute-start(f32[64,256]{1,0:T(8,128)S(1)} %get-tuple-element.87.old_hi_y), channel_id=1, source_target_pairs={{0,7},{1,0},{2,1},{3,2},{4,3},{5,4},{6,5},{7,6},{8,15},{9,8},{10,9... | collective-permute-start | bytes 196616 | tf_op jit(solution)/shard_map/ppermute | solution.py:283
  96.9 0.6 shard_map.97.local_ref
  97.8 0.6 collective-permute-done.30.lo_y_ref
  98.4 0.9 shard_map.98
  99.6 0.9 broadcast_select_fusion.2
  (95 shorter events, 4.5 us)
Async XLA Ops:
  0.0 0.7 slice-start
  3.2 1.0 copy-start
  5.6 30.4 %collective-permute-start.1 = (f32[64,128]{1,0:T(8,128)S(1)}, f32[64,128]{1,0:T(8,128)S(1)}, u32[]{:S(2)}, u32[]{:S(2)}) collective-permute-start(f32[64,128]{1,0:T(8,128)S(1)} %reshape_squeeze.13.old_hi_x), channel_id=1, source_target_pairs={{0,24},{8,0},{16,8},{24,16},{1,25},{9,1},{17,9},{25,17},{2,26},{10... | collective-permute-start | bytes 98312 | tf_op jit(solution)/shard_map/ppermute | solution.py:279
  5.9 30.2 %collective-permute-start = (f32[64,128]{1,0:T(8,128)S(1)}, f32[64,128]{1,0:T(8,128)S(1)}, u32[]{:S(2)}, u32[]{:S(2)}) collective-permute-start(f32[64,128]{1,0:T(8,128)S(1)} %reshape_squeeze.12.old_lo_x), channel_id=1, source_target_pairs={{0,8},{8,16},{16,24},{24,0},{1,9},{9,17},{17,25},{25,1},{2,10},{10... | collective-permute-start | bytes 98312 | tf_op jit(solution)/shard_map/ppermute | solution.py:278
  8.7 5.2 %copy-start.1 = (f32[4,2,2,4096]{3,2,1,0:T(2,128)S(1)}, f32[4,2,2,4096]{3,2,1,0:T(2,128)}, u32[]{:S(2)}) copy-start(f32[4,2,2,4096]{3,2,1,0:T(2,128)} %param.10) | copy-start | bytes 786436
  8.7 27.4 %collective-permute-start.3 = (f32[64,256]{1,0:T(8,128)S(1)}, f32[64,256]{1,0:T(8,128)S(1)}, u32[]{:S(2)}, u32[]{:S(2)}) collective-permute-start(f32[64,256]{1,0:T(8,128)S(1)} %reshape_squeeze.15.old_hi_y), channel_id=1, source_target_pairs={{0,7},{1,0},{2,1},{3,2},{4,3},{5,4},{6,5},{7,6},{8,15},{9,8},{10,9... | collective-permute-start | bytes 196616 | tf_op jit(solution)/shard_map/ppermute | solution.py:283
  13.1 0.7 copy-start.3
  13.1 0.7 copy-start.4
  13.2 0.7 copy-start.5
  13.3 22.8 %collective-permute-start.2 = (f32[64,256]{1,0:T(8,128)S(1)}, f32[64,256]{1,0:T(8,128)S(1)}, u32[]{:S(2)}, u32[]{:S(2)}) collective-permute-start(f32[64,256]{1,0:T(8,128)S(1)} %reshape_squeeze.14.old_lo_y), channel_id=1, source_target_pairs={{0,1},{1,2},{2,3},{3,4},{4,5},{5,6},{6,7},{7,0},{8,9},{9,10},{10,1... | collective-permute-start | bytes 196616 | tf_op jit(solution)/shard_map/ppermute | solution.py:282
  33.7 0.9 copy-start.2
  37.0 8.9 %collective-permute-start.6 = (f32[64,256]{1,0:T(8,128)S(1)}, f32[64,256]{1,0:T(8,128)S(1)}, u32[]{:S(2)}, u32[]{:S(2)}) collective-permute-start(f32[64,256]{1,0:T(8,128)S(1)} %get-tuple-element.54.old_lo_y), channel_id=1, source_target_pairs={{0,1},{1,2},{2,3},{3,4},{4,5},{5,6},{6,7},{7,0},{8,9},{9,10},{10,1... | collective-permute-start | bytes 196616 | tf_op jit(solution)/shard_map/ppermute | solution.py:282
  37.1 8.8 %collective-permute-start.7 = (f32[64,256]{1,0:T(8,128)S(1)}, f32[64,256]{1,0:T(8,128)S(1)}, u32[]{:S(2)}, u32[]{:S(2)}) collective-permute-start(f32[64,256]{1,0:T(8,128)S(1)} %get-tuple-element.55.old_hi_y), channel_id=1, source_target_pairs={{0,7},{1,0},{2,1},{3,2},{4,3},{5,4},{6,5},{7,6},{8,15},{9,8},{10,9... | collective-permute-start | bytes 196616 | tf_op jit(solution)/shard_map/ppermute | solution.py:283
  41.3 2.4 %collective-permute-start.4 = (f32[64,128]{1,0:T(8,128)S(1)}, f32[64,128]{1,0:T(8,128)S(1)}, u32[]{:S(2)}, u32[]{:S(2)}) collective-permute-start(f32[64,128]{1,0:T(8,128)S(1)} %get-tuple-element.52.old_lo_x), channel_id=1, source_target_pairs={{0,8},{8,16},{16,24},{24,0},{1,9},{9,17},{17,25},{25,1},{2,10},{10... | collective-permute-start | bytes 98312 | tf_op jit(solution)/shard_map/ppermute | solution.py:278
  42.6 3.3 %collective-permute-start.5 = (f32[64,128]{1,0:T(8,128)S(1)}, f32[64,128]{1,0:T(8,128)S(1)}, u32[]{:S(2)}, u32[]{:S(2)}) collective-permute-start(f32[64,128]{1,0:T(8,128)S(1)} %get-tuple-element.53.old_hi_x), channel_id=1, source_target_pairs={{0,24},{8,0},{16,8},{24,16},{1,25},{9,1},{17,9},{25,17},{2,26},{10... | collective-permute-start | bytes 98312 | tf_op jit(solution)/shard_map/ppermute | solution.py:279
  46.8 8.1 %collective-permute-start.10 = (f32[64,256]{1,0:T(8,128)S(1)}, f32[64,256]{1,0:T(8,128)S(1)}, u32[]{:S(2)}, u32[]{:S(2)}) collective-permute-start(f32[64,256]{1,0:T(8,128)S(1)} %get-tuple-element.61.old_lo_y), channel_id=1, source_target_pairs={{0,1},{1,2},{2,3},{3,4},{4,5},{5,6},{6,7},{7,0},{8,9},{9,10},{10,1... | collective-permute-start | bytes 196616 | tf_op jit(solution)/shard_map/ppermute | solution.py:282
  46.9 8.1 %collective-permute-start.11 = (f32[64,256]{1,0:T(8,128)S(1)}, f32[64,256]{1,0:T(8,128)S(1)}, u32[]{:S(2)}, u32[]{:S(2)}) collective-permute-start(f32[64,256]{1,0:T(8,128)S(1)} %get-tuple-element.62.old_hi_y), channel_id=1, source_target_pairs={{0,7},{1,0},{2,1},{3,2},{4,3},{5,4},{6,5},{7,6},{8,15},{9,8},{10,9... | collective-permute-start | bytes 196616 | tf_op jit(solution)/shard_map/ppermute | solution.py:283
  51.0 1.6 %collective-permute-start.8 = (f32[64,128]{1,0:T(8,128)S(1)}, f32[64,128]{1,0:T(8,128)S(1)}, u32[]{:S(2)}, u32[]{:S(2)}) collective-permute-start(f32[64,128]{1,0:T(8,128)S(1)} %get-tuple-element.59.old_lo_x), channel_id=1, source_target_pairs={{0,8},{8,16},{16,24},{24,0},{1,9},{9,17},{17,25},{25,1},{2,10},{10... | collective-permute-start | bytes 98312 | tf_op jit(solution)/shard_map/ppermute | solution.py:278
  51.6 3.3 %collective-permute-start.9 = (f32[64,128]{1,0:T(8,128)S(1)}, f32[64,128]{1,0:T(8,128)S(1)}, u32[]{:S(2)}, u32[]{:S(2)}) collective-permute-start(f32[64,128]{1,0:T(8,128)S(1)} %get-tuple-element.60.old_hi_x), channel_id=1, source_target_pairs={{0,24},{8,0},{16,8},{24,16},{1,25},{9,1},{17,9},{25,17},{2,26},{10... | collective-permute-start | bytes 98312 | tf_op jit(solution)/shard_map/ppermute | solution.py:279
  55.9 8.1 %collective-permute-start.14 = (f32[64,256]{1,0:T(8,128)S(1)}, f32[64,256]{1,0:T(8,128)S(1)}, u32[]{:S(2)}, u32[]{:S(2)}) collective-permute-start(f32[64,256]{1,0:T(8,128)S(1)} %get-tuple-element.66.old_lo_y), channel_id=1, source_target_pairs={{0,1},{1,2},{2,3},{3,4},{4,5},{5,6},{6,7},{7,0},{8,9},{9,10},{10,1... | collective-permute-start | bytes 196616 | tf_op jit(solution)/shard_map/ppermute | solution.py:282
  55.9 8.1 %collective-permute-start.15 = (f32[64,256]{1,0:T(8,128)S(1)}, f32[64,256]{1,0:T(8,128)S(1)}, u32[]{:S(2)}, u32[]{:S(2)}) collective-permute-start(f32[64,256]{1,0:T(8,128)S(1)} %get-tuple-element.67.old_hi_y), channel_id=1, source_target_pairs={{0,7},{1,0},{2,1},{3,2},{4,3},{5,4},{6,5},{7,6},{8,15},{9,8},{10,9... | collective-permute-start | bytes 196616 | tf_op jit(solution)/shard_map/ppermute | solution.py:283
  60.1 1.6 %collective-permute-start.12 = (f32[64,128]{1,0:T(8,128)S(1)}, f32[64,128]{1,0:T(8,128)S(1)}, u32[]{:S(2)}, u32[]{:S(2)}) collective-permute-start(f32[64,128]{1,0:T(8,128)S(1)} %get-tuple-element.64.old_lo_x), channel_id=1, source_target_pairs={{0,8},{8,16},{16,24},{24,0},{1,9},{9,17},{17,25},{25,1},{2,10},{10... | collective-permute-start | bytes 98312 | tf_op jit(solution)/shard_map/ppermute | solution.py:278
  60.6 3.3 %collective-permute-start.13 = (f32[64,128]{1,0:T(8,128)S(1)}, f32[64,128]{1,0:T(8,128)S(1)}, u32[]{:S(2)}, u32[]{:S(2)}) collective-permute-start(f32[64,128]{1,0:T(8,128)S(1)} %get-tuple-element.65.old_hi_x), channel_id=1, source_target_pairs={{0,24},{8,0},{16,8},{24,16},{1,25},{9,1},{17,9},{25,17},{2,26},{10... | collective-permute-start | bytes 98312 | tf_op jit(solution)/shard_map/ppermute | solution.py:279
  64.9 8.1 %collective-permute-start.18 = (f32[64,256]{1,0:T(8,128)S(1)}, f32[64,256]{1,0:T(8,128)S(1)}, u32[]{:S(2)}, u32[]{:S(2)}) collective-permute-start(f32[64,256]{1,0:T(8,128)S(1)} %get-tuple-element.71.old_lo_y), channel_id=1, source_target_pairs={{0,1},{1,2},{2,3},{3,4},{4,5},{5,6},{6,7},{7,0},{8,9},{9,10},{10,1... | collective-permute-start | bytes 196616 | tf_op jit(solution)/shard_map/ppermute | solution.py:282
  65.0 8.1 %collective-permute-start.19 = (f32[64,256]{1,0:T(8,128)S(1)}, f32[64,256]{1,0:T(8,128)S(1)}, u32[]{:S(2)}, u32[]{:S(2)}) collective-permute-start(f32[64,256]{1,0:T(8,128)S(1)} %get-tuple-element.72.old_hi_y), channel_id=1, source_target_pairs={{0,7},{1,0},{2,1},{3,2},{4,3},{5,4},{6,5},{7,6},{8,15},{9,8},{10,9... | collective-permute-start | bytes 196616 | tf_op jit(solution)/shard_map/ppermute | solution.py:283
  69.1 1.6 %collective-permute-start.16 = (f32[64,128]{1,0:T(8,128)S(1)}, f32[64,128]{1,0:T(8,128)S(1)}, u32[]{:S(2)}, u32[]{:S(2)}) collective-permute-start(f32[64,128]{1,0:T(8,128)S(1)} %get-tuple-element.69.old_lo_x), channel_id=1, source_target_pairs={{0,8},{8,16},{16,24},{24,0},{1,9},{9,17},{17,25},{25,1},{2,10},{10... | collective-permute-start | bytes 98312 | tf_op jit(solution)/shard_map/ppermute | solution.py:278
  69.7 3.3 %collective-permute-start.17 = (f32[64,128]{1,0:T(8,128)S(1)}, f32[64,128]{1,0:T(8,128)S(1)}, u32[]{:S(2)}, u32[]{:S(2)}) collective-permute-start(f32[64,128]{1,0:T(8,128)S(1)} %get-tuple-element.70.old_hi_x), channel_id=1, source_target_pairs={{0,24},{8,0},{16,8},{24,16},{1,25},{9,1},{17,9},{25,17},{2,26},{10... | collective-permute-start | bytes 98312 | tf_op jit(solution)/shard_map/ppermute | solution.py:279
  73.9 8.1 %collective-permute-start.22 = (f32[64,256]{1,0:T(8,128)S(1)}, f32[64,256]{1,0:T(8,128)S(1)}, u32[]{:S(2)}, u32[]{:S(2)}) collective-permute-start(f32[64,256]{1,0:T(8,128)S(1)} %get-tuple-element.76.old_lo_y), channel_id=1, source_target_pairs={{0,1},{1,2},{2,3},{3,4},{4,5},{5,6},{6,7},{7,0},{8,9},{9,10},{10,1... | collective-permute-start | bytes 196616 | tf_op jit(solution)/shard_map/ppermute | solution.py:282
  74.0 8.1 %collective-permute-start.23 = (f32[64,256]{1,0:T(8,128)S(1)}, f32[64,256]{1,0:T(8,128)S(1)}, u32[]{:S(2)}, u32[]{:S(2)}) collective-permute-start(f32[64,256]{1,0:T(8,128)S(1)} %get-tuple-element.77.old_hi_y), channel_id=1, source_target_pairs={{0,7},{1,0},{2,1},{3,2},{4,3},{5,4},{6,5},{7,6},{8,15},{9,8},{10,9... | collective-permute-start | bytes 196616 | tf_op jit(solution)/shard_map/ppermute | solution.py:283
  78.1 1.6 %collective-permute-start.20 = (f32[64,128]{1,0:T(8,128)S(1)}, f32[64,128]{1,0:T(8,128)S(1)}, u32[]{:S(2)}, u32[]{:S(2)}) collective-permute-start(f32[64,128]{1,0:T(8,128)S(1)} %get-tuple-element.74.old_lo_x), channel_id=1, source_target_pairs={{0,8},{8,16},{16,24},{24,0},{1,9},{9,17},{17,25},{25,1},{2,10},{10... | collective-permute-start | bytes 98312 | tf_op jit(solution)/shard_map/ppermute | solution.py:278
  78.7 3.3 %collective-permute-start.21 = (f32[64,128]{1,0:T(8,128)S(1)}, f32[64,128]{1,0:T(8,128)S(1)}, u32[]{:S(2)}, u32[]{:S(2)}) collective-permute-start(f32[64,128]{1,0:T(8,128)S(1)} %get-tuple-element.75.old_hi_x), channel_id=1, source_target_pairs={{0,24},{8,0},{16,8},{24,16},{1,25},{9,1},{17,9},{25,17},{2,26},{10... | collective-permute-start | bytes 98312 | tf_op jit(solution)/shard_map/ppermute | solution.py:279
  83.0 8.1 %collective-permute-start.26 = (f32[64,256]{1,0:T(8,128)S(1)}, f32[64,256]{1,0:T(8,128)S(1)}, u32[]{:S(2)}, u32[]{:S(2)}) collective-permute-start(f32[64,256]{1,0:T(8,128)S(1)} %get-tuple-element.81.old_lo_y), channel_id=1, source_target_pairs={{0,1},{1,2},{2,3},{3,4},{4,5},{5,6},{6,7},{7,0},{8,9},{9,10},{10,1... | collective-permute-start | bytes 196616 | tf_op jit(solution)/shard_map/ppermute | solution.py:282
  83.0 8.1 %collective-permute-start.27 = (f32[64,256]{1,0:T(8,128)S(1)}, f32[64,256]{1,0:T(8,128)S(1)}, u32[]{:S(2)}, u32[]{:S(2)}) collective-permute-start(f32[64,256]{1,0:T(8,128)S(1)} %get-tuple-element.82.old_hi_y), channel_id=1, source_target_pairs={{0,7},{1,0},{2,1},{3,2},{4,3},{5,4},{6,5},{7,6},{8,15},{9,8},{10,9... | collective-permute-start | bytes 196616 | tf_op jit(solution)/shard_map/ppermute | solution.py:283
  87.2 1.6 %collective-permute-start.24 = (f32[64,128]{1,0:T(8,128)S(1)}, f32[64,128]{1,0:T(8,128)S(1)}, u32[]{:S(2)}, u32[]{:S(2)}) collective-permute-start(f32[64,128]{1,0:T(8,128)S(1)} %get-tuple-element.79.old_lo_x), channel_id=1, source_target_pairs={{0,8},{8,16},{16,24},{24,0},{1,9},{9,17},{17,25},{25,1},{2,10},{10... | collective-permute-start | bytes 98312 | tf_op jit(solution)/shard_map/ppermute | solution.py:278
  87.8 3.3 %collective-permute-start.25 = (f32[64,128]{1,0:T(8,128)S(1)}, f32[64,128]{1,0:T(8,128)S(1)}, u32[]{:S(2)}, u32[]{:S(2)}) collective-permute-start(f32[64,128]{1,0:T(8,128)S(1)} %get-tuple-element.80.old_hi_x), channel_id=1, source_target_pairs={{0,24},{8,0},{16,8},{24,16},{1,25},{9,1},{17,9},{25,17},{2,26},{10... | collective-permute-start | bytes 98312 | tf_op jit(solution)/shard_map/ppermute | solution.py:279
  92.0 5.8 %collective-permute-start.28 = (f32[64,128]{1,0:T(8,128)S(1)}, f32[64,128]{1,0:T(8,128)S(1)}, u32[]{:S(2)}, u32[]{:S(2)}) collective-permute-start(f32[64,128]{1,0:T(8,128)S(1)} %get-tuple-element.84.old_lo_x), channel_id=1, source_target_pairs={{0,8},{8,16},{16,24},{24,0},{1,9},{9,17},{17,25},{25,1},{2,10},{10... | collective-permute-start | bytes 98312 | tf_op jit(solution)/shard_map/ppermute | solution.py:278
  92.1 4.7 %copy-start.6 = (s32[4,2,2]{0,2,1:T(2,128)S(1)}, s32[4,2,2]{0,2,1:T(2,128)}, u32[]{:S(2)}) copy-start(s32[4,2,2]{0,2,1:T(2,128)} %param.14) | copy-start | bytes 196
  92.1 5.7 %collective-permute-start.29 = (f32[64,128]{1,0:T(8,128)S(1)}, f32[64,128]{1,0:T(8,128)S(1)}, u32[]{:S(2)}, u32[]{:S(2)}) collective-permute-start(f32[64,128]{1,0:T(8,128)S(1)} %get-tuple-element.85.old_hi_x), channel_id=1, source_target_pairs={{0,24},{8,0},{16,8},{24,16},{1,25},{9,1},{17,9},{25,17},{2,26},{10... | collective-permute-start | bytes 98312 | tf_op jit(solution)/shard_map/ppermute | solution.py:279
  92.6 5.8 %collective-permute-start.30 = (f32[64,256]{1,0:T(8,128)S(1)}, f32[64,256]{1,0:T(8,128)S(1)}, u32[]{:S(2)}, u32[]{:S(2)}) collective-permute-start(f32[64,256]{1,0:T(8,128)S(1)} %get-tuple-element.86.old_lo_y), channel_id=1, source_target_pairs={{0,1},{1,2},{2,3},{3,4},{4,5},{5,6},{6,7},{7,0},{8,9},{9,10},{10,1... | collective-permute-start | bytes 196616 | tf_op jit(solution)/shard_map/ppermute | solution.py:282
  92.6 5.8 %collective-permute-start.31 = (f32[64,256]{1,0:T(8,128)S(1)}, f32[64,256]{1,0:T(8,128)S(1)}, u32[]{:S(2)}, u32[]{:S(2)}) collective-permute-start(f32[64,256]{1,0:T(8,128)S(1)} %get-tuple-element.87.old_hi_y), channel_id=1, source_target_pairs={{0,7},{1,0},{2,1},{3,2},{4,3},{5,4},{6,5},{7,6},{8,15},{9,8},{10,9... | collective-permute-start | bytes 196616 | tf_op jit(solution)/shard_map/ppermute | solution.py:283

commit v12 on v10

--- a/solution.py
+++ b/solution.py
@@ -122,7 +122,14 @@
         high = lax.index_in_dim(values, 1, axis=axis, keepdims=False)
         return jnp.where(mask, low, high)
 
-    member_inverse = [inverse[:, paint * columns * P_SIZE:(paint + 1) * columns * P_SIZE] for paint in (0, 1)]
+    member_inverse = [
+        jnp.where(
+            first_is[paint].reshape(1, columns, 1),
+            inverse[:, :, 0],
+            inverse[:, :, 1],
+        ).reshape(P_SIZE, columns * P_SIZE)
+        for paint in (0, 1)
+    ]
     face_row = jnp.transpose(face_blocks, (1, 0, 2)).reshape(P_SIZE, 6 * P_SIZE)
     member_target = [pick(forcing, paint).reshape(columns, P_SIZE, R) for paint in (0, 1)]
     member_weight = [pick(weight, paint, axis=3)[..., None] for paint in (0, 1)]
@@ -278,10 +285,18 @@
     start_state = to_lanes(pick(initial, 1))
     first_sends = send_buffers(start_state, span_x)
     first_halos = trade(first_sends)
-    by_colour = jnp.stack([pick(blocks, paint) for paint in (0, 1)]).reshape(count, P_SIZE, P_SIZE)
-    inverse = block_inverses(by_colour, lanes_out=True)
+    inverse = block_inverses(blocks.reshape(count, P_SIZE, P_SIZE), lanes_out=True).reshape(
+        P_SIZE, columns, span_z, P_SIZE
+    )
     weight = jnp.where(neighbours == empty_slot, 0.0, strength * strong.astype(jnp.float32))
-    member_inverse = [inverse[:, paint * columns * P_SIZE:(paint + 1) * columns * P_SIZE] for paint in (0, 1)]
+    member_inverse = [
+        jnp.where(
+            first_is[paint].reshape(1, columns, 1),
+            inverse[:, :, 0],
+            inverse[:, :, 1],
+        ).reshape(P_SIZE, columns * P_SIZE)
+        for paint in (0, 1)
+    ]
     face_row = jnp.transpose(face_blocks, (1, 0, 2)).reshape(P_SIZE, 6 * P_SIZE)
     member_target = [to_lanes(pick(forcing, paint)) for paint in (0, 1)]
     member_weight = [

time: 103 us -> 104 us (level); the launches traced: 101 us -> 104 us
  waiting for transfers between devices: 20.7 us -> 22.4 us
  starting transfers between devices: 41.2 us -> 42.6 us
    ppermute x8, waiting for transfers between devices: 13.9 us -> 16.2 us  [trade(): lax.ppermute(sends[1], 'gx', shift_pairs('gx', -1))]
    ppermute x8, starting transfers between devices: 0.39 us -> 2.51 us  [trade(): lax.ppermute(sends[2], 'gy', shift_pairs('gy', 1))]
    ppermute x8, starting transfers between devices: 33.4 us -> 32.1 us  [trade(): lax.ppermute(sends[3], 'gy', shift_pairs('gy', -1))]
    ppermute x8, waiting for transfers between devices: 1.2 us -> 0.02 us  [trade(): lax.ppermute(sends[2], 'gy', shift_pairs('gy', 1))]
    ppermute x8, starting transfers between devices: 6.78 us -> 7.92 us  [trade(): lax.ppermute(sends[0], 'gx', shift_pairs('gx', 1))]
  transfers between devices with their start and end apart: 32 -> 32, of which waited for: 13 -> 14; matrix products, arithmetic and copies ran while one was open for 5% -> 5% of each run, Pallas kernels for 17% -> 17%
where the time goes in v12:
time: 104 us
  starting transfers between devices  42.6 us (41%)
  Pallas kernels  25.5 us (25%)
  waiting for transfers between devices  22.4 us (22%)
  local copies, waits for them, and re-layouts  11.9 us (11%)
  other arithmetic  1.15 us (1%)
    ppermute x8, starting transfers between devices, trade(): lax.ppermute(sends[3], 'gy', shift_pairs('gy', -1))  32.1 us
    pallas_call x1, Pallas kernels, block_inverses(): pl.pallas_call(functools.partial(_gauss_jordan_kernel, n=n, nb=nb), out_s...  17.5 us
    ppermute x8, waiting for transfers between devices, trade(): lax.ppermute(sends[1], 'gx', shift_pairs('gx', -1))  16.2 us
    pallas_call x8, Pallas kernels, half_sweep(): pl.pallas_call(functools.partial(_half_sweep_kernel, span_x=span_x), out_...  7.98 us
    ppermute x8, starting transfers between devices, trade(): lax.ppermute(sends[0], 'gx', shift_pairs('gx', 1))  7.92 us
    ppermute x8, waiting for transfers between devices, trade(): lax.ppermute(sends[0], 'gx', shift_pairs('gx', 1))  6.19 us
    slice x3, local copies, waits for them, and re-layouts, pick(): high = lax.index_in_dim(values, 1, axis=axis, keepdims=False)  2.68 us
    ppermute x8, starting transfers between devices, trade(): lax.ppermute(sends[2], 'gy', shift_pairs('gy', 1))  2.51 us
  transfers between devices with their start and end apart: 32, of which 14 were waited for; matrix products, arithmetic and copies ran while one was open for 5% of the time, Pallas kernels for 17%

profile of v12, /device:TPU:1, one launch (start us, length us, event | category | flops | bytes accessed | tf_op | source)
XLA Modules:
  0.0 104.0 jit_solution(2388745262572112639)
XLA Ops:
  0.0 0.7 slice-done
  1.1 1.9 %slice_reduce_fusion.2 = (f32[4,2,4096]{2,1,0:T(2,128)S(1)}, f32[4,2,4096]{2,1,0:T(2,128)S(1)}) fusion(f32[4,2,2,4096]{3,2,1,0:T(2,128)} %param.9), kind=kLoop, calls=%fused_computation.7 | loop fusion | bytes 524288 | tf_op jit(solution)/shard_map/slice | solution.py:279
  3.0 0.2 squeeze.32
  3.2 0.2 squeeze.33
  3.4 0.7 copy-done.1
  4.1 0.8 slice_reduce_fusion
  4.9 0.2 squeeze.36
  5.1 0.2 squeeze.37
  5.6 0.1 reshape_squeeze.14.old_lo_y
  5.7 2.1 %collective-permute-start.2 = (f32[64,256]{1,0:T(8,128)S(1)}, f32[64,256]{1,0:T(8,128)S(1)}, u32[]{:S(2)}, u32[]{:S(2)}) collective-permute-start(f32[64,256]{1,0:T(8,128)S(1)} %reshape_squeeze.14.old_lo_y), channel_id=1, source_target_pairs={{0,1},{1,2},{2,3},{3,4},{4,5},{5,6},{6,7},{7,0},{8,9},{9,10},{10,1... | collective-permute-start | bytes 196616 | tf_op jit(solution)/shard_map/ppermute | solution.py:257
  8.1 3.1 %collective-permute-start.3 = (f32[64,256]{1,0:T(8,128)S(1)}, f32[64,256]{1,0:T(8,128)S(1)}, u32[]{:S(2)}, u32[]{:S(2)}) collective-permute-start(f32[64,256]{1,0:T(8,128)S(1)} %reshape_squeeze.15.old_hi_y), channel_id=1, source_target_pairs={{0,7},{1,0},{2,1},{3,2},{4,3},{5,4},{6,5},{7,6},{8,15},{9,8},{10,9... | collective-permute-start | bytes 196616 | tf_op jit(solution)/shard_map/ppermute | solution.py:258
  11.3 2.2 %collective-permute-start = (f32[64,128]{1,0:T(8,128)S(1)}, f32[64,128]{1,0:T(8,128)S(1)}, u32[]{:S(2)}, u32[]{:S(2)}) collective-permute-start(f32[64,128]{1,0:T(8,128)S(1)} %reshape_squeeze.12.old_lo_x), channel_id=1, source_target_pairs={{0,8},{8,16},{16,24},{24,0},{1,9},{9,17},{17,25},{25,1},{2,10},{10... | collective-permute-start | bytes 98312 | tf_op jit(solution)/shard_map/ppermute | solution.py:253
  14.1 0.3 reshape.104
  14.4 0.3 copy.98
  14.7 0.2 copy.99.a_ref
  14.9 17.5 %shard_map.82 = f32[64,1024]{1,0:T(8,128)S(1)} custom-call(f32[64,1024]{1,0:T(8,128)S(1)} %copy.99.a_ref), custom_call_target="tpu_custom_call", output_to_operand_aliasing={{}: (0, {})} | custom-call | flops 8388608000 | bytes 524288 | tf_op jit(solution)/shard_map/pallas_call | solution.py:75
  32.4 0.2 copy.100
  32.6 0.3 copy.101
  32.9 0.2 copy.102
  33.2 0.2 copy.103
  33.5 0.5 copy-done.3
  34.2 0.2 copy.104
  34.7 0.2 copy.91
  35.0 0.8 copy-done.2
  36.1 1.0 shard_map.83
  37.2 4.1 %collective-permute-start.7 = (f32[64,256]{1,0:T(8,128)S(1)}, f32[64,256]{1,0:T(8,128)S(1)}, u32[]{:S(2)}, u32[]{:S(2)}) collective-permute-start(f32[64,256]{1,0:T(8,128)S(1)} %get-tuple-element.54.old_hi_y), channel_id=1, source_target_pairs={{0,7},{1,0},{2,1},{3,2},{4,3},{5,4},{6,5},{7,6},{8,15},{9,8},{10,9... | collective-permute-start | bytes 196616 | tf_op jit(solution)/shard_map/ppermute | solution.py:258
  41.3 2.3 %collective-permute-start.4 = (f32[64,128]{1,0:T(8,128)S(1)}, f32[64,128]{1,0:T(8,128)S(1)}, u32[]{:S(2)}, u32[]{:S(2)}) collective-permute-start(f32[64,128]{1,0:T(8,128)S(1)} %get-tuple-element.51.old_lo_x), channel_id=1, source_target_pairs={{0,8},{8,16},{16,24},{24,0},{1,9},{9,17},{17,25},{25,1},{2,10},{10... | collective-permute-start | bytes 98312 | tf_op jit(solution)/shard_map/ppermute | solution.py:253
  43.6 0.2 copy.106
  44.1 0.5 collective-permute-done.4.lo_x_ref
  44.6 2.3 %collective-permute-done.5.hi_x_ref = f32[64,128]{1,0:T(8,128)S(1)} collective-permute-done((f32[64,128]{1,0:T(8,128)S(1)}, f32[64,128]{1,0:T(8,128)S(1)}, u32[]{:S(2)}, u32[]{:S(2)}) %collective-permute-start.5) | collective-permute-done | bytes 32800 | tf_op jit(solution)/shard_map/ppermute | solution.py:254
  47.0 1.0 shard_map.84
  48.0 4.1 %collective-permute-start.11 = (f32[64,256]{1,0:T(8,128)S(1)}, f32[64,256]{1,0:T(8,128)S(1)}, u32[]{:S(2)}, u32[]{:S(2)}) collective-permute-start(f32[64,256]{1,0:T(8,128)S(1)} %get-tuple-element.62.old_hi_y), channel_id=1, source_target_pairs={{0,7},{1,0},{2,1},{3,2},{4,3},{5,4},{6,5},{7,6},{8,15},{9,8},{10,9... | collective-permute-start | bytes 196616 | tf_op jit(solution)/shard_map/ppermute | solution.py:258
  52.2 0.6 collective-permute-start.8
  52.8 1.0 collective-permute-done.8.lo_x_ref
  53.8 2.3 %collective-permute-done.9.hi_x_ref = f32[64,128]{1,0:T(8,128)S(1)} collective-permute-done((f32[64,128]{1,0:T(8,128)S(1)}, f32[64,128]{1,0:T(8,128)S(1)}, u32[]{:S(2)}, u32[]{:S(2)}) %collective-permute-start.9) | collective-permute-done | bytes 32800 | tf_op jit(solution)/shard_map/ppermute | solution.py:254
  56.1 1.0 shard_map.85
  57.2 4.1 %collective-permute-start.15 = (f32[64,256]{1,0:T(8,128)S(1)}, f32[64,256]{1,0:T(8,128)S(1)}, u32[]{:S(2)}, u32[]{:S(2)}) collective-permute-start(f32[64,256]{1,0:T(8,128)S(1)} %get-tuple-element.67.old_hi_y), channel_id=1, source_target_pairs={{0,7},{1,0},{2,1},{3,2},{4,3},{5,4},{6,5},{7,6},{8,15},{9,8},{10,9... | collective-permute-start | bytes 196616 | tf_op jit(solution)/shard_map/ppermute | solution.py:258
  61.3 0.6 collective-permute-start.12
  61.9 1.0 collective-permute-done.12.lo_x_ref
  62.9 2.3 %collective-permute-done.13.hi_x_ref = f32[64,128]{1,0:T(8,128)S(1)} collective-permute-done((f32[64,128]{1,0:T(8,128)S(1)}, f32[64,128]{1,0:T(8,128)S(1)}, u32[]{:S(2)}, u32[]{:S(2)}) %collective-permute-start.13) | collective-permute-done | bytes 32800 | tf_op jit(solution)/shard_map/ppermute | solution.py:254
  65.2 1.0 shard_map.86
  66.3 4.1 %collective-permute-start.19 = (f32[64,256]{1,0:T(8,128)S(1)}, f32[64,256]{1,0:T(8,128)S(1)}, u32[]{:S(2)}, u32[]{:S(2)}) collective-permute-start(f32[64,256]{1,0:T(8,128)S(1)} %get-tuple-element.72.old_hi_y), channel_id=1, source_target_pairs={{0,7},{1,0},{2,1},{3,2},{4,3},{5,4},{6,5},{7,6},{8,15},{9,8},{10,9... | collective-permute-start | bytes 196616 | tf_op jit(solution)/shard_map/ppermute | solution.py:258
  70.5 0.6 collective-permute-start.16
  71.0 1.0 collective-permute-done.16.lo_x_ref
  72.1 2.3 %collective-permute-done.17.hi_x_ref = f32[64,128]{1,0:T(8,128)S(1)} collective-permute-done((f32[64,128]{1,0:T(8,128)S(1)}, f32[64,128]{1,0:T(8,128)S(1)}, u32[]{:S(2)}, u32[]{:S(2)}) %collective-permute-start.17) | collective-permute-done | bytes 32800 | tf_op jit(solution)/shard_map/ppermute | solution.py:254
  74.4 1.0 shard_map.87
  75.4 4.1 %collective-permute-start.23 = (f32[64,256]{1,0:T(8,128)S(1)}, f32[64,256]{1,0:T(8,128)S(1)}, u32[]{:S(2)}, u32[]{:S(2)}) collective-permute-start(f32[64,256]{1,0:T(8,128)S(1)} %get-tuple-element.77.old_hi_y), channel_id=1, source_target_pairs={{0,7},{1,0},{2,1},{3,2},{4,3},{5,4},{6,5},{7,6},{8,15},{9,8},{10,9... | collective-permute-start | bytes 196616 | tf_op jit(solution)/shard_map/ppermute | solution.py:258
  79.6 0.6 collective-permute-start.20
  80.2 1.0 collective-permute-done.20.lo_x_ref
  81.2 2.3 %collective-permute-done.21.hi_x_ref = f32[64,128]{1,0:T(8,128)S(1)} collective-permute-done((f32[64,128]{1,0:T(8,128)S(1)}, f32[64,128]{1,0:T(8,128)S(1)}, u32[]{:S(2)}, u32[]{:S(2)}) %collective-permute-start.21) | collective-permute-done | bytes 32800 | tf_op jit(solution)/shard_map/ppermute | solution.py:254
  83.5 1.0 shard_map.88
  84.6 4.1 %collective-permute-start.27 = (f32[64,256]{1,0:T(8,128)S(1)}, f32[64,256]{1,0:T(8,128)S(1)}, u32[]{:S(2)}, u32[]{:S(2)}) collective-permute-start(f32[64,256]{1,0:T(8,128)S(1)} %get-tuple-element.82.old_hi_y), channel_id=1, source_target_pairs={{0,7},{1,0},{2,1},{3,2},{4,3},{5,4},{6,5},{7,6},{8,15},{9,8},{10,9... | collective-permute-start | bytes 196616 | tf_op jit(solution)/shard_map/ppermute | solution.py:258
  88.7 0.6 collective-permute-start.24
  89.3 1.0 collective-permute-done.24.lo_x_ref
  90.3 2.3 %collective-permute-done.25.hi_x_ref = f32[64,128]{1,0:T(8,128)S(1)} collective-permute-done((f32[64,128]{1,0:T(8,128)S(1)}, f32[64,128]{1,0:T(8,128)S(1)}, u32[]{:S(2)}, u32[]{:S(2)}) %collective-permute-start.25) | collective-permute-done | bytes 32800 | tf_op jit(solution)/shard_map/ppermute | solution.py:254
  92.7 1.0 shard_map.89
  93.7 4.1 %collective-permute-start.31 = (f32[64,256]{1,0:T(8,128)S(1)}, f32[64,256]{1,0:T(8,128)S(1)}, u32[]{:S(2)}, u32[]{:S(2)}) collective-permute-start(f32[64,256]{1,0:T(8,128)S(1)} %get-tuple-element.87.old_hi_y), channel_id=1, source_target_pairs={{0,7},{1,0},{2,1},{3,2},{4,3},{5,4},{6,5},{7,6},{8,15},{9,8},{10,9... | collective-permute-start | bytes 196616 | tf_op jit(solution)/shard_map/ppermute | solution.py:258
  97.9 0.6 collective-permute-start.28
  98.7 0.1 broadcast_in_dim.110
  98.9 0.6 collective-permute-done.28.lo_x_ref
  99.5 2.3 %collective-permute-done.29.hi_x_ref = f32[64,128]{1,0:T(8,128)S(1)} collective-permute-done((f32[64,128]{1,0:T(8,128)S(1)}, f32[64,128]{1,0:T(8,128)S(1)}, u32[]{:S(2)}, u32[]{:S(2)}) %collective-permute-start.29) | collective-permute-done | bytes 32800 | tf_op jit(solution)/shard_map/ppermute | solution.py:254
  101.8 1.0 shard_map.90
  103.0 0.1 broadcast_in_dim.112
  103.1 0.9 broadcast_select_fusion
  (91 shorter events, 3.9 us)
Async XLA Ops:
  0.0 0.7 slice-start
  3.2 1.0 copy-start.1
  5.7 30.3 %collective-permute-start.2 = (f32[64,256]{1,0:T(8,128)S(1)}, f32[64,256]{1,0:T(8,128)S(1)}, u32[]{:S(2)}, u32[]{:S(2)}) collective-permute-start(f32[64,256]{1,0:T(8,128)S(1)} %reshape_squeeze.14.old_lo_y), channel_id=1, source_target_pairs={{0,1},{1,2},{2,3},{3,4},{4,5},{5,6},{6,7},{7,0},{8,9},{9,10},{10,1... | collective-permute-start | bytes 196616 | tf_op jit(solution)/shard_map/ppermute | solution.py:257
  8.1 28.0 %collective-permute-start.3 = (f32[64,256]{1,0:T(8,128)S(1)}, f32[64,256]{1,0:T(8,128)S(1)}, u32[]{:S(2)}, u32[]{:S(2)}) collective-permute-start(f32[64,256]{1,0:T(8,128)S(1)} %reshape_squeeze.15.old_hi_y), channel_id=1, source_target_pairs={{0,7},{1,0},{2,1},{3,2},{4,3},{5,4},{6,5},{7,6},{8,15},{9,8},{10,9... | collective-permute-start | bytes 196616 | tf_op jit(solution)/shard_map/ppermute | solution.py:258
  11.2 2.9 %copy-start = (f32[4,2,2,4096]{3,2,1,0:T(2,128)S(1)}, f32[4,2,2,4096]{3,2,1,0:T(2,128)}, u32[]{:S(2)}) copy-start(f32[4,2,2,4096]{3,2,1,0:T(2,128)} %param.10) | copy-start | bytes 786436
  11.3 24.7 %collective-permute-start = (f32[64,128]{1,0:T(8,128)S(1)}, f32[64,128]{1,0:T(8,128)S(1)}, u32[]{:S(2)}, u32[]{:S(2)}) collective-permute-start(f32[64,128]{1,0:T(8,128)S(1)} %reshape_squeeze.12.old_lo_x), channel_id=1, source_target_pairs={{0,8},{8,16},{16,24},{24,0},{1,9},{9,17},{17,25},{25,1},{2,10},{10... | collective-permute-start | bytes 98312 | tf_op jit(solution)/shard_map/ppermute | solution.py:253
  13.7 22.3 %collective-permute-start.1 = (f32[64,128]{1,0:T(8,128)S(1)}, f32[64,128]{1,0:T(8,128)S(1)}, u32[]{:S(2)}, u32[]{:S(2)}) collective-permute-start(f32[64,128]{1,0:T(8,128)S(1)} %reshape_squeeze.13.old_hi_x), channel_id=1, source_target_pairs={{0,24},{8,0},{16,8},{24,16},{1,25},{9,1},{17,9},{25,17},{2,26},{10... | collective-permute-start | bytes 98312 | tf_op jit(solution)/shard_map/ppermute | solution.py:254
  33.3 0.7 copy-start.3
  33.4 0.7 copy-start.4
  33.4 0.7 copy-start.5
  34.9 0.9 copy-start.2
  37.1 9.9 %collective-permute-start.6 = (f32[64,256]{1,0:T(8,128)S(1)}, f32[64,256]{1,0:T(8,128)S(1)}, u32[]{:S(2)}, u32[]{:S(2)}) collective-permute-start(f32[64,256]{1,0:T(8,128)S(1)} %get-tuple-element.53.old_lo_y), channel_id=1, source_target_pairs={{0,1},{1,2},{2,3},{3,4},{4,5},{5,6},{6,7},{7,0},{8,9},{9,10},{10,1... | collective-permute-start | bytes 196616 | tf_op jit(solution)/shard_map/ppermute | solution.py:257
  37.2 9.8 %collective-permute-start.7 = (f32[64,256]{1,0:T(8,128)S(1)}, f32[64,256]{1,0:T(8,128)S(1)}, u32[]{:S(2)}, u32[]{:S(2)}) collective-permute-start(f32[64,256]{1,0:T(8,128)S(1)} %get-tuple-element.54.old_hi_y), channel_id=1, source_target_pairs={{0,7},{1,0},{2,1},{3,2},{4,3},{5,4},{6,5},{7,6},{8,15},{9,8},{10,9... | collective-permute-start | bytes 196616 | tf_op jit(solution)/shard_map/ppermute | solution.py:258
  41.3 3.3 %collective-permute-start.4 = (f32[64,128]{1,0:T(8,128)S(1)}, f32[64,128]{1,0:T(8,128)S(1)}, u32[]{:S(2)}, u32[]{:S(2)}) collective-permute-start(f32[64,128]{1,0:T(8,128)S(1)} %get-tuple-element.51.old_lo_x), channel_id=1, source_target_pairs={{0,8},{8,16},{16,24},{24,0},{1,9},{9,17},{17,25},{25,1},{2,10},{10... | collective-permute-start | bytes 98312 | tf_op jit(solution)/shard_map/ppermute | solution.py:253
  43.6 3.3 %collective-permute-start.5 = (f32[64,128]{1,0:T(8,128)S(1)}, f32[64,128]{1,0:T(8,128)S(1)}, u32[]{:S(2)}, u32[]{:S(2)}) collective-permute-start(f32[64,128]{1,0:T(8,128)S(1)} %get-tuple-element.52.old_hi_x), channel_id=1, source_target_pairs={{0,24},{8,0},{16,8},{24,16},{1,25},{9,1},{17,9},{25,17},{2,26},{10... | collective-permute-start | bytes 98312 | tf_op jit(solution)/shard_map/ppermute | solution.py:254
  48.0 8.1 %collective-permute-start.10 = (f32[64,256]{1,0:T(8,128)S(1)}, f32[64,256]{1,0:T(8,128)S(1)}, u32[]{:S(2)}, u32[]{:S(2)}) collective-permute-start(f32[64,256]{1,0:T(8,128)S(1)} %get-tuple-element.61.old_lo_y), channel_id=1, source_target_pairs={{0,1},{1,2},{2,3},{3,4},{4,5},{5,6},{6,7},{7,0},{8,9},{9,10},{10,1... | collective-permute-start | bytes 196616 | tf_op jit(solution)/shard_map/ppermute | solution.py:257
  48.0 8.1 %collective-permute-start.11 = (f32[64,256]{1,0:T(8,128)S(1)}, f32[64,256]{1,0:T(8,128)S(1)}, u32[]{:S(2)}, u32[]{:S(2)}) collective-permute-start(f32[64,256]{1,0:T(8,128)S(1)} %get-tuple-element.62.old_hi_y), channel_id=1, source_target_pairs={{0,7},{1,0},{2,1},{3,2},{4,3},{5,4},{6,5},{7,6},{8,15},{9,8},{10,9... | collective-permute-start | bytes 196616 | tf_op jit(solution)/shard_map/ppermute | solution.py:258
  52.2 1.6 %collective-permute-start.8 = (f32[64,128]{1,0:T(8,128)S(1)}, f32[64,128]{1,0:T(8,128)S(1)}, u32[]{:S(2)}, u32[]{:S(2)}) collective-permute-start(f32[64,128]{1,0:T(8,128)S(1)} %get-tuple-element.59.old_lo_x), channel_id=1, source_target_pairs={{0,8},{8,16},{16,24},{24,0},{1,9},{9,17},{17,25},{25,1},{2,10},{10... | collective-permute-start | bytes 98312 | tf_op jit(solution)/shard_map/ppermute | solution.py:253
  52.8 3.3 %collective-permute-start.9 = (f32[64,128]{1,0:T(8,128)S(1)}, f32[64,128]{1,0:T(8,128)S(1)}, u32[]{:S(2)}, u32[]{:S(2)}) collective-permute-start(f32[64,128]{1,0:T(8,128)S(1)} %get-tuple-element.60.old_hi_x), channel_id=1, source_target_pairs={{0,24},{8,0},{16,8},{24,16},{1,25},{9,1},{17,9},{25,17},{2,26},{10... | collective-permute-start | bytes 98312 | tf_op jit(solution)/shard_map/ppermute | solution.py:254
  57.1 8.1 %collective-permute-start.14 = (f32[64,256]{1,0:T(8,128)S(1)}, f32[64,256]{1,0:T(8,128)S(1)}, u32[]{:S(2)}, u32[]{:S(2)}) collective-permute-start(f32[64,256]{1,0:T(8,128)S(1)} %get-tuple-element.66.old_lo_y), channel_id=1, source_target_pairs={{0,1},{1,2},{2,3},{3,4},{4,5},{5,6},{6,7},{7,0},{8,9},{9,10},{10,1... | collective-permute-start | bytes 196616 | tf_op jit(solution)/shard_map/ppermute | solution.py:257
  57.2 8.1 %collective-permute-start.15 = (f32[64,256]{1,0:T(8,128)S(1)}, f32[64,256]{1,0:T(8,128)S(1)}, u32[]{:S(2)}, u32[]{:S(2)}) collective-permute-start(f32[64,256]{1,0:T(8,128)S(1)} %get-tuple-element.67.old_hi_y), channel_id=1, source_target_pairs={{0,7},{1,0},{2,1},{3,2},{4,3},{5,4},{6,5},{7,6},{8,15},{9,8},{10,9... | collective-permute-start | bytes 196616 | tf_op jit(solution)/shard_map/ppermute | solution.py:258
  61.3 1.6 %collective-permute-start.12 = (f32[64,128]{1,0:T(8,128)S(1)}, f32[64,128]{1,0:T(8,128)S(1)}, u32[]{:S(2)}, u32[]{:S(2)}) collective-permute-start(f32[64,128]{1,0:T(8,128)S(1)} %get-tuple-element.64.old_lo_x), channel_id=1, source_target_pairs={{0,8},{8,16},{16,24},{24,0},{1,9},{9,17},{17,25},{25,1},{2,10},{10... | collective-permute-start | bytes 98312 | tf_op jit(solution)/shard_map/ppermute | solution.py:253
  61.9 3.3 %collective-permute-start.13 = (f32[64,128]{1,0:T(8,128)S(1)}, f32[64,128]{1,0:T(8,128)S(1)}, u32[]{:S(2)}, u32[]{:S(2)}) collective-permute-start(f32[64,128]{1,0:T(8,128)S(1)} %get-tuple-element.65.old_hi_x), channel_id=1, source_target_pairs={{0,24},{8,0},{16,8},{24,16},{1,25},{9,1},{17,9},{25,17},{2,26},{10... | collective-permute-start | bytes 98312 | tf_op jit(solution)/shard_map/ppermute | solution.py:254
  66.2 8.1 %collective-permute-start.18 = (f32[64,256]{1,0:T(8,128)S(1)}, f32[64,256]{1,0:T(8,128)S(1)}, u32[]{:S(2)}, u32[]{:S(2)}) collective-permute-start(f32[64,256]{1,0:T(8,128)S(1)} %get-tuple-element.71.old_lo_y), channel_id=1, source_target_pairs={{0,1},{1,2},{2,3},{3,4},{4,5},{5,6},{6,7},{7,0},{8,9},{9,10},{10,1... | collective-permute-start | bytes 196616 | tf_op jit(solution)/shard_map/ppermute | solution.py:257
  66.3 8.1 %collective-permute-start.19 = (f32[64,256]{1,0:T(8,128)S(1)}, f32[64,256]{1,0:T(8,128)S(1)}, u32[]{:S(2)}, u32[]{:S(2)}) collective-permute-start(f32[64,256]{1,0:T(8,128)S(1)} %get-tuple-element.72.old_hi_y), channel_id=1, source_target_pairs={{0,7},{1,0},{2,1},{3,2},{4,3},{5,4},{6,5},{7,6},{8,15},{9,8},{10,9... | collective-permute-start | bytes 196616 | tf_op jit(solution)/shard_map/ppermute | solution.py:258
  70.5 1.6 %collective-permute-start.16 = (f32[64,128]{1,0:T(8,128)S(1)}, f32[64,128]{1,0:T(8,128)S(1)}, u32[]{:S(2)}, u32[]{:S(2)}) collective-permute-start(f32[64,128]{1,0:T(8,128)S(1)} %get-tuple-element.69.old_lo_x), channel_id=1, source_target_pairs={{0,8},{8,16},{16,24},{24,0},{1,9},{9,17},{17,25},{25,1},{2,10},{10... | collective-permute-start | bytes 98312 | tf_op jit(solution)/shard_map/ppermute | solution.py:253
  71.0 3.3 %collective-permute-start.17 = (f32[64,128]{1,0:T(8,128)S(1)}, f32[64,128]{1,0:T(8,128)S(1)}, u32[]{:S(2)}, u32[]{:S(2)}) collective-permute-start(f32[64,128]{1,0:T(8,128)S(1)} %get-tuple-element.70.old_hi_x), channel_id=1, source_target_pairs={{0,24},{8,0},{16,8},{24,16},{1,25},{9,1},{17,9},{25,17},{2,26},{10... | collective-permute-start | bytes 98312 | tf_op jit(solution)/shard_map/ppermute | solution.py:254
  75.4 8.1 %collective-permute-start.22 = (f32[64,256]{1,0:T(8,128)S(1)}, f32[64,256]{1,0:T(8,128)S(1)}, u32[]{:S(2)}, u32[]{:S(2)}) collective-permute-start(f32[64,256]{1,0:T(8,128)S(1)} %get-tuple-element.76.old_lo_y), channel_id=1, source_target_pairs={{0,1},{1,2},{2,3},{3,4},{4,5},{5,6},{6,7},{7,0},{8,9},{9,10},{10,1... | collective-permute-start | bytes 196616 | tf_op jit(solution)/shard_map/ppermute | solution.py:257
  75.4 8.1 %collective-permute-start.23 = (f32[64,256]{1,0:T(8,128)S(1)}, f32[64,256]{1,0:T(8,128)S(1)}, u32[]{:S(2)}, u32[]{:S(2)}) collective-permute-start(f32[64,256]{1,0:T(8,128)S(1)} %get-tuple-element.77.old_hi_y), channel_id=1, source_target_pairs={{0,7},{1,0},{2,1},{3,2},{4,3},{5,4},{6,5},{7,6},{8,15},{9,8},{10,9... | collective-permute-start | bytes 196616 | tf_op jit(solution)/shard_map/ppermute | solution.py:258
  79.6 1.6 %collective-permute-start.20 = (f32[64,128]{1,0:T(8,128)S(1)}, f32[64,128]{1,0:T(8,128)S(1)}, u32[]{:S(2)}, u32[]{:S(2)}) collective-permute-start(f32[64,128]{1,0:T(8,128)S(1)} %get-tuple-element.74.old_lo_x), channel_id=1, source_target_pairs={{0,8},{8,16},{16,24},{24,0},{1,9},{9,17},{17,25},{25,1},{2,10},{10... | collective-permute-start | bytes 98312 | tf_op jit(solution)/shard_map/ppermute | solution.py:253
  80.2 3.3 %collective-permute-start.21 = (f32[64,128]{1,0:T(8,128)S(1)}, f32[64,128]{1,0:T(8,128)S(1)}, u32[]{:S(2)}, u32[]{:S(2)}) collective-permute-start(f32[64,128]{1,0:T(8,128)S(1)} %get-tuple-element.75.old_hi_x), channel_id=1, source_target_pairs={{0,24},{8,0},{16,8},{24,16},{1,25},{9,1},{17,9},{25,17},{2,26},{10... | collective-permute-start | bytes 98312 | tf_op jit(solution)/shard_map/ppermute | solution.py:254
  84.5 8.1 %collective-permute-start.26 = (f32[64,256]{1,0:T(8,128)S(1)}, f32[64,256]{1,0:T(8,128)S(1)}, u32[]{:S(2)}, u32[]{:S(2)}) collective-permute-start(f32[64,256]{1,0:T(8,128)S(1)} %get-tuple-element.81.old_lo_y), channel_id=1, source_target_pairs={{0,1},{1,2},{2,3},{3,4},{4,5},{5,6},{6,7},{7,0},{8,9},{9,10},{10,1... | collective-permute-start | bytes 196616 | tf_op jit(solution)/shard_map/ppermute | solution.py:257
  84.6 8.1 %collective-permute-start.27 = (f32[64,256]{1,0:T(8,128)S(1)}, f32[64,256]{1,0:T(8,128)S(1)}, u32[]{:S(2)}, u32[]{:S(2)}) collective-permute-start(f32[64,256]{1,0:T(8,128)S(1)} %get-tuple-element.82.old_hi_y), channel_id=1, source_target_pairs={{0,7},{1,0},{2,1},{3,2},{4,3},{5,4},{6,5},{7,6},{8,15},{9,8},{10,9... | collective-permute-start | bytes 196616 | tf_op jit(solution)/shard_map/ppermute | solution.py:258
  88.7 1.6 %collective-permute-start.24 = (f32[64,128]{1,0:T(8,128)S(1)}, f32[64,128]{1,0:T(8,128)S(1)}, u32[]{:S(2)}, u32[]{:S(2)}) collective-permute-start(f32[64,128]{1,0:T(8,128)S(1)} %get-tuple-element.79.old_lo_x), channel_id=1, source_target_pairs={{0,8},{8,16},{16,24},{24,0},{1,9},{9,17},{17,25},{25,1},{2,10},{10... | collective-permute-start | bytes 98312 | tf_op jit(solution)/shard_map/ppermute | solution.py:253
  89.3 3.3 %collective-permute-start.25 = (f32[64,128]{1,0:T(8,128)S(1)}, f32[64,128]{1,0:T(8,128)S(1)}, u32[]{:S(2)}, u32[]{:S(2)}) collective-permute-start(f32[64,128]{1,0:T(8,128)S(1)} %get-tuple-element.80.old_hi_x), channel_id=1, source_target_pairs={{0,24},{8,0},{16,8},{24,16},{1,25},{9,1},{17,9},{25,17},{2,26},{10... | collective-permute-start | bytes 98312 | tf_op jit(solution)/shard_map/ppermute | solution.py:254
  93.7 8.1 %collective-permute-start.30 = (f32[64,256]{1,0:T(8,128)S(1)}, f32[64,256]{1,0:T(8,128)S(1)}, u32[]{:S(2)}, u32[]{:S(2)}) collective-permute-start(f32[64,256]{1,0:T(8,128)S(1)} %get-tuple-element.86.old_lo_y), channel_id=1, source_target_pairs={{0,1},{1,2},{2,3},{3,4},{4,5},{5,6},{6,7},{7,0},{8,9},{9,10},{10,1... | collective-permute-start | bytes 196616 | tf_op jit(solution)/shard_map/ppermute | solution.py:257
  93.7 4.7 %copy-start.6 = (s32[4,2,2]{0,2,1:T(2,128)S(1)}, s32[4,2,2]{0,2,1:T(2,128)}, u32[]{:S(2)}) copy-start(s32[4,2,2]{0,2,1:T(2,128)} %param.14) | copy-start | bytes 196
  93.7 8.1 %collective-permute-start.31 = (f32[64,256]{1,0:T(8,128)S(1)}, f32[64,256]{1,0:T(8,128)S(1)}, u32[]{:S(2)}, u32[]{:S(2)}) collective-permute-start(f32[64,256]{1,0:T(8,128)S(1)} %get-tuple-element.87.old_hi_y), channel_id=1, source_target_pairs={{0,7},{1,0},{2,1},{3,2},{4,3},{5,4},{6,5},{7,6},{8,15},{9,8},{10,9... | collective-permute-start | bytes 196616 | tf_op jit(solution)/shard_map/ppermute | solution.py:258
  97.9 1.6 %collective-permute-start.28 = (f32[64,128]{1,0:T(8,128)S(1)}, f32[64,128]{1,0:T(8,128)S(1)}, u32[]{:S(2)}, u32[]{:S(2)}) collective-permute-start(f32[64,128]{1,0:T(8,128)S(1)} %get-tuple-element.84.old_lo_x), channel_id=1, source_target_pairs={{0,8},{8,16},{16,24},{24,0},{1,9},{9,17},{17,25},{25,1},{2,10},{10... | collective-permute-start | bytes 98312 | tf_op jit(solution)/shard_map/ppermute | solution.py:253
  98.4 3.3 %collective-permute-start.29 = (f32[64,128]{1,0:T(8,128)S(1)}, f32[64,128]{1,0:T(8,128)S(1)}, u32[]{:S(2)}, u32[]{:S(2)}) collective-permute-start(f32[64,128]{1,0:T(8,128)S(1)} %get-tuple-element.85.old_hi_x), channel_id=1, source_target_pairs={{0,24},{8,0},{16,8},{24,16},{1,25},{9,1},{17,9},{25,17},{2,26},{10... | collective-permute-start | bytes 98312 | tf_op jit(solution)/shard_map/ppermute | solution.py:254

commit v13 on v10

--- a/solution.py
+++ b/solution.py
@@ -275,14 +275,14 @@
     def to_lanes(values):
         return jnp.transpose(values.reshape(columns, P_SIZE, R), (1, 0, 2)).reshape(P_SIZE, columns * R)
 
-    start_state = to_lanes(pick(initial, 1))
+    face_row = jnp.transpose(face_blocks, (1, 0, 2)).reshape(P_SIZE, 6 * P_SIZE)
+    start_state, face_row = lax.optimization_barrier((to_lanes(pick(initial, 1)), face_row))
     first_sends = send_buffers(start_state, span_x)
     first_halos = trade(first_sends)
     by_colour = jnp.stack([pick(blocks, paint) for paint in (0, 1)]).reshape(count, P_SIZE, P_SIZE)
     inverse = block_inverses(by_colour, lanes_out=True)
     weight = jnp.where(neighbours == empty_slot, 0.0, strength * strong.astype(jnp.float32))
     member_inverse = [inverse[:, paint * columns * P_SIZE:(paint + 1) * columns * P_SIZE] for paint in (0, 1)]
-    face_row = jnp.transpose(face_blocks, (1, 0, 2)).reshape(P_SIZE, 6 * P_SIZE)
     member_target = [to_lanes(pick(forcing, paint)) for paint in (0, 1)]
     member_weight = [
         jnp.pad(jnp.repeat(pick(weight, paint, axis=3).reshape(6, columns), R, axis=1), ((0, 2), (0, 0)))

time: 103 us -> 104 us (level); the launches traced: 101 us -> 103 us
  starting transfers between devices: 41.2 us -> 42.6 us
    ppermute x8, starting transfers between devices: 6.78 us -> 8.21 us  [trade(): lax.ppermute(sends[0], 'gx', shift_pairs('gx', 1))]
    ppermute x8, starting transfers between devices: 0.39 us -> 1.63 us  [trade(): lax.ppermute(sends[2], 'gy', shift_pairs('gy', 1))]
    ppermute x8, starting transfers between devices: 33.4 us -> 32.2 us  [trade(): lax.ppermute(sends[3], 'gy', shift_pairs('gy', -1))]
    slice x3, local copies, waits for them, and re-layouts: 2.68 us -> 1.6 us  [pick(): high = lax.index_in_dim(values, 1, axis=axis, keepdims=False)]
    unnamed x18 -> x14, local copies, waits for them, and re-layouts: 2.14 us -> 1.62 us
where the time goes in v13:
time: 104 us; the launch traced here: 103 us
  starting transfers between devices  42.6 us (41%)
  Pallas kernels  25.5 us (25%)
  waiting for transfers between devices  21.3 us (20%)
  local copies, waits for them, and re-layouts  11.6 us (11%)
  other arithmetic  1.65 us (2%)
    ppermute x8, starting transfers between devices, trade(): lax.ppermute(sends[3], 'gy', shift_pairs('gy', -1))  32.2 us
    pallas_call x1, Pallas kernels, block_inverses(): pl.pallas_call(functools.partial(_gauss_jordan_kernel, n=n, nb=nb), out_s...  17.5 us
    ppermute x8, waiting for transfers between devices, trade(): lax.ppermute(sends[1], 'gx', shift_pairs('gx', -1))  13.9 us
    ppermute x8, starting transfers between devices, trade(): lax.ppermute(sends[0], 'gx', shift_pairs('gx', 1))  8.21 us
    pallas_call x8, Pallas kernels, half_sweep(): pl.pallas_call(functools.partial(_half_sweep_kernel, span_x=span_x), out_...  7.98 us
    ppermute x8, waiting for transfers between devices, trade(): lax.ppermute(sends[0], 'gx', shift_pairs('gx', 1))  5.61 us
  transfers between devices with their start and end apart: 32, of which 13 were waited for; matrix products, arithmetic and copies ran while one was open for 5% of the time, Pallas kernels for 17%

profile of v13, /device:TPU:1, one launch (start us, length us, event | category | flops | bytes accessed | tf_op | source)
XLA Modules:
  0.0 102.9 jit_solution(13521143052413462842)
XLA Ops:
  0.0 0.7 slice-done
  1.1 1.1 %copy.87 = f32[64,6,64]{2,1,0:T(8,128)S(1)} copy(f32[64,6,64]{2,0,1:T(8,128)} %bitcast.38) | data formatting | bytes 196608 | tf_op jit(solution)/shard_map/transpose | solution.py:278
  2.2 0.8 copy-done
  3.1 0.8 slice_reduce_fusion.2
  3.9 0.2 squeeze.37
  4.1 0.2 squeeze.36
  4.3 0.7 copy-done.1
  5.0 0.8 slice_reduce_fusion.4
  5.8 0.2 squeeze.33
  6.0 0.2 squeeze.32
  6.4 0.2 copy.86
  6.7 0.2 reshape.126
  7.0 2.6 %collective-permute-start = (f32[64,128]{1,0:T(8,128)S(1)}, f32[64,128]{1,0:T(8,128)S(1)}, u32[]{:S(2)}, u32[]{:S(2)}) collective-permute-start(f32[64,128]{1,0:T(8,128)S(1)} %reshape_squeeze.12.old_lo_x), channel_id=1, source_target_pairs={{0,8},{8,16},{16,24},{24,0},{1,9},{9,17},{17,25},{25,1},{2,10},{10... | collective-permute-start | bytes 98312 | tf_op jit(solution)/shard_map/ppermute | solution.py:246
  9.8 0.8 slice_reduce_fusion
  10.7 1.3 %collective-permute-start.2 = (f32[64,256]{1,0:T(8,128)S(1)}, f32[64,256]{1,0:T(8,128)S(1)}, u32[]{:S(2)}, u32[]{:S(2)}) collective-permute-start(f32[64,256]{1,0:T(8,128)S(1)} %reshape_squeeze.14.old_lo_y), channel_id=1, source_target_pairs={{0,1},{1,2},{2,3},{3,4},{4,5},{5,6},{6,7},{7,0},{8,9},{9,10},{10,1... | collective-permute-start | bytes 196616 | tf_op jit(solution)/shard_map/ppermute | solution.py:250
  12.1 3.1 %collective-permute-start.3 = (f32[64,256]{1,0:T(8,128)S(1)}, f32[64,256]{1,0:T(8,128)S(1)}, u32[]{:S(2)}, u32[]{:S(2)}) collective-permute-start(f32[64,256]{1,0:T(8,128)S(1)} %reshape_squeeze.15.old_hi_y), channel_id=1, source_target_pairs={{0,7},{1,0},{2,1},{3,2},{4,3},{5,4},{6,5},{7,6},{8,15},{9,8},{10,9... | collective-permute-start | bytes 196616 | tf_op jit(solution)/shard_map/ppermute | solution.py:251
  15.3 0.3 broadcast_select_fusion.1
  15.6 0.2 pad_maximum_fusion
  15.8 0.2 copy.90
  16.0 0.3 reshape.127
  16.4 0.3 copy.91
  16.7 0.2 copy.92.a_ref
  16.9 17.5 %shard_map.82 = f32[64,1024]{1,0:T(8,128)S(1)} custom-call(f32[64,1024]{1,0:T(8,128)S(1)} %copy.92.a_ref), custom_call_target="tpu_custom_call", output_to_operand_aliasing={{}: (0, {})} | custom-call | flops 8388608000 | bytes 524288 | tf_op jit(solution)/shard_map/pallas_call | solution.py:75
  34.4 0.2 copy.93
  34.6 0.4 copy.94
  34.9 0.2 reshape.130
  35.5 0.2 copy.96
  35.8 1.0 shard_map.83
  36.9 4.1 %collective-permute-start.7 = (f32[64,256]{1,0:T(8,128)S(1)}, f32[64,256]{1,0:T(8,128)S(1)}, u32[]{:S(2)}, u32[]{:S(2)}) collective-permute-start(f32[64,256]{1,0:T(8,128)S(1)} %get-tuple-element.58.old_hi_y), channel_id=1, source_target_pairs={{0,7},{1,0},{2,1},{3,2},{4,3},{5,4},{6,5},{7,6},{8,15},{9,8},{10,9... | collective-permute-start | bytes 196616 | tf_op jit(solution)/shard_map/ppermute | solution.py:251
  41.0 2.7 %collective-permute-start.4 = (f32[64,128]{1,0:T(8,128)S(1)}, f32[64,128]{1,0:T(8,128)S(1)}, u32[]{:S(2)}, u32[]{:S(2)}) collective-permute-start(f32[64,128]{1,0:T(8,128)S(1)} %get-tuple-element.55.old_lo_x), channel_id=1, source_target_pairs={{0,8},{8,16},{16,24},{24,0},{1,9},{9,17},{17,25},{25,1},{2,10},{10... | collective-permute-start | bytes 98312 | tf_op jit(solution)/shard_map/ppermute | solution.py:246
  44.0 0.2 copy.98
  44.2 0.5 collective-permute-done.4.lo_x_ref
  44.7 2.3 %collective-permute-done.5.hi_x_ref = f32[64,128]{1,0:T(8,128)S(1)} collective-permute-done((f32[64,128]{1,0:T(8,128)S(1)}, f32[64,128]{1,0:T(8,128)S(1)}, u32[]{:S(2)}, u32[]{:S(2)}) %collective-permute-start.5) | collective-permute-done | bytes 32800 | tf_op jit(solution)/shard_map/ppermute | solution.py:247
  47.1 1.0 shard_map.84
  48.1 4.1 %collective-permute-start.11 = (f32[64,256]{1,0:T(8,128)S(1)}, f32[64,256]{1,0:T(8,128)S(1)}, u32[]{:S(2)}, u32[]{:S(2)}) collective-permute-start(f32[64,256]{1,0:T(8,128)S(1)} %get-tuple-element.66.old_hi_y), channel_id=1, source_target_pairs={{0,7},{1,0},{2,1},{3,2},{4,3},{5,4},{6,5},{7,6},{8,15},{9,8},{10,9... | collective-permute-start | bytes 196616 | tf_op jit(solution)/shard_map/ppermute | solution.py:251
  52.3 0.6 collective-permute-start.8
  52.9 1.0 collective-permute-done.8.lo_x_ref
  53.9 2.3 %collective-permute-done.9.hi_x_ref = f32[64,128]{1,0:T(8,128)S(1)} collective-permute-done((f32[64,128]{1,0:T(8,128)S(1)}, f32[64,128]{1,0:T(8,128)S(1)}, u32[]{:S(2)}, u32[]{:S(2)}) %collective-permute-start.9) | collective-permute-done | bytes 32800 | tf_op jit(solution)/shard_map/ppermute | solution.py:247
  56.2 1.0 shard_map.85
  57.3 4.1 %collective-permute-start.15 = (f32[64,256]{1,0:T(8,128)S(1)}, f32[64,256]{1,0:T(8,128)S(1)}, u32[]{:S(2)}, u32[]{:S(2)}) collective-permute-start(f32[64,256]{1,0:T(8,128)S(1)} %get-tuple-element.71.old_hi_y), channel_id=1, source_target_pairs={{0,7},{1,0},{2,1},{3,2},{4,3},{5,4},{6,5},{7,6},{8,15},{9,8},{10,9... | collective-permute-start | bytes 196616 | tf_op jit(solution)/shard_map/ppermute | solution.py:251
  61.4 0.6 collective-permute-start.12
  62.0 1.0 collective-permute-done.12.lo_x_ref
  63.0 2.3 %collective-permute-done.13.hi_x_ref = f32[64,128]{1,0:T(8,128)S(1)} collective-permute-done((f32[64,128]{1,0:T(8,128)S(1)}, f32[64,128]{1,0:T(8,128)S(1)}, u32[]{:S(2)}, u32[]{:S(2)}) %collective-permute-start.13) | collective-permute-done | bytes 32800 | tf_op jit(solution)/shard_map/ppermute | solution.py:247
  65.3 1.0 shard_map.86
  66.4 4.1 %collective-permute-start.19 = (f32[64,256]{1,0:T(8,128)S(1)}, f32[64,256]{1,0:T(8,128)S(1)}, u32[]{:S(2)}, u32[]{:S(2)}) collective-permute-start(f32[64,256]{1,0:T(8,128)S(1)} %get-tuple-element.76.old_hi_y), channel_id=1, source_target_pairs={{0,7},{1,0},{2,1},{3,2},{4,3},{5,4},{6,5},{7,6},{8,15},{9,8},{10,9... | collective-permute-start | bytes 196616 | tf_op jit(solution)/shard_map/ppermute | solution.py:251
  70.6 0.6 collective-permute-start.16
  71.1 1.0 collective-permute-done.16.lo_x_ref
  72.2 2.3 %collective-permute-done.17.hi_x_ref = f32[64,128]{1,0:T(8,128)S(1)} collective-permute-done((f32[64,128]{1,0:T(8,128)S(1)}, f32[64,128]{1,0:T(8,128)S(1)}, u32[]{:S(2)}, u32[]{:S(2)}) %collective-permute-start.17) | collective-permute-done | bytes 32800 | tf_op jit(solution)/shard_map/ppermute | solution.py:247
  74.5 1.0 shard_map.87
  75.6 4.1 %collective-permute-start.23 = (f32[64,256]{1,0:T(8,128)S(1)}, f32[64,256]{1,0:T(8,128)S(1)}, u32[]{:S(2)}, u32[]{:S(2)}) collective-permute-start(f32[64,256]{1,0:T(8,128)S(1)} %get-tuple-element.81.old_hi_y), channel_id=1, source_target_pairs={{0,7},{1,0},{2,1},{3,2},{4,3},{5,4},{6,5},{7,6},{8,15},{9,8},{10,9... | collective-permute-start | bytes 196616 | tf_op jit(solution)/shard_map/ppermute | solution.py:251
  79.7 0.6 collective-permute-start.20
  80.3 1.0 collective-permute-done.20.lo_x_ref
  81.3 2.3 %collective-permute-done.21.hi_x_ref = f32[64,128]{1,0:T(8,128)S(1)} collective-permute-done((f32[64,128]{1,0:T(8,128)S(1)}, f32[64,128]{1,0:T(8,128)S(1)}, u32[]{:S(2)}, u32[]{:S(2)}) %collective-permute-start.21) | collective-permute-done | bytes 32800 | tf_op jit(solution)/shard_map/ppermute | solution.py:247
  83.6 1.0 shard_map.88
  84.7 4.1 %collective-permute-start.27 = (f32[64,256]{1,0:T(8,128)S(1)}, f32[64,256]{1,0:T(8,128)S(1)}, u32[]{:S(2)}, u32[]{:S(2)}) collective-permute-start(f32[64,256]{1,0:T(8,128)S(1)} %get-tuple-element.86.old_hi_y), channel_id=1, source_target_pairs={{0,7},{1,0},{2,1},{3,2},{4,3},{5,4},{6,5},{7,6},{8,15},{9,8},{10,9... | collective-permute-start | bytes 196616 | tf_op jit(solution)/shard_map/ppermute | solution.py:251
  88.8 0.6 collective-permute-start.24
  89.4 1.0 collective-permute-done.24.lo_x_ref
  90.4 2.3 %collective-permute-done.25.hi_x_ref = f32[64,128]{1,0:T(8,128)S(1)} collective-permute-done((f32[64,128]{1,0:T(8,128)S(1)}, f32[64,128]{1,0:T(8,128)S(1)}, u32[]{:S(2)}, u32[]{:S(2)}) %collective-permute-start.25) | collective-permute-done | bytes 32800 | tf_op jit(solution)/shard_map/ppermute | solution.py:247
  92.8 1.0 shard_map.89
  93.8 0.5 collective-permute-start.29
  94.3 4.2 %collective-permute-start.31 = (f32[64,256]{1,0:T(8,128)S(1)}, f32[64,256]{1,0:T(8,128)S(1)}, u32[]{:S(2)}, u32[]{:S(2)}) collective-permute-start(f32[64,256]{1,0:T(8,128)S(1)} %get-tuple-element.91.old_hi_y), channel_id=1, source_target_pairs={{0,7},{1,0},{2,1},{3,2},{4,3},{5,4},{6,5},{7,6},{8,15},{9,8},{10,9... | collective-permute-start | bytes 196616 | tf_op jit(solution)/shard_map/ppermute | solution.py:251
  99.0 1.7 %collective-permute-done.30.lo_y_ref = f32[64,256]{1,0:T(8,128)S(1)} collective-permute-done((f32[64,256]{1,0:T(8,128)S(1)}, f32[64,256]{1,0:T(8,128)S(1)}, u32[]{:S(2)}, u32[]{:S(2)}) %collective-permute-start.30) | collective-permute-done | bytes 65568 | tf_op jit(solution)/shard_map/ppermute | solution.py:250
  100.7 1.0 shard_map.90
  102.0 0.9 broadcast_select_fusion.2
  (83 shorter events, 3.4 us)
Async XLA Ops:
  0.0 0.7 slice-start
  2.1 1.0 copy-start
  4.1 1.0 copy-start.1
  7.0 28.7 %collective-permute-start = (f32[64,128]{1,0:T(8,128)S(1)}, f32[64,128]{1,0:T(8,128)S(1)}, u32[]{:S(2)}, u32[]{:S(2)}) collective-permute-start(f32[64,128]{1,0:T(8,128)S(1)} %reshape_squeeze.12.old_lo_x), channel_id=1, source_target_pairs={{0,8},{8,16},{16,24},{24,0},{1,9},{9,17},{17,25},{25,1},{2,10},{10... | collective-permute-start | bytes 98312 | tf_op jit(solution)/shard_map/ppermute | solution.py:246
  9.7 26.0 %collective-permute-start.1 = (f32[64,128]{1,0:T(8,128)S(1)}, f32[64,128]{1,0:T(8,128)S(1)}, u32[]{:S(2)}, u32[]{:S(2)}) collective-permute-start(f32[64,128]{1,0:T(8,128)S(1)} %reshape_squeeze.13.old_hi_x), channel_id=1, source_target_pairs={{0,24},{8,0},{16,8},{24,16},{1,25},{9,1},{17,9},{25,17},{2,26},{10... | collective-permute-start | bytes 98312 | tf_op jit(solution)/shard_map/ppermute | solution.py:247
  10.6 4.7 %copy-start.2 = (f32[4,2,2,4096]{3,2,1,0:T(2,128)S(1)}, f32[4,2,2,4096]{3,2,1,0:T(2,128)}, u32[]{:S(2)}) copy-start(f32[4,2,2,4096]{3,2,1,0:T(2,128)} %param.10) | copy-start | bytes 786436
  10.7 25.1 %collective-permute-start.2 = (f32[64,256]{1,0:T(8,128)S(1)}, f32[64,256]{1,0:T(8,128)S(1)}, u32[]{:S(2)}, u32[]{:S(2)}) collective-permute-start(f32[64,256]{1,0:T(8,128)S(1)} %reshape_squeeze.14.old_lo_y), channel_id=1, source_target_pairs={{0,1},{1,2},{2,3},{3,4},{4,5},{5,6},{6,7},{7,0},{8,9},{9,10},{10,1... | collective-permute-start | bytes 196616 | tf_op jit(solution)/shard_map/ppermute | solution.py:250
  12.0 3.3 %copy-start.3 = (s32[6,4,2,2]{0,3,2,1:T(2,128)S(1)}, s32[6,4,2,2]{0,3,2,1:T(2,128)}, u32[]{:S(2)}) copy-start(s32[6,4,2,2]{0,3,2,1:T(2,128)} %param.15) | copy-start | bytes 1156
  12.0 3.3 %copy-start.4 = (f32[6,4,2,2]{0,3,2,1:T(2,128)S(1)}, f32[6,4,2,2]{0,3,2,1:T(2,128)}, u32[]{:S(2)}) copy-start(f32[6,4,2,2]{0,3,2,1:T(2,128)} %param.12) | copy-start | bytes 1156
  12.0 3.3 %copy-start.5 = (s32[6,4,2,2]{0,3,2,1:T(2,128)S(1)}, s32[6,4,2,2]{0,3,2,1:T(2,128)}, u32[]{:S(2)}) copy-start(s32[6,4,2,2]{0,3,2,1:T(2,128)} %param.13) | copy-start | bytes 1156
  12.1 23.7 %collective-permute-start.3 = (f32[64,256]{1,0:T(8,128)S(1)}, f32[64,256]{1,0:T(8,128)S(1)}, u32[]{:S(2)}, u32[]{:S(2)}) collective-permute-start(f32[64,256]{1,0:T(8,128)S(1)} %reshape_squeeze.15.old_hi_y), channel_id=1, source_target_pairs={{0,7},{1,0},{2,1},{3,2},{4,3},{5,4},{6,5},{7,6},{8,15},{9,8},{10,9... | collective-permute-start | bytes 196616 | tf_op jit(solution)/shard_map/ppermute | solution.py:251
  36.8 10.2 %collective-permute-start.6 = (f32[64,256]{1,0:T(8,128)S(1)}, f32[64,256]{1,0:T(8,128)S(1)}, u32[]{:S(2)}, u32[]{:S(2)}) collective-permute-start(f32[64,256]{1,0:T(8,128)S(1)} %get-tuple-element.57.old_lo_y), channel_id=1, source_target_pairs={{0,1},{1,2},{2,3},{3,4},{4,5},{5,6},{6,7},{7,0},{8,9},{9,10},{10,1... | collective-permute-start | bytes 196616 | tf_op jit(solution)/shard_map/ppermute | solution.py:250
  36.9 10.2 %collective-permute-start.7 = (f32[64,256]{1,0:T(8,128)S(1)}, f32[64,256]{1,0:T(8,128)S(1)}, u32[]{:S(2)}, u32[]{:S(2)}) collective-permute-start(f32[64,256]{1,0:T(8,128)S(1)} %get-tuple-element.58.old_hi_y), channel_id=1, source_target_pairs={{0,7},{1,0},{2,1},{3,2},{4,3},{5,4},{6,5},{7,6},{8,15},{9,8},{10,9... | collective-permute-start | bytes 196616 | tf_op jit(solution)/shard_map/ppermute | solution.py:251
  41.0 3.7 %collective-permute-start.4 = (f32[64,128]{1,0:T(8,128)S(1)}, f32[64,128]{1,0:T(8,128)S(1)}, u32[]{:S(2)}, u32[]{:S(2)}) collective-permute-start(f32[64,128]{1,0:T(8,128)S(1)} %get-tuple-element.55.old_lo_x), channel_id=1, source_target_pairs={{0,8},{8,16},{16,24},{24,0},{1,9},{9,17},{17,25},{25,1},{2,10},{10... | collective-permute-start | bytes 98312 | tf_op jit(solution)/shard_map/ppermute | solution.py:246
  43.7 3.3 %collective-permute-start.5 = (f32[64,128]{1,0:T(8,128)S(1)}, f32[64,128]{1,0:T(8,128)S(1)}, u32[]{:S(2)}, u32[]{:S(2)}) collective-permute-start(f32[64,128]{1,0:T(8,128)S(1)} %get-tuple-element.56.old_hi_x), channel_id=1, source_target_pairs={{0,24},{8,0},{16,8},{24,16},{1,25},{9,1},{17,9},{25,17},{2,26},{10... | collective-permute-start | bytes 98312 | tf_op jit(solution)/shard_map/ppermute | solution.py:247
  48.1 8.1 %collective-permute-start.10 = (f32[64,256]{1,0:T(8,128)S(1)}, f32[64,256]{1,0:T(8,128)S(1)}, u32[]{:S(2)}, u32[]{:S(2)}) collective-permute-start(f32[64,256]{1,0:T(8,128)S(1)} %get-tuple-element.65.old_lo_y), channel_id=1, source_target_pairs={{0,1},{1,2},{2,3},{3,4},{4,5},{5,6},{6,7},{7,0},{8,9},{9,10},{10,1... | collective-permute-start | bytes 196616 | tf_op jit(solution)/shard_map/ppermute | solution.py:250
  48.1 8.1 %collective-permute-start.11 = (f32[64,256]{1,0:T(8,128)S(1)}, f32[64,256]{1,0:T(8,128)S(1)}, u32[]{:S(2)}, u32[]{:S(2)}) collective-permute-start(f32[64,256]{1,0:T(8,128)S(1)} %get-tuple-element.66.old_hi_y), channel_id=1, source_target_pairs={{0,7},{1,0},{2,1},{3,2},{4,3},{5,4},{6,5},{7,6},{8,15},{9,8},{10,9... | collective-permute-start | bytes 196616 | tf_op jit(solution)/shard_map/ppermute | solution.py:251
  52.3 1.6 %collective-permute-start.8 = (f32[64,128]{1,0:T(8,128)S(1)}, f32[64,128]{1,0:T(8,128)S(1)}, u32[]{:S(2)}, u32[]{:S(2)}) collective-permute-start(f32[64,128]{1,0:T(8,128)S(1)} %get-tuple-element.63.old_lo_x), channel_id=1, source_target_pairs={{0,8},{8,16},{16,24},{24,0},{1,9},{9,17},{17,25},{25,1},{2,10},{10... | collective-permute-start | bytes 98312 | tf_op jit(solution)/shard_map/ppermute | solution.py:246
  52.9 3.3 %collective-permute-start.9 = (f32[64,128]{1,0:T(8,128)S(1)}, f32[64,128]{1,0:T(8,128)S(1)}, u32[]{:S(2)}, u32[]{:S(2)}) collective-permute-start(f32[64,128]{1,0:T(8,128)S(1)} %get-tuple-element.64.old_hi_x), channel_id=1, source_target_pairs={{0,24},{8,0},{16,8},{24,16},{1,25},{9,1},{17,9},{25,17},{2,26},{10... | collective-permute-start | bytes 98312 | tf_op jit(solution)/shard_map/ppermute | solution.py:247
  57.2 8.1 %collective-permute-start.14 = (f32[64,256]{1,0:T(8,128)S(1)}, f32[64,256]{1,0:T(8,128)S(1)}, u32[]{:S(2)}, u32[]{:S(2)}) collective-permute-start(f32[64,256]{1,0:T(8,128)S(1)} %get-tuple-element.70.old_lo_y), channel_id=1, source_target_pairs={{0,1},{1,2},{2,3},{3,4},{4,5},{5,6},{6,7},{7,0},{8,9},{9,10},{10,1... | collective-permute-start | bytes 196616 | tf_op jit(solution)/shard_map/ppermute | solution.py:250
  57.3 8.1 %collective-permute-start.15 = (f32[64,256]{1,0:T(8,128)S(1)}, f32[64,256]{1,0:T(8,128)S(1)}, u32[]{:S(2)}, u32[]{:S(2)}) collective-permute-start(f32[64,256]{1,0:T(8,128)S(1)} %get-tuple-element.71.old_hi_y), channel_id=1, source_target_pairs={{0,7},{1,0},{2,1},{3,2},{4,3},{5,4},{6,5},{7,6},{8,15},{9,8},{10,9... | collective-permute-start | bytes 196616 | tf_op jit(solution)/shard_map/ppermute | solution.py:251
  61.4 1.6 %collective-permute-start.12 = (f32[64,128]{1,0:T(8,128)S(1)}, f32[64,128]{1,0:T(8,128)S(1)}, u32[]{:S(2)}, u32[]{:S(2)}) collective-permute-start(f32[64,128]{1,0:T(8,128)S(1)} %get-tuple-element.68.old_lo_x), channel_id=1, source_target_pairs={{0,8},{8,16},{16,24},{24,0},{1,9},{9,17},{17,25},{25,1},{2,10},{10... | collective-permute-start | bytes 98312 | tf_op jit(solution)/shard_map/ppermute | solution.py:246
  62.0 3.3 %collective-permute-start.13 = (f32[64,128]{1,0:T(8,128)S(1)}, f32[64,128]{1,0:T(8,128)S(1)}, u32[]{:S(2)}, u32[]{:S(2)}) collective-permute-start(f32[64,128]{1,0:T(8,128)S(1)} %get-tuple-element.69.old_hi_x), channel_id=1, source_target_pairs={{0,24},{8,0},{16,8},{24,16},{1,25},{9,1},{17,9},{25,17},{2,26},{10... | collective-permute-start | bytes 98312 | tf_op jit(solution)/shard_map/ppermute | solution.py:247
  66.3 8.1 %collective-permute-start.18 = (f32[64,256]{1,0:T(8,128)S(1)}, f32[64,256]{1,0:T(8,128)S(1)}, u32[]{:S(2)}, u32[]{:S(2)}) collective-permute-start(f32[64,256]{1,0:T(8,128)S(1)} %get-tuple-element.75.old_lo_y), channel_id=1, source_target_pairs={{0,1},{1,2},{2,3},{3,4},{4,5},{5,6},{6,7},{7,0},{8,9},{9,10},{10,1... | collective-permute-start | bytes 196616 | tf_op jit(solution)/shard_map/ppermute | solution.py:250
  66.4 8.1 %collective-permute-start.19 = (f32[64,256]{1,0:T(8,128)S(1)}, f32[64,256]{1,0:T(8,128)S(1)}, u32[]{:S(2)}, u32[]{:S(2)}) collective-permute-start(f32[64,256]{1,0:T(8,128)S(1)} %get-tuple-element.76.old_hi_y), channel_id=1, source_target_pairs={{0,7},{1,0},{2,1},{3,2},{4,3},{5,4},{6,5},{7,6},{8,15},{9,8},{10,9... | collective-permute-start | bytes 196616 | tf_op jit(solution)/shard_map/ppermute | solution.py:251
  70.6 1.6 %collective-permute-start.16 = (f32[64,128]{1,0:T(8,128)S(1)}, f32[64,128]{1,0:T(8,128)S(1)}, u32[]{:S(2)}, u32[]{:S(2)}) collective-permute-start(f32[64,128]{1,0:T(8,128)S(1)} %get-tuple-element.73.old_lo_x), channel_id=1, source_target_pairs={{0,8},{8,16},{16,24},{24,0},{1,9},{9,17},{17,25},{25,1},{2,10},{10... | collective-permute-start | bytes 98312 | tf_op jit(solution)/shard_map/ppermute | solution.py:246
  71.1 3.3 %collective-permute-start.17 = (f32[64,128]{1,0:T(8,128)S(1)}, f32[64,128]{1,0:T(8,128)S(1)}, u32[]{:S(2)}, u32[]{:S(2)}) collective-permute-start(f32[64,128]{1,0:T(8,128)S(1)} %get-tuple-element.74.old_hi_x), channel_id=1, source_target_pairs={{0,24},{8,0},{16,8},{24,16},{1,25},{9,1},{17,9},{25,17},{2,26},{10... | collective-permute-start | bytes 98312 | tf_op jit(solution)/shard_map/ppermute | solution.py:247
  75.5 8.1 %collective-permute-start.22 = (f32[64,256]{1,0:T(8,128)S(1)}, f32[64,256]{1,0:T(8,128)S(1)}, u32[]{:S(2)}, u32[]{:S(2)}) collective-permute-start(f32[64,256]{1,0:T(8,128)S(1)} %get-tuple-element.80.old_lo_y), channel_id=1, source_target_pairs={{0,1},{1,2},{2,3},{3,4},{4,5},{5,6},{6,7},{7,0},{8,9},{9,10},{10,1... | collective-permute-start | bytes 196616 | tf_op jit(solution)/shard_map/ppermute | solution.py:250
  75.6 8.1 %collective-permute-start.23 = (f32[64,256]{1,0:T(8,128)S(1)}, f32[64,256]{1,0:T(8,128)S(1)}, u32[]{:S(2)}, u32[]{:S(2)}) collective-permute-start(f32[64,256]{1,0:T(8,128)S(1)} %get-tuple-element.81.old_hi_y), channel_id=1, source_target_pairs={{0,7},{1,0},{2,1},{3,2},{4,3},{5,4},{6,5},{7,6},{8,15},{9,8},{10,9... | collective-permute-start | bytes 196616 | tf_op jit(solution)/shard_map/ppermute | solution.py:251
  79.7 1.6 %collective-permute-start.20 = (f32[64,128]{1,0:T(8,128)S(1)}, f32[64,128]{1,0:T(8,128)S(1)}, u32[]{:S(2)}, u32[]{:S(2)}) collective-permute-start(f32[64,128]{1,0:T(8,128)S(1)} %get-tuple-element.78.old_lo_x), channel_id=1, source_target_pairs={{0,8},{8,16},{16,24},{24,0},{1,9},{9,17},{17,25},{25,1},{2,10},{10... | collective-permute-start | bytes 98312 | tf_op jit(solution)/shard_map/ppermute | solution.py:246
  80.3 3.3 %collective-permute-start.21 = (f32[64,128]{1,0:T(8,128)S(1)}, f32[64,128]{1,0:T(8,128)S(1)}, u32[]{:S(2)}, u32[]{:S(2)}) collective-permute-start(f32[64,128]{1,0:T(8,128)S(1)} %get-tuple-element.79.old_hi_x), channel_id=1, source_target_pairs={{0,24},{8,0},{16,8},{24,16},{1,25},{9,1},{17,9},{25,17},{2,26},{10... | collective-permute-start | bytes 98312 | tf_op jit(solution)/shard_map/ppermute | solution.py:247
  84.6 8.1 %collective-permute-start.26 = (f32[64,256]{1,0:T(8,128)S(1)}, f32[64,256]{1,0:T(8,128)S(1)}, u32[]{:S(2)}, u32[]{:S(2)}) collective-permute-start(f32[64,256]{1,0:T(8,128)S(1)} %get-tuple-element.85.old_lo_y), channel_id=1, source_target_pairs={{0,1},{1,2},{2,3},{3,4},{4,5},{5,6},{6,7},{7,0},{8,9},{9,10},{10,1... | collective-permute-start | bytes 196616 | tf_op jit(solution)/shard_map/ppermute | solution.py:250
  84.7 8.1 %collective-permute-start.27 = (f32[64,256]{1,0:T(8,128)S(1)}, f32[64,256]{1,0:T(8,128)S(1)}, u32[]{:S(2)}, u32[]{:S(2)}) collective-permute-start(f32[64,256]{1,0:T(8,128)S(1)} %get-tuple-element.86.old_hi_y), channel_id=1, source_target_pairs={{0,7},{1,0},{2,1},{3,2},{4,3},{5,4},{6,5},{7,6},{8,15},{9,8},{10,9... | collective-permute-start | bytes 196616 | tf_op jit(solution)/shard_map/ppermute | solution.py:251
  88.8 1.6 %collective-permute-start.24 = (f32[64,128]{1,0:T(8,128)S(1)}, f32[64,128]{1,0:T(8,128)S(1)}, u32[]{:S(2)}, u32[]{:S(2)}) collective-permute-start(f32[64,128]{1,0:T(8,128)S(1)} %get-tuple-element.83.old_lo_x), channel_id=1, source_target_pairs={{0,8},{8,16},{16,24},{24,0},{1,9},{9,17},{17,25},{25,1},{2,10},{10... | collective-permute-start | bytes 98312 | tf_op jit(solution)/shard_map/ppermute | solution.py:246
  89.4 3.3 %collective-permute-start.25 = (f32[64,128]{1,0:T(8,128)S(1)}, f32[64,128]{1,0:T(8,128)S(1)}, u32[]{:S(2)}, u32[]{:S(2)}) collective-permute-start(f32[64,128]{1,0:T(8,128)S(1)} %get-tuple-element.84.old_hi_x), channel_id=1, source_target_pairs={{0,24},{8,0},{16,8},{24,16},{1,25},{9,1},{17,9},{25,17},{2,26},{10... | collective-permute-start | bytes 98312 | tf_op jit(solution)/shard_map/ppermute | solution.py:247
  93.8 5.2 %collective-permute-start.28 = (f32[64,128]{1,0:T(8,128)S(1)}, f32[64,128]{1,0:T(8,128)S(1)}, u32[]{:S(2)}, u32[]{:S(2)}) collective-permute-start(f32[64,128]{1,0:T(8,128)S(1)} %get-tuple-element.88.old_lo_x), channel_id=1, source_target_pairs={{0,8},{8,16},{16,24},{24,0},{1,9},{9,17},{17,25},{25,1},{2,10},{10... | collective-permute-start | bytes 98312 | tf_op jit(solution)/shard_map/ppermute | solution.py:246
  93.8 4.7 %copy-start.6 = (s32[4,2,2]{0,2,1:T(2,128)S(1)}, s32[4,2,2]{0,2,1:T(2,128)}, u32[]{:S(2)}) copy-start(s32[4,2,2]{0,2,1:T(2,128)} %param.14) | copy-start | bytes 196
  93.8 5.1 %collective-permute-start.29 = (f32[64,128]{1,0:T(8,128)S(1)}, f32[64,128]{1,0:T(8,128)S(1)}, u32[]{:S(2)}, u32[]{:S(2)}) collective-permute-start(f32[64,128]{1,0:T(8,128)S(1)} %get-tuple-element.89.old_hi_x), channel_id=1, source_target_pairs={{0,24},{8,0},{16,8},{24,16},{1,25},{9,1},{17,9},{25,17},{2,26},{10... | collective-permute-start | bytes 98312 | tf_op jit(solution)/shard_map/ppermute | solution.py:247
  94.3 6.3 %collective-permute-start.30 = (f32[64,256]{1,0:T(8,128)S(1)}, f32[64,256]{1,0:T(8,128)S(1)}, u32[]{:S(2)}, u32[]{:S(2)}) collective-permute-start(f32[64,256]{1,0:T(8,128)S(1)} %get-tuple-element.90.old_lo_y), channel_id=1, source_target_pairs={{0,1},{1,2},{2,3},{3,4},{4,5},{5,6},{6,7},{7,0},{8,9},{9,10},{10,1... | collective-permute-start | bytes 196616 | tf_op jit(solution)/shard_map/ppermute | solution.py:250
  94.3 6.3 %collective-permute-start.31 = (f32[64,256]{1,0:T(8,128)S(1)}, f32[64,256]{1,0:T(8,128)S(1)}, u32[]{:S(2)}, u32[]{:S(2)}) collective-permute-start(f32[64,256]{1,0:T(8,128)S(1)} %get-tuple-element.91.old_hi_y), channel_id=1, source_target_pairs={{0,7},{1,0},{2,1},{3,2},{4,3},{5,4},{6,5},{7,6},{8,15},{9,8},{10,9... | collective-permute-start | bytes 196616 | tf_op jit(solution)/shard_map/ppermute | solution.py:251
